TPU v7x, 128 devices: a whole 4x4x4 slice. The times are simulated.
128 devices in a mesh: row: 8 (over x, core), col: 16 (over y, z).
Axes of the slice: x: 4, y: 4, z: 4, core: 2. Of those that a mesh axis runs over, the one named last changes fastest.
Arguments:
- image: bfloat16 [768, 512, 384], P('row', 'col'), may hold values from -6 to 6
- depth_kernel: bfloat16 [7, 7, 384], replicated, may hold values from -0.875 to 0.875
- weight_in: bfloat16 [384, 1536], replicated, may hold values from -0.3125 to 0.3125
- weight_out: bfloat16 [1536, 384], replicated, may hold values from -0.15625 to 0.15625
- weight_down: bfloat16 [2, 2, 384, 768], replicated, may hold values from -0.15625 to 0.15625
- tissue_mask: int32 [96, 64], P('row', 'col'), may hold values from 0 to 1, as said below
- tile_counts: int32 [8, 16, 16], P('row'), may hold values from 0 to 3, as said below
- tile_owner: int32 [96, 64], P('row', 'col'), may hold values from -1 to 15, as said below
- tile_slot: int32 [96, 64], P('row', 'col'), may hold values from -1 to 17, as said below
- cotangent: bfloat16 [384, 256, 768], P('row', 'col'), may hold values from -6 to 6
Outputs:
- reduced: bfloat16 [384, 256, 768], P('row', 'col')
- grad_image: bfloat16 [768, 512, 384], P('row', 'col')
Inputs may be any that keep to these rules, and one draw needn't show every extreme that they name: `tissue_mask`: exactly 288 tiles of each row of devices have tissue; in each row of devices one device, drawn from the seed, is all tissue. `tile_counts`: counts[r, s, o] is the number of tissue tiles of device (r, s) with owner o; each owner receives exactly 18 tiles from its row of devices. `tile_owner`: -1 exactly on tiles without tissue; the tissue tiles of a row of devices, in order of device column and then row-major within a device, go to owners 0, 1, 2, ... in turn. `tile_slot`: -1 exactly on tiles without tissue; else the tile's place among its owner's 18 tiles, in the same order.
All inputs are finite; a program needn't handle non-finite values.
Results may differ from a plain program's by a relative error of at most 0.0057.
Values may be sent and summed in bfloat16 or wider, within the bound.
No kernel may reach another device: no remote copies, remote signals or barrier semaphores. Data moves between devices by JAX's collectives and lax.ppermute only.
A program may use at most 128 MiB of HBM per device.

v0:
```python
import jax
import jax.numpy as jnp
from jax import lax
from jax.sharding import PartitionSpec as P

KS = 7
LIVE_DEV = 18


EPSILON = 1e-06
ROOT_HALF = 0.7071067811865476
INV_ROOT_TAU = 0.3989422804014327


def with_halo(cells, sides, width):
    for axis, dim in sides:
        count = lax.axis_size(axis)
        ends = count - 1
        head = lax.slice_in_dim(cells, 0, width, axis=dim)
        tail = lax.slice_in_dim(cells, cells.shape[dim] - width, cells.shape[dim], axis=dim)
        cells = jnp.concatenate(
            [
                lax.ppermute(tail, axis, [(i, (i + 1) % count) for i in range(ends)]),
                cells,
                lax.ppermute(head, axis, [((i + 1) % count, i) for i in range(ends)]),
            ],
            axis=dim,
        )
    return cells


def gelu_exact(hidden):
    return 0.5 * hidden * (1.0 + jax.scipy.special.erf(hidden * ROOT_HALF))


def gelu_slope(hidden):
    return 0.5 * (
        1.0 + jax.scipy.special.erf(hidden * ROOT_HALF)
    ) + hidden * INV_ROOT_TAU * jnp.exp(-0.5 * hidden * hidden)


def depthwise(padded, kernel, height, breadth):
    reach = kernel.shape[0]
    total = jnp.zeros((height, breadth, padded.shape[2]), jnp.float32)
    for shift_r in range(reach):
        for shift_c in range(reach):
            window = padded[shift_r : shift_r + height, shift_c : shift_c + breadth, :].astype(
                jnp.float32
            )
            total = total + window * kernel[shift_r, shift_c, :].astype(jnp.float32)
    return total


def normalize(values):
    average = jnp.mean(values, axis=-1, keepdims=True)
    centered = values - average
    inv_std = lax.rsqrt(jnp.mean(centered * centered, axis=-1, keepdims=True) + EPSILON)
    return (centered * inv_std, inv_std)


def normalize_back(gradient, normed, inv_std):
    return inv_std * (
        gradient
        - jnp.mean(gradient, axis=-1, keepdims=True)
        - normed * jnp.mean(gradient * normed, axis=-1, keepdims=True)
    )


def to_tiles(field, tile_side):
    height, breadth, channels = field.shape
    blocks = field.reshape(
        height // tile_side, tile_side, breadth // tile_side, tile_side, channels
    )
    return blocks.transpose(0, 2, 1, 3, 4).reshape(
        height // tile_side * (breadth // tile_side), tile_side * tile_side * channels
    )


def from_tiles(tiles, height, breadth, tile_side, channels):
    blocks = tiles.reshape(
        height // tile_side, breadth // tile_side, tile_side, tile_side, channels
    )
    return blocks.transpose(0, 2, 1, 3, 4).reshape(height, breadth, channels)


def to_patches(field):
    height, breadth, channels = field.shape
    return (
        field.reshape(height // 2, 2, breadth // 2, 2, channels)
        .transpose(0, 2, 1, 3, 4)
        .reshape(height // 2 * (breadth // 2), 4 * channels)
    )


def from_patches(patches, height, breadth, channels):
    return (
        patches.reshape(height // 2, breadth // 2, 2, 2, channels)
        .transpose(0, 2, 1, 3, 4)
        .reshape(height, breadth, channels)
    )


def times_transposed(left, right):
    return lax.dot_general(
        left, right, (((1,), (1,)), ((), ())), preferred_element_type=jnp.float32
    )


def select_rows(selector, source):
    return jnp.dot(selector, source, preferred_element_type=jnp.float32).astype(jnp.bfloat16)


def return_rows(selector, source):
    return lax.dot_general(
        selector, source, (((0,), (0,)), ((), ())), preferred_element_type=jnp.float32
    )


def branch_start(owned, channels, weight_in):
    normed, inv_std = normalize(owned.reshape(-1, channels).astype(jnp.float32))
    hidden = jnp.dot(normed.astype(jnp.bfloat16), weight_in, preferred_element_type=jnp.float32)
    return (normed, inv_std, hidden)


def on_device(
    image,
    depth_kernel,
    weight_in,
    weight_out,
    weight_down,
    tissue_mask,
    tile_counts,
    tile_owner,
    tile_slot,
    cotangent,
):
    height, breadth, channels = image.shape
    tile_side = height // tissue_mask.shape[0]
    outputs = weight_down.shape[3]
    reach = KS // 2
    peer_count = lax.axis_size("col")
    my_column = lax.axis_index("col")
    tiles_dev = tissue_mask.shape[0] * tissue_mask.shape[1]
    capacity = tiles_dev // peer_count
    tile_width = tile_side * tile_side * channels
    slot_count = peer_count * capacity
    count_table = tile_counts[0]
    before = jnp.cumsum(count_table, axis=0) - count_table
    column_ids = jnp.arange(peer_count, dtype=jnp.int32)
    own_column = column_ids == my_column
    my_bases = jnp.sum(jnp.where(own_column[:, None], before, 0), axis=0)
    in_bases = jnp.sum(jnp.where(own_column[None, :], before, 0), axis=1)
    in_counts = jnp.sum(jnp.where(own_column[None, :], count_table, 0), axis=1)
    owner_flat = tile_owner.reshape(-1)
    slot_flat = tile_slot.reshape(-1)
    owner_hits = owner_flat[:, None] == column_ids[None, :]
    send_rank = slot_flat - jnp.sum(jnp.where(owner_hits, my_bases[None, :], 0), axis=1)
    target = owner_flat * capacity + send_rank
    usable = (owner_flat >= 0) & (send_rank >= 0) & (send_rank < capacity)
    slot_ids = jnp.arange(slot_count, dtype=jnp.int32)
    packer = ((slot_ids[:, None] == target[None, :]) & usable[None, :]).astype(jnp.bfloat16)
    arrival_rank = slot_ids % capacity
    source_hits = (slot_ids // capacity)[:, None] == column_ids[None, :]
    arrival_base = jnp.sum(jnp.where(source_hits, in_bases[None, :], 0), axis=1)
    arrival_count = jnp.sum(jnp.where(source_hits, in_counts[None, :], 0), axis=1)
    position = arrival_base + arrival_rank
    filled = arrival_rank < arrival_count
    place_ids = jnp.arange(LIVE_DEV, dtype=jnp.int32)
    placer = ((place_ids[:, None] == position[None, :]) & filled[None, :]).astype(jnp.bfloat16)
    mask_column = tissue_mask.reshape(-1, 1).astype(jnp.float32)
    padded = with_halo(image, (("row", 0), ("col", 1)), reach)
    mixed = depthwise(padded, depth_kernel, height, breadth).astype(jnp.bfloat16)
    outgoing = select_rows(packer, to_tiles(mixed, tile_side)).reshape(
        peer_count, capacity, tile_width
    )
    arrived = lax.all_to_all(outgoing, "col", split_axis=0, concat_axis=0, tiled=True)
    owned = select_rows(placer, arrived.reshape(slot_count, tile_width))
    normed, inv_std, hidden = branch_start(owned, channels, weight_in)
    activated = gelu_exact(hidden).astype(jnp.bfloat16)
    branch = jnp.dot(activated, weight_out, preferred_element_type=jnp.float32).astype(jnp.bfloat16)
    homeward = return_rows(placer, branch.reshape(LIVE_DEV, tile_width)).astype(jnp.bfloat16)
    returned = lax.all_to_all(
        homeward.reshape(peer_count, capacity, tile_width),
        "col",
        split_axis=0,
        concat_axis=0,
        tiled=True,
    )
    branch_tiles = return_rows(packer, returned.reshape(slot_count, tile_width)) * mask_column
    summed = (
        image.astype(jnp.float32) + from_tiles(branch_tiles, height, breadth, tile_side, channels)
    ).astype(jnp.bfloat16)
    down_normed, down_inv = normalize(summed.astype(jnp.float32))
    weight_flat = weight_down.reshape(4 * channels, outputs)
    reduced = jnp.dot(
        to_patches(down_normed.astype(jnp.bfloat16)),
        weight_flat,
        preferred_element_type=jnp.float32,
    )
    reduced = reduced.astype(jnp.bfloat16).reshape(height // 2, breadth // 2, outputs)
    grad_patches = times_transposed(cotangent.reshape(-1, outputs), weight_flat)
    grad_normed = from_patches(grad_patches, height, breadth, channels)
    grad_summed = normalize_back(grad_normed, down_normed, down_inv).astype(jnp.bfloat16)
    grad_out = select_rows(packer, to_tiles(grad_summed, tile_side)).reshape(
        peer_count, capacity, tile_width
    )
    grad_in, resent = (
        lax.all_to_all(grad_out, "col", split_axis=0, concat_axis=0, tiled=True),
        lax.all_to_all(outgoing, "col", split_axis=0, concat_axis=0, tiled=True),
    )
    again_owned = select_rows(placer, resent.reshape(slot_count, tile_width))
    normed, inv_std, hidden = branch_start(again_owned, channels, weight_in)
    grad_owned = select_rows(placer, grad_in.reshape(slot_count, tile_width)).reshape(-1, channels)
    grad_hidden = (times_transposed(grad_owned, weight_out) * gelu_slope(hidden)).astype(
        jnp.bfloat16
    )
    grad_norm_in = times_transposed(grad_hidden, weight_in)
    grad_owned_mixed = normalize_back(grad_norm_in, normed, inv_std).astype(jnp.bfloat16)
    grad_homeward = return_rows(placer, grad_owned_mixed.reshape(LIVE_DEV, tile_width)).astype(
        jnp.bfloat16
    )
    grad_returned = lax.all_to_all(
        grad_homeward.reshape(peer_count, capacity, tile_width),
        "col",
        split_axis=0,
        concat_axis=0,
        tiled=True,
    )
    grad_tiles = (
        return_rows(packer, grad_returned.reshape(slot_count, tile_width)) * mask_column
    ).astype(jnp.bfloat16)
    grad_mixed = from_tiles(grad_tiles, height, breadth, tile_side, channels)
    grad_padded = with_halo(grad_mixed, (("row", 0), ("col", 1)), reach)
    grad_image = (
        grad_summed.astype(jnp.float32)
        + depthwise(grad_padded, depth_kernel[::-1, ::-1, :], height, breadth)
    ).astype(jnp.bfloat16)
    return (reduced, grad_image)


def solution(mesh):
    in_specs = (
        P("row", "col", None),
        P(),
        P(),
        P(),
        P(),
        P("row", "col"),
        P("row", None, None),
        P("row", "col"),
        P("row", "col"),
        P("row", "col", None),
    )
    out_specs = (P("row", "col", None), P("row", "col", None))
    return jax.shard_map(
        on_device, mesh=mesh, in_specs=in_specs, out_specs=out_specs, check_vma=False
    )
```

profile of v0, /device:TPU:1, one launch (start us, length us, event | category | flops | bytes accessed | tf_op | source)
XLA Modules:
  0.0 509.8 jit_solution(17493525063692882408)
XLA Ops:
  1.7 4.5 collective-permute-start
  6.2 1.9 collective-permute-start.1
  15.5 4.6 constant_dynamic-update-slice_fusion.3
  20.8 1.5 copy-done.7
  22.5 3.6 collective-permute-start.2
  27.4 1.6 convert_reduce_fusion.47
  29.4 2.4 collective-permute-done.2
  31.8 4.1 collective-permute-done.3
  36.3 73.7 %fusion.42 = bf16[96,32,384]{2,1,0:T(8,128)(2,1)} fusion(bf16[96,32,384]{2,1,0:T(8,128)(2,1)} %param.10, bf16[102,3,384]{2,1,0:T(4,128)(2,1)S(1)} %collective-permute-done.3, bf16[102,3,384]{2,1,0:T(4,128)(2,1)S(1)} %collective-permute-done.2, bf16[102,32,384]{2,1,0:T(8,128)(2,1)} %copy-done.7, bf16[99,32,384]{2,1,0:T(8,128)(2,1)} %get-tuple-element.77, ...), kind=kLoop, calls=%fused_computation.99 | loop fusion | flops 322043904 | bytes 21926400 | tf_op jit(solution)/shard_map/convert_element_type | solution.py:172
  110.0 3.5 copy.80
  113.5 4.4 reshape.220
  117.9 3.9 convolution_convert_fusion.3
  121.8 3.7 reshape.221
  125.5 8.2 %all-to-all-start = ((bf16[16,3,24576]{2,1,0:T(4,128)(2,1)}), bf16[16,3,24576]{2,1,0:T(4,128)(2,1)}, u32[]{:S(2)}, u32[]{:S(2)}) async-start(bf16[16,3,24576]{2,1,0:T(4,128)(2,1)} %reshape.221), calls=%async_computation | async-start | bytes 6291456 | tf_op jit(solution)/shard_map/all_to_all | solution.py:176
  133.8 42.8 %all-to-all-done = bf16[16,3,24576]{2,1,0:T(4,128)(2,1)} async-done(((bf16[16,3,24576]{2,1,0:T(4,128)(2,1)}), bf16[16,3,24576]{2,1,0:T(4,128)(2,1)}, u32[]{:S(2)}, u32[]{:S(2)}) %all-to-all-start) | async-done | bytes 2359328 | tf_op jit(solution)/shard_map/all_to_all | solution.py:176
  176.6 4.4 reshape.222
  181.0 3.5 fusion.1
  184.5 2.9 reshape.292
  187.5 2.9 copy.59
  190.3 1.7 reduce_sum.140
  192.1 1.7 multiply_reduce_fusion.1
  193.8 3.6 fusion.98
  197.4 2.9 copy-done.6
  200.3 3.3 fusion.45
  203.6 1.7 reshape.223
  205.3 2.9 convolution_convert_fusion.2
  208.2 3.8 reshape.224
  212.0 9.9 %all-to-all-start.1 = ((bf16[16,3,24576]{2,1,0:T(4,128)(2,1)}), bf16[16,3,24576]{2,1,0:T(4,128)(2,1)}, u32[]{:S(2)}, u32[]{:S(2)}) async-start(bf16[16,3,24576]{2,1,0:T(4,128)(2,1)} %reshape.224), calls=%async_computation.1 | async-start | bytes 6291456 | tf_op jit(solution)/shard_map/all_to_all | solution.py:182
  222.1 3.4 fusion.139
  225.6 4.7 copy.63
  230.2 6.9 %reshape.232 = f32[96,32,384]{2,1,0:T(8,128)} reshape(f32[48,2,16,2,384]{4,3,2,1,0:T(2,128)} %copy.63) | data formatting | bytes 9437184 | tf_op jit(solution)/shard_map/reshape | solution.py:99
  238.3 24.2 %all-to-all-done.1 = bf16[16,3,24576]{2,1,0:T(4,128)(2,1)} async-done(((bf16[16,3,24576]{2,1,0:T(4,128)(2,1)}), bf16[16,3,24576]{2,1,0:T(4,128)(2,1)}, u32[]{:S(2)}, u32[]{:S(2)}) %all-to-all-start.1) | async-done | bytes 2359328 | tf_op jit(solution)/shard_map/all_to_all | solution.py:182
  262.5 4.4 reshape.225
  266.9 2.5 convolution_multiply_fusion.1
  272.6 1.4 fusion.15
  274.1 1.5 fusion.11
  275.6 3.5 fusion.14
  280.4 1.8 copy.78
  282.2 4.5 reshape.234
  286.8 3.8 convolution_convert_fusion.1
  290.6 3.8 reshape.235
  294.4 47.6 %all_to_all.21 = bf16[16,3,24576]{2,1,0:T(4,128)(2,1)} all-to-all(bf16[16,3,24576]{2,1,0:T(4,128)(2,1)} %reshape.235), channel_id=1, replica_groups=mesh['row'=8,'col'=16] {'col'}, dimensions={0} | all-to-all | bytes 4718592 | tf_op jit(solution)/shard_map/all_to_all | solution.py:208
  342.0 4.5 reshape.236
  346.5 2.1 convolution_convert_fusion.4
  348.6 1.4 reshape.237
  350.0 10.0 %fusion.134 = (f32[1152]{0:T(1024)S(1)}, f32[1152]{0:T(1024)S(1)}, f32[1152,384]{0,1:T(8,128)}) fusion(f32[1152]{0:T(1024)S(1)} %add_rsqrt_fusion.1, f32[1152,384]{0,1:T(8,128)} %copy.59, f32[1152]{0:T(1024)S(1)} %broadcast_multiply_fusion.5, bf16[384,1536]{1,0:T(8,128)(2,1)} %param.12, bf16[1152,384]{1,0:T(8,128)(2,1)} %reshape.237, ...), kind=kOutput, calls=%fused_computation.319 | convolution fusion | flops 2737813504 | bytes 13879296 | tf_op jit(solution)/shard_map/dot_general | solution.py:104
  360.0 2.4 multiply_convert_fusion.4
  363.7 1.7 reshape.238
  365.4 2.9 convolution_convert_fusion
  368.4 3.7 reshape.239
  372.1 40.8 %all_to_all.22 = bf16[16,3,24576]{2,1,0:T(4,128)(2,1)} all-to-all(bf16[16,3,24576]{2,1,0:T(4,128)(2,1)} %reshape.239), channel_id=1, replica_groups=mesh['row'=8,'col'=16] {'col'}, dimensions={0} | all-to-all | bytes 4718592 | tf_op jit(solution)/shard_map/all_to_all | solution.py:222
  412.9 4.4 reshape.240
  417.3 2.5 fusion
  422.0 1.9 collective-permute-start.4
  424.0 5.8 %collective-permute-start.5 = (bf16[3,32,384]{2,1,0:T(8,128)(2,1)S(1)}, bf16[3,32,384]{2,1,0:T(8,128)(2,1)S(1)}, u32[]{:S(2)}, u32[]{:S(2)}) collective-permute-start(bf16[3,32,384]{2,1,0:T(8,128)(2,1)S(1)} %get-tuple-element.69), channel_id=1, source_target_pairs={{16,0},{32,16},{48,32},{64,48},{80,64},{96,80},{112,96},{17,1},{33... | collective-permute-start | bytes 221192 | tf_op jit(solution)/shard_map/ppermute | solution.py:25
  429.8 5.9 %reshape.228 = bf16[48,2,16,2,384]{4,3,2,1,0:T(2,128)(2,1)} reshape(bf16[96,32,384]{2,1,0:T(8,128)(2,1)} %get-tuple-element.67) | data formatting | bytes 4718592 | tf_op jit(solution)/shard_map/reshape | solution.py:89
  435.7 5.1 copy.79
  440.8 6.3 %reshape.229 = bf16[768,1536]{1,0:T(8,128)(2,1)} reshape(bf16[48,16,2,2,384]{4,3,2,1,0:T(2,128)(2,1)} %bitcast.80) | data formatting | bytes 4718592 | tf_op jit(solution)/shard_map/reshape | solution.py:91
  447.1 1.5 pad_maximum_fusion.7
  448.6 2.2 collective-permute-start.6
  452.1 4.8 convolution_convert_fusion.6
  457.9 4.1 collective-permute-done.7
  462.0 2.1 maximum_maximum_fusion
  464.5 45.2 %add_convert_fusion = bf16[96,32,384]{2,1,0:T(8,128)(2,1)} fusion(bf16[96,32,384]{2,1,0:T(8,128)(2,1)S(1)} %bitcast.72, bf16[96,32,384]{2,1,0:T(8,128)(2,1)S(1)} %copy-done.5, bf16[3,32,384]{2,1,0:T(8,128)(2,1)S(1)} %collective-permute-done.5, bf16[3,32,384]{2,1,0:T(8,128)(2,1)S(1)} %collective-permute-done.4, ...), kind=kLoop, calls=%fused_computation.98 | loop fusion | flops 182845440 | bytes 106391040 | tf_op jit(solution)/shard_map/convert_element_type | solution.py:237
  (234 shorter events, 22.4 us)
Async XLA Ops:
  0.6 221.5 %copy-start = (bf16[2,2,384,768]{3,2,1,0:T(8,128)(2,1)S(1)}, bf16[2,2,384,768]{3,2,1,0:T(8,128)(2,1)}, u32[]{:S(2)}) copy-start(bf16[2,2,384,768]{3,2,1,0:T(8,128)(2,1)} %param.14) | copy-start | bytes 7077892
  1.7 13.1 %collective-permute-start = (bf16[3,32,384]{2,1,0:T(8,128)(2,1)S(1)}, bf16[3,32,384]{2,1,0:T(8,128)(2,1)S(1)}, u32[]{:S(2)}, u32[]{:S(2)}) collective-permute-start(bf16[3,32,384]{2,1,0:T(8,128)(2,1)S(1)} %get-tuple-element.74), channel_id=1, source_target_pairs={{0,16},{16,32},{32,48},{48,64},{64,80},{80,96},{96,112},{1,17},{17... | collective-permute-start | bytes 221192 | tf_op jit(solution)/shard_map/ppermute | solution.py:23
  6.2 13.9 %collective-permute-start.1 = (bf16[3,32,384]{2,1,0:T(8,128)(2,1)S(1)}, bf16[3,32,384]{2,1,0:T(8,128)(2,1)S(1)}, u32[]{:S(2)}, u32[]{:S(2)}) collective-permute-start(bf16[3,32,384]{2,1,0:T(8,128)(2,1)S(1)} %get-tuple-element.73), channel_id=1, source_target_pairs={{16,0},{32,16},{48,32},{64,48},{80,64},{96,80},{112,96},{17,1},{33... | collective-permute-start | bytes 221192 | tf_op jit(solution)/shard_map/ppermute | solution.py:25
  9.3 26.6 %copy-start.9 = (f32[384]{0:T(512)}, f32[384]{0:T(512)S(1)}, u32[]{:S(2)}) copy-start(f32[384]{0:T(512)S(1)} %get-tuple-element.23) | copy-start | bytes 4612
  9.3 26.6 %copy-start.11 = (f32[384]{0:T(512)}, f32[384]{0:T(512)S(1)}, u32[]{:S(2)}) copy-start(f32[384]{0:T(512)S(1)} %get-tuple-element.24) | copy-start | bytes 4612
  9.3 26.6 %copy-start.13 = (f32[384]{0:T(512)}, f32[384]{0:T(512)S(1)}, u32[]{:S(2)}) copy-start(f32[384]{0:T(512)S(1)} %get-tuple-element.25) | copy-start | bytes 4612
  9.3 26.6 %copy-start.15 = (f32[384]{0:T(512)}, f32[384]{0:T(512)S(1)}, u32[]{:S(2)}) copy-start(f32[384]{0:T(512)S(1)} %get-tuple-element.26) | copy-start | bytes 4612
  9.3 26.6 %copy-start.17 = (f32[384]{0:T(512)}, f32[384]{0:T(512)S(1)}, u32[]{:S(2)}) copy-start(f32[384]{0:T(512)S(1)} %get-tuple-element.27) | copy-start | bytes 4612
  9.3 26.6 %copy-start.19 = (f32[384]{0:T(512)}, f32[384]{0:T(512)S(1)}, u32[]{:S(2)}) copy-start(f32[384]{0:T(512)S(1)} %get-tuple-element.28) | copy-start | bytes 4612
  9.4 26.6 %copy-start.21 = (f32[384]{0:T(512)}, f32[384]{0:T(512)S(1)}, u32[]{:S(2)}) copy-start(f32[384]{0:T(512)S(1)} %get-tuple-element.29) | copy-start | bytes 4612
  9.4 26.6 %copy-start.23 = (f32[384]{0:T(512)}, f32[384]{0:T(512)S(1)}, u32[]{:S(2)}) copy-start(f32[384]{0:T(512)S(1)} %get-tuple-element.30) | copy-start | bytes 4612
  9.4 26.6 %copy-start.25 = (f32[384]{0:T(512)}, f32[384]{0:T(512)S(1)}, u32[]{:S(2)}) copy-start(f32[384]{0:T(512)S(1)} %get-tuple-element.31) | copy-start | bytes 4612
  9.4 26.6 %copy-start.27 = (f32[384]{0:T(512)}, f32[384]{0:T(512)S(1)}, u32[]{:S(2)}) copy-start(f32[384]{0:T(512)S(1)} %get-tuple-element.32) | copy-start | bytes 4612
  9.4 26.6 %copy-start.29 = (f32[384]{0:T(512)}, f32[384]{0:T(512)S(1)}, u32[]{:S(2)}) copy-start(f32[384]{0:T(512)S(1)} %get-tuple-element.33) | copy-start | bytes 4612
  9.4 26.6 %copy-start.31 = (f32[384]{0:T(512)}, f32[384]{0:T(512)S(1)}, u32[]{:S(2)}) copy-start(f32[384]{0:T(512)S(1)} %get-tuple-element.34) | copy-start | bytes 4612
  9.4 26.6 %copy-start.33 = (f32[384]{0:T(512)}, f32[384]{0:T(512)S(1)}, u32[]{:S(2)}) copy-start(f32[384]{0:T(512)S(1)} %get-tuple-element.35) | copy-start | bytes 4612
  9.4 26.6 %copy-start.35 = (f32[384]{0:T(512)}, f32[384]{0:T(512)S(1)}, u32[]{:S(2)}) copy-start(f32[384]{0:T(512)S(1)} %get-tuple-element.36) | copy-start | bytes 4612
  9.4 26.6 %copy-start.37 = (f32[384]{0:T(512)}, f32[384]{0:T(512)S(1)}, u32[]{:S(2)}) copy-start(f32[384]{0:T(512)S(1)} %get-tuple-element.37) | copy-start | bytes 4612
  9.4 26.6 %copy-start.39 = (f32[384]{0:T(512)}, f32[384]{0:T(512)S(1)}, u32[]{:S(2)}) copy-start(f32[384]{0:T(512)S(1)} %get-tuple-element.38) | copy-start | bytes 4612
  9.5 26.6 %copy-start.41 = (f32[384]{0:T(512)}, f32[384]{0:T(512)S(1)}, u32[]{:S(2)}) copy-start(f32[384]{0:T(512)S(1)} %get-tuple-element.39) | copy-start | bytes 4612
  9.5 26.6 %copy-start.43 = (f32[384]{0:T(512)}, f32[384]{0:T(512)S(1)}, u32[]{:S(2)}) copy-start(f32[384]{0:T(512)S(1)} %get-tuple-element.40) | copy-start | bytes 4612
  9.5 26.6 %copy-start.45 = (f32[384]{0:T(512)}, f32[384]{0:T(512)S(1)}, u32[]{:S(2)}) copy-start(f32[384]{0:T(512)S(1)} %get-tuple-element.41) | copy-start | bytes 4612
  14.7 21.4 %copy-start.47 = (f32[384]{0:T(512)}, f32[384]{0:T(512)S(1)}, u32[]{:S(2)}) copy-start(f32[384]{0:T(512)S(1)} %get-tuple-element.4) | copy-start | bytes 4612
  14.7 21.4 %copy-start.49 = (f32[384]{0:T(512)}, f32[384]{0:T(512)S(1)}, u32[]{:S(2)}) copy-start(f32[384]{0:T(512)S(1)} %get-tuple-element.5) | copy-start | bytes 4612
  14.7 21.4 %copy-start.51 = (f32[384]{0:T(512)}, f32[384]{0:T(512)S(1)}, u32[]{:S(2)}) copy-start(f32[384]{0:T(512)S(1)} %get-tuple-element.6) | copy-start | bytes 4612
  14.7 21.4 %copy-start.53 = (f32[384]{0:T(512)}, f32[384]{0:T(512)S(1)}, u32[]{:S(2)}) copy-start(f32[384]{0:T(512)S(1)} %get-tuple-element.7) | copy-start | bytes 4612
  14.7 21.4 %copy-start.55 = (f32[384]{0:T(512)}, f32[384]{0:T(512)S(1)}, u32[]{:S(2)}) copy-start(f32[384]{0:T(512)S(1)} %get-tuple-element.8) | copy-start | bytes 4612
  14.7 21.4 %copy-start.57 = (f32[384]{0:T(512)}, f32[384]{0:T(512)S(1)}, u32[]{:S(2)}) copy-start(f32[384]{0:T(512)S(1)} %get-tuple-element.9) | copy-start | bytes 4612
  14.8 21.4 %copy-start.59 = (f32[384]{0:T(512)}, f32[384]{0:T(512)S(1)}, u32[]{:S(2)}) copy-start(f32[384]{0:T(512)S(1)} %get-tuple-element.10) | copy-start | bytes 4612
  14.8 21.4 %copy-start.61 = (f32[384]{0:T(512)}, f32[384]{0:T(512)S(1)}, u32[]{:S(2)}) copy-start(f32[384]{0:T(512)S(1)} %get-tuple-element.11) | copy-start | bytes 4612
  14.8 21.4 %copy-start.63 = (f32[384]{0:T(512)}, f32[384]{0:T(512)S(1)}, u32[]{:S(2)}) copy-start(f32[384]{0:T(512)S(1)} %get-tuple-element.12) | copy-start | bytes 4612
  14.8 21.4 %copy-start.65 = (f32[384]{0:T(512)}, f32[384]{0:T(512)S(1)}, u32[]{:S(2)}) copy-start(f32[384]{0:T(512)S(1)} %get-tuple-element.13) | copy-start | bytes 4612
  14.8 21.4 %copy-start.67 = (f32[384]{0:T(512)}, f32[384]{0:T(512)S(1)}, u32[]{:S(2)}) copy-start(f32[384]{0:T(512)S(1)} %get-tuple-element.14) | copy-start | bytes 4612
  14.8 21.4 %copy-start.69 = (f32[384]{0:T(512)}, f32[384]{0:T(512)S(1)}, u32[]{:S(2)}) copy-start(f32[384]{0:T(512)S(1)} %get-tuple-element.15) | copy-start | bytes 4612
  14.8 21.4 %copy-start.71 = (f32[384]{0:T(512)}, f32[384]{0:T(512)S(1)}, u32[]{:S(2)}) copy-start(f32[384]{0:T(512)S(1)} %get-tuple-element.16) | copy-start | bytes 4612
  14.8 21.4 %copy-start.73 = (f32[384]{0:T(512)}, f32[384]{0:T(512)S(1)}, u32[]{:S(2)}) copy-start(f32[384]{0:T(512)S(1)} %get-tuple-element.17) | copy-start | bytes 4612
  14.8 21.4 %copy-start.75 = (f32[384]{0:T(512)}, f32[384]{0:T(512)S(1)}, u32[]{:S(2)}) copy-start(f32[384]{0:T(512)S(1)} %get-tuple-element.18) | copy-start | bytes 4612
  14.8 21.4 %copy-start.77 = (f32[384]{0:T(512)}, f32[384]{0:T(512)S(1)}, u32[]{:S(2)}) copy-start(f32[384]{0:T(512)S(1)} %get-tuple-element.19) | copy-start | bytes 4612
  14.9 21.4 %copy-start.79 = (f32[384]{0:T(512)}, f32[384]{0:T(512)S(1)}, u32[]{:S(2)}) copy-start(f32[384]{0:T(512)S(1)} %get-tuple-element.20) | copy-start | bytes 4612
  14.9 21.4 %copy-start.81 = (f32[384]{0:T(512)}, f32[384]{0:T(512)S(1)}, u32[]{:S(2)}) copy-start(f32[384]{0:T(512)S(1)} %get-tuple-element.21) | copy-start | bytes 4612
  14.9 21.4 %copy-start.83 = (f32[384]{0:T(512)}, f32[384]{0:T(512)S(1)}, u32[]{:S(2)}) copy-start(f32[384]{0:T(512)S(1)} %get-tuple-element.22) | copy-start | bytes 4612
  22.5 9.3 %collective-permute-start.2 = (bf16[102,3,384]{2,1,0:T(4,128)(2,1)S(1)}, bf16[102,3,384]{2,1,0:T(4,128)(2,1)S(1)}, u32[]{:S(2)}, u32[]{:S(2)}) collective-permute-start(bf16[102,3,384]{2,1,0:T(4,128)(2,1)S(1)} %get-tuple-element.64), channel_id=1, source_target_pairs={{0,1},{1,2},{2,3},{3,4},{4,5},{5,6},{6,7},{7,8},{8,9},{9,10},{10,1... | collective-permute-start | bytes 705032 | tf_op jit(solution)/shard_map/ppermute | solution.py:23
  26.1 9.9 %collective-permute-start.3 = (bf16[102,3,384]{2,1,0:T(4,128)(2,1)S(1)}, bf16[102,3,384]{2,1,0:T(4,128)(2,1)S(1)}, u32[]{:S(2)}, u32[]{:S(2)}) collective-permute-start(bf16[102,3,384]{2,1,0:T(4,128)(2,1)S(1)} %get-tuple-element.65), channel_id=1, source_target_pairs={{1,0},{2,1},{3,2},{4,3},{5,4},{6,5},{7,6},{8,7},{9,8},{10,9},{11,1... | collective-permute-start | bytes 705032 | tf_op jit(solution)/shard_map/ppermute | solution.py:25
  28.9 81.0 %copy-start.85 = (f32[384]{0:T(512)}, f32[384]{0:T(512)S(1)}, u32[]{:S(2)}) copy-start(f32[384]{0:T(512)S(1)} %get-tuple-element.42) | copy-start | bytes 4612
  125.5 51.1 %all-to-all-start = ((bf16[16,3,24576]{2,1,0:T(4,128)(2,1)}), bf16[16,3,24576]{2,1,0:T(4,128)(2,1)}, u32[]{:S(2)}, u32[]{:S(2)}) async-start(bf16[16,3,24576]{2,1,0:T(4,128)(2,1)} %reshape.221), calls=%async_computation | async-start | bytes 6291456 | tf_op jit(solution)/shard_map/all_to_all | solution.py:176
  133.7 47.3 %copy-start.86 = (pred[48]{0:T(512)(128)(4,1)}, pred[48]{0:T(512)(128)(4,1)S(1)}, u32[]{:S(2)}) copy-start(pred[48]{0:T(512)(128)(4,1)S(1)} %fusion.128) | copy-start | bytes 148
  133.7 47.3 %copy-start.87 = (s32[48]{0:T(128)}, s32[48]{0:T(128)S(1)}, u32[]{:S(2)}) copy-start(s32[48]{0:T(128)S(1)} %fusion.129) | copy-start | bytes 580
  184.5 9.2 %copy-start.8 = (bf16[384,1536]{1,0:T(8,128)(2,1)S(1)}, bf16[384,1536]{1,0:T(8,128)(2,1)}, u32[]{:S(2)}) copy-start(bf16[384,1536]{1,0:T(8,128)(2,1)} %param.12) | copy-start | bytes 3538948
  208.2 13.7 %copy-start.90 = (s32[12,4]{0,1:T(4,128)S(1)}, s32[12,4]{0,1:T(4,128)}, u32[]{:S(2)}) copy-start(s32[12,4]{0,1:T(4,128)} %param.15) | copy-start | bytes 580
  212.0 50.5 %all-to-all-start.1 = ((bf16[16,3,24576]{2,1,0:T(4,128)(2,1)}), bf16[16,3,24576]{2,1,0:T(4,128)(2,1)}, u32[]{:S(2)}, u32[]{:S(2)}) async-start(bf16[16,3,24576]{2,1,0:T(4,128)(2,1)} %reshape.224), calls=%async_computation.1 | async-start | bytes 6291456 | tf_op jit(solution)/shard_map/all_to_all | solution.py:182
  222.1 44.8 %copy-start.88 = (f32[48]{0:T(128)}, f32[48]{0:T(128)S(1)}, u32[]{:S(2)}) copy-start(f32[48]{0:T(128)S(1)} %convert_element_type.632) | copy-start | bytes 580
  372.1 45.2 %copy-start.89 = (f32[48]{0:T(128)S(1)}, f32[48]{0:T(128)}, u32[]{:S(2)}) copy-start(f32[48]{0:T(128)} %copy-done.88) | copy-start | bytes 580
  422.0 25.1 %collective-permute-start.4 = (bf16[3,32,384]{2,1,0:T(8,128)(2,1)S(1)}, bf16[3,32,384]{2,1,0:T(8,128)(2,1)S(1)}, u32[]{:S(2)}, u32[]{:S(2)}) collective-permute-start(bf16[3,32,384]{2,1,0:T(8,128)(2,1)S(1)} %get-tuple-element.68), channel_id=1, source_target_pairs={{0,16},{16,32},{32,48},{48,64},{64,80},{80,96},{96,112},{1,17},{17... | collective-permute-start | bytes 221192 | tf_op jit(solution)/shard_map/ppermute | solution.py:23
  424.0 23.1 %collective-permute-start.5 = (bf16[3,32,384]{2,1,0:T(8,128)(2,1)S(1)}, bf16[3,32,384]{2,1,0:T(8,128)(2,1)S(1)}, u32[]{:S(2)}, u32[]{:S(2)}) collective-permute-start(bf16[3,32,384]{2,1,0:T(8,128)(2,1)S(1)} %get-tuple-element.69), channel_id=1, source_target_pairs={{16,0},{32,16},{48,32},{64,48},{80,64},{96,80},{112,96},{17,1},{33... | collective-permute-start | bytes 221192 | tf_op jit(solution)/shard_map/ppermute | solution.py:25
  448.6 9.3 %collective-permute-start.6 = (bf16[102,3,384]{2,1,0:T(4,128)(2,1)S(1)}, bf16[102,3,384]{2,1,0:T(4,128)(2,1)S(1)}, u32[]{:S(2)}, u32[]{:S(2)}) collective-permute-start(bf16[102,3,384]{2,1,0:T(4,128)(2,1)S(1)} %get-tuple-element.62), channel_id=1, source_target_pairs={{0,1},{1,2},{2,3},{3,4},{4,5},{5,6},{6,7},{7,8},{8,9},{9,10},{10,1... | collective-permute-start | bytes 705032 | tf_op jit(solution)/shard_map/ppermute | solution.py:23
  450.8 11.2 %collective-permute-start.7 = (bf16[102,3,384]{2,1,0:T(4,128)(2,1)S(1)}, bf16[102,3,384]{2,1,0:T(4,128)(2,1)S(1)}, u32[]{:S(2)}, u32[]{:S(2)}) collective-permute-start(bf16[102,3,384]{2,1,0:T(4,128)(2,1)S(1)} %get-tuple-element.63), channel_id=1, source_target_pairs={{1,0},{2,1},{3,2},{4,3},{5,4},{6,5},{7,6},{8,7},{9,8},{10,9},{11,1... | collective-permute-start | bytes 705032 | tf_op jit(solution)/shard_map/ppermute | solution.py:25
  452.1 9.9 %copy-start.2 = (bf16[12,8,4,8,384]{4,3,2,1,0:T(8,128)(2,1)S(1)}, bf16[12,8,4,8,384]{4,3,2,1,0:T(8,128)(2,1)}, u32[]{:S(2)}) copy-start(bf16[12,8,4,8,384]{4,3,2,1,0:T(8,128)(2,1)} %copy-done.1) | copy-start | bytes 7077892
  457.0 7.2 %copy-start.16 = (f32[384]{0:T(512)S(1)}, f32[384]{0:T(512)}, u32[]{:S(2)}) copy-start(f32[384]{0:T(512)} %copy-done.15) | copy-start | bytes 4612
  457.0 7.2 %copy-start.18 = (f32[384]{0:T(512)S(1)}, f32[384]{0:T(512)}, u32[]{:S(2)}) copy-start(f32[384]{0:T(512)} %copy-done.17) | copy-start | bytes 4612
  457.0 7.2 %copy-start.20 = (f32[384]{0:T(512)S(1)}, f32[384]{0:T(512)}, u32[]{:S(2)}) copy-start(f32[384]{0:T(512)} %copy-done.19) | copy-start | bytes 4612
  457.0 7.2 %copy-start.22 = (f32[384]{0:T(512)S(1)}, f32[384]{0:T(512)}, u32[]{:S(2)}) copy-start(f32[384]{0:T(512)} %copy-done.21) | copy-start | bytes 4612
  457.0 7.2 %copy-start.24 = (f32[384]{0:T(512)S(1)}, f32[384]{0:T(512)}, u32[]{:S(2)}) copy-start(f32[384]{0:T(512)} %copy-done.23) | copy-start | bytes 4612
  457.0 7.2 %copy-start.26 = (f32[384]{0:T(512)S(1)}, f32[384]{0:T(512)}, u32[]{:S(2)}) copy-start(f32[384]{0:T(512)} %copy-done.25) | copy-start | bytes 4612
  457.0 7.2 %copy-start.28 = (f32[384]{0:T(512)S(1)}, f32[384]{0:T(512)}, u32[]{:S(2)}) copy-start(f32[384]{0:T(512)} %copy-done.27) | copy-start | bytes 4612
  (40 other events, 249.5 us)
where the time goes:
time: 518 us; the launch traced here: 510 us
  other arithmetic  142 us (27%)
  local copies, waits for them, and re-layouts  109 us (21%)
  blocking collectives  88.4 us (17%)
  waiting for transfers between devices  78.3 us (15%)
  matrix products  49.2 us (9%)
  starting transfers between devices  40.6 us (8%)
    convert_element_type x1, other arithmetic, on_device(): depthwise(padded, depth_kernel, height, breadth).astype(jnp.bfloat16)  73.7 us
    all_to_all x1, blocking collectives, on_device(): lax.all_to_all(grad_out, 'col', split_axis=0, concat_axis=0, tiled=True)  47.6 us
    convert_element_type x1, other arithmetic, on_device(): grad_image = (grad_summed.astype(jnp.float32) + depthwise(grad_padded, de...  45.2 us
    all_to_all x1, waiting for transfers between devices, on_device(): lax.all_to_all(outgoing, 'col', split_axis=0, concat_axis=0, tiled=True)  42.8 us
    all_to_all x1, blocking collectives, on_device(): lax.all_to_all(grad_homeward.reshape(peer_count, capacity, tile_width), '...  40.8 us
    all_to_all x1, waiting for transfers between devices, on_device(): lax.all_to_all(homeward.reshape(peer_count, capacity, tile_width), 'col',...  24.2 us
    dot_general x2, matrix products, times_transposed(): lax.dot_general(left, right, (((1,), (1,)), ((), ())), preferred_element_...  13.4 us
    dot_general x4, matrix products, select_rows(): jnp.dot(selector, source, preferred_element_type=jnp.float32)  13.3 us
  transfers between devices with their start and end apart: 10, of which 6 were waited for; matrix products, arithmetic and copies ran while one was open for 10% of the time, Pallas kernels for 0%

commit v1 on v0

v1 whole, which is shorter than its diff:
```python
import jax
import jax.numpy as jnp
from jax import lax
from jax.sharding import PartitionSpec as P

KS = 7
LIVE_DEV = 18


EPSILON = 1e-06
ROOT_HALF = 0.7071067811865476
INV_ROOT_TAU = 0.3989422804014327


def with_halo(cells, sides, width):
    for axis, dim in sides:
        count = lax.axis_size(axis)
        ends = count - 1
        head = lax.slice_in_dim(cells, 0, width, axis=dim)
        tail = lax.slice_in_dim(cells, cells.shape[dim] - width, cells.shape[dim], axis=dim)
        cells = jnp.concatenate(
            [
                lax.ppermute(tail, axis, [(i, (i + 1) % count) for i in range(ends)]),
                cells,
                lax.ppermute(head, axis, [((i + 1) % count, i) for i in range(ends)]),
            ],
            axis=dim,
        )
    return cells


def depthwise(padded, kernel, height, breadth):
    reach = kernel.shape[0]
    total = jnp.zeros((height, breadth, padded.shape[2]), jnp.float32)
    for shift_r in range(reach):
        for shift_c in range(reach):
            window = padded[shift_r : shift_r + height, shift_c : shift_c + breadth, :].astype(
                jnp.float32
            )
            total = total + window * kernel[shift_r, shift_c, :].astype(jnp.float32)
    return total


def normalize(values):
    average = jnp.mean(values, axis=-1, keepdims=True)
    centered = values - average
    inv_std = lax.rsqrt(jnp.mean(centered * centered, axis=-1, keepdims=True) + EPSILON)
    return (centered * inv_std, inv_std)


def normalize_back(gradient, normed, inv_std):
    return inv_std * (
        gradient
        - jnp.mean(gradient, axis=-1, keepdims=True)
        - normed * jnp.mean(gradient * normed, axis=-1, keepdims=True)
    )


def times_transposed(left, right):
    return lax.dot_general(
        left, right, (((1,), (1,)), ((), ())), preferred_element_type=jnp.float32
    )


def routed_tiles(tile_counts, tile_owner, tile_slot, peer_count, capacity):
    count_table = tile_counts[0]
    before = jnp.cumsum(count_table, axis=0) - count_table
    column_ids = jnp.arange(peer_count, dtype=jnp.int32)
    own_column = column_ids == lax.axis_index("col")
    my_bases = jnp.sum(jnp.where(own_column[:, None], before, 0), axis=0)
    my_counts = jnp.sum(jnp.where(own_column[:, None], count_table, 0), axis=0)
    owner_hits = tile_owner[:, :, None] == column_ids[None, None, :]
    base = jnp.sum(jnp.where(owner_hits, my_bases[None, None, :], 0), axis=2)
    quota = jnp.sum(jnp.where(owner_hits, my_counts[None, None, :], 0), axis=2)
    rank = tile_slot - base
    return (
        (tile_owner >= 0)
        & (rank >= 0)
        & (rank < capacity)
        & (rank < quota)
        & (tile_slot < LIVE_DEV)
    )


def on_device(
    image,
    depth_kernel,
    weight_in,
    weight_out,
    weight_down,
    tissue_mask,
    tile_counts,
    tile_owner,
    tile_slot,
    cotangent,
):
    height, breadth, channels = image.shape
    tile_rows, tile_cols = tissue_mask.shape
    tile_side = height // tile_rows
    outputs = weight_down.shape[3]
    reach = KS // 2
    peer_count = lax.axis_size("col")
    capacity = tile_rows * tile_cols // peer_count
    pixels = height * breadth
    routed = routed_tiles(tile_counts, tile_owner, tile_slot, peer_count, capacity)
    live = routed & (tissue_mask != 0)
    live_px = jnp.broadcast_to(
        live[:, None, :, None], (tile_rows, tile_side, tile_cols, tile_side)
    ).reshape(pixels, 1)
    padded = with_halo(image, (("row", 0), ("col", 1)), reach)
    mixed = depthwise(padded, depth_kernel, height, breadth).astype(jnp.bfloat16)
    normed, inv_std = normalize(mixed.reshape(pixels, channels).astype(jnp.float32))
    hidden = jnp.dot(normed.astype(jnp.bfloat16), weight_in, preferred_element_type=jnp.float32)
    cdf = 0.5 * (1.0 + jax.scipy.special.erf(hidden * ROOT_HALF))
    activated = (hidden * cdf).astype(jnp.bfloat16)
    branch = jnp.dot(activated, weight_out, preferred_element_type=jnp.float32).astype(jnp.bfloat16)
    branch_px = jnp.where(live_px, branch.astype(jnp.float32), 0.0)
    summed = (image.reshape(pixels, channels).astype(jnp.float32) + branch_px).astype(jnp.bfloat16)
    down_normed, down_inv = normalize(summed.astype(jnp.float32))
    down_low = down_normed.astype(jnp.bfloat16).reshape(height // 2, 2, breadth // 2, 2 * channels)
    weight_pair = weight_down.reshape(2, 2 * channels, outputs)
    reduced = jnp.dot(down_low[:, 0], weight_pair[0], preferred_element_type=jnp.float32) + jnp.dot(
        down_low[:, 1], weight_pair[1], preferred_element_type=jnp.float32
    )
    reduced = reduced.astype(jnp.bfloat16)
    grad_pair = [
        lax.dot_general(
            cotangent, weight_pair[a], (((2,), (1,)), ((), ())), preferred_element_type=jnp.float32
        )
        for a in range(2)
    ]
    grad_normed = jnp.stack(grad_pair, axis=1).reshape(pixels, channels)
    grad_summed = normalize_back(grad_normed, down_normed, down_inv).astype(jnp.bfloat16)
    slope = cdf + hidden * INV_ROOT_TAU * jnp.exp(-0.5 * hidden * hidden)
    grad_hidden = (times_transposed(grad_summed, weight_out) * slope).astype(jnp.bfloat16)
    grad_norm_in = times_transposed(grad_hidden, weight_in)
    grad_owned_mixed = normalize_back(grad_norm_in, normed, inv_std).astype(jnp.bfloat16)
    grad_mixed = jnp.where(live_px, grad_owned_mixed, jnp.zeros_like(grad_owned_mixed))
    grad_padded = with_halo(grad_mixed.reshape(height, breadth, channels), (("row", 0), ("col", 1)), reach)
    grad_image = (
        grad_summed.reshape(height, breadth, channels).astype(jnp.float32)
        + depthwise(grad_padded, depth_kernel[::-1, ::-1, :], height, breadth)
    ).astype(jnp.bfloat16)
    return (reduced, grad_image)


def solution(mesh):
    in_specs = (
        P("row", "col", None),
        P(),
        P(),
        P(),
        P(),
        P("row", "col"),
        P("row", None, None),
        P("row", "col"),
        P("row", "col"),
        P("row", "col", None),
    )
    out_specs = (P("row", "col", None), P("row", "col", None))
    return jax.shard_map(
        on_device, mesh=mesh, in_specs=in_specs, out_specs=out_specs, check_vma=False
    )
```

time: 518 us -> 247 us (0.48)
  the two profiles are of different devices: /device:TPU:1 before, /device:TPU:26 now
where the time goes in v1:
time: 247 us; the launch traced here: 242 us
  other arithmetic  125 us (51%)
  local copies, waits for them, and re-layouts  45.5 us (18%)
  matrix products  40.5 us (16%)
  starting transfers between devices  26.7 us (11%)
  between operations  2.79 us (1%)
    reduce_sum x1, other arithmetic, normalize(): average = jnp.mean(values, axis=-1, keepdims=True)  40.8 us
    convert_element_type x1, other arithmetic, on_device(): grad_image = (grad_summed.reshape(height, breadth, channels).astype(jnp.f...  39.6 us
    dot_general x1, matrix products, times_transposed(): lax.dot_general(left, right, (((1,), (1,)), ((), ())), preferred_element_...  21.4 us
    ppermute x4, starting transfers between devices, with_halo(): lax.ppermute(head, axis, [((i + 1) % count, i) for i in range(ends)])  16.6 us
    ppermute x4, starting transfers between devices, with_halo(): lax.ppermute(tail, axis, [(i, (i + 1) % count) for i in range(ends)])  10.1 us
    dot_general x1, matrix products, on_device(): jnp.dot(activated, weight_out, preferred_element_type=jnp.float32)  8.51 us
    unnamed x233, local copies, waits for them, and re-layouts  7.84 us
    convert_element_type x1, local copies, waits for them, and re-layouts, on_device(): image.reshape(pixels, channels).astype(jnp.float32) + branch_px  7.24 us
  transfers between devices with their start and end apart: 8, of which 1 were waited for; matrix products, arithmetic and copies ran while one was open for 18% of the time, Pallas kernels for 0%

profile of v1, /device:TPU:26, one launch (start us, length us, event | category | flops | bytes accessed | tf_op | source)
XLA Modules:
  0.0 241.8 jit_solution(273132203441296649)
XLA Ops:
  0.7 5.7 %constant_dynamic-update-slice_fusion.1 = (bf16[99,32,384]{2,0,1:T(8,128)(2,1)}, f32[96,32,384]{2,0,1:T(8,128)}, bf16[96,32,384]{2,0,1:T(8,128)(2,1)S(1)}) fusion(bf16[96,32,384]{2,1,0:T(8,128)(2,1)} %param.10), kind=kLoop, calls=%fused_computation.68 | loop fusion | flops 1179647 | bytes 11796480
  6.4 0.8 fusion.31
  7.1 1.9 collective-permute-start
  9.0 3.6 %collective-permute-start.1 = (bf16[3,32,384]{2,0,1:T(4,128)(2,1)}, bf16[3,32,384]{2,0,1:T(4,128)(2,1)}, u32[]{:S(2)}, u32[]{:S(2)}) collective-permute-start(bf16[3,32,384]{2,0,1:T(4,128)(2,1)} %get-tuple-element.89), channel_id=1, source_target_pairs={{16,0},{32,16},{48,32},{64,48},{80,64},{96,80},{112,96},{17,1},{33... | collective-permute-start | bytes 221192 | tf_op jit(solution)/shard_map/ppermute | solution.py:25
  12.7 0.5 iota_compare_fusion.1
  13.2 0.8 copy.95
  14.0 0.6 reduce_window_sum.11
  14.6 0.8 select_reduce_fusion.3
  15.4 1.0 select_reduce_fusion.1
  16.4 0.8 copy.96
  17.2 0.1 copy.97
  17.2 1.9 fusion.30
  19.1 0.1 copy-done.109
  19.2 1.1 convolution_bitcast_fusion.1
  20.4 0.2 copy-done.5
  20.6 1.1 convolution_bitcast_fusion
  21.7 2.5 %pad_maximum_fusion = f32[48,2,16,768]{3,2,0,1:T(8,128)} fusion(f32[48,1,16,768]{3,2,0,1:T(8,128)S(1)} %convolution_bitcast_fusion, f32[48,1,16,768]{3,2,0,1:T(8,128)S(1)} %convolution_bitcast_fusion.1), kind=kLoop, calls=%fused_computation.21 | loop fusion | flops 1179648 | bytes 9437184 | tf_op jit(solution)/shard_map/stack | solution.py:132
  24.2 0.5 compare_and_fusion
  24.8 0.7 convert_reduce_fusion.50
  25.5 1.7 pad_maximum_fusion.10
  27.2 3.8 %collective-permute-start.2 = (bf16[102,3,384]{2,0,1:T(8,128)(2,1)}, bf16[102,3,384]{2,0,1:T(8,128)(2,1)}, u32[]{:S(2)}, u32[]{:S(2)}) collective-permute-start(bf16[102,3,384]{2,0,1:T(8,128)(2,1)} %get-tuple-element.75), channel_id=1, source_target_pairs={{0,1},{1,2},{2,3},{3,4},{4,5},{5,6},{6,7},{7,8},{8,9},{9,10},{10,1... | collective-permute-start | bytes 705032 | tf_op jit(solution)/shard_map/ppermute | solution.py:23
  31.0 4.7 %collective-permute-start.3 = (bf16[102,3,384]{2,0,1:T(8,128)(2,1)}, bf16[102,3,384]{2,0,1:T(8,128)(2,1)}, u32[]{:S(2)}, u32[]{:S(2)}) collective-permute-start(bf16[102,3,384]{2,0,1:T(8,128)(2,1)} %get-tuple-element.76), channel_id=1, source_target_pairs={{1,0},{2,1},{3,2},{4,3},{5,4},{6,5},{7,6},{8,7},{9,8},{10,9},{11,1... | collective-permute-start | bytes 705032 | tf_op jit(solution)/shard_map/ppermute | solution.py:25
  35.7 0.7 convert_reduce_fusion.48
  36.4 1.3 copy.98
  37.7 1.4 broadcast_in_dim.56
  39.1 1.5 broadcast_in_dim.57
  40.6 5.0 %copy.109 = f32[48,2,16,768]{3,2,1,0:T(8,128)} copy(f32[48,2,16,768]{3,2,0,1:T(8,128)} %pad_maximum_fusion) | data formatting | bytes 9437184 | tf_op jit(solution)/shard_map/stack | solution.py:132
  45.6 6.0 %reshape.100 = f32[3072,384]{1,0:T(8,128)} reshape(f32[48,2,16,768]{3,2,1,0:T(8,128)} %copy.109) | data formatting | bytes 9437184 | tf_op jit(solution)/shard_map/reshape | solution.py:132
  51.6 7.2 %copy.94 = f32[96,32,384]{2,1,0:T(8,128)} copy(f32[96,32,384]{2,0,1:T(8,128)} %get-tuple-element.86) | data formatting | bytes 9437184 | tf_op jit(solution)/shard_map/convert_element_type | solution.py:118
  59.1 0.1 convert_reduce_fusion.49
  59.4 1.6 constant_dynamic-update-slice_fusion
  61.0 3.7 %maximum_maximum_fusion = (bf16[102,35,384]{2,0,1:T(8,128)(2,1)S(1)}, bf16[102,35,384]{2,0,1:T(8,128)(2,1)S(1)}) fusion(bf16[3,32,384]{2,0,1:T(4,128)(2,1)} %collective-permute-done.1, bf16[96,32,384]{2,0,1:T(8,128)(2,1)S(1)} %get-tuple-element.87, bf16[3,32,384]{2,0,1:T(4,128)(2,1)} %collective-permute-done, ...), kind=kLoop, calls=%fused_computation.38 | loop fusion | flops 21934080 | bytes 8460288 | tf_op jit(solution)/shard_map/concatenate | solution.py:21
  65.0 40.8 %convert_reduce_fusion.1 = (f32[96,32]{0,1:T(8,128)S(1)}, bf16[96,32,384]{2,0,1:T(8,128)(2,1)}) fusion(f32[384]{0:T(512)S(1)} %copy-done.69, bf16[102,35,384]{2,0,1:T(8,128)(2,1)S(1)} %get-tuple-element.74, f32[384]{0:T(512)S(1)} %copy-done.71, f32[384]{0:T(512)S(1)} %get-tuple-element.15, f32[384]{0:T(512)S(1)} %get-tuple-element.16, ...), kind=kLoop, calls=%fused_computation.49 | loop fusion | flops 186381312 | bytes 111048192 | tf_op jit(solution)/shard_map/reduce_sum | solution.py:45
  106.0 0.1 copy.105
  106.1 2.8 %multiply_reduce_fusion.1 = f32[96,32]{0,1:T(8,128)S(1)} fusion(bf16[96,32,384]{2,0,1:T(8,128)(2,1)} %get-tuple-element.68, f32[96,32]{0,1:T(8,128)S(1)} %broadcast_multiply_fusion), kind=kLoop, calls=%fused_computation.30 | loop fusion | flops 4715520 | bytes 2383872 | tf_op jit(solution)/shard_map/reduce_sum | solution.py:47
  108.9 4.7 %copy.104 = f32[96,32,384]{2,1,0:T(8,128)} copy(bf16[96,32,384]{2,0,1:T(8,128)(2,1)} %get-tuple-element.68) | data formatting | bytes 7077888 | tf_op jit(solution)/shard_map/convert_element_type | solution.py:112
  113.6 0.1 copy.106
  113.7 0.1 rsqrt.20
  113.7 0.1 div.27
  113.8 3.7 %fusion.20 = bf16[3072,384]{1,0:T(8,128)(2,1)S(1)} fusion(f32[96,32,384]{2,1,0:T(8,128)} %copy.104, f32[3072]{0:T(1024)S(1)} %rsqrt.20, f32[3072]{0:T(1024)S(1)} %div.27), kind=kLoop, calls=%fused_computation.33 | loop fusion | flops 3538944 | bytes 7102464 | tf_op jit(solution)/shard_map/convert_element_type | solution.py:113
  117.6 5.1 %fusion.32 = f32[3072,1536]{1,0:T(8,128)S(1)} fusion(bf16[3072,384]{1,0:T(8,128)(2,1)S(1)} %fusion.20, bf16[384,1536]{1,0:T(8,128)(2,1)S(1)} %copy-done), kind=kOutput, calls=%fused_computation.136 | convolution fusion | flops 3623878656 | bytes 22413312 | tf_op jit(solution)/shard_map/dot_general | solution.py:113
  122.7 8.5 %convert_reduce_fusion = (f32[3072]{0:T(1024)S(1)}, bf16[3072,384]{1,0:T(8,128)(2,1)S(1)}) fusion(bf16[1536,384]{1,0:T(8,128)(2,1)S(1)} %copy-done.110, f32[3072,1536]{1,0:T(8,128)S(1)} %fusion.32, pred[3072]{0:T(1024)(128)(4,1)S(1)} %copy-done.102, f32[96,32,384]{2,1,0:T(8,128)S(1)} %bitcast.72), kind=kOutput, calls=%fused_computation.10 | convolution fusion | flops 3655726080 | bytes 27147264 | tf_op jit(solution)/shard_map/dot_general | solution.py:116
  131.3 1.1 fusion.15
  132.4 2.7 %fusion.28 = (f32[3072]{0:T(1024)S(1)}, f32[3072]{0:T(1024)S(1)}) fusion(f32[3072,384]{1,0:T(8,128)S(1)} %bitcast.68, f32[3072]{0:T(1024)S(1)} %add_rsqrt_fusion.1, f32[3072]{0:T(1024)S(1)} %broadcast_multiply_fusion.5, bf16[3072,384]{1,0:T(8,128)(2,1)S(1)} %get-tuple-element.91), kind=kLoop, calls=%fused_computation.132 | loop fusion | flops 7071744 | bytes 7127040 | tf_op jit(solution)/shard_map/reduce_sum | solution.py:54
  135.1 3.8 %fusion.14 = (bf16[3072,384]{1,0:T(8,128)(2,1)S(1)}, bf16[3072,384]{1,0:T(8,128)(2,1)}) fusion(bf16[3072,384]{1,0:T(8,128)(2,1)S(1)} %get-tuple-element.91, f32[3072,384]{1,0:T(8,128)S(1)} %bitcast.68, f32[3072]{0:T(1024)S(1)} %get-tuple-element.93, f32[3072]{0:T(1024)S(1)} %get-tuple-element.94, f32[3072]{0:T(1024)S(1)} %add_rsqrt_fusion.1, ...), kind=kLoop, calls=%fused_computation.19 | loop fusion | flops 10616832 | bytes 11845632 | tf_op jit(solution)/shard_map/convert_element_type | solution.py:133
  138.9 21.4 %fusion.27 = (f32[3072]{0:T(1024)}, f32[3072]{0:T(1024)}, f32[3072,384]{1,0:T(8,128)}) fusion(f32[3072]{0:T(1024)S(1)} %rsqrt.20, f32[3072]{0:T(1024)} %copy-done.12, f32[96,32,384]{2,1,0:T(8,128)} %copy.104, bf16[384,1536]{1,0:T(8,128)(2,1)S(1)} %copy-done, f32[3072,1536]{1,0:T(8,128)} %copy-done.2, bf16[3072,384]{1,0:T(8,128)(2,1)S(1)} %get-tuple-element.77, ...), kind=kOutput, calls=%fused_computation.131 | convolution fusion | flops 7300835328 | bytes 33079296 | tf_op jit(solution)/shard_map/dot_general | solution.py:60
  160.3 4.9 %reshape.99 = bf16[48,2,16,768]{3,2,1,0:T(8,128)(2,1)} reshape(bf16[3072,384]{1,0:T(8,128)(2,1)} %get-tuple-element.78) | data formatting | bytes 4718592 | tf_op jit(solution)/shard_map/reshape | solution.py:120
  165.3 6.4 %fusion.25 = bf16[3072,384]{1,0:T(8,128)(2,1)S(1)} fusion(f32[96,32,384]{2,1,0:T(8,128)} %copy.104, f32[3072,384]{1,0:T(8,128)} %get-tuple-element.92, f32[3072]{0:T(1024)S(1)} %broadcast_multiply_fusion.1, f32[3072]{0:T(1024)S(1)} %broadcast_multiply_fusion.2, f32[3072]{0:T(1024)S(1)} %rsqrt.20, f32[3072]{0:T(1024)S(1)} %copy-done.13, ...), kind=kLoop, calls=%fused_computation.46 | loop fusion | flops 9437184 | bytes 11848704 | tf_op jit(solution)/shard_map/jit(_where)/select_n | solution.py:138
  171.7 0.1 copy.110
  171.8 2.2 collective-permute-start.5
  174.0 2.4 collective-permute-start.4
  176.4 0.9 constant_dynamic-update-slice_fusion.3
  177.4 1.1 fusion.26
  178.5 1.4 collective-permute-done.4
  179.9 0.1 pad_maximum_fusion.7
  180.1 1.9 collective-permute-start.6
  182.0 6.0 %collective-permute-start.7 = (bf16[102,3,384]{2,0,1:T(8,128)(2,1)S(1)}, bf16[102,3,384]{2,0,1:T(8,128)(2,1)S(1)}, u32[]{:S(2)}, u32[]{:S(2)}) collective-permute-start(bf16[102,3,384]{2,0,1:T(8,128)(2,1)S(1)} %get-tuple-element.72), channel_id=1, source_target_pairs={{1,0},{2,1},{3,2},{4,3},{5,4},{6,5},{7,6},{8,7},{9,8},{10,9},{11,1... | collective-permute-start | bytes 705032 | tf_op jit(solution)/shard_map/ppermute | solution.py:25
  188.0 2.1 add_convert_fusion.1
  190.2 2.8 %convert.52 = f32[96,32,384]{2,1,0:T(8,128)} convert(bf16[96,32,384]{2,1,0:T(8,128)(2,1)S(1)} %bitcast.70) | non-fusion elementwise | flops 1179648 | bytes 7077888 | tf_op jit(solution)/shard_map/convert_element_type | solution.py:141
  193.3 0.1 constant_dynamic-update-slice_fusion.2
  193.4 1.5 copy-done.3
  194.9 2.8 %maximum_maximum_fusion.1 = (bf16[102,35,384]{2,0,1:T(8,128)(2,1)S(1)}, bf16[102,35,384]{2,0,1:T(8,128)(2,1)S(1)}) fusion(bf16[3,32,384]{2,0,1:T(4,128)(2,1)S(1)} %collective-permute-done.5, bf16[96,32,384]{2,0,1:T(8,128)(2,1)S(1)} %get-tuple-element.80, bf16[3,32,384]{2,0,1:T(4,128)(2,1)S(1)} %collective-permute-done.4, ...), kind=kLoop, calls=%fused_computation.40 | loop fusion | flops 21934080 | bytes 8460288 | tf_op jit(solution)/shard_map/concatenate | solution.py:21
  198.1 39.6 %fusion.18 = bf16[96,32,384]{2,0,1:T(8,128)(2,1)} fusion(f32[96,32,384]{2,1,0:T(8,128)} %convert.52, bf16[96,32,384]{2,0,1:T(8,128)(2,1)S(1)} %get-tuple-element.80, bf16[3,32,384]{2,0,1:T(4,128)(2,1)} %copy-done.9, bf16[102,35,384]{2,0,1:T(8,128)(2,1)S(1)} %get-tuple-element.70, bf16[99,32,384]{2,0,1:T(8,128)(2,1)} %copy-done.3, ...), kind=kLoop, calls=%fused_computation.27 | loop fusion | flops 185204736 | bytes 115754496 | tf_op jit(solution)/shard_map/convert_element_type | solution.py:143
  237.6 3.9 %copy.117 = bf16[96,32,384]{2,1,0:T(8,128)(2,1)} copy(bf16[96,32,384]{2,0,1:T(8,128)(2,1)} %fusion.18) | data formatting | bytes 4718592
  (245 shorter events, 0.6 us)
Async XLA Ops:
  0.6 116.9 %copy-start = (bf16[384,1536]{1,0:T(8,128)(2,1)S(1)}, bf16[384,1536]{1,0:T(8,128)(2,1)}, u32[]{:S(2)}) copy-start(bf16[384,1536]{1,0:T(8,128)(2,1)} %param.12) | copy-start | bytes 3538948
  0.6 13.4 %copy-start.14 = (s32[1,16,16]{2,1,0:T(8,128)S(1)}, s32[1,16,16]{2,1,0:T(8,128)}, u32[]{:S(2)}) copy-start(s32[1,16,16]{2,1,0:T(8,128)} %param.16) | copy-start | bytes 3076
  7.1 18.3 %collective-permute-start = (bf16[3,32,384]{2,0,1:T(4,128)(2,1)}, bf16[3,32,384]{2,0,1:T(4,128)(2,1)}, u32[]{:S(2)}, u32[]{:S(2)}) collective-permute-start(bf16[3,32,384]{2,0,1:T(4,128)(2,1)} %get-tuple-element.88), channel_id=1, source_target_pairs={{0,16},{16,32},{32,48},{48,64},{64,80},{80,96},{96,112},{1,17},{17... | collective-permute-start | bytes 221192 | tf_op jit(solution)/shard_map/ppermute | solution.py:23
  9.0 16.4 %collective-permute-start.1 = (bf16[3,32,384]{2,0,1:T(4,128)(2,1)}, bf16[3,32,384]{2,0,1:T(4,128)(2,1)}, u32[]{:S(2)}, u32[]{:S(2)}) collective-permute-start(bf16[3,32,384]{2,0,1:T(4,128)(2,1)} %get-tuple-element.89), channel_id=1, source_target_pairs={{16,0},{32,16},{48,32},{64,48},{80,64},{96,80},{112,96},{17,1},{33... | collective-permute-start | bytes 221192 | tf_op jit(solution)/shard_map/ppermute | solution.py:25
  25.4 39.2 %copy-start.15 = (f32[384]{0:T(512)}, f32[384]{0:T(512)S(1)}, u32[]{:S(2)}) copy-start(f32[384]{0:T(512)S(1)} %get-tuple-element.15) | copy-start | bytes 4612
  25.4 39.2 %copy-start.17 = (f32[384]{0:T(512)}, f32[384]{0:T(512)S(1)}, u32[]{:S(2)}) copy-start(f32[384]{0:T(512)S(1)} %get-tuple-element.16) | copy-start | bytes 4612
  25.5 39.2 %copy-start.19 = (f32[384]{0:T(512)}, f32[384]{0:T(512)S(1)}, u32[]{:S(2)}) copy-start(f32[384]{0:T(512)S(1)} %get-tuple-element.17) | copy-start | bytes 4612
  27.2 33.8 %collective-permute-start.2 = (bf16[102,3,384]{2,0,1:T(8,128)(2,1)}, bf16[102,3,384]{2,0,1:T(8,128)(2,1)}, u32[]{:S(2)}, u32[]{:S(2)}) collective-permute-start(bf16[102,3,384]{2,0,1:T(8,128)(2,1)} %get-tuple-element.75), channel_id=1, source_target_pairs={{0,1},{1,2},{2,3},{3,4},{4,5},{5,6},{6,7},{7,8},{8,9},{9,10},{10,1... | collective-permute-start | bytes 705032 | tf_op jit(solution)/shard_map/ppermute | solution.py:23
  31.0 30.0 %collective-permute-start.3 = (bf16[102,3,384]{2,0,1:T(8,128)(2,1)}, bf16[102,3,384]{2,0,1:T(8,128)(2,1)}, u32[]{:S(2)}, u32[]{:S(2)}) collective-permute-start(bf16[102,3,384]{2,0,1:T(8,128)(2,1)} %get-tuple-element.76), channel_id=1, source_target_pairs={{1,0},{2,1},{3,2},{4,3},{5,4},{6,5},{7,6},{8,7},{9,8},{10,9},{11,1... | collective-permute-start | bytes 705032 | tf_op jit(solution)/shard_map/ppermute | solution.py:25
  51.6 7.2 %copy-start.11 = (bf16[7,7,384]{2,1,0:T(8,128)(2,1)S(1)}, bf16[7,7,384]{2,1,0:T(8,128)(2,1)}, u32[]{:S(2)}) copy-start(bf16[7,7,384]{2,1,0:T(8,128)(2,1)} %param.11) | copy-start | bytes 112900
  58.8 5.9 %copy-start.27 = (f32[384]{0:T(512)S(1)}, f32[384]{0:T(512)}, u32[]{:S(2)}) copy-start(f32[384]{0:T(512)} %get-tuple-element.21) | copy-start | bytes 4612
  58.9 5.9 %copy-start.29 = (f32[384]{0:T(512)S(1)}, f32[384]{0:T(512)}, u32[]{:S(2)}) copy-start(f32[384]{0:T(512)} %get-tuple-element.22) | copy-start | bytes 4612
  58.9 5.9 %copy-start.31 = (f32[384]{0:T(512)S(1)}, f32[384]{0:T(512)}, u32[]{:S(2)}) copy-start(f32[384]{0:T(512)} %get-tuple-element.23) | copy-start | bytes 4612
  58.9 5.9 %copy-start.33 = (f32[384]{0:T(512)S(1)}, f32[384]{0:T(512)}, u32[]{:S(2)}) copy-start(f32[384]{0:T(512)} %get-tuple-element.24) | copy-start | bytes 4612
  58.9 5.9 %copy-start.35 = (f32[384]{0:T(512)S(1)}, f32[384]{0:T(512)}, u32[]{:S(2)}) copy-start(f32[384]{0:T(512)} %get-tuple-element.25) | copy-start | bytes 4612
  58.9 5.9 %copy-start.37 = (f32[384]{0:T(512)S(1)}, f32[384]{0:T(512)}, u32[]{:S(2)}) copy-start(f32[384]{0:T(512)} %get-tuple-element.26) | copy-start | bytes 4612
  58.9 5.9 %copy-start.39 = (f32[384]{0:T(512)S(1)}, f32[384]{0:T(512)}, u32[]{:S(2)}) copy-start(f32[384]{0:T(512)} %get-tuple-element.27) | copy-start | bytes 4612
  58.9 5.9 %copy-start.41 = (f32[384]{0:T(512)S(1)}, f32[384]{0:T(512)}, u32[]{:S(2)}) copy-start(f32[384]{0:T(512)} %get-tuple-element.28) | copy-start | bytes 4612
  58.9 5.9 %copy-start.43 = (f32[384]{0:T(512)S(1)}, f32[384]{0:T(512)}, u32[]{:S(2)}) copy-start(f32[384]{0:T(512)} %get-tuple-element.29) | copy-start | bytes 4612
  58.9 5.9 %copy-start.45 = (f32[384]{0:T(512)S(1)}, f32[384]{0:T(512)}, u32[]{:S(2)}) copy-start(f32[384]{0:T(512)} %get-tuple-element.30) | copy-start | bytes 4612
  58.9 5.9 %copy-start.47 = (f32[384]{0:T(512)S(1)}, f32[384]{0:T(512)}, u32[]{:S(2)}) copy-start(f32[384]{0:T(512)} %get-tuple-element.31) | copy-start | bytes 4612
  59.0 5.9 %copy-start.49 = (f32[384]{0:T(512)S(1)}, f32[384]{0:T(512)}, u32[]{:S(2)}) copy-start(f32[384]{0:T(512)} %get-tuple-element.32) | copy-start | bytes 4612
  59.0 5.9 %copy-start.51 = (f32[384]{0:T(512)S(1)}, f32[384]{0:T(512)}, u32[]{:S(2)}) copy-start(f32[384]{0:T(512)} %get-tuple-element.52) | copy-start | bytes 4612
  59.0 5.9 %copy-start.53 = (f32[384]{0:T(512)S(1)}, f32[384]{0:T(512)}, u32[]{:S(2)}) copy-start(f32[384]{0:T(512)} %get-tuple-element.53) | copy-start | bytes 4612
  59.0 5.9 %copy-start.55 = (f32[384]{0:T(512)S(1)}, f32[384]{0:T(512)}, u32[]{:S(2)}) copy-start(f32[384]{0:T(512)} %get-tuple-element.54) | copy-start | bytes 4612
  59.0 5.9 %copy-start.57 = (f32[384]{0:T(512)S(1)}, f32[384]{0:T(512)}, u32[]{:S(2)}) copy-start(f32[384]{0:T(512)} %get-tuple-element.55) | copy-start | bytes 4612
  59.0 5.9 %copy-start.59 = (f32[384]{0:T(512)S(1)}, f32[384]{0:T(512)}, u32[]{:S(2)}) copy-start(f32[384]{0:T(512)} %get-tuple-element.56) | copy-start | bytes 4612
  59.0 5.9 %copy-start.61 = (f32[384]{0:T(512)S(1)}, f32[384]{0:T(512)}, u32[]{:S(2)}) copy-start(f32[384]{0:T(512)} %get-tuple-element.57) | copy-start | bytes 4612
  59.0 5.9 %copy-start.63 = (f32[384]{0:T(512)S(1)}, f32[384]{0:T(512)}, u32[]{:S(2)}) copy-start(f32[384]{0:T(512)} %get-tuple-element.58) | copy-start | bytes 4612
  59.0 5.9 %copy-start.65 = (f32[384]{0:T(512)S(1)}, f32[384]{0:T(512)}, u32[]{:S(2)}) copy-start(f32[384]{0:T(512)} %get-tuple-element.59) | copy-start | bytes 4612
  59.0 5.9 %copy-start.67 = (f32[384]{0:T(512)S(1)}, f32[384]{0:T(512)}, u32[]{:S(2)}) copy-start(f32[384]{0:T(512)} %get-tuple-element.60) | copy-start | bytes 4612
  59.1 5.9 %copy-start.69 = (f32[384]{0:T(512)S(1)}, f32[384]{0:T(512)}, u32[]{:S(2)}) copy-start(f32[384]{0:T(512)} %get-tuple-element.61) | copy-start | bytes 4612
  59.1 5.9 %copy-start.71 = (f32[384]{0:T(512)S(1)}, f32[384]{0:T(512)}, u32[]{:S(2)}) copy-start(f32[384]{0:T(512)} %get-tuple-element.62) | copy-start | bytes 4612
  59.2 46.6 %copy-start.73 = (f32[384]{0:T(512)}, f32[384]{0:T(512)S(1)}, u32[]{:S(2)}) copy-start(f32[384]{0:T(512)S(1)} %get-tuple-element.33) | copy-start | bytes 4612
  59.2 46.6 %copy-start.75 = (f32[384]{0:T(512)}, f32[384]{0:T(512)S(1)}, u32[]{:S(2)}) copy-start(f32[384]{0:T(512)S(1)} %get-tuple-element.34) | copy-start | bytes 4612
  59.2 46.6 %copy-start.77 = (f32[384]{0:T(512)}, f32[384]{0:T(512)S(1)}, u32[]{:S(2)}) copy-start(f32[384]{0:T(512)S(1)} %get-tuple-element.35) | copy-start | bytes 4612
  59.2 46.6 %copy-start.79 = (f32[384]{0:T(512)}, f32[384]{0:T(512)S(1)}, u32[]{:S(2)}) copy-start(f32[384]{0:T(512)S(1)} %get-tuple-element.36) | copy-start | bytes 4612
  59.2 46.6 %copy-start.81 = (f32[384]{0:T(512)}, f32[384]{0:T(512)S(1)}, u32[]{:S(2)}) copy-start(f32[384]{0:T(512)S(1)} %get-tuple-element.37) | copy-start | bytes 4612
  59.2 46.6 %copy-start.83 = (f32[384]{0:T(512)}, f32[384]{0:T(512)S(1)}, u32[]{:S(2)}) copy-start(f32[384]{0:T(512)S(1)} %get-tuple-element.38) | copy-start | bytes 4612
  59.2 46.6 %copy-start.85 = (f32[384]{0:T(512)}, f32[384]{0:T(512)S(1)}, u32[]{:S(2)}) copy-start(f32[384]{0:T(512)S(1)} %get-tuple-element.39) | copy-start | bytes 4612
  59.2 46.6 %copy-start.87 = (f32[384]{0:T(512)}, f32[384]{0:T(512)S(1)}, u32[]{:S(2)}) copy-start(f32[384]{0:T(512)S(1)} %get-tuple-element.40) | copy-start | bytes 4612
  59.3 46.6 %copy-start.89 = (f32[384]{0:T(512)}, f32[384]{0:T(512)S(1)}, u32[]{:S(2)}) copy-start(f32[384]{0:T(512)S(1)} %get-tuple-element.41) | copy-start | bytes 4612
  59.3 46.6 %copy-start.91 = (f32[384]{0:T(512)}, f32[384]{0:T(512)S(1)}, u32[]{:S(2)}) copy-start(f32[384]{0:T(512)S(1)} %get-tuple-element.42) | copy-start | bytes 4612
  59.3 46.6 %copy-start.93 = (f32[384]{0:T(512)}, f32[384]{0:T(512)S(1)}, u32[]{:S(2)}) copy-start(f32[384]{0:T(512)S(1)} %get-tuple-element.43) | copy-start | bytes 4612
  59.3 46.6 %copy-start.94 = (f32[384]{0:T(512)}, f32[384]{0:T(512)S(1)}, u32[]{:S(2)}) copy-start(f32[384]{0:T(512)S(1)} %get-tuple-element.44) | copy-start | bytes 4612
  59.3 46.6 %copy-start.95 = (f32[384]{0:T(512)}, f32[384]{0:T(512)S(1)}, u32[]{:S(2)}) copy-start(f32[384]{0:T(512)S(1)} %get-tuple-element.45) | copy-start | bytes 4612
  59.3 46.6 %copy-start.96 = (f32[384]{0:T(512)}, f32[384]{0:T(512)S(1)}, u32[]{:S(2)}) copy-start(f32[384]{0:T(512)S(1)} %get-tuple-element.46) | copy-start | bytes 4612
  59.3 46.6 %copy-start.97 = (f32[384]{0:T(512)}, f32[384]{0:T(512)S(1)}, u32[]{:S(2)}) copy-start(f32[384]{0:T(512)S(1)} %get-tuple-element.47) | copy-start | bytes 4612
  59.3 46.6 %copy-start.98 = (f32[384]{0:T(512)}, f32[384]{0:T(512)S(1)}, u32[]{:S(2)}) copy-start(f32[384]{0:T(512)S(1)} %get-tuple-element.48) | copy-start | bytes 4612
  59.3 46.6 %copy-start.99 = (f32[384]{0:T(512)}, f32[384]{0:T(512)S(1)}, u32[]{:S(2)}) copy-start(f32[384]{0:T(512)S(1)} %get-tuple-element.49) | copy-start | bytes 4612
  59.3 46.6 %copy-start.100 = (f32[384]{0:T(512)}, f32[384]{0:T(512)S(1)}, u32[]{:S(2)}) copy-start(f32[384]{0:T(512)S(1)} %get-tuple-element.50) | copy-start | bytes 4612
  59.4 46.6 %copy-start.101 = (f32[384]{0:T(512)}, f32[384]{0:T(512)S(1)}, u32[]{:S(2)}) copy-start(f32[384]{0:T(512)S(1)} %get-tuple-element.51) | copy-start | bytes 4612
  113.8 8.8 %copy-start.12 = (f32[3072]{0:T(1024)}, f32[3072]{0:T(1024)S(1)}, u32[]{:S(2)}) copy-start(f32[3072]{0:T(1024)S(1)} %div.27) | copy-start | bytes 36868
  113.8 8.8 %slice-start.2 = ((s8[4718592]{0:T(1024)(128)(4,1)}), s8[4194304]{0:T(1024)(128)(4,1)S(1)}, s32[]{:S(2)}) async-start(s8[4718592]{0:T(1024)(128)(4,1)} %bitcast.71), calls=%async_computation.2 | async-start | bytes 8388608
  117.6 14.8 %slice-start = ((s8[4718592]{0:T(1024)(128)(4,1)}), s8[524288]{0:T(1024)(128)(4,1)S(1)}, s32[]{:S(2)}) async-start(s8[4718592]{0:T(1024)(128)(4,1)} %bitcast.67), calls=%async_computation | async-start | bytes 1048576
  122.7 8.5 %copy-start.2 = (f32[3072,1536]{1,0:T(8,128)}, f32[3072,1536]{1,0:T(8,128)S(1)}, u32[]{:S(2)}) copy-start(f32[3072,1536]{1,0:T(8,128)S(1)} %fusion.32) | copy-start | bytes 56623108
  122.7 9.7 %slice-start.1 = ((s8[4718592]{0:T(1024)(128)(4,1)}), s8[4194304]{0:T(1024)(128)(4,1)S(1)}, s32[]{:S(2)}) async-start(s8[4718592]{0:T(1024)(128)(4,1)} %bitcast.67), calls=%async_computation.1 | async-start | bytes 8388608
  171.8 6.7 %collective-permute-start.5 = (bf16[3,32,384]{2,0,1:T(4,128)(2,1)S(1)}, bf16[3,32,384]{2,0,1:T(4,128)(2,1)S(1)}, u32[]{:S(2)}, u32[]{:S(2)}) collective-permute-start(bf16[3,32,384]{2,0,1:T(4,128)(2,1)S(1)} %copy.111), channel_id=1, source_target_pairs={{16,0},{32,16},{48,32},{64,48},{80,64},{96,80},{112,96},{17,1},{33... | collective-permute-start | bytes 221192 | tf_op jit(solution)/shard_map/ppermute | solution.py:25
  174.0 5.9 %collective-permute-start.4 = (bf16[3,32,384]{2,0,1:T(4,128)(2,1)S(1)}, bf16[3,32,384]{2,0,1:T(4,128)(2,1)S(1)}, u32[]{:S(2)}, u32[]{:S(2)}) collective-permute-start(bf16[3,32,384]{2,0,1:T(4,128)(2,1)S(1)} %copy.110), channel_id=1, source_target_pairs={{0,16},{16,32},{32,48},{48,64},{64,80},{80,96},{96,112},{1,17},{17... | collective-permute-start | bytes 221192 | tf_op jit(solution)/shard_map/ppermute | solution.py:23
  177.4 10.7 %copy-start.6 = (bf16[1,2,384,768]{3,2,1,0:T(8,128)(2,1)S(1)}, bf16[1,2,384,768]{3,2,1,0:T(8,128)(2,1)}, u32[]{:S(2)}) copy-start(bf16[1,2,384,768]{3,2,1,0:T(8,128)(2,1)} %copy-done.5) | copy-start | bytes 3538948
  179.9 14.9 %copy-start.9 = (bf16[3,32,384]{2,0,1:T(4,128)(2,1)}, bf16[3,32,384]{2,0,1:T(4,128)(2,1)S(1)}, u32[]{:S(2)}) copy-start(bf16[3,32,384]{2,0,1:T(4,128)(2,1)S(1)} %collective-permute-done.4) | copy-start | bytes 221188
  180.1 13.3 %collective-permute-start.6 = (bf16[102,3,384]{2,0,1:T(8,128)(2,1)S(1)}, bf16[102,3,384]{2,0,1:T(8,128)(2,1)S(1)}, u32[]{:S(2)}, u32[]{:S(2)}) collective-permute-start(bf16[102,3,384]{2,0,1:T(8,128)(2,1)S(1)} %get-tuple-element.71), channel_id=1, source_target_pairs={{0,1},{1,2},{2,3},{3,4},{4,5},{5,6},{6,7},{7,8},{8,9},{9,10},{10,1... | collective-permute-start | bytes 705032 | tf_op jit(solution)/shard_map/ppermute | solution.py:23
  182.0 12.9 %collective-permute-start.7 = (bf16[102,3,384]{2,0,1:T(8,128)(2,1)S(1)}, bf16[102,3,384]{2,0,1:T(8,128)(2,1)S(1)}, u32[]{:S(2)}, u32[]{:S(2)}) collective-permute-start(bf16[102,3,384]{2,0,1:T(8,128)(2,1)S(1)} %get-tuple-element.72), channel_id=1, source_target_pairs={{1,0},{2,1},{3,2},{4,3},{5,4},{6,5},{7,6},{8,7},{9,8},{10,9},{11,1... | collective-permute-start | bytes 705032 | tf_op jit(solution)/shard_map/ppermute | solution.py:25
  198.0 43.5 %copy-start.1 = (bf16[384,1536]{1,0:T(8,128)(2,1)S(1)}, bf16[384,1536]{1,0:T(8,128)(2,1)}, u32[]{:S(2)}) copy-start(bf16[384,1536]{1,0:T(8,128)(2,1)} %param.12) | copy-start | bytes 3538948
  (59 other events, 266.0 us)

commit v2 on v1

--- a/solution.py
+++ b/solution.py
@@ -2,6 +2,8 @@
 import jax.numpy as jnp
 from jax import lax
 from jax.sharding import PartitionSpec as P
+from jax.experimental import pallas as pl
+from jax.experimental.pallas import tpu as pltpu
 
 KS = 7
 LIVE_DEV = 18
@@ -29,16 +31,61 @@
     return cells
 
 
-def depthwise(padded, kernel, height, breadth):
-    reach = kernel.shape[0]
-    total = jnp.zeros((height, breadth, padded.shape[2]), jnp.float32)
-    for shift_r in range(reach):
-        for shift_c in range(reach):
-            window = padded[shift_r : shift_r + height, shift_c : shift_c + breadth, :].astype(
-                jnp.float32
-            )
-            total = total + window * kernel[shift_r, shift_c, :].astype(jnp.float32)
-    return total
+def depthwise_kernel(x_ref, k_ref, *rest, reach, chunk):
+    if len(rest) == 4:
+        base_ref, out_ref, shifted_ref, total_ref = rest
+    else:
+        base_ref = None
+        out_ref, shifted_ref, total_ref = rest
+    height, breadth, _ = out_ref.shape
+    side = 2 * reach + 1
+    for shift_c in range(side):
+        shifted_ref[...] = x_ref[:, shift_c : shift_c + breadth, :].astype(jnp.float32)
+
+        def body(step, carry, shift_c=shift_c):
+            start = pl.multiple_of(step * chunk, chunk)
+            if shift_c > 0:
+                total = total_ref[pl.ds(start, chunk)]
+            elif base_ref is not None:
+                total = base_ref[pl.ds(start, chunk)].astype(jnp.float32)
+            else:
+                total = jnp.zeros((chunk, breadth, out_ref.shape[2]), jnp.float32)
+            for shift_r in range(side):
+                tap = k_ref[pl.ds(shift_r * side + shift_c, 1), :]
+                total = total + shifted_ref[pl.ds(start + shift_r, chunk)] * tap[None]
+            if shift_c == side - 1:
+                out_ref[pl.ds(start, chunk)] = total.astype(out_ref.dtype)
+            else:
+                total_ref[pl.ds(start, chunk)] = total
+            return carry
+
+        lax.fori_loop(0, height // chunk, body, 0)
+
+
+def depthwise(padded, kernel, height, breadth, base=None, lanes=128, chunk=8):
+    side = kernel.shape[0]
+    reach = side // 2
+    channels = padded.shape[2]
+    taps = kernel.reshape(side * side, channels).astype(jnp.float32)
+    in_specs = [
+        pl.BlockSpec((height + 2 * reach, breadth + 2 * reach, lanes), lambda c: (0, 0, c)),
+        pl.BlockSpec((side * side, lanes), lambda c: (0, c)),
+    ]
+    operands = [padded, taps]
+    if base is not None:
+        in_specs.append(pl.BlockSpec((height, breadth, lanes), lambda c: (0, 0, c)))
+        operands.append(base)
+    return pl.pallas_call(
+        lambda *refs: depthwise_kernel(*refs, reach=reach, chunk=chunk),
+        grid=(channels // lanes,),
+        in_specs=in_specs,
+        out_specs=pl.BlockSpec((height, breadth, lanes), lambda c: (0, 0, c)),
+        out_shape=jax.ShapeDtypeStruct((height, breadth, channels), jnp.bfloat16),
+        scratch_shapes=[
+            pltpu.VMEM((height + 2 * reach, breadth, lanes), jnp.float32),
+            pltpu.VMEM((height, breadth, lanes), jnp.float32),
+        ],
+    )(*operands)
 
 
 def normalize(values):
@@ -108,7 +155,7 @@
         live[:, None, :, None], (tile_rows, tile_side, tile_cols, tile_side)
     ).reshape(pixels, 1)
     padded = with_halo(image, (("row", 0), ("col", 1)), reach)
-    mixed = depthwise(padded, depth_kernel, height, breadth).astype(jnp.bfloat16)
+    mixed = depthwise(padded, depth_kernel, height, breadth)
     normed, inv_std = normalize(mixed.reshape(pixels, channels).astype(jnp.float32))
     hidden = jnp.dot(normed.astype(jnp.bfloat16), weight_in, preferred_element_type=jnp.float32)
     cdf = 0.5 * (1.0 + jax.scipy.special.erf(hidden * ROOT_HALF))
@@ -137,10 +184,9 @@
     grad_owned_mixed = normalize_back(grad_norm_in, normed, inv_std).astype(jnp.bfloat16)
     grad_mixed = jnp.where(live_px, grad_owned_mixed, jnp.zeros_like(grad_owned_mixed))
     grad_padded = with_halo(grad_mixed.reshape(height, breadth, channels), (("row", 0), ("col", 1)), reach)
-    grad_image = (
-        grad_summed.reshape(height, breadth, channels).astype(jnp.float32)
-        + depthwise(grad_padded, depth_kernel[::-1, ::-1, :], height, breadth)
-    ).astype(jnp.bfloat16)
+    grad_image = depthwise(
+        grad_padded, depth_kernel[::-1, ::-1, :], height, breadth, base=grad_summed.reshape(height, breadth, channels)
+    )
     return (reduced, grad_image)
 
 

time: 247 us -> 195 us (0.79); the launches traced: 242 us -> 193 us
  other arithmetic: 125 us -> 42.2 us
  Pallas kernels: 0 us -> 44.1 us
  local copies, waits for them, and re-layouts: 45.5 us -> 30.6 us
  matrix products: 40.5 us -> 43.8 us
  waiting for transfers between devices: 1.46 us -> 4.3 us
    pallas_call x0 -> x2, Pallas kernels: none -> 44.1 us  [depthwise(): pl.pallas_call(lambda *refs: depthwise_kernel(*refs, reach=reach, chunk=c...]
    convert_element_type x2 -> x0, other arithmetic: 42.3 us -> none  [the longest x1 39.6 us: on_device(): grad_image = (grad_summed.reshape(height, breadth, channels).astype(jnp.f...]
    reduce_sum x1, other arithmetic: 40.8 us -> 2.3 us  [normalize(): average = jnp.mean(values, axis=-1, keepdims=True)]
    convert_element_type x2, local copies, waits for them, and re-layouts: 11.9 us -> 2.1 us  [depthwise(): taps = kernel.reshape(side * side, channels).astype(jnp.float32)]
    unnamed x3 -> x1, other arithmetic: 5.71 us -> 0.01 us
    concatenate x2, other arithmetic: 6.45 us -> 11.3 us  [with_halo(): jnp.concatenate([lax.ppermute(tail, axis, [(i, (i + 1) % count) for i in...]
    dot_general x2, matrix products: 2.25 us -> 5.07 us  [on_device(): lax.dot_general(cotangent, weight_pair[a], (((2,), (1,)), ((), ())), pref...]
    unnamed x233 -> x47, local copies, waits for them, and re-layouts: 7.84 us -> 5.77 us
  transfers between devices with their start and end apart: 8 -> 8, of which waited for: 1 -> 2; matrix products, arithmetic and copies ran while one was open for 18% -> 19% of each run, Pallas kernels for 0% -> 0%
where the time goes in v2:
time: 195 us; the launch traced here: 193 us
  Pallas kernels  44.1 us (23%)
  matrix products  43.8 us (22%)
  other arithmetic  42.2 us (22%)
  local copies, waits for them, and re-layouts  30.6 us (16%)
  starting transfers between devices  27.3 us (14%)
  waiting for transfers between devices  4.3 us (2%)
    pallas_call x2, Pallas kernels, depthwise(): pl.pallas_call(lambda *refs: depthwise_kernel(*refs, reach=reach, chunk=c...  44.1 us
    dot_general x1, matrix products, times_transposed(): lax.dot_general(left, right, (((1,), (1,)), ((), ())), preferred_element_...  20.8 us
    ppermute x4, starting transfers between devices, with_halo(): lax.ppermute(head, axis, [((i + 1) % count, i) for i in range(ends)])  17.7 us
    concatenate x2, other arithmetic, with_halo(): jnp.concatenate([lax.ppermute(tail, axis, [(i, (i + 1) % count) for i in...  11.3 us
    ppermute x4, starting transfers between devices, with_halo(): lax.ppermute(tail, axis, [(i, (i + 1) % count) for i in range(ends)])  9.57 us
    dot_general x1, matrix products, on_device(): jnp.dot(activated, weight_out, preferred_element_type=jnp.float32)  8.22 us
    select_n x1, other arithmetic, on_device(): jnp.where(live_px, grad_owned_mixed, jnp.zeros_like(grad_owned_mixed))  6.09 us
    reshape x1, local copies, waits for them, and re-layouts, on_device(): grad_normed = jnp.stack(grad_pair, axis=1).reshape(pixels, channels)  5.95 us
  transfers between devices with their start and end apart: 8, of which 2 were waited for; matrix products, arithmetic and copies ran while one was open for 19% of the time, Pallas kernels for 0%

profile of v2, /device:TPU:26, one launch (start us, length us, event | category | flops | bytes accessed | tf_op | source)
XLA Modules:
  0.0 193.4 jit_solution(5539323378470507438)
XLA Ops:
  0.6 0.0 copy-start
  0.6 0.0 copy-start.17
  0.7 1.7 fusion.27
  2.4 1.9 collective-permute-start
  4.3 3.6 %collective-permute-start.1 = (bf16[3,32,384]{2,1,0:T(8,128)(2,1)}, bf16[3,32,384]{2,1,0:T(8,128)(2,1)}, u32[]{:S(2)}, u32[]{:S(2)}) collective-permute-start(bf16[3,32,384]{2,1,0:T(8,128)(2,1)} %get-tuple-element.20), channel_id=1, source_target_pairs={{16,0},{32,16},{48,32},{64,48},{80,64},{96,80},{112,96},{17,1},{33... | collective-permute-start | bytes 221192 | tf_op jit(solution)/shard_map/ppermute | solution.py:27
  8.0 0.5 iota_compare_fusion.1
  8.5 0.8 copy.30
  9.3 1.8 fusion.26
  11.1 0.0 copy-start.11
  11.1 2.5 %convolution_bitcast_fusion = f32[48,1,16,768]{3,2,0,1:T(8,128)} fusion(bf16[48,16,768]{2,1,0:T(8,128)(2,1)S(1)} %copy-done.17, bf16[768,768,1]{1,0,2:T(8,128)(2,1)S(1)} %bitcast.70), kind=kOutput, calls=%fused_computation.36 | convolution fusion | flops 905969664 | bytes 4718592 | tf_op jit(solution)/shard_map/dot_general | solution.py:174
  13.6 2.5 %convolution_bitcast_fusion.1 = f32[48,1,16,768]{3,2,0,1:T(8,128)} fusion(bf16[48,16,768]{2,1,0:T(8,128)(2,1)S(1)} %copy-done.18, bf16[768,768,1]{1,0,2:T(8,128)(2,1)S(1)} %bitcast.72), kind=kOutput, calls=%fused_computation.37 | convolution fusion | flops 905969664 | bytes 4718592 | tf_op jit(solution)/shard_map/dot_general | solution.py:174
  16.2 0.6 reduce_window_sum.11
  16.8 0.8 select_reduce_fusion.3
  17.6 1.0 select_reduce_fusion.1
  18.5 0.8 copy.31
  19.3 0.1 copy.32
  19.4 0.9 constant_dynamic-update-slice_fusion.2
  20.4 0.5 constant_dynamic-update-slice_fusion.1
  20.8 0.9 constant_dynamic-update-slice_fusion
  21.8 1.5 copy-done.6
  23.2 0.2 fusion.24
  23.5 3.8 %collective-permute-start.2 = (bf16[102,3,384]{2,1,0:T(4,128)(2,1)S(1)}, bf16[102,3,384]{2,1,0:T(4,128)(2,1)S(1)}, u32[]{:S(2)}, u32[]{:S(2)}) collective-permute-start(bf16[102,3,384]{2,1,0:T(4,128)(2,1)S(1)} %get-tuple-element.12), channel_id=1, source_target_pairs={{0,1},{1,2},{2,3},{3,4},{4,5},{5,6},{6,7},{7,8},{8,9},{9,10},{10,1... | collective-permute-start | bytes 705032 | tf_op jit(solution)/shard_map/ppermute | solution.py:25
  27.3 4.4 %collective-permute-start.3 = (bf16[102,3,384]{2,1,0:T(4,128)(2,1)S(1)}, bf16[102,3,384]{2,1,0:T(4,128)(2,1)S(1)}, u32[]{:S(2)}, u32[]{:S(2)}) collective-permute-start(bf16[102,3,384]{2,1,0:T(4,128)(2,1)S(1)} %get-tuple-element.13), channel_id=1, source_target_pairs={{1,0},{2,1},{3,2},{4,3},{5,4},{6,5},{7,6},{8,7},{9,8},{10,9},{11,1... | collective-permute-start | bytes 705032 | tf_op jit(solution)/shard_map/ppermute | solution.py:27
  31.8 1.5 reshape.110.refs_1_
  33.2 1.5 rev.3
  34.8 0.1 copy.33
  34.9 0.1 broadcast_in_dim.82
  35.0 0.1 broadcast_in_dim.83
  35.1 2.7 %pad_maximum_fusion = f32[48,2,16,768]{3,2,0,1:T(8,128)S(1)} fusion(f32[48,1,16,768]{3,2,0,1:T(8,128)} %convolution_bitcast_fusion, f32[48,1,16,768]{3,2,0,1:T(8,128)} %convolution_bitcast_fusion.1), kind=kLoop, calls=%fused_computation.21 | loop fusion | flops 1179648 | bytes 9437184 | tf_op jit(solution)/shard_map/stack | solution.py:179
  37.8 2.6 %copy.36 = f32[48,2,16,768]{3,2,1,0:T(8,128)} copy(f32[48,2,16,768]{3,2,0,1:T(8,128)S(1)} %pad_maximum_fusion) | data formatting | bytes 9437184 | tf_op jit(solution)/shard_map/stack | solution.py:179
  40.4 5.9 %reshape.106 = f32[3072,384]{1,0:T(8,128)} reshape(f32[48,2,16,768]{3,2,1,0:T(8,128)} %copy.36) | data formatting | bytes 9437184 | tf_op jit(solution)/shard_map/reshape | solution.py:179
  46.4 0.6 reshape.112.refs_1_
  47.0 5.3 %pad_maximum_fusion.1.refs_0_ = bf16[102,38,384]{2,1,0:T(8,128)(2,1)} fusion(bf16[102,3,384]{2,1,0:T(4,128)(2,1)S(1)} %collective-permute-done.3, bf16[102,32,384]{2,1,0:T(8,128)(2,1)} %copy-done.6, bf16[102,3,384]{2,1,0:T(4,128)(2,1)S(1)} %collective-permute-done.2), kind=kLoop, calls=%fused_computation.32 | loop fusion | flops 8930304 | bytes 5953536 | tf_op jit(solution)/shard_map/concatenate | solution.py:23
  52.3 21.7 %shard_map.113 = bf16[96,32,384]{2,1,0:T(8,128)(2,1)} custom-call(bf16[102,38,384]{2,1,0:T(8,128)(2,1)} %pad_maximum_fusion.1.refs_0_, f32[49,384]{1,0:T(8,128)} %reshape.110.refs_1_), custom_call_target="tpu_custom_call" | custom-call | tf_op jit(solution)/shard_map/pallas_call | solution.py:78
  74.1 2.3 %convert_reduce_fusion.1 = f32[96,32]{1,0:T(8,128)S(1)} fusion(bf16[96,32,384]{2,1,0:T(8,128)(2,1)} %shard_map.113), kind=kLoop, calls=%fused_computation.31 | loop fusion | flops 2356224 | bytes 2371584 | tf_op jit(solution)/shard_map/reduce_sum | solution.py:92
  76.4 0.6 copy-done.12
  77.0 2.0 %multiply_reduce_fusion.1 = f32[96,32]{1,0:T(8,128)} fusion(bf16[96,32,384]{2,1,0:T(8,128)(2,1)S(1)} %copy-done.2, f32[96,32]{1,0:T(8,128)S(1)} %broadcast_multiply_fusion), kind=kLoop, calls=%fused_computation.28 | loop fusion | flops 4715520 | bytes 2383872 | tf_op jit(solution)/shard_map/reduce_sum | solution.py:94
  79.0 0.9 div.27
  79.9 1.4 add_rsqrt_fusion
  81.3 1.5 rsqrt.20
  82.8 3.1 %fusion.19 = bf16[3072,384]{1,0:T(8,128)(2,1)S(1)} fusion(bf16[96,32,384]{2,1,0:T(8,128)(2,1)S(1)} %copy-done.2, f32[3072]{0:T(1024)} %rsqrt.20, f32[3072]{0:T(1024)S(1)} %div.27), kind=kLoop, calls=%fused_computation.30 | loop fusion | flops 4718592 | bytes 4743168 | tf_op jit(solution)/shard_map/convert_element_type | solution.py:160
  85.9 5.1 %fusion.28 = f32[3072,1536]{1,0:T(8,128)S(1)} fusion(bf16[3072,384]{1,0:T(8,128)(2,1)S(1)} %fusion.19, bf16[384,1536]{1,0:T(8,128)(2,1)S(1)} %copy-done), kind=kOutput, calls=%fused_computation.68 | convolution fusion | flops 3623878656 | bytes 22413312 | tf_op jit(solution)/shard_map/dot_general | solution.py:160
  91.1 8.2 %convert_reduce_fusion = (f32[3072]{0:T(1024)S(1)}, bf16[3072,384]{1,0:T(8,128)(2,1)S(1)}) fusion(bf16[1536,384]{1,0:T(8,128)(2,1)S(1)} %copy-done.19, f32[3072,1536]{1,0:T(8,128)S(1)} %fusion.28, pred[3072]{0:T(1024)(128)(4,1)S(1)} %broadcast_in_dim.83, bf16[3072,384]{1,0:T(8,128)(2,1)S(1)} %bitcast.69), kind=kOutput, calls=%fused_computation.10 | convolution fusion | flops 3656905728 | bytes 24787968 | tf_op jit(solution)/shard_map/dot_general | solution.py:163
  99.3 1.1 fusion.15
  100.4 2.7 %fusion.23 = (f32[3072]{0:T(1024)S(1)}, f32[3072]{0:T(1024)S(1)}) fusion(f32[3072,384]{1,0:T(8,128)S(1)} %bitcast.65, f32[3072]{0:T(1024)S(1)} %add_rsqrt_fusion.1, f32[3072]{0:T(1024)S(1)} %broadcast_multiply_fusion.5, bf16[3072,384]{1,0:T(8,128)(2,1)S(1)} %get-tuple-element.23), kind=kLoop, calls=%fused_computation.63 | loop fusion | flops 7071744 | bytes 7127040 | tf_op jit(solution)/shard_map/reduce_sum | solution.py:101
  103.2 4.2 %fusion.14 = (bf16[3072,384]{1,0:T(8,128)(2,1)}, bf16[3072,384]{1,0:T(8,128)(2,1)}) fusion(bf16[3072,384]{1,0:T(8,128)(2,1)S(1)} %get-tuple-element.23, f32[3072,384]{1,0:T(8,128)S(1)} %bitcast.65, f32[3072]{0:T(1024)S(1)} %get-tuple-element.25, f32[3072]{0:T(1024)S(1)} %get-tuple-element.26, f32[3072]{0:T(1024)S(1)} %add_rsqrt_fusion.1, ...), kind=kLoop, calls=%fused_computation.19 | loop fusion | flops 10616832 | bytes 11845632 | tf_op jit(solution)/shard_map/convert_element_type | solution.py:180
  107.3 20.8 %fusion.22 = (f32[3072]{0:T(1024)}, f32[3072]{0:T(1024)}, f32[3072,384]{1,0:T(8,128)}) fusion(f32[3072]{0:T(1024)} %rsqrt.20, f32[3072]{0:T(1024)S(1)} %div.27, bf16[96,32,384]{2,1,0:T(8,128)(2,1)S(1)} %copy-done.2, bf16[384,1536]{1,0:T(8,128)(2,1)S(1)} %copy-done, f32[3072,1536]{1,0:T(8,128)} %copy-done.3, bf16[3072,384]{1,0:T(8,128)(2,1)} %get-tuple-element.14, ...), kind=kOutput, calls=%fused_computation.62 | convolution fusion | flops 7302014976 | bytes 30720000 | tf_op jit(solution)/shard_map/dot_general | solution.py:107
  128.2 0.7 broadcast_multiply_fusion.1
  128.9 0.7 broadcast_multiply_fusion.2
  129.6 6.1 %fusion.20 = bf16[3072,384]{1,0:T(8,128)(2,1)S(1)} fusion(bf16[96,32,384]{2,1,0:T(8,128)(2,1)S(1)} %copy-done.2, f32[3072,384]{1,0:T(8,128)} %get-tuple-element.24, f32[3072]{0:T(1024)S(1)} %broadcast_multiply_fusion.1, f32[3072]{0:T(1024)S(1)} %broadcast_multiply_fusion.2, f32[3072]{0:T(1024)} %rsqrt.20, f32[3072]{0:T(1024)S(1)} %div.27, ...), kind=kLoop, calls=%fused_computation.34 | loop fusion | flops 10616832 | bytes 9489408 | tf_op jit(solution)/shard_map/jit(_where)/select_n | solution.py:185
  135.7 1.4 copy-done.4
  137.1 0.7 fusion.25
  137.8 1.9 collective-permute-start.4
  139.7 3.6 %collective-permute-start.5 = (bf16[3,32,384]{2,1,0:T(8,128)(2,1)}, bf16[3,32,384]{2,1,0:T(8,128)(2,1)}, u32[]{:S(2)}, u32[]{:S(2)}) collective-permute-start(bf16[3,32,384]{2,1,0:T(8,128)(2,1)} %bitcast.15), channel_id=1, source_target_pairs={{16,0},{32,16},{48,32},{64,48},{80,64},{96,80},{112,96},{17,1},{33... | collective-permute-start | bytes 221192 | tf_op jit(solution)/shard_map/ppermute | solution.py:27
  143.3 3.8 %reshape.105 = bf16[48,2,16,768]{3,2,1,0:T(8,128)(2,1)S(1)} reshape(bf16[3072,384]{1,0:T(8,128)(2,1)} %get-tuple-element.15) | data formatting | bytes 4718592 | tf_op jit(solution)/shard_map/reshape | solution.py:167
  147.1 2.5 %fusion.21 = f32[48,16,768]{2,1,0:T(8,128)S(1)} fusion(bf16[768,768,1]{1,0,2:T(8,128)(2,1)} %bitcast.73, bf16[48,2,16,768]{3,2,1,0:T(8,128)(2,1)S(1)} %reshape.105), kind=kOutput, calls=%fused_computation.40 | convolution fusion | flops 905969664 | bytes 4718592 | tf_op jit(solution)/shard_map/dot_general | solution.py:169
  149.7 1.0 pad_maximum_fusion.5
  150.7 1.9 collective-permute-start.6
  152.6 6.0 %collective-permute-start.7 = (bf16[102,3,384]{2,1,0:T(4,128)(2,1)S(1)}, bf16[102,3,384]{2,1,0:T(4,128)(2,1)S(1)}, u32[]{:S(2)}, u32[]{:S(2)}) collective-permute-start(bf16[102,3,384]{2,1,0:T(4,128)(2,1)S(1)} %get-tuple-element.11), channel_id=1, source_target_pairs={{1,0},{2,1},{3,2},{4,3},{5,4},{6,5},{7,6},{8,7},{9,8},{10,9},{11,1... | collective-permute-start | bytes 705032 | tf_op jit(solution)/shard_map/ppermute | solution.py:27
  158.7 2.1 %add_convert_fusion = bf16[48,16,768]{2,1,0:T(8,128)(2,1)} fusion(f32[48,16,768]{2,1,0:T(8,128)S(1)} %fusion.21, bf16[768,768,1]{1,0,2:T(8,128)(2,1)S(1)} %bitcast.71, bf16[48,2,16,768]{3,2,1,0:T(8,128)(2,1)S(1)} %reshape.105), kind=kOutput, calls=%fused_computation.35 | convolution fusion | flops 907149312 | bytes 5898240 | tf_op jit(solution)/shard_map/dot_general | solution.py:169
  160.8 3.1 %collective-permute-done.6 = bf16[102,3,384]{2,1,0:T(4,128)(2,1)S(1)} collective-permute-done((bf16[102,3,384]{2,1,0:T(4,128)(2,1)S(1)}, bf16[102,3,384]{2,1,0:T(4,128)(2,1)S(1)}, u32[]{:S(2)}, u32[]{:S(2)}) %collective-permute-start.6) | collective-permute-done | bytes 235040 | tf_op jit(solution)/shard_map/ppermute | solution.py:25
  163.9 1.2 collective-permute-done.7
  165.1 5.9 %pad_maximum_fusion.2.refs_0_ = bf16[102,38,384]{2,1,0:T(8,128)(2,1)} fusion(bf16[102,3,384]{2,1,0:T(4,128)(2,1)S(1)} %collective-permute-done.7, bf16[3,32,384]{2,1,0:T(8,128)(2,1)} %collective-permute-done.5, bf16[96,32,384]{2,1,0:T(8,128)(2,1)S(1)} %bitcast.67, bf16[3,32,384]{2,1,0:T(8,128)(2,1)} %collective-permute-done.4, ...), kind=kLoop, calls=%fused_computation.33 | loop fusion | flops 14883840 | bytes 5953536 | tf_op jit(solution)/shard_map/concatenate | solution.py:23
  171.0 22.4 %shard_map.114 = bf16[96,32,384]{2,1,0:T(8,128)(2,1)} custom-call(bf16[102,38,384]{2,1,0:T(8,128)(2,1)} %pad_maximum_fusion.2.refs_0_, f32[49,384]{1,0:T(8,128)} %reshape.112.refs_1_, bf16[96,32,384]{2,1,0:T(8,128)(2,1)} %bitcast.68), custom_call_target="tpu_custom_call" | custom-call | tf_op jit(solution)/shard_map/pallas_call | solution.py:78
  (50 shorter events, 0.1 us)
Async XLA Ops:
  0.6 85.3 %copy-start = (bf16[384,1536]{1,0:T(8,128)(2,1)S(1)}, bf16[384,1536]{1,0:T(8,128)(2,1)}, u32[]{:S(2)}) copy-start(bf16[384,1536]{1,0:T(8,128)(2,1)} %param.12) | copy-start | bytes 3538948
  0.6 10.4 %copy-start.17 = (bf16[48,16,768]{2,1,0:T(8,128)(2,1)S(1)}, bf16[48,16,768]{2,1,0:T(8,128)(2,1)}, u32[]{:S(2)}) copy-start(bf16[48,16,768]{2,1,0:T(8,128)(2,1)} %param.19) | copy-start | bytes 3538948
  2.4 17.0 %collective-permute-start = (bf16[3,32,384]{2,1,0:T(8,128)(2,1)}, bf16[3,32,384]{2,1,0:T(8,128)(2,1)}, u32[]{:S(2)}, u32[]{:S(2)}) collective-permute-start(bf16[3,32,384]{2,1,0:T(8,128)(2,1)} %get-tuple-element.21), channel_id=1, source_target_pairs={{0,16},{16,32},{32,48},{48,64},{64,80},{80,96},{96,112},{1,17},{17... | collective-permute-start | bytes 221192 | tf_op jit(solution)/shard_map/ppermute | solution.py:25
  4.3 16.5 %collective-permute-start.1 = (bf16[3,32,384]{2,1,0:T(8,128)(2,1)}, bf16[3,32,384]{2,1,0:T(8,128)(2,1)}, u32[]{:S(2)}, u32[]{:S(2)}) collective-permute-start(bf16[3,32,384]{2,1,0:T(8,128)(2,1)} %get-tuple-element.20), channel_id=1, source_target_pairs={{16,0},{32,16},{48,32},{64,48},{80,64},{96,80},{112,96},{17,1},{33... | collective-permute-start | bytes 221192 | tf_op jit(solution)/shard_map/ppermute | solution.py:27
  11.1 5.1 %copy-start.9 = (bf16[1,2,384,768]{3,2,1,0:T(8,128)(2,1)}, bf16[1,2,384,768]{3,2,1,0:T(8,128)(2,1)S(1)}, u32[]{:S(2)}) copy-start(bf16[1,2,384,768]{3,2,1,0:T(8,128)(2,1)S(1)} %get-tuple-element.18) | copy-start | bytes 3538948
  11.1 5.1 %copy-start.11 = (bf16[1,2,384,768]{3,2,1,0:T(8,128)(2,1)}, bf16[1,2,384,768]{3,2,1,0:T(8,128)(2,1)S(1)}, u32[]{:S(2)}) copy-start(bf16[1,2,384,768]{3,2,1,0:T(8,128)(2,1)S(1)} %get-tuple-element.19) | copy-start | bytes 3538948
  11.1 2.6 %copy-start.18 = (bf16[48,16,768]{2,1,0:T(8,128)(2,1)S(1)}, bf16[48,16,768]{2,1,0:T(8,128)(2,1)}, u32[]{:S(2)}) copy-start(bf16[48,16,768]{2,1,0:T(8,128)(2,1)} %param.19) | copy-start | bytes 3538948
  13.6 2.6 %copy-start.13 = (s32[1,16,16]{2,1,0:T(8,128)S(1)}, s32[1,16,16]{2,1,0:T(8,128)}, u32[]{:S(2)}) copy-start(s32[1,16,16]{2,1,0:T(8,128)} %param.16) | copy-start | bytes 3076
  13.6 6.7 %copy-start.7 = (bf16[96,32,384]{2,1,0:T(8,128)(2,1)S(1)}, bf16[96,32,384]{2,1,0:T(8,128)(2,1)}, u32[]{:S(2)}) copy-start(bf16[96,32,384]{2,1,0:T(8,128)(2,1)} %param.10) | copy-start | bytes 7077892
  19.4 12.3 %copy-start.14 = (s32[12,4]{0,1:T(4,128)S(1)}, s32[12,4]{0,1:T(4,128)}, u32[]{:S(2)}) copy-start(s32[12,4]{0,1:T(4,128)} %param.17) | copy-start | bytes 580
  19.4 12.3 %copy-start.15 = (s32[12,4]{0,1:T(4,128)S(1)}, s32[12,4]{0,1:T(4,128)}, u32[]{:S(2)}) copy-start(s32[12,4]{0,1:T(4,128)} %param.15) | copy-start | bytes 580
  19.4 12.3 %copy-start.16 = (s32[12,4]{0,1:T(4,128)S(1)}, s32[12,4]{0,1:T(4,128)}, u32[]{:S(2)}) copy-start(s32[12,4]{0,1:T(4,128)} %param.18) | copy-start | bytes 580
  21.7 1.5 copy-start.6
  23.5 23.5 %collective-permute-start.2 = (bf16[102,3,384]{2,1,0:T(4,128)(2,1)S(1)}, bf16[102,3,384]{2,1,0:T(4,128)(2,1)S(1)}, u32[]{:S(2)}, u32[]{:S(2)}) collective-permute-start(bf16[102,3,384]{2,1,0:T(4,128)(2,1)S(1)} %get-tuple-element.12), channel_id=1, source_target_pairs={{0,1},{1,2},{2,3},{3,4},{4,5},{5,6},{6,7},{7,8},{8,9},{9,10},{10,1... | collective-permute-start | bytes 705032 | tf_op jit(solution)/shard_map/ppermute | solution.py:25
  27.3 19.7 %collective-permute-start.3 = (bf16[102,3,384]{2,1,0:T(4,128)(2,1)S(1)}, bf16[102,3,384]{2,1,0:T(4,128)(2,1)S(1)}, u32[]{:S(2)}, u32[]{:S(2)}) collective-permute-start(bf16[102,3,384]{2,1,0:T(4,128)(2,1)S(1)} %get-tuple-element.13), channel_id=1, source_target_pairs={{1,0},{2,1},{3,2},{4,3},{5,4},{6,5},{7,6},{8,7},{9,8},{10,9},{11,1... | collective-permute-start | bytes 705032 | tf_op jit(solution)/shard_map/ppermute | solution.py:27
  74.1 3.0 %copy-start.2 = (bf16[96,32,384]{2,1,0:T(8,128)(2,1)S(1)}, bf16[96,32,384]{2,1,0:T(8,128)(2,1)}, u32[]{:S(2)}) copy-start(bf16[96,32,384]{2,1,0:T(8,128)(2,1)} %shard_map.113) | copy-start | bytes 7077892
  76.4 0.6 copy-start.12
  85.9 5.1 %copy-start.8 = (bf16[96,32,384]{2,1,0:T(8,128)(2,1)S(1)}, bf16[96,32,384]{2,1,0:T(8,128)(2,1)}, u32[]{:S(2)}) copy-start(bf16[96,32,384]{2,1,0:T(8,128)(2,1)} %param.10) | copy-start | bytes 7077892
  85.9 5.1 %copy-start.19 = (bf16[1536,384]{1,0:T(8,128)(2,1)S(1)}, bf16[1536,384]{1,0:T(8,128)(2,1)}, u32[]{:S(2)}) copy-start(bf16[1536,384]{1,0:T(8,128)(2,1)} %param.13) | copy-start | bytes 3538948
  91.0 8.3 %copy-start.3 = (f32[3072,1536]{1,0:T(8,128)}, f32[3072,1536]{1,0:T(8,128)S(1)}, u32[]{:S(2)}) copy-start(f32[3072,1536]{1,0:T(8,128)S(1)} %fusion.28) | copy-start | bytes 56623108
  91.0 9.4 %slice-start = ((s8[4718592]{0:T(1024)(128)(4,1)}), s8[4194304]{0:T(1024)(128)(4,1)S(1)}, s32[]{:S(2)}) async-start(s8[4718592]{0:T(1024)(128)(4,1)} %bitcast.64), calls=%async_computation | async-start | bytes 8388608
  91.1 9.4 %slice-start.1 = ((s8[4718592]{0:T(1024)(128)(4,1)}), s8[524288]{0:T(1024)(128)(4,1)S(1)}, s32[]{:S(2)}) async-start(s8[4718592]{0:T(1024)(128)(4,1)} %bitcast.64), calls=%async_computation.1 | async-start | bytes 1048576
  135.7 1.4 copy-start.4
  137.8 11.9 %collective-permute-start.4 = (bf16[3,32,384]{2,1,0:T(8,128)(2,1)}, bf16[3,32,384]{2,1,0:T(8,128)(2,1)}, u32[]{:S(2)}, u32[]{:S(2)}) collective-permute-start(bf16[3,32,384]{2,1,0:T(8,128)(2,1)} %bitcast.13), channel_id=1, source_target_pairs={{0,16},{16,32},{32,48},{48,64},{64,80},{80,96},{96,112},{1,17},{17... | collective-permute-start | bytes 221192 | tf_op jit(solution)/shard_map/ppermute | solution.py:25
  139.7 10.0 %collective-permute-start.5 = (bf16[3,32,384]{2,1,0:T(8,128)(2,1)}, bf16[3,32,384]{2,1,0:T(8,128)(2,1)}, u32[]{:S(2)}, u32[]{:S(2)}) collective-permute-start(bf16[3,32,384]{2,1,0:T(8,128)(2,1)} %bitcast.15), channel_id=1, source_target_pairs={{16,0},{32,16},{48,32},{64,48},{80,64},{96,80},{112,96},{17,1},{33... | collective-permute-start | bytes 221192 | tf_op jit(solution)/shard_map/ppermute | solution.py:27
  147.1 2.6 %copy-start.5 = (bf16[3072,384]{1,0:T(8,128)(2,1)S(1)}, bf16[3072,384]{1,0:T(8,128)(2,1)}, u32[]{:S(2)}) copy-start(bf16[3072,384]{1,0:T(8,128)(2,1)} %copy-done.4) | copy-start | bytes 7077892
  147.1 11.5 %copy-start.10 = (bf16[1,2,384,768]{3,2,1,0:T(8,128)(2,1)S(1)}, bf16[1,2,384,768]{3,2,1,0:T(8,128)(2,1)}, u32[]{:S(2)}) copy-start(bf16[1,2,384,768]{3,2,1,0:T(8,128)(2,1)} %copy-done.9) | copy-start | bytes 3538948
  150.7 13.2 %collective-permute-start.6 = (bf16[102,3,384]{2,1,0:T(4,128)(2,1)S(1)}, bf16[102,3,384]{2,1,0:T(4,128)(2,1)S(1)}, u32[]{:S(2)}, u32[]{:S(2)}) collective-permute-start(bf16[102,3,384]{2,1,0:T(4,128)(2,1)S(1)} %get-tuple-element.10), channel_id=1, source_target_pairs={{0,1},{1,2},{2,3},{3,4},{4,5},{5,6},{6,7},{7,8},{8,9},{9,10},{10,1... | collective-permute-start | bytes 705032 | tf_op jit(solution)/shard_map/ppermute | solution.py:25
  152.6 12.4 %collective-permute-start.7 = (bf16[102,3,384]{2,1,0:T(4,128)(2,1)S(1)}, bf16[102,3,384]{2,1,0:T(4,128)(2,1)S(1)}, u32[]{:S(2)}, u32[]{:S(2)}) collective-permute-start(bf16[102,3,384]{2,1,0:T(4,128)(2,1)S(1)} %get-tuple-element.11), channel_id=1, source_target_pairs={{1,0},{2,1},{3,2},{4,3},{5,4},{6,5},{7,6},{8,7},{9,8},{10,9},{11,1... | collective-permute-start | bytes 705032 | tf_op jit(solution)/shard_map/ppermute | solution.py:27
  171.0 22.4 %copy-start.1 = (bf16[384,1536]{1,0:T(8,128)(2,1)S(1)}, bf16[384,1536]{1,0:T(8,128)(2,1)}, u32[]{:S(2)}) copy-start(bf16[384,1536]{1,0:T(8,128)(2,1)} %param.12) | copy-start | bytes 3538948

commit v3 on v2

--- a/solution.py
+++ b/solution.py
@@ -127,6 +127,52 @@
         & (rank < quota)
         & (tile_slot < LIVE_DEV)
     )
+
+
+def mlp_forward_kernel(mixed_ref, image_ref, live_ref, w_in_ref, w_out_ref, summed_ref, low_ref):
+    normed, _ = normalize(mixed_ref[...].astype(jnp.float32))
+    hidden = jnp.dot(normed.astype(jnp.bfloat16), w_in_ref[...], preferred_element_type=jnp.float32)
+    cdf = 0.5 * (1.0 + lax.erf(hidden * ROOT_HALF))
+    activated = (hidden * cdf).astype(jnp.bfloat16)
+    branch = jnp.dot(activated, w_out_ref[...], preferred_element_type=jnp.float32)
+    branch = jnp.where(live_ref[...] > 0, branch.astype(jnp.bfloat16).astype(jnp.float32), 0.0)
+    summed = (image_ref[...].astype(jnp.float32) + branch).astype(jnp.bfloat16)
+    summed_ref[...] = summed
+    down_normed, _ = normalize(summed.astype(jnp.float32))
+    low_ref[...] = down_normed.astype(jnp.bfloat16)
+
+
+def mlp_backward_kernel(
+    mixed_ref, summed_ref, grad_ref, live_ref, w_in_ref, w_out_ref, grad_summed_ref, grad_mixed_ref
+):
+    normed, inv_std = normalize(mixed_ref[...].astype(jnp.float32))
+    hidden = jnp.dot(normed.astype(jnp.bfloat16), w_in_ref[...], preferred_element_type=jnp.float32)
+    cdf = 0.5 * (1.0 + lax.erf(hidden * ROOT_HALF))
+    slope = cdf + hidden * INV_ROOT_TAU * jnp.exp(-0.5 * hidden * hidden)
+    down_normed, down_inv = normalize(summed_ref[...].astype(jnp.float32))
+    grad_summed = normalize_back(grad_ref[...], down_normed, down_inv).astype(jnp.bfloat16)
+    grad_summed_ref[...] = grad_summed
+    grad_hidden = (times_transposed(grad_summed, w_out_ref[...]) * slope).astype(jnp.bfloat16)
+    grad_norm_in = times_transposed(grad_hidden, w_in_ref[...])
+    grad_owned_mixed = normalize_back(grad_norm_in, normed, inv_std)
+    grad_mixed_ref[...] = jnp.where(live_ref[...] > 0, grad_owned_mixed, 0.0).astype(jnp.bfloat16)
+
+
+def pixel_call(kernel, operands, widths, outputs, block=256):
+    pixels = operands[0].shape[0]
+    specs = []
+    for operand, blocked in zip(operands, widths):
+        if blocked:
+            specs.append(pl.BlockSpec((block, operand.shape[1]), lambda i: (i, 0)))
+        else:
+            specs.append(pl.BlockSpec(operand.shape, lambda i: (0, 0)))
+    return pl.pallas_call(
+        kernel,
+        grid=(pixels // block,),
+        in_specs=specs,
+        out_specs=[pl.BlockSpec((block, width), lambda i: (i, 0)) for width, _ in outputs],
+        out_shape=[jax.ShapeDtypeStruct((pixels, width), dtype) for width, dtype in outputs],
+    )(*operands)
 
 
 def on_device(
@@ -156,15 +202,15 @@
     ).reshape(pixels, 1)
     padded = with_halo(image, (("row", 0), ("col", 1)), reach)
     mixed = depthwise(padded, depth_kernel, height, breadth)
-    normed, inv_std = normalize(mixed.reshape(pixels, channels).astype(jnp.float32))
-    hidden = jnp.dot(normed.astype(jnp.bfloat16), weight_in, preferred_element_type=jnp.float32)
-    cdf = 0.5 * (1.0 + jax.scipy.special.erf(hidden * ROOT_HALF))
-    activated = (hidden * cdf).astype(jnp.bfloat16)
-    branch = jnp.dot(activated, weight_out, preferred_element_type=jnp.float32).astype(jnp.bfloat16)
-    branch_px = jnp.where(live_px, branch.astype(jnp.float32), 0.0)
-    summed = (image.reshape(pixels, channels).astype(jnp.float32) + branch_px).astype(jnp.bfloat16)
-    down_normed, down_inv = normalize(summed.astype(jnp.float32))
-    down_low = down_normed.astype(jnp.bfloat16).reshape(height // 2, 2, breadth // 2, 2 * channels)
+    live_px = live_px.astype(jnp.float32)
+    mixed = mixed.reshape(pixels, channels)
+    summed, down_low = pixel_call(
+        mlp_forward_kernel,
+        (mixed, image.reshape(pixels, channels), live_px, weight_in, weight_out),
+        (True, True, True, False, False),
+        ((channels, jnp.bfloat16), (channels, jnp.bfloat16)),
+    )
+    down_low = down_low.reshape(height // 2, 2, breadth // 2, 2 * channels)
     weight_pair = weight_down.reshape(2, 2 * channels, outputs)
     reduced = jnp.dot(down_low[:, 0], weight_pair[0], preferred_element_type=jnp.float32) + jnp.dot(
         down_low[:, 1], weight_pair[1], preferred_element_type=jnp.float32
@@ -177,12 +223,12 @@
         for a in range(2)
     ]
     grad_normed = jnp.stack(grad_pair, axis=1).reshape(pixels, channels)
-    grad_summed = normalize_back(grad_normed, down_normed, down_inv).astype(jnp.bfloat16)
-    slope = cdf + hidden * INV_ROOT_TAU * jnp.exp(-0.5 * hidden * hidden)
-    grad_hidden = (times_transposed(grad_summed, weight_out) * slope).astype(jnp.bfloat16)
-    grad_norm_in = times_transposed(grad_hidden, weight_in)
-    grad_owned_mixed = normalize_back(grad_norm_in, normed, inv_std).astype(jnp.bfloat16)
-    grad_mixed = jnp.where(live_px, grad_owned_mixed, jnp.zeros_like(grad_owned_mixed))
+    grad_summed, grad_mixed = pixel_call(
+        mlp_backward_kernel,
+        (mixed, summed, grad_normed, live_px, weight_in, weight_out),
+        (True, True, True, True, False, False),
+        ((channels, jnp.bfloat16), (channels, jnp.bfloat16)),
+    )
     grad_padded = with_halo(grad_mixed.reshape(height, breadth, channels), (("row", 0), ("col", 1)), reach)
     grad_image = depthwise(
         grad_padded, depth_kernel[::-1, ::-1, :], height, breadth, base=grad_summed.reshape(height, breadth, channels)

time: 195 us -> 184 us (0.944)
  Pallas kernels: 44.1 us -> 88.7 us
  matrix products: 43.8 us -> 9.56 us
  other arithmetic: 42.2 us -> 16 us
  waiting for transfers between devices: 4.3 us -> 10.2 us
    pallas_call x0 -> x2, Pallas kernels: none -> 44.7 us  [pixel_call(): pl.pallas_call(kernel, grid=(pixels // block,), in_specs=specs, out_specs...]
    dot_general x3 -> x0, matrix products: 34.1 us -> none  [the longest x1 20.8 us: times_transposed(): lax.dot_general(left, right, (((1,), (1,)), ((), ())), preferred_element_...]
    reduce_sum x4 -> x0, other arithmetic: 8.09 us -> none  [the longest x2 3.1 us: normalize(): jnp.mean(centered * centered, axis=-1, keepdims=True) + EPSILON]
    convert_element_type x2 -> x1, other arithmetic: 7.25 us -> 0.01 us  [on_device(): live_px = live_px.astype(jnp.float32)]
    select_n x1 -> x0, other arithmetic: 6.09 us -> none  [on_device(): jnp.where(live_px, grad_owned_mixed, jnp.zeros_like(grad_owned_mixed))]
    ppermute x4, waiting for transfers between devices: 3.11 us -> 6.93 us  [with_halo(): lax.ppermute(tail, axis, [(i, (i + 1) % count) for i in range(ends)])]
    unnamed x47 -> x31, local copies, waits for them, and re-layouts: 5.77 us -> 2.96 us
    convert_element_type x0 -> x2, local copies, waits for them, and re-layouts: none -> 2.72 us  [on_device(): live_px = live_px.astype(jnp.float32)]
  transfers between devices with their start and end apart: 8 -> 8, of which waited for: 2 -> 3; matrix products, arithmetic and copies ran while one was open for 19% -> 20% of each run, Pallas kernels for 0% -> 0%
where the time goes in v3:
time: 184 us; the launch traced here: 183 us
  Pallas kernels  88.7 us (48%)
  local copies, waits for them, and re-layouts  31.2 us (17%)
  starting transfers between devices  26.2 us (14%)
  other arithmetic  16 us (9%)
  waiting for transfers between devices  10.2 us (6%)
  matrix products  9.56 us (5%)
    pallas_call x2, Pallas kernels, pixel_call(): pl.pallas_call(kernel, grid=(pixels // block,), in_specs=specs, out_specs...  44.7 us
    pallas_call x2, Pallas kernels, depthwise(): pl.pallas_call(lambda *refs: depthwise_kernel(*refs, reach=reach, chunk=c...  44 us
    ppermute x4, starting transfers between devices, with_halo(): lax.ppermute(head, axis, [((i + 1) % count, i) for i in range(ends)])  17.7 us
    concatenate x2, other arithmetic, with_halo(): jnp.concatenate([lax.ppermute(tail, axis, [(i, (i + 1) % count) for i in...  10.7 us
    ppermute x4, starting transfers between devices, with_halo(): lax.ppermute(tail, axis, [(i, (i + 1) % count) for i in range(ends)])  8.47 us
    ppermute x4, waiting for transfers between devices, with_halo(): lax.ppermute(tail, axis, [(i, (i + 1) % count) for i in range(ends)])  6.93 us
    reshape x1, local copies, waits for them, and re-layouts, on_device(): grad_normed = jnp.stack(grad_pair, axis=1).reshape(pixels, channels)  5.96 us
    dot_general x2, matrix products, on_device(): lax.dot_general(cotangent, weight_pair[a], (((2,), (1,)), ((), ())), pref...  5.07 us
  transfers between devices with their start and end apart: 8, of which 3 were waited for; matrix products, arithmetic and copies ran while one was open for 20% of the time, Pallas kernels for 0%

profile of v3, /device:TPU:26, one launch (start us, length us, event | category | flops | bytes accessed | tf_op | source)
XLA Modules:
  0.0 182.7 jit_solution(4575321835414403547)
XLA Ops:
  0.6 0.0 copy-start
  0.6 1.7 fusion.4
  2.3 1.9 %collective-permute-start = (bf16[3,32,384]{2,1,0:T(8,128)(2,1)}, bf16[3,32,384]{2,1,0:T(8,128)(2,1)}, u32[]{:S(2)}, u32[]{:S(2)}) collective-permute-start(bf16[3,32,384]{2,1,0:T(8,128)(2,1)} %get-tuple-element.23), channel_id=1, source_target_pairs={{0,16},{16,32},{32,48},{48,64},{64,80},{80,96},{96,112},{1,17},{17... | collective-permute-start | bytes 221192 | tf_op jit(solution)/shard_map/ppermute | solution.py:25
  4.3 3.6 %collective-permute-start.1 = (bf16[3,32,384]{2,1,0:T(8,128)(2,1)}, bf16[3,32,384]{2,1,0:T(8,128)(2,1)}, u32[]{:S(2)}, u32[]{:S(2)}) collective-permute-start(bf16[3,32,384]{2,1,0:T(8,128)(2,1)} %get-tuple-element.22), channel_id=1, source_target_pairs={{16,0},{32,16},{48,32},{64,48},{80,64},{96,80},{112,96},{17,1},{33... | collective-permute-start | bytes 221192 | tf_op jit(solution)/shard_map/ppermute | solution.py:27
  7.9 0.0 copy-start.10
  7.9 2.8 %fusion.3 = (bf16[1,2,384,768]{3,2,1,0:T(8,128)(2,1)S(1)}, bf16[1,2,384,768]{3,2,1,0:T(8,128)(2,1)}) fusion(bf16[2,2,384,768]{3,2,1,0:T(8,128)(2,1)} %param.14), kind=kLoop, calls=%fused_computation.24 | loop fusion | bytes 4718592 | tf_op jit(solution)/shard_map/slice | solution.py:216
  10.7 0.5 iota_compare_fusion.1
  11.2 0.1 copy.34
  11.3 2.5 %convolution_bitcast_fusion = f32[48,1,16,768]{3,2,0,1:T(8,128)} fusion(bf16[48,16,768]{2,1,0:T(8,128)(2,1)S(1)} %copy-done, bf16[768,768,1]{1,0,2:T(8,128)(2,1)S(1)} %bitcast.43), kind=kOutput, calls=%fused_computation.4 | convolution fusion | flops 905969664 | bytes 4718592 | tf_op jit(solution)/shard_map/dot_general | solution.py:220
  13.9 0.0 copy-done.7
  13.9 2.6 %convolution_bitcast_fusion.1 = f32[48,1,16,768]{3,2,0,1:T(8,128)} fusion(bf16[48,16,768]{2,1,0:T(8,128)(2,1)S(1)} %copy-done, bf16[768,768,1]{1,0,2:T(8,128)(2,1)S(1)} %bitcast.46), kind=kOutput, calls=%fused_computation.5 | convolution fusion | flops 905969664 | bytes 4718592 | tf_op jit(solution)/shard_map/dot_general | solution.py:220
  16.4 0.6 reduce_window_sum.11
  17.0 0.8 select_reduce_fusion.3
  17.8 1.1 select_reduce_fusion.1
  19.0 0.8 copy.36
  19.7 0.1 copy.35
  19.8 0.0 collective-permute-done
  19.8 0.9 constant_dynamic-update-slice_fusion.2
  20.7 0.0 copy-start.11
  20.8 0.0 copy-start.12
  20.8 0.0 copy-start.13
  20.8 0.5 constant_dynamic-update-slice_fusion.1
  21.3 0.0 copy-start.4
  21.3 0.0 collective-permute-done.1
  21.3 1.1 constant_dynamic-update-slice_fusion
  22.3 1.4 copy-done.3
  23.8 1.1 fusion.1
  24.9 6.1 %collective-permute-start.3 = (bf16[102,3,384]{2,1,0:T(4,128)(2,1)}, bf16[102,3,384]{2,1,0:T(4,128)(2,1)}, u32[]{:S(2)}, u32[]{:S(2)}) collective-permute-start(bf16[102,3,384]{2,1,0:T(4,128)(2,1)} %get-tuple-element.17), channel_id=1, source_target_pairs={{1,0},{2,1},{3,2},{4,3},{5,4},{6,5},{7,6},{8,7},{9,8},{10,9},{11,1... | collective-permute-start | bytes 705032 | tf_op jit(solution)/shard_map/ppermute | solution.py:27
  31.0 1.9 %collective-permute-start.2 = (bf16[102,3,384]{2,1,0:T(4,128)(2,1)}, bf16[102,3,384]{2,1,0:T(4,128)(2,1)}, u32[]{:S(2)}, u32[]{:S(2)}) collective-permute-start(bf16[102,3,384]{2,1,0:T(4,128)(2,1)} %get-tuple-element.16), channel_id=1, source_target_pairs={{0,1},{1,2},{2,3},{3,4},{4,5},{5,6},{6,7},{7,8},{8,9},{9,10},{10,1... | collective-permute-start | bytes 705032 | tf_op jit(solution)/shard_map/ppermute | solution.py:25
  32.9 0.0 copy-done.11
  32.9 0.0 copy-done.12
  32.9 0.0 copy-done.13
  33.0 1.5 reshape.63.refs_1_
  34.4 2.1 %rev.3 = bf16[7,7,384]{2,1,0:T(8,128)(2,1)} reverse(bf16[7,7,384]{2,1,0:T(8,128)(2,1)} %param.11), dimensions={0,1} | reverse | bytes 75264 | tf_op jit(solution)/shard_map/rev | solution.py:234
  36.5 0.1 copy.37
  36.6 0.8 broadcast_in_dim.51
  37.4 2.6 %convert_element_type.27.live_ref = f32[3072,1]{1,0:T(8,128)} reshape(f32[12,8,4,8]{3,2,1,0:T(4,128)} %broadcast_in_dim.51) | data formatting | bytes 24576 | tf_op jit(solution)/shard_map/convert_element_type | solution.py:205
  40.0 0.0 copy-done.4
  40.0 2.0 %pad_maximum_fusion = f32[48,2,16,768]{3,2,0,1:T(8,128)S(1)} fusion(f32[48,1,16,768]{3,2,0,1:T(8,128)S(1)} %copy-done.4, f32[48,1,16,768]{3,2,0,1:T(8,128)} %convolution_bitcast_fusion.1), kind=kLoop, calls=%fused_computation | loop fusion | flops 1179648 | bytes 9437184 | tf_op jit(solution)/shard_map/stack | solution.py:225
  42.0 2.6 %copy.41 = f32[48,2,16,768]{3,2,1,0:T(8,128)} copy(f32[48,2,16,768]{3,2,0,1:T(8,128)S(1)} %pad_maximum_fusion) | data formatting | bytes 9437184 | tf_op jit(solution)/shard_map/stack | solution.py:225
  44.6 6.0 %reshape.60.grad_ref = f32[3072,384]{1,0:T(8,128)} reshape(f32[48,2,16,768]{3,2,1,0:T(8,128)} %copy.41) | data formatting | bytes 9437184 | tf_op jit(solution)/shard_map/reshape | solution.py:225
  50.6 0.6 reshape.64.refs_1_
  51.2 0.0 collective-permute-done.3
  51.2 0.0 collective-permute-done.2
  51.2 5.4 %pad_maximum_fusion.1.refs_0_ = bf16[102,38,384]{2,1,0:T(8,128)(2,1)} fusion(bf16[102,3,384]{2,1,0:T(4,128)(2,1)} %collective-permute-done.3, bf16[102,32,384]{2,1,0:T(8,128)(2,1)} %copy-done.3, bf16[102,3,384]{2,1,0:T(4,128)(2,1)} %collective-permute-done.2), kind=kLoop, calls=%fused_computation.1 | loop fusion | flops 8930304 | bytes 5953536 | tf_op jit(solution)/shard_map/concatenate | solution.py:23
  56.6 21.7 %shard_map.113 = bf16[96,32,384]{2,1,0:T(8,128)(2,1)} custom-call(bf16[102,38,384]{2,1,0:T(8,128)(2,1)} %pad_maximum_fusion.1.refs_0_, f32[49,384]{1,0:T(8,128)} %reshape.63.refs_1_), custom_call_target="tpu_custom_call" | custom-call | tf_op jit(solution)/shard_map/pallas_call | solution.py:78
  78.4 19.9 %shard_map.114 = (bf16[3072,384]{1,0:T(8,128)(2,1)}, bf16[3072,384]{1,0:T(8,128)(2,1)}) custom-call(bf16[3072,384]{1,0:T(8,128)(2,1)} %bitcast.37, bf16[3072,384]{1,0:T(8,128)(2,1)} %bitcast.41, f32[3072,1]{1,0:T(8,128)} %convert_element_type.27.live_ref, bf16[384,1536]{1,0:T(8,128)(2,1)} %w_in_ref.3, bf16[1536,384]{1,0:T(8,128)(2,1)} %w_out_ref.3), custom_call_target="tpu_custom_call" | custom-call | tf_op jit(solution)/shard_map/pallas_call | solution.py:169
  98.3 3.5 %reshape.59 = bf16[48,2,16,768]{3,2,1,0:T(8,128)(2,1)S(1)} reshape(bf16[3072,384]{1,0:T(8,128)(2,1)} %get-tuple-element.6) | data formatting | bytes 4718592 | tf_op jit(solution)/shard_map/reshape | solution.py:213
  101.8 24.8 %shard_map.115 = (bf16[3072,384]{1,0:T(8,128)(2,1)}, bf16[3072,384]{1,0:T(8,128)(2,1)}) custom-call(bf16[3072,384]{1,0:T(8,128)(2,1)} %bitcast.38, bf16[3072,384]{1,0:T(8,128)(2,1)} %get-tuple-element.7.summed_ref, f32[3072,384]{1,0:T(8,128)} %reshape.60.grad_ref, f32[3072,1]{1,0:T(8,128)} %convert_element_type.27.live_ref, bf16[384,1536]{1,0:T(8,128)(2,1)} %w_in_ref.3, ...), custom_call_target="tpu_custom_call" | custom-call | tf_op jit(solution)/shard_map/pallas_call | solution.py:169
  126.6 0.9 fusion.2
  127.5 1.9 %collective-permute-start.5 = (bf16[3,32,384]{2,1,0:T(8,128)(2,1)S(1)}, bf16[3,32,384]{2,1,0:T(8,128)(2,1)S(1)}, u32[]{:S(2)}, u32[]{:S(2)}) collective-permute-start(bf16[3,32,384]{2,1,0:T(8,128)(2,1)S(1)} %bitcast.48), channel_id=1, source_target_pairs={{16,0},{32,16},{48,32},{64,48},{80,64},{96,80},{112,96},{17,1},{33... | collective-permute-start | bytes 221192 | tf_op jit(solution)/shard_map/ppermute | solution.py:27
  129.4 2.7 %collective-permute-start.4 = (bf16[3,32,384]{2,1,0:T(8,128)(2,1)S(1)}, bf16[3,32,384]{2,1,0:T(8,128)(2,1)S(1)}, u32[]{:S(2)}, u32[]{:S(2)}) collective-permute-start(bf16[3,32,384]{2,1,0:T(8,128)(2,1)S(1)} %bitcast.47), channel_id=1, source_target_pairs={{0,16},{16,32},{32,48},{48,64},{64,80},{80,96},{96,112},{1,17},{17... | collective-permute-start | bytes 221192 | tf_op jit(solution)/shard_map/ppermute | solution.py:25
  132.2 2.4 %fusion = f32[48,16,768]{2,1,0:T(8,128)S(1)} fusion(bf16[768,768,1]{1,0,2:T(8,128)(2,1)} %bitcast.45, bf16[48,2,16,768]{3,2,1,0:T(8,128)(2,1)S(1)} %reshape.59), kind=kOutput, calls=%fused_computation.8 | convolution fusion | flops 905969664 | bytes 4718592 | tf_op jit(solution)/shard_map/dot_general | solution.py:215
  134.5 0.0 collective-permute-done.5
  134.5 0.7 collective-permute-done.4
  135.2 0.0 copy-done.1
  135.2 0.2 pad_maximum_fusion.5
  135.5 6.0 %collective-permute-start.7 = (bf16[102,3,384]{2,1,0:T(4,128)(2,1)S(1)}, bf16[102,3,384]{2,1,0:T(4,128)(2,1)S(1)}, u32[]{:S(2)}, u32[]{:S(2)}) collective-permute-start(bf16[102,3,384]{2,1,0:T(4,128)(2,1)S(1)} %get-tuple-element.15), channel_id=1, source_target_pairs={{1,0},{2,1},{3,2},{4,3},{5,4},{6,5},{7,6},{8,7},{9,8},{10,9},{11,1... | collective-permute-start | bytes 705032 | tf_op jit(solution)/shard_map/ppermute | solution.py:27
  141.5 1.9 %collective-permute-start.6 = (bf16[102,3,384]{2,1,0:T(4,128)(2,1)S(1)}, bf16[102,3,384]{2,1,0:T(4,128)(2,1)S(1)}, u32[]{:S(2)}, u32[]{:S(2)}) collective-permute-start(bf16[102,3,384]{2,1,0:T(4,128)(2,1)S(1)} %get-tuple-element.14), channel_id=1, source_target_pairs={{0,1},{1,2},{2,3},{3,4},{4,5},{5,6},{6,7},{7,8},{8,9},{9,10},{10,1... | collective-permute-start | bytes 705032 | tf_op jit(solution)/shard_map/ppermute | solution.py:25
  143.5 2.1 %add_convert_fusion = bf16[48,16,768]{2,1,0:T(8,128)(2,1)} fusion(f32[48,16,768]{2,1,0:T(8,128)S(1)} %fusion, bf16[768,768,1]{1,0,2:T(8,128)(2,1)S(1)} %bitcast.44, bf16[48,2,16,768]{3,2,1,0:T(8,128)(2,1)S(1)} %reshape.59), kind=kOutput, calls=%fused_computation.3 | convolution fusion | flops 907149312 | bytes 5898240 | tf_op jit(solution)/shard_map/dot_general | solution.py:215
  145.6 3.3 %collective-permute-done.7 = bf16[102,3,384]{2,1,0:T(4,128)(2,1)S(1)} collective-permute-done((bf16[102,3,384]{2,1,0:T(4,128)(2,1)S(1)}, bf16[102,3,384]{2,1,0:T(4,128)(2,1)S(1)}, u32[]{:S(2)}, u32[]{:S(2)}) %collective-permute-start.7) | collective-permute-done | bytes 235040 | tf_op jit(solution)/shard_map/ppermute | solution.py:27
  148.9 6.2 %collective-permute-done.6 = bf16[102,3,384]{2,1,0:T(4,128)(2,1)S(1)} collective-permute-done((bf16[102,3,384]{2,1,0:T(4,128)(2,1)S(1)}, bf16[102,3,384]{2,1,0:T(4,128)(2,1)S(1)}, u32[]{:S(2)}, u32[]{:S(2)}) %collective-permute-start.6) | collective-permute-done | bytes 235040 | tf_op jit(solution)/shard_map/ppermute | solution.py:25
  155.1 5.3 %pad_maximum_fusion.2.refs_0_ = bf16[102,38,384]{2,1,0:T(8,128)(2,1)} fusion(bf16[102,3,384]{2,1,0:T(4,128)(2,1)S(1)} %collective-permute-done.7, bf16[3,32,384]{2,1,0:T(8,128)(2,1)S(1)} %collective-permute-done.5, bf16[96,32,384]{2,1,0:T(8,128)(2,1)S(1)} %bitcast.40, bf16[3,32,384]{2,1,0:T(8,128)(2,1)S(1)} %collective-permute-done.4, ...), kind=kLoop, calls=%fused_computation.2 | loop fusion | flops 14883840 | bytes 5953536 | tf_op jit(solution)/shard_map/concatenate | solution.py:23
  160.4 22.3 %shard_map.116 = bf16[96,32,384]{2,1,0:T(8,128)(2,1)} custom-call(bf16[102,38,384]{2,1,0:T(8,128)(2,1)} %pad_maximum_fusion.2.refs_0_, f32[49,384]{1,0:T(8,128)} %reshape.64.refs_1_, bf16[96,32,384]{2,1,0:T(8,128)(2,1)} %bitcast.42), custom_call_target="tpu_custom_call" | custom-call | tf_op jit(solution)/shard_map/pallas_call | solution.py:78
  (16 shorter events, 0.0 us)
Async XLA Ops:
  0.6 10.7 %copy-start = (bf16[48,16,768]{2,1,0:T(8,128)(2,1)S(1)}, bf16[48,16,768]{2,1,0:T(8,128)(2,1)}, u32[]{:S(2)}) copy-start(bf16[48,16,768]{2,1,0:T(8,128)(2,1)} %param.19) | copy-start | bytes 3538948
  2.3 17.5 %collective-permute-start = (bf16[3,32,384]{2,1,0:T(8,128)(2,1)}, bf16[3,32,384]{2,1,0:T(8,128)(2,1)}, u32[]{:S(2)}, u32[]{:S(2)}) collective-permute-start(bf16[3,32,384]{2,1,0:T(8,128)(2,1)} %get-tuple-element.23), channel_id=1, source_target_pairs={{0,16},{16,32},{32,48},{48,64},{64,80},{80,96},{96,112},{1,17},{17... | collective-permute-start | bytes 221192 | tf_op jit(solution)/shard_map/ppermute | solution.py:25
  4.3 17.0 %collective-permute-start.1 = (bf16[3,32,384]{2,1,0:T(8,128)(2,1)}, bf16[3,32,384]{2,1,0:T(8,128)(2,1)}, u32[]{:S(2)}, u32[]{:S(2)}) collective-permute-start(bf16[3,32,384]{2,1,0:T(8,128)(2,1)} %get-tuple-element.22), channel_id=1, source_target_pairs={{16,0},{32,16},{48,32},{64,48},{80,64},{96,80},{112,96},{17,1},{33... | collective-permute-start | bytes 221192 | tf_op jit(solution)/shard_map/ppermute | solution.py:27
  7.9 3.3 %copy-start.10 = (s32[12,4]{0,1:T(4,128)S(1)}, s32[12,4]{0,1:T(4,128)}, u32[]{:S(2)}) copy-start(s32[12,4]{0,1:T(4,128)} %param.17) | copy-start | bytes 580
  10.7 3.1 %copy-start.5 = (bf16[1,2,384,768]{3,2,1,0:T(8,128)(2,1)}, bf16[1,2,384,768]{3,2,1,0:T(8,128)(2,1)S(1)}, u32[]{:S(2)}) copy-start(bf16[1,2,384,768]{3,2,1,0:T(8,128)(2,1)S(1)} %get-tuple-element.20) | copy-start | bytes 3538948
  11.3 2.5 %copy-start.7 = (bf16[1,2,384,768]{3,2,1,0:T(8,128)(2,1)S(1)}, bf16[1,2,384,768]{3,2,1,0:T(8,128)(2,1)}, u32[]{:S(2)}) copy-start(bf16[1,2,384,768]{3,2,1,0:T(8,128)(2,1)} %get-tuple-element.21) | copy-start | bytes 3538948
  13.9 2.6 %copy-start.9 = (s32[1,16,16]{2,1,0:T(8,128)S(1)}, s32[1,16,16]{2,1,0:T(8,128)}, u32[]{:S(2)}) copy-start(s32[1,16,16]{2,1,0:T(8,128)} %param.16) | copy-start | bytes 3076
  13.9 6.9 %copy-start.2 = (bf16[96,32,384]{2,1,0:T(8,128)(2,1)S(1)}, bf16[96,32,384]{2,1,0:T(8,128)(2,1)}, u32[]{:S(2)}) copy-start(bf16[96,32,384]{2,1,0:T(8,128)(2,1)} %param.10) | copy-start | bytes 7077892
  20.7 12.2 %copy-start.11 = (s32[12,4]{0,1:T(4,128)S(1)}, s32[12,4]{0,1:T(4,128)}, u32[]{:S(2)}) copy-start(s32[12,4]{0,1:T(4,128)} %param.17) | copy-start | bytes 580
  20.8 12.2 %copy-start.12 = (s32[12,4]{0,1:T(4,128)S(1)}, s32[12,4]{0,1:T(4,128)}, u32[]{:S(2)}) copy-start(s32[12,4]{0,1:T(4,128)} %param.15) | copy-start | bytes 580
  20.8 12.2 %copy-start.13 = (s32[12,4]{0,1:T(4,128)S(1)}, s32[12,4]{0,1:T(4,128)}, u32[]{:S(2)}) copy-start(s32[12,4]{0,1:T(4,128)} %param.18) | copy-start | bytes 580
  21.3 18.7 %copy-start.4 = (f32[48,1,16,768]{3,2,0,1:T(8,128)S(1)}, f32[48,1,16,768]{3,2,0,1:T(8,128)}, u32[]{:S(2)}) copy-start(f32[48,1,16,768]{3,2,0,1:T(8,128)} %convolution_bitcast_fusion) | copy-start | bytes 7077892
  22.3 1.4 copy-start.3
  24.9 26.4 %collective-permute-start.3 = (bf16[102,3,384]{2,1,0:T(4,128)(2,1)}, bf16[102,3,384]{2,1,0:T(4,128)(2,1)}, u32[]{:S(2)}, u32[]{:S(2)}) collective-permute-start(bf16[102,3,384]{2,1,0:T(4,128)(2,1)} %get-tuple-element.17), channel_id=1, source_target_pairs={{1,0},{2,1},{3,2},{4,3},{5,4},{6,5},{7,6},{8,7},{9,8},{10,9},{11,1... | collective-permute-start | bytes 705032 | tf_op jit(solution)/shard_map/ppermute | solution.py:27
  31.0 20.2 %collective-permute-start.2 = (bf16[102,3,384]{2,1,0:T(4,128)(2,1)}, bf16[102,3,384]{2,1,0:T(4,128)(2,1)}, u32[]{:S(2)}, u32[]{:S(2)}) collective-permute-start(bf16[102,3,384]{2,1,0:T(4,128)(2,1)} %get-tuple-element.16), channel_id=1, source_target_pairs={{0,1},{1,2},{2,3},{3,4},{4,5},{5,6},{6,7},{7,8},{8,9},{9,10},{10,1... | collective-permute-start | bytes 705032 | tf_op jit(solution)/shard_map/ppermute | solution.py:25
  44.6 6.0 %copy-start.8 = (bf16[7,7,384]{2,1,0:T(8,128)(2,1)S(1)}, bf16[7,7,384]{2,1,0:T(8,128)(2,1)}, u32[]{:S(2)}) copy-start(bf16[7,7,384]{2,1,0:T(8,128)(2,1)} %rev.3) | copy-start | bytes 112900
  127.5 7.0 %collective-permute-start.5 = (bf16[3,32,384]{2,1,0:T(8,128)(2,1)S(1)}, bf16[3,32,384]{2,1,0:T(8,128)(2,1)S(1)}, u32[]{:S(2)}, u32[]{:S(2)}) collective-permute-start(bf16[3,32,384]{2,1,0:T(8,128)(2,1)S(1)} %bitcast.48), channel_id=1, source_target_pairs={{16,0},{32,16},{48,32},{64,48},{80,64},{96,80},{112,96},{17,1},{33... | collective-permute-start | bytes 221192 | tf_op jit(solution)/shard_map/ppermute | solution.py:27
  129.4 5.8 %copy-start.1 = (bf16[3072,384]{1,0:T(8,128)(2,1)S(1)}, bf16[3072,384]{1,0:T(8,128)(2,1)}, u32[]{:S(2)}) copy-start(bf16[3072,384]{1,0:T(8,128)(2,1)} %get-tuple-element.8) | copy-start | bytes 7077892
  129.4 5.8 %collective-permute-start.4 = (bf16[3,32,384]{2,1,0:T(8,128)(2,1)S(1)}, bf16[3,32,384]{2,1,0:T(8,128)(2,1)S(1)}, u32[]{:S(2)}, u32[]{:S(2)}) collective-permute-start(bf16[3,32,384]{2,1,0:T(8,128)(2,1)S(1)} %bitcast.47), channel_id=1, source_target_pairs={{0,16},{16,32},{32,48},{48,64},{64,80},{80,96},{96,112},{1,17},{17... | collective-permute-start | bytes 221192 | tf_op jit(solution)/shard_map/ppermute | solution.py:25
  134.5 8.9 %copy-start.6 = (bf16[1,2,384,768]{3,2,1,0:T(8,128)(2,1)S(1)}, bf16[1,2,384,768]{3,2,1,0:T(8,128)(2,1)}, u32[]{:S(2)}) copy-start(bf16[1,2,384,768]{3,2,1,0:T(8,128)(2,1)} %copy-done.5) | copy-start | bytes 3538948
  135.5 13.4 %collective-permute-start.7 = (bf16[102,3,384]{2,1,0:T(4,128)(2,1)S(1)}, bf16[102,3,384]{2,1,0:T(4,128)(2,1)S(1)}, u32[]{:S(2)}, u32[]{:S(2)}) collective-permute-start(bf16[102,3,384]{2,1,0:T(4,128)(2,1)S(1)} %get-tuple-element.15), channel_id=1, source_target_pairs={{1,0},{2,1},{3,2},{4,3},{5,4},{6,5},{7,6},{8,7},{9,8},{10,9},{11,1... | collective-permute-start | bytes 705032 | tf_op jit(solution)/shard_map/ppermute | solution.py:27
  141.5 13.6 %collective-permute-start.6 = (bf16[102,3,384]{2,1,0:T(4,128)(2,1)S(1)}, bf16[102,3,384]{2,1,0:T(4,128)(2,1)S(1)}, u32[]{:S(2)}, u32[]{:S(2)}) collective-permute-start(bf16[102,3,384]{2,1,0:T(4,128)(2,1)S(1)} %get-tuple-element.14), channel_id=1, source_target_pairs={{0,1},{1,2},{2,3},{3,4},{4,5},{5,6},{6,7},{7,8},{8,9},{9,10},{10,1... | collective-permute-start | bytes 705032 | tf_op jit(solution)/shard_map/ppermute | solution.py:25

commit v4 on v3

--- a/solution.py
+++ b/solution.py
@@ -14,33 +14,36 @@
 INV_ROOT_TAU = 0.3989422804014327
 
 
-def with_halo(cells, sides, width):
-    for axis, dim in sides:
-        count = lax.axis_size(axis)
-        ends = count - 1
-        head = lax.slice_in_dim(cells, 0, width, axis=dim)
-        tail = lax.slice_in_dim(cells, cells.shape[dim] - width, cells.shape[dim], axis=dim)
-        cells = jnp.concatenate(
-            [
-                lax.ppermute(tail, axis, [(i, (i + 1) % count) for i in range(ends)]),
-                cells,
-                lax.ppermute(head, axis, [((i + 1) % count, i) for i in range(ends)]),
-            ],
-            axis=dim,
-        )
-    return cells
-
-
-def depthwise_kernel(x_ref, k_ref, *rest, reach, chunk):
-    if len(rest) == 4:
-        base_ref, out_ref, shifted_ref, total_ref = rest
+def halo_pieces(cells, width):
+    rows = lax.axis_size("row")
+    cols = lax.axis_size("col")
+    down = [(i, i + 1) for i in range(rows - 1)]
+    up = [(i + 1, i) for i in range(rows - 1)]
+    top = lax.ppermute(cells[cells.shape[0] - width :], "row", down)
+    bottom = lax.ppermute(cells[:width], "row", up)
+    framed = jnp.concatenate([top, cells, bottom], axis=0)
+    left = lax.ppermute(framed[:, cells.shape[1] - width :], "col", [(i, i + 1) for i in range(cols - 1)])
+    right = lax.ppermute(framed[:, :width], "col", [(i + 1, i) for i in range(cols - 1)])
+    return (cells, top, bottom, left, right)
+
+
+def depthwise_kernel(
+    image_ref, top_ref, bottom_ref, left_ref, right_ref, k_ref, *rest, reach, chunk, flip
+):
+    if len(rest) == 5:
+        base_ref, out_ref, framed_ref, shifted_ref, total_ref = rest
     else:
         base_ref = None
-        out_ref, shifted_ref, total_ref = rest
+        out_ref, framed_ref, shifted_ref, total_ref = rest
     height, breadth, _ = out_ref.shape
     side = 2 * reach + 1
+    framed_ref[reach : reach + height, reach : reach + breadth, :] = image_ref[...].astype(jnp.float32)
+    framed_ref[:reach, reach : reach + breadth, :] = top_ref[...].astype(jnp.float32)
+    framed_ref[reach + height :, reach : reach + breadth, :] = bottom_ref[...].astype(jnp.float32)
+    framed_ref[:, :reach, :] = left_ref[...].astype(jnp.float32)
+    framed_ref[:, reach + breadth :, :] = right_ref[...].astype(jnp.float32)
     for shift_c in range(side):
-        shifted_ref[...] = x_ref[:, shift_c : shift_c + breadth, :].astype(jnp.float32)
+        shifted_ref[...] = framed_ref[:, shift_c : shift_c + breadth, :]
 
         def body(step, carry, shift_c=shift_c):
             start = pl.multiple_of(step * chunk, chunk)
@@ -51,7 +54,11 @@
             else:
                 total = jnp.zeros((chunk, breadth, out_ref.shape[2]), jnp.float32)
             for shift_r in range(side):
-                tap = k_ref[pl.ds(shift_r * side + shift_c, 1), :]
+                if flip:
+                    index = (side - 1 - shift_r) * side + (side - 1 - shift_c)
+                else:
+                    index = shift_r * side + shift_c
+                tap = k_ref[pl.ds(index, 1), :]
                 total = total + shifted_ref[pl.ds(start + shift_r, chunk)] * tap[None]
             if shift_c == side - 1:
                 out_ref[pl.ds(start, chunk)] = total.astype(out_ref.dtype)
@@ -62,27 +69,31 @@
         lax.fori_loop(0, height // chunk, body, 0)
 
 
-def depthwise(padded, kernel, height, breadth, base=None, lanes=128, chunk=8):
-    side = kernel.shape[0]
-    reach = side // 2
-    channels = padded.shape[2]
-    taps = kernel.reshape(side * side, channels).astype(jnp.float32)
+def depthwise(pieces, taps, reach, base=None, flip=False, lanes=128, chunk=8):
+    image = pieces[0]
+    height, breadth, channels = image.shape
+    framed = (height + 2 * reach, breadth + 2 * reach)
     in_specs = [
-        pl.BlockSpec((height + 2 * reach, breadth + 2 * reach, lanes), lambda c: (0, 0, c)),
-        pl.BlockSpec((side * side, lanes), lambda c: (0, c)),
+        pl.BlockSpec((height, breadth, lanes), lambda c: (0, 0, c)),
+        pl.BlockSpec((reach, breadth, lanes), lambda c: (0, 0, c)),
+        pl.BlockSpec((reach, breadth, lanes), lambda c: (0, 0, c)),
+        pl.BlockSpec((framed[0], reach, lanes), lambda c: (0, 0, c)),
+        pl.BlockSpec((framed[0], reach, lanes), lambda c: (0, 0, c)),
+        pl.BlockSpec((taps.shape[0], lanes), lambda c: (0, c)),
     ]
-    operands = [padded, taps]
+    operands = list(pieces) + [taps]
     if base is not None:
         in_specs.append(pl.BlockSpec((height, breadth, lanes), lambda c: (0, 0, c)))
         operands.append(base)
     return pl.pallas_call(
-        lambda *refs: depthwise_kernel(*refs, reach=reach, chunk=chunk),
+        lambda *refs: depthwise_kernel(*refs, reach=reach, chunk=chunk, flip=flip),
         grid=(channels // lanes,),
         in_specs=in_specs,
         out_specs=pl.BlockSpec((height, breadth, lanes), lambda c: (0, 0, c)),
         out_shape=jax.ShapeDtypeStruct((height, breadth, channels), jnp.bfloat16),
         scratch_shapes=[
-            pltpu.VMEM((height + 2 * reach, breadth, lanes), jnp.float32),
+            pltpu.VMEM((framed[0], framed[1], lanes), jnp.float32),
+            pltpu.VMEM((framed[0], breadth, lanes), jnp.float32),
             pltpu.VMEM((height, breadth, lanes), jnp.float32),
         ],
     )(*operands)
@@ -129,13 +140,13 @@
     )
 
 
-def mlp_forward_kernel(mixed_ref, image_ref, live_ref, w_in_ref, w_out_ref, summed_ref, low_ref):
+def mlp_forward_kernel(live, mixed_ref, image_ref, w_in_ref, w_out_ref, summed_ref, low_ref, *, layout):
     normed, _ = normalize(mixed_ref[...].astype(jnp.float32))
     hidden = jnp.dot(normed.astype(jnp.bfloat16), w_in_ref[...], preferred_element_type=jnp.float32)
     cdf = 0.5 * (1.0 + lax.erf(hidden * ROOT_HALF))
     activated = (hidden * cdf).astype(jnp.bfloat16)
     branch = jnp.dot(activated, w_out_ref[...], preferred_element_type=jnp.float32)
-    branch = jnp.where(live_ref[...] > 0, branch.astype(jnp.bfloat16).astype(jnp.float32), 0.0)
+    branch = jnp.where(pixel_live(live, layout), branch.astype(jnp.bfloat16).astype(jnp.float32), 0.0)
     summed = (image_ref[...].astype(jnp.float32) + branch).astype(jnp.bfloat16)
     summed_ref[...] = summed
     down_normed, _ = normalize(summed.astype(jnp.float32))
@@ -143,7 +154,7 @@
 
 
 def mlp_backward_kernel(
-    mixed_ref, summed_ref, grad_ref, live_ref, w_in_ref, w_out_ref, grad_summed_ref, grad_mixed_ref
+    live, mixed_ref, summed_ref, grad_ref, w_in_ref, w_out_ref, grad_summed_ref, grad_mixed_ref, *, layout
 ):
     normed, inv_std = normalize(mixed_ref[...].astype(jnp.float32))
     hidden = jnp.dot(normed.astype(jnp.bfloat16), w_in_ref[...], preferred_element_type=jnp.float32)
@@ -155,24 +166,39 @@
     grad_hidden = (times_transposed(grad_summed, w_out_ref[...]) * slope).astype(jnp.bfloat16)
     grad_norm_in = times_transposed(grad_hidden, w_in_ref[...])
     grad_owned_mixed = normalize_back(grad_norm_in, normed, inv_std)
-    grad_mixed_ref[...] = jnp.where(live_ref[...] > 0, grad_owned_mixed, 0.0).astype(jnp.bfloat16)
-
-
-def pixel_call(kernel, operands, widths, outputs, block=256):
+    grad_mixed_ref[...] = jnp.where(pixel_live(live, layout), grad_owned_mixed, 0.0).astype(jnp.bfloat16)
+
+
+def pixel_live(live, layout):
+    block, breadth, tile_side, tile_cols = layout
+    place = lax.broadcasted_iota(jnp.int32, (block, 1), 0)
+    tile = (place % breadth) // tile_side
+    first = pl.program_id(0) * tile_cols
+    flag = jnp.zeros((block, 1), jnp.int32)
+    for column in range(tile_cols):
+        flag = jnp.where(tile == column, live[first + column], flag)
+    return flag > 0
+
+
+def pixel_call(kernel, live, operands, widths, outputs, layout):
+    block = layout[0]
     pixels = operands[0].shape[0]
     specs = []
     for operand, blocked in zip(operands, widths):
         if blocked:
-            specs.append(pl.BlockSpec((block, operand.shape[1]), lambda i: (i, 0)))
+            specs.append(pl.BlockSpec((block, operand.shape[1]), lambda i, live: (i, 0)))
         else:
-            specs.append(pl.BlockSpec(operand.shape, lambda i: (0, 0)))
+            specs.append(pl.BlockSpec(operand.shape, lambda i, live: (0, 0)))
     return pl.pallas_call(
-        kernel,
-        grid=(pixels // block,),
-        in_specs=specs,
-        out_specs=[pl.BlockSpec((block, width), lambda i: (i, 0)) for width, _ in outputs],
+        lambda *refs: kernel(*refs, layout=layout),
+        grid_spec=pltpu.PrefetchScalarGridSpec(
+            num_scalar_prefetch=1,
+            grid=(pixels // block,),
+            in_specs=specs,
+            out_specs=[pl.BlockSpec((block, width), lambda i, live: (i, 0)) for width, _ in outputs],
+        ),
         out_shape=[jax.ShapeDtypeStruct((pixels, width), dtype) for width, dtype in outputs],
-    )(*operands)
+    )(live, *operands)
 
 
 def on_device(
@@ -197,18 +223,18 @@
     pixels = height * breadth
     routed = routed_tiles(tile_counts, tile_owner, tile_slot, peer_count, capacity)
     live = routed & (tissue_mask != 0)
-    live_px = jnp.broadcast_to(
-        live[:, None, :, None], (tile_rows, tile_side, tile_cols, tile_side)
-    ).reshape(pixels, 1)
-    padded = with_halo(image, (("row", 0), ("col", 1)), reach)
-    mixed = depthwise(padded, depth_kernel, height, breadth)
-    live_px = live_px.astype(jnp.float32)
+    live = live.reshape(-1).astype(jnp.int32)
+    layout = (tile_side * breadth, breadth, tile_side, tile_cols)
+    taps = depth_kernel.reshape(KS * KS, channels).astype(jnp.float32)
+    mixed = depthwise(halo_pieces(image, reach), taps, reach)
     mixed = mixed.reshape(pixels, channels)
     summed, down_low = pixel_call(
         mlp_forward_kernel,
-        (mixed, image.reshape(pixels, channels), live_px, weight_in, weight_out),
-        (True, True, True, False, False),
+        live,
+        (mixed, image.reshape(pixels, channels), weight_in, weight_out),
+        (True, True, False, False),
         ((channels, jnp.bfloat16), (channels, jnp.bfloat16)),
+        layout,
     )
     down_low = down_low.reshape(height // 2, 2, breadth // 2, 2 * channels)
     weight_pair = weight_down.reshape(2, 2 * channels, outputs)
@@ -225,13 +251,18 @@
     grad_normed = jnp.stack(grad_pair, axis=1).reshape(pixels, channels)
     grad_summed, grad_mixed = pixel_call(
         mlp_backward_kernel,
-        (mixed, summed, grad_normed, live_px, weight_in, weight_out),
-        (True, True, True, True, False, False),
+        live,
+        (mixed, summed, grad_normed, weight_in, weight_out),
+        (True, True, True, False, False),
         ((channels, jnp.bfloat16), (channels, jnp.bfloat16)),
-    )
-    grad_padded = with_halo(grad_mixed.reshape(height, breadth, channels), (("row", 0), ("col", 1)), reach)
+        layout,
+    )
     grad_image = depthwise(
-        grad_padded, depth_kernel[::-1, ::-1, :], height, breadth, base=grad_summed.reshape(height, breadth, channels)
+        halo_pieces(grad_mixed.reshape(height, breadth, channels), reach),
+        taps,
+        reach,
+        base=grad_summed.reshape(height, breadth, channels),
+        flip=True,
     )
     return (reduced, grad_image)
 

time: 184 us -> 165 us (0.90)
  other arithmetic: 16 us -> 6.09 us
  local copies, waits for them, and re-layouts: 31.2 us -> 24.7 us
  waiting for transfers between devices: 10.2 us -> 5.47 us
    concatenate x2 -> x1, other arithmetic: 10.7 us -> 0.25 us  [halo_pieces(): framed = jnp.concatenate([top, cells, bottom], axis=0)]
    ppermute x8, waiting for transfers between devices: 10.2 us -> 5.47 us  [the longest x2 4.18 us: halo_pieces(): lax.ppermute(framed[:, cells.shape[1] - width:], 'col', [(i, i + 1) for i...]
    convert_element_type x4 -> x3, local copies, waits for them, and re-layouts: 4.82 us -> 2.19 us  [the longest x1 1.44 us: on_device(): taps = depth_kernel.reshape(KS * KS, channels).astype(jnp.float32)]
    rev x1 -> x0, local copies, waits for them, and re-layouts: 2.07 us -> none  [on_device(): depth_kernel[::-1, ::-1, :]]
  transfers between devices with their start and end apart: 8 -> 8, of which waited for: 3 -> 2; matrix products, arithmetic and copies ran while one was open for 20% -> 19% of each run, Pallas kernels for 0% -> 0%
where the time goes in v4:
time: 165 us; the launch traced here: 164 us
  Pallas kernels  89.5 us (54%)
  starting transfers between devices  27.4 us (17%)
  local copies, waits for them, and re-layouts  24.7 us (15%)
  matrix products  9.54 us (6%)
  other arithmetic  6.09 us (4%)
  waiting for transfers between devices  5.47 us (3%)
    pallas_call x2, Pallas kernels, pixel_call(): pl.pallas_call(lambda *refs: kernel(*refs, layout=layout), grid_spec=pltp...  45.3 us
    pallas_call x2, Pallas kernels, depthwise(): pl.pallas_call(lambda *refs: depthwise_kernel(*refs, reach=reach, chunk=c...  44.2 us
    ppermute x2, starting transfers between devices, halo_pieces(): lax.ppermute(framed[:, :width], 'col', [(i + 1, i) for i in range(cols -...  10.3 us
    ppermute x2, starting transfers between devices, halo_pieces(): bottom = lax.ppermute(cells[:width], 'row', up)  7.42 us
    reshape x1, local copies, waits for them, and re-layouts, on_device(): grad_normed = jnp.stack(grad_pair, axis=1).reshape(pixels, channels)  5.94 us
    ppermute x2, starting transfers between devices, halo_pieces(): lax.ppermute(framed[:, cells.shape[1] - width:], 'col', [(i, i + 1) for i...  5.88 us
    dot_general x2, matrix products, on_device(): lax.dot_general(cotangent, weight_pair[a], (((2,), (1,)), ((), ())), pref...  5.07 us
    ppermute x2, waiting for transfers between devices, halo_pieces(): lax.ppermute(framed[:, cells.shape[1] - width:], 'col', [(i, i + 1) for i...  4.18 us
  transfers between devices with their start and end apart: 8, of which 2 were waited for; matrix products, arithmetic and copies ran while one was open for 19% of the time, Pallas kernels for 0%

profile of v4, /device:TPU:26, one launch (start us, length us, event | category | flops | bytes accessed | tf_op | source)
XLA Modules:
  0.0 163.7 jit_solution(8012287689304529404)
XLA Ops:
  0.6 0.0 copy-start
  0.6 1.7 %fusion.4 = (bf16[3,32,384]{2,1,0:T(8,128)(2,1)}, bf16[3,32,384]{2,1,0:T(8,128)(2,1)}) fusion(bf16[96,32,384]{2,1,0:T(8,128)(2,1)} %refs_0_.1), kind=kLoop, calls=%fused_computation.23 | loop fusion | bytes 294912 | tf_op jit(solution)/shard_map/slice | solution.py:23
  2.3 1.9 %collective-permute-start = (bf16[3,32,384]{2,1,0:T(8,128)(2,1)}, bf16[3,32,384]{2,1,0:T(8,128)(2,1)}, u32[]{:S(2)}, u32[]{:S(2)}) collective-permute-start(bf16[3,32,384]{2,1,0:T(8,128)(2,1)} %get-tuple-element.23), channel_id=1, source_target_pairs={{0,16},{16,32},{32,48},{48,64},{64,80},{80,96},{96,112},{1,17},{17... | collective-permute-start | bytes 221192 | tf_op jit(solution)/shard_map/ppermute | solution.py:22
  4.3 3.6 %collective-permute-start.1 = (bf16[3,32,384]{2,1,0:T(8,128)(2,1)}, bf16[3,32,384]{2,1,0:T(8,128)(2,1)}, u32[]{:S(2)}, u32[]{:S(2)}) collective-permute-start(bf16[3,32,384]{2,1,0:T(8,128)(2,1)} %get-tuple-element.22), channel_id=1, source_target_pairs={{16,0},{32,16},{48,32},{64,48},{80,64},{96,80},{112,96},{17,1},{33... | collective-permute-start | bytes 221192 | tf_op jit(solution)/shard_map/ppermute | solution.py:23
  7.9 0.0 copy-start.11
  7.9 2.8 %fusion.3 = (bf16[1,2,384,768]{3,2,1,0:T(8,128)(2,1)S(1)}, bf16[1,2,384,768]{3,2,1,0:T(8,128)(2,1)}) fusion(bf16[2,2,384,768]{3,2,1,0:T(8,128)(2,1)} %param.14), kind=kLoop, calls=%fused_computation.22 | loop fusion | bytes 4718592 | tf_op jit(solution)/shard_map/slice | solution.py:242
  10.7 0.6 iota_compare_fusion.1
  11.3 0.0 copy-done.11
  11.3 0.1 copy.30
  11.4 0.0 copy-done
  11.4 2.5 %convolution_bitcast_fusion = f32[48,1,16,768]{3,2,0,1:T(8,128)} fusion(bf16[48,16,768]{2,1,0:T(8,128)(2,1)S(1)} %copy-done, bf16[768,768,1]{1,0,2:T(8,128)(2,1)S(1)} %bitcast.43), kind=kOutput, calls=%fused_computation.2 | convolution fusion | flops 905969664 | bytes 4718592 | tf_op jit(solution)/shard_map/dot_general | solution.py:246
  13.9 0.0 copy-done.3
  13.9 0.0 copy-done.5
  13.9 2.6 %convolution_bitcast_fusion.1 = f32[48,1,16,768]{3,2,0,1:T(8,128)} fusion(bf16[48,16,768]{2,1,0:T(8,128)(2,1)S(1)} %copy-done, bf16[768,768,1]{1,0,2:T(8,128)(2,1)S(1)} %bitcast.46), kind=kOutput, calls=%fused_computation.3 | convolution fusion | flops 905969664 | bytes 4718592 | tf_op jit(solution)/shard_map/dot_general | solution.py:246
  16.5 0.0 copy-done.10
  16.5 0.6 reduce_window_sum.11
  17.1 0.8 select_reduce_fusion.3
  17.9 1.2 select_reduce_fusion.1
  19.1 0.8 copy.32
  19.8 0.1 copy.31
  19.9 0.0 collective-permute-done.refs_1_
  19.9 0.9 constant_dynamic-update-slice_fusion.2
  20.8 0.0 copy-done.1
  20.8 0.0 copy-start.12
  20.8 0.0 copy-start.13
  20.8 0.0 copy-start.14
  20.9 0.5 constant_dynamic-update-slice_fusion.1
  21.3 0.0 collective-permute-done.1.refs_2_
  21.4 0.9 constant_dynamic-update-slice_fusion
  22.3 0.2 fusion.1
  22.5 3.8 %collective-permute-start.2 = (bf16[102,3,384]{2,1,0:T(4,128)(2,1)S(1)}, bf16[102,3,384]{2,1,0:T(4,128)(2,1)S(1)}, u32[]{:S(2)}, u32[]{:S(2)}) collective-permute-start(bf16[102,3,384]{2,1,0:T(4,128)(2,1)S(1)} %get-tuple-element.17), channel_id=1, source_target_pairs={{0,1},{1,2},{2,3},{3,4},{4,5},{5,6},{6,7},{7,8},{8,9},{9,10},{10,1... | collective-permute-start | bytes 705032 | tf_op jit(solution)/shard_map/ppermute | solution.py:25
  26.3 4.2 %collective-permute-start.3 = (bf16[102,3,384]{2,1,0:T(4,128)(2,1)S(1)}, bf16[102,3,384]{2,1,0:T(4,128)(2,1)S(1)}, u32[]{:S(2)}, u32[]{:S(2)}) collective-permute-start(bf16[102,3,384]{2,1,0:T(4,128)(2,1)S(1)} %get-tuple-element.16), channel_id=1, source_target_pairs={{1,0},{2,1},{3,2},{4,3},{5,4},{6,5},{7,6},{8,7},{9,8},{10,9},{11,1... | collective-permute-start | bytes 705032 | tf_op jit(solution)/shard_map/ppermute | solution.py:26
  30.6 0.0 copy-done.12
  30.6 0.0 copy-done.13
  30.6 0.1 copy.33
  30.7 0.7 reshape.48.refs_0_
  31.4 1.4 reshape.49.refs_5_
  32.8 2.7 %pad_maximum_fusion = f32[48,2,16,768]{3,2,0,1:T(8,128)S(1)} fusion(f32[48,1,16,768]{3,2,0,1:T(8,128)} %convolution_bitcast_fusion, f32[48,1,16,768]{3,2,0,1:T(8,128)} %convolution_bitcast_fusion.1), kind=kLoop, calls=%fused_computation | loop fusion | flops 1179648 | bytes 9437184 | tf_op jit(solution)/shard_map/stack | solution.py:251
  35.5 2.6 %copy.36 = f32[48,2,16,768]{3,2,1,0:T(8,128)} copy(f32[48,2,16,768]{3,2,0,1:T(8,128)S(1)} %pad_maximum_fusion) | data formatting | bytes 9437184 | tf_op jit(solution)/shard_map/stack | solution.py:251
  38.1 5.9 %reshape.45.refs_3_ = f32[3072,384]{1,0:T(8,128)} reshape(f32[48,2,16,768]{3,2,1,0:T(8,128)} %copy.36) | data formatting | bytes 9437184 | tf_op jit(solution)/shard_map/reshape | solution.py:251
  44.1 0.0 collective-permute-done.2.refs_3_
  44.1 0.0 collective-permute-done.3.refs_4_
  44.1 0.7 copy-done.6
  44.8 0.7 copy-done.7
  45.6 21.8 %shard_map.113 = bf16[96,32,384]{2,1,0:T(8,128)(2,1)} custom-call(bf16[96,32,384]{2,1,0:T(8,128)(2,1)} %refs_0_.1, bf16[3,32,384]{2,1,0:T(8,128)(2,1)} %collective-permute-done.refs_1_, bf16[3,32,384]{2,1,0:T(8,128)(2,1)} %collective-permute-done.1.refs_2_, bf16[102,3,384]{2,1,0:T(4,128)(2,1)} %copy-done.6, bf16[102,3,384]{2,1,0:T(4,128)(2,1)} %copy-done.7, ...), custom_call_target="tpu_custom_call" | custom-call | tf_op jit(solution)/shard_map/pallas_call | solution.py:88
  67.4 20.3 %shard_map.114 = (bf16[3072,384]{1,0:T(8,128)(2,1)}, bf16[3072,384]{1,0:T(8,128)(2,1)}) custom-call(s32[48]{0:T(128)} %reshape.48.refs_0_, bf16[3072,384]{1,0:T(8,128)(2,1)} %bitcast.38, bf16[3072,384]{1,0:T(8,128)(2,1)} %bitcast.37, bf16[384,1536]{1,0:T(8,128)(2,1)} %refs_4_.3, bf16[1536,384]{1,0:T(8,128)(2,1)} %refs_5_.1), custom_call_target="tpu_custom_call" | custom-call | tf_op jit(solution)/shard_map/pallas_call | solution.py:192
  87.7 3.5 %reshape.44 = bf16[48,2,16,768]{3,2,1,0:T(8,128)(2,1)S(1)} reshape(bf16[3072,384]{1,0:T(8,128)(2,1)} %get-tuple-element.6) | data formatting | bytes 4718592 | tf_op jit(solution)/shard_map/reshape | solution.py:239
  91.2 25.0 %shard_map.115 = (bf16[3072,384]{1,0:T(8,128)(2,1)}, bf16[3072,384]{1,0:T(8,128)(2,1)}) custom-call(s32[48]{0:T(128)} %reshape.48.refs_0_, bf16[3072,384]{1,0:T(8,128)(2,1)} %bitcast.39, bf16[3072,384]{1,0:T(8,128)(2,1)} %get-tuple-element.7.refs_2_, f32[3072,384]{1,0:T(8,128)} %reshape.45.refs_3_, bf16[384,1536]{1,0:T(8,128)(2,1)} %refs_4_.3, ...), custom_call_target="tpu_custom_call" | custom-call | tf_op jit(solution)/shard_map/pallas_call | solution.py:192
  116.2 0.9 fusion.2
  117.2 1.9 %collective-permute-start.4 = (bf16[3,32,384]{2,1,0:T(8,128)(2,1)S(1)}, bf16[3,32,384]{2,1,0:T(8,128)(2,1)S(1)}, u32[]{:S(2)}, u32[]{:S(2)}) collective-permute-start(bf16[3,32,384]{2,1,0:T(8,128)(2,1)S(1)} %bitcast.48), channel_id=1, source_target_pairs={{0,16},{16,32},{32,48},{48,64},{64,80},{80,96},{96,112},{1,17},{17... | collective-permute-start | bytes 221192 | tf_op jit(solution)/shard_map/ppermute | solution.py:22
  119.1 3.8 %collective-permute-start.5 = (bf16[3,32,384]{2,1,0:T(8,128)(2,1)S(1)}, bf16[3,32,384]{2,1,0:T(8,128)(2,1)S(1)}, u32[]{:S(2)}, u32[]{:S(2)}) collective-permute-start(bf16[3,32,384]{2,1,0:T(8,128)(2,1)S(1)} %bitcast.47), channel_id=1, source_target_pairs={{16,0},{32,16},{48,32},{64,48},{80,64},{96,80},{112,96},{17,1},{33... | collective-permute-start | bytes 221192 | tf_op jit(solution)/shard_map/ppermute | solution.py:23
  122.9 2.4 %fusion = f32[48,16,768]{2,1,0:T(8,128)S(1)} fusion(bf16[768,768,1]{1,0,2:T(8,128)(2,1)} %bitcast.45, bf16[48,2,16,768]{3,2,1,0:T(8,128)(2,1)S(1)} %reshape.44), kind=kOutput, calls=%fused_computation.6 | convolution fusion | flops 905969664 | bytes 4718592 | tf_op jit(solution)/shard_map/dot_general | solution.py:241
  125.3 0.0 collective-permute-done.4.refs_1_
  125.3 0.0 collective-permute-done.5.refs_2_
  125.3 0.0 copy-start.9
  125.3 0.0 copy-done.2
  125.3 0.2 pad_maximum_fusion.1
  125.6 2.1 %collective-permute-start.6 = (bf16[102,3,384]{2,1,0:T(4,128)(2,1)S(1)}, bf16[102,3,384]{2,1,0:T(4,128)(2,1)}, u32[]{:S(2)}, u32[]{:S(2)}) collective-permute-start(bf16[102,3,384]{2,1,0:T(4,128)(2,1)S(1)} %get-tuple-element.15), channel_id=1, source_target_pairs={{0,1},{1,2},{2,3},{3,4},{4,5},{5,6},{6,7},{7,8},{8,9},{9,10},{10,1... | collective-permute-start | bytes 705032 | tf_op jit(solution)/shard_map/ppermute | solution.py:25
  127.6 6.0 %collective-permute-start.7 = (bf16[102,3,384]{2,1,0:T(4,128)(2,1)S(1)}, bf16[102,3,384]{2,1,0:T(4,128)(2,1)}, u32[]{:S(2)}, u32[]{:S(2)}) collective-permute-start(bf16[102,3,384]{2,1,0:T(4,128)(2,1)S(1)} %get-tuple-element.14), channel_id=1, source_target_pairs={{1,0},{2,1},{3,2},{4,3},{5,4},{6,5},{7,6},{8,7},{9,8},{10,9},{11,1... | collective-permute-start | bytes 705032 | tf_op jit(solution)/shard_map/ppermute | solution.py:26
  133.7 0.0 copy-done.4
  133.7 2.1 %add_convert_fusion = bf16[48,16,768]{2,1,0:T(8,128)(2,1)} fusion(f32[48,16,768]{2,1,0:T(8,128)S(1)} %fusion, bf16[768,768,1]{1,0,2:T(8,128)(2,1)S(1)} %bitcast.44, bf16[48,2,16,768]{3,2,1,0:T(8,128)(2,1)S(1)} %reshape.44), kind=kOutput, calls=%fused_computation.1 | convolution fusion | flops 907149312 | bytes 5898240 | tf_op jit(solution)/shard_map/dot_general | solution.py:241
  135.8 4.2 %collective-permute-done.6.refs_3_ = bf16[102,3,384]{2,1,0:T(4,128)(2,1)} collective-permute-done((bf16[102,3,384]{2,1,0:T(4,128)(2,1)S(1)}, bf16[102,3,384]{2,1,0:T(4,128)(2,1)}, u32[]{:S(2)}, u32[]{:S(2)}) %collective-permute-start.6) | collective-permute-done | bytes 235040 | tf_op jit(solution)/shard_map/ppermute | solution.py:25
  140.0 1.3 collective-permute-done.7.refs_4_
  141.3 22.4 %shard_map.116 = bf16[96,32,384]{2,1,0:T(8,128)(2,1)} custom-call(bf16[96,32,384]{2,1,0:T(8,128)(2,1)} %bitcast.40, bf16[3,32,384]{2,1,0:T(8,128)(2,1)} %copy-done.8, bf16[3,32,384]{2,1,0:T(8,128)(2,1)} %copy-done.9, bf16[102,3,384]{2,1,0:T(4,128)(2,1)} %collective-permute-done.6.refs_3_, bf16[102,3,384]{2,1,0:T(4,128)(2,1)} %collective-permute-done.7.refs_4_, ...), custom_call_target="tpu_custom_call" | custom-call | tf_op jit(solution)/shard_map/pallas_call | solution.py:88
  (13 shorter events, 0.0 us)
Async XLA Ops:
  0.6 10.8 %copy-start = (bf16[48,16,768]{2,1,0:T(8,128)(2,1)S(1)}, bf16[48,16,768]{2,1,0:T(8,128)(2,1)}, u32[]{:S(2)}) copy-start(bf16[48,16,768]{2,1,0:T(8,128)(2,1)} %param.19) | copy-start | bytes 3538948
  2.3 17.6 %collective-permute-start = (bf16[3,32,384]{2,1,0:T(8,128)(2,1)}, bf16[3,32,384]{2,1,0:T(8,128)(2,1)}, u32[]{:S(2)}, u32[]{:S(2)}) collective-permute-start(bf16[3,32,384]{2,1,0:T(8,128)(2,1)} %get-tuple-element.23), channel_id=1, source_target_pairs={{0,16},{16,32},{32,48},{48,64},{64,80},{80,96},{96,112},{1,17},{17... | collective-permute-start | bytes 221192 | tf_op jit(solution)/shard_map/ppermute | solution.py:22
  4.3 17.1 %collective-permute-start.1 = (bf16[3,32,384]{2,1,0:T(8,128)(2,1)}, bf16[3,32,384]{2,1,0:T(8,128)(2,1)}, u32[]{:S(2)}, u32[]{:S(2)}) collective-permute-start(bf16[3,32,384]{2,1,0:T(8,128)(2,1)} %get-tuple-element.22), channel_id=1, source_target_pairs={{16,0},{32,16},{48,32},{64,48},{80,64},{96,80},{112,96},{17,1},{33... | collective-permute-start | bytes 221192 | tf_op jit(solution)/shard_map/ppermute | solution.py:23
  7.9 3.4 %copy-start.11 = (s32[12,4]{0,1:T(4,128)S(1)}, s32[12,4]{0,1:T(4,128)}, u32[]{:S(2)}) copy-start(s32[12,4]{0,1:T(4,128)} %param.17) | copy-start | bytes 580
  10.7 3.2 %copy-start.3 = (bf16[1,2,384,768]{3,2,1,0:T(8,128)(2,1)}, bf16[1,2,384,768]{3,2,1,0:T(8,128)(2,1)S(1)}, u32[]{:S(2)}) copy-start(bf16[1,2,384,768]{3,2,1,0:T(8,128)(2,1)S(1)} %get-tuple-element.20) | copy-start | bytes 3538948
  11.4 2.5 %copy-start.5 = (bf16[1,2,384,768]{3,2,1,0:T(8,128)(2,1)S(1)}, bf16[1,2,384,768]{3,2,1,0:T(8,128)(2,1)}, u32[]{:S(2)}) copy-start(bf16[1,2,384,768]{3,2,1,0:T(8,128)(2,1)} %get-tuple-element.21) | copy-start | bytes 3538948
  13.9 2.6 %copy-start.10 = (s32[1,16,16]{2,1,0:T(8,128)S(1)}, s32[1,16,16]{2,1,0:T(8,128)}, u32[]{:S(2)}) copy-start(s32[1,16,16]{2,1,0:T(8,128)} %param.16) | copy-start | bytes 3076
  13.9 6.9 %copy-start.1 = (bf16[96,32,384]{2,1,0:T(8,128)(2,1)S(1)}, bf16[96,32,384]{2,1,0:T(8,128)(2,1)}, u32[]{:S(2)}) copy-start(bf16[96,32,384]{2,1,0:T(8,128)(2,1)} %refs_0_.1) | copy-start | bytes 7077892
  20.8 9.7 %copy-start.12 = (s32[12,4]{0,1:T(4,128)S(1)}, s32[12,4]{0,1:T(4,128)}, u32[]{:S(2)}) copy-start(s32[12,4]{0,1:T(4,128)} %param.17) | copy-start | bytes 580
  20.8 9.7 %copy-start.13 = (s32[12,4]{0,1:T(4,128)S(1)}, s32[12,4]{0,1:T(4,128)}, u32[]{:S(2)}) copy-start(s32[12,4]{0,1:T(4,128)} %param.15) | copy-start | bytes 580
  20.8 9.7 %copy-start.14 = (s32[12,4]{0,1:T(4,128)S(1)}, s32[12,4]{0,1:T(4,128)}, u32[]{:S(2)}) copy-start(s32[12,4]{0,1:T(4,128)} %param.18) | copy-start | bytes 580
  22.5 21.6 %collective-permute-start.2 = (bf16[102,3,384]{2,1,0:T(4,128)(2,1)S(1)}, bf16[102,3,384]{2,1,0:T(4,128)(2,1)S(1)}, u32[]{:S(2)}, u32[]{:S(2)}) collective-permute-start(bf16[102,3,384]{2,1,0:T(4,128)(2,1)S(1)} %get-tuple-element.17), channel_id=1, source_target_pairs={{0,1},{1,2},{2,3},{3,4},{4,5},{5,6},{6,7},{7,8},{8,9},{9,10},{10,1... | collective-permute-start | bytes 705032 | tf_op jit(solution)/shard_map/ppermute | solution.py:25
  26.3 17.7 %collective-permute-start.3 = (bf16[102,3,384]{2,1,0:T(4,128)(2,1)S(1)}, bf16[102,3,384]{2,1,0:T(4,128)(2,1)S(1)}, u32[]{:S(2)}, u32[]{:S(2)}) collective-permute-start(bf16[102,3,384]{2,1,0:T(4,128)(2,1)S(1)} %get-tuple-element.16), channel_id=1, source_target_pairs={{1,0},{2,1},{3,2},{4,3},{5,4},{6,5},{7,6},{8,7},{9,8},{10,9},{11,1... | collective-permute-start | bytes 705032 | tf_op jit(solution)/shard_map/ppermute | solution.py:26
  44.1 0.7 copy-start.6
  44.8 0.7 copy-start.7
  117.2 8.1 %collective-permute-start.4 = (bf16[3,32,384]{2,1,0:T(8,128)(2,1)S(1)}, bf16[3,32,384]{2,1,0:T(8,128)(2,1)S(1)}, u32[]{:S(2)}, u32[]{:S(2)}) collective-permute-start(bf16[3,32,384]{2,1,0:T(8,128)(2,1)S(1)} %bitcast.48), channel_id=1, source_target_pairs={{0,16},{16,32},{32,48},{48,64},{64,80},{80,96},{96,112},{1,17},{17... | collective-permute-start | bytes 221192 | tf_op jit(solution)/shard_map/ppermute | solution.py:22
  119.1 6.2 %copy-start.2 = (bf16[3072,384]{1,0:T(8,128)(2,1)S(1)}, bf16[3072,384]{1,0:T(8,128)(2,1)}, u32[]{:S(2)}) copy-start(bf16[3072,384]{1,0:T(8,128)(2,1)} %get-tuple-element.8) | copy-start | bytes 7077892
  119.1 6.2 %collective-permute-start.5 = (bf16[3,32,384]{2,1,0:T(8,128)(2,1)S(1)}, bf16[3,32,384]{2,1,0:T(8,128)(2,1)S(1)}, u32[]{:S(2)}, u32[]{:S(2)}) collective-permute-start(bf16[3,32,384]{2,1,0:T(8,128)(2,1)S(1)} %bitcast.47), channel_id=1, source_target_pairs={{16,0},{32,16},{48,32},{64,48},{80,64},{96,80},{112,96},{17,1},{33... | collective-permute-start | bytes 221192 | tf_op jit(solution)/shard_map/ppermute | solution.py:23
  125.2 8.4 %copy-start.4 = (bf16[1,2,384,768]{3,2,1,0:T(8,128)(2,1)S(1)}, bf16[1,2,384,768]{3,2,1,0:T(8,128)(2,1)}, u32[]{:S(2)}) copy-start(bf16[1,2,384,768]{3,2,1,0:T(8,128)(2,1)} %copy-done.3) | copy-start | bytes 3538948
  125.3 2.4 %copy-start.8 = (bf16[3,32,384]{2,1,0:T(8,128)(2,1)}, bf16[3,32,384]{2,1,0:T(8,128)(2,1)S(1)}, u32[]{:S(2)}) copy-start(bf16[3,32,384]{2,1,0:T(8,128)(2,1)S(1)} %collective-permute-done.4.refs_1_) | copy-start | bytes 221188
  125.3 2.3 %copy-start.9 = (bf16[3,32,384]{2,1,0:T(8,128)(2,1)}, bf16[3,32,384]{2,1,0:T(8,128)(2,1)S(1)}, u32[]{:S(2)}) copy-start(bf16[3,32,384]{2,1,0:T(8,128)(2,1)S(1)} %collective-permute-done.5.refs_2_) | copy-start | bytes 221188
  125.6 14.4 %collective-permute-start.6 = (bf16[102,3,384]{2,1,0:T(4,128)(2,1)S(1)}, bf16[102,3,384]{2,1,0:T(4,128)(2,1)}, u32[]{:S(2)}, u32[]{:S(2)}) collective-permute-start(bf16[102,3,384]{2,1,0:T(4,128)(2,1)S(1)} %get-tuple-element.15), channel_id=1, source_target_pairs={{0,1},{1,2},{2,3},{3,4},{4,5},{5,6},{6,7},{7,8},{8,9},{9,10},{10,1... | collective-permute-start | bytes 705032 | tf_op jit(solution)/shard_map/ppermute | solution.py:25
  127.6 13.6 %collective-permute-start.7 = (bf16[102,3,384]{2,1,0:T(4,128)(2,1)S(1)}, bf16[102,3,384]{2,1,0:T(4,128)(2,1)}, u32[]{:S(2)}, u32[]{:S(2)}) collective-permute-start(bf16[102,3,384]{2,1,0:T(4,128)(2,1)S(1)} %get-tuple-element.14), channel_id=1, source_target_pairs={{1,0},{2,1},{3,2},{4,3},{5,4},{6,5},{7,6},{8,7},{9,8},{10,9},{11,1... | collective-permute-start | bytes 705032 | tf_op jit(solution)/shard_map/ppermute | solution.py:26

commit v5 on v4

--- a/solution.py
+++ b/solution.py
@@ -140,7 +140,14 @@
     )
 
 
-def mlp_forward_kernel(live, mixed_ref, image_ref, w_in_ref, w_out_ref, summed_ref, low_ref, *, layout):
+def patch_rows(row, column, breadth):
+    return pl.ds(row * breadth + column, breadth // 2, stride=2)
+
+
+def mlp_forward_kernel(
+    live, mixed_ref, image_ref, w_in_ref, w_out_ref, w_down_ref, summed_ref, reduced_ref, low_ref,
+    *, layout
+):
     normed, _ = normalize(mixed_ref[...].astype(jnp.float32))
     hidden = jnp.dot(normed.astype(jnp.bfloat16), w_in_ref[...], preferred_element_type=jnp.float32)
     cdf = 0.5 * (1.0 + lax.erf(hidden * ROOT_HALF))
@@ -150,18 +157,52 @@
     summed = (image_ref[...].astype(jnp.float32) + branch).astype(jnp.bfloat16)
     summed_ref[...] = summed
     down_normed, _ = normalize(summed.astype(jnp.float32))
-    low_ref[...] = down_normed.astype(jnp.bfloat16)
+    low = down_normed.astype(jnp.bfloat16).astype(jnp.float32)
+    for k in range(low_ref.shape[0]):
+        low_ref[k] = low[:, k * 128 : (k + 1) * 128]
+    breadth = layout[1]
+    pair_rows = layout[0] // breadth // 2
+    total = jnp.zeros(reduced_ref.shape, jnp.float32)
+    for a in range(2):
+        for e in range(2):
+            patch = jnp.concatenate(
+                [
+                    jnp.concatenate(
+                        [low_ref[k, patch_rows(2 * y + a, e, breadth), :] for k in range(low_ref.shape[0])],
+                        axis=1,
+                    )
+                    for y in range(pair_rows)
+                ],
+                axis=0,
+            )
+            total = total + jnp.dot(
+                patch.astype(jnp.bfloat16), w_down_ref[2 * a + e], preferred_element_type=jnp.float32
+            )
+    reduced_ref[...] = total.astype(jnp.bfloat16)
 
 
 def mlp_backward_kernel(
-    live, mixed_ref, summed_ref, grad_ref, w_in_ref, w_out_ref, grad_summed_ref, grad_mixed_ref, *, layout
+    live, mixed_ref, summed_ref, cot_ref, w_in_ref, w_out_ref, w_down_ref, grad_summed_ref,
+    grad_mixed_ref, grad_ref, *, layout
 ):
+    breadth = layout[1]
+    pair_rows = layout[0] // breadth // 2
+    half = breadth // 2
+    for a in range(2):
+        for e in range(2):
+            part = times_transposed(cot_ref[...], w_down_ref[2 * a + e])
+            for y in range(pair_rows):
+                for k in range(grad_ref.shape[0]):
+                    grad_ref[k, patch_rows(2 * y + a, e, breadth), :] = part[
+                        y * half : (y + 1) * half, k * 128 : (k + 1) * 128
+                    ]
     normed, inv_std = normalize(mixed_ref[...].astype(jnp.float32))
     hidden = jnp.dot(normed.astype(jnp.bfloat16), w_in_ref[...], preferred_element_type=jnp.float32)
     cdf = 0.5 * (1.0 + lax.erf(hidden * ROOT_HALF))
     slope = cdf + hidden * INV_ROOT_TAU * jnp.exp(-0.5 * hidden * hidden)
     down_normed, down_inv = normalize(summed_ref[...].astype(jnp.float32))
-    grad_summed = normalize_back(grad_ref[...], down_normed, down_inv).astype(jnp.bfloat16)
+    grad_normed = jnp.concatenate([grad_ref[k] for k in range(grad_ref.shape[0])], axis=1)
+    grad_summed = normalize_back(grad_normed, down_normed, down_inv).astype(jnp.bfloat16)
     grad_summed_ref[...] = grad_summed
     grad_hidden = (times_transposed(grad_summed, w_out_ref[...]) * slope).astype(jnp.bfloat16)
     grad_norm_in = times_transposed(grad_hidden, w_in_ref[...])
@@ -180,24 +221,28 @@
     return flag > 0
 
 
-def pixel_call(kernel, live, operands, widths, outputs, layout):
+def pixel_call(kernel, live, operands, kinds, outputs, layout, scratch):
     block = layout[0]
-    pixels = operands[0].shape[0]
+    steps = operands[0].shape[0] // block
     specs = []
-    for operand, blocked in zip(operands, widths):
-        if blocked:
-            specs.append(pl.BlockSpec((block, operand.shape[1]), lambda i, live: (i, 0)))
+    for operand, kind in zip(operands, kinds):
+        if kind == "whole":
+            specs.append(pl.BlockSpec(operand.shape, lambda i, live, n=operand.ndim: (0,) * n))
         else:
-            specs.append(pl.BlockSpec(operand.shape, lambda i, live: (0, 0)))
+            rows = operand.shape[0] // steps
+            specs.append(pl.BlockSpec((rows, operand.shape[1]), lambda i, live: (i, 0)))
     return pl.pallas_call(
         lambda *refs: kernel(*refs, layout=layout),
         grid_spec=pltpu.PrefetchScalarGridSpec(
             num_scalar_prefetch=1,
-            grid=(pixels // block,),
+            grid=(steps,),
             in_specs=specs,
-            out_specs=[pl.BlockSpec((block, width), lambda i, live: (i, 0)) for width, _ in outputs],
+            out_specs=[
+                pl.BlockSpec((rows // steps, width), lambda i, live: (i, 0)) for rows, width, _ in outputs
+            ],
+            scratch_shapes=[pltpu.VMEM((width // 128, block, 128), jnp.float32) for width in scratch],
         ),
-        out_shape=[jax.ShapeDtypeStruct((pixels, width), dtype) for width, dtype in outputs],
+        out_shape=[jax.ShapeDtypeStruct((rows, width), dtype) for rows, width, dtype in outputs],
     )(live, *operands)
 
 
@@ -228,34 +273,26 @@
     taps = depth_kernel.reshape(KS * KS, channels).astype(jnp.float32)
     mixed = depthwise(halo_pieces(image, reach), taps, reach)
     mixed = mixed.reshape(pixels, channels)
-    summed, down_low = pixel_call(
+    weight_quad = weight_down.reshape(4, channels, outputs)
+    patches = pixels // 4
+    summed, reduced = pixel_call(
         mlp_forward_kernel,
         live,
-        (mixed, image.reshape(pixels, channels), weight_in, weight_out),
-        (True, True, False, False),
-        ((channels, jnp.bfloat16), (channels, jnp.bfloat16)),
+        (mixed, image.reshape(pixels, channels), weight_in, weight_out, weight_quad),
+        ("rows", "rows", "whole", "whole", "whole"),
+        ((pixels, channels, jnp.bfloat16), (patches, outputs, jnp.bfloat16)),
         layout,
-    )
-    down_low = down_low.reshape(height // 2, 2, breadth // 2, 2 * channels)
-    weight_pair = weight_down.reshape(2, 2 * channels, outputs)
-    reduced = jnp.dot(down_low[:, 0], weight_pair[0], preferred_element_type=jnp.float32) + jnp.dot(
-        down_low[:, 1], weight_pair[1], preferred_element_type=jnp.float32
-    )
-    reduced = reduced.astype(jnp.bfloat16)
-    grad_pair = [
-        lax.dot_general(
-            cotangent, weight_pair[a], (((2,), (1,)), ((), ())), preferred_element_type=jnp.float32
-        )
-        for a in range(2)
-    ]
-    grad_normed = jnp.stack(grad_pair, axis=1).reshape(pixels, channels)
+        (channels,),
+    )
+    reduced = reduced.reshape(height // 2, breadth // 2, outputs)
     grad_summed, grad_mixed = pixel_call(
         mlp_backward_kernel,
         live,
-        (mixed, summed, grad_normed, weight_in, weight_out),
-        (True, True, True, False, False),
-        ((channels, jnp.bfloat16), (channels, jnp.bfloat16)),
+        (mixed, summed, cotangent.reshape(patches, outputs), weight_in, weight_out, weight_quad),
+        ("rows", "rows", "rows", "whole", "whole", "whole"),
+        ((pixels, channels, jnp.bfloat16), (pixels, channels, jnp.bfloat16)),
         layout,
+        (channels,),
     )
     grad_image = depthwise(
         halo_pieces(grad_mixed.reshape(height, breadth, channels), reach),

time: 165 us -> 164 us (level)
  local copies, waits for them, and re-layouts: 24.7 us -> 8.19 us
  waiting for transfers between devices: 5.47 us -> 21.7 us
  Pallas kernels: 89.5 us -> 105 us
  matrix products: 9.54 us -> 0 us
  starting transfers between devices: 27.4 us -> 23.8 us
  other arithmetic: 6.09 us -> 3.6 us
    pallas_call x2, Pallas kernels: 45.3 us -> 60.6 us  [pixel_call(): pl.pallas_call(lambda *refs: kernel(*refs, layout=layout), grid_spec=pltp...]
    dot_general x4 -> x0, matrix products: 9.54 us -> none  [the longest x2 5.07 us: on_device(): lax.dot_general(cotangent, weight_pair[a], (((2,), (1,)), ((), ())), pref...]
    reshape x2 -> x0, local copies, waits for them, and re-layouts: 9.46 us -> none  [the longest x1 5.94 us: on_device(): grad_normed = jnp.stack(grad_pair, axis=1).reshape(pixels, channels)]
    ppermute x2, waiting for transfers between devices: 1.27 us -> 8.52 us  [halo_pieces(): lax.ppermute(framed[:, :width], 'col', [(i + 1, i) for i in range(cols -...]
    ppermute x2, waiting for transfers between devices: 4.18 us -> 10.3 us  [halo_pieces(): lax.ppermute(framed[:, cells.shape[1] - width:], 'col', [(i, i + 1) for i...]
    slice x1 -> x0, local copies, waits for them, and re-layouts: 2.8 us -> none  [on_device(): weight_pair[1]]
    another operation x1 -> x0, other arithmetic: 2.7 us -> none  [on_device(): grad_normed = jnp.stack(grad_pair, axis=1).reshape(pixels, channels)]
    another operation x1 -> x0, local copies, waits for them, and re-layouts: 2.62 us -> none  [on_device(): grad_normed = jnp.stack(grad_pair, axis=1).reshape(pixels, channels)]
  transfers between devices with their start and end apart: 8 -> 8, of which waited for: 2 -> 7; matrix products, arithmetic and copies ran while one was open for 19% -> 4% of each run, Pallas kernels for 0% -> 0%
where the time goes in v5:
time: 164 us; the launch traced here: 163 us
  Pallas kernels  105 us (64%)
  starting transfers between devices  23.8 us (15%)
  waiting for transfers between devices  21.7 us (13%)
  local copies, waits for them, and re-layouts  8.19 us (5%)
  other arithmetic  3.6 us (2%)
    pallas_call x2, Pallas kernels, pixel_call(): pl.pallas_call(lambda *refs: kernel(*refs, layout=layout), grid_spec=pltp...  60.6 us
    pallas_call x2, Pallas kernels, depthwise(): pl.pallas_call(lambda *refs: depthwise_kernel(*refs, reach=reach, chunk=c...  44.2 us
    ppermute x2, waiting for transfers between devices, halo_pieces(): lax.ppermute(framed[:, cells.shape[1] - width:], 'col', [(i, i + 1) for i...  10.3 us
    ppermute x2, waiting for transfers between devices, halo_pieces(): lax.ppermute(framed[:, :width], 'col', [(i + 1, i) for i in range(cols -...  8.52 us
    ppermute x2, starting transfers between devices, halo_pieces(): lax.ppermute(framed[:, :width], 'col', [(i + 1, i) for i in range(cols -...  8.05 us
    ppermute x2, starting transfers between devices, halo_pieces(): lax.ppermute(framed[:, cells.shape[1] - width:], 'col', [(i, i + 1) for i...  5.84 us
    ppermute x2, starting transfers between devices, halo_pieces(): bottom = lax.ppermute(cells[:width], 'row', up)  5.56 us
    unnamed x27, local copies, waits for them, and re-layouts  4.46 us
  transfers between devices with their start and end apart: 8, of which 7 were waited for; matrix products, arithmetic and copies ran while one was open for 4% of the time, Pallas kernels for 0%

profile of v5, /device:TPU:26, one launch (start us, length us, event | category | flops | bytes accessed | tf_op | source)
XLA Modules:
  0.0 162.9 jit_solution(5641887218250325561)
XLA Ops:
  0.6 0.9 fusion.2
  1.6 1.9 %collective-permute-start.1 = (bf16[3,32,384]{2,1,0:T(8,128)(2,1)S(1)}, bf16[3,32,384]{2,1,0:T(8,128)(2,1)S(1)}, u32[]{:S(2)}, u32[]{:S(2)}) collective-permute-start(bf16[3,32,384]{2,1,0:T(8,128)(2,1)S(1)} %get-tuple-element.20), channel_id=1, source_target_pairs={{16,0},{32,16},{48,32},{64,48},{80,64},{96,80},{112,96},{17,1},{33... | collective-permute-start | bytes 221192 | tf_op jit(solution)/shard_map/ppermute | solution.py:23
  3.5 2.4 %collective-permute-start = (bf16[3,32,384]{2,1,0:T(8,128)(2,1)S(1)}, bf16[3,32,384]{2,1,0:T(8,128)(2,1)S(1)}, u32[]{:S(2)}, u32[]{:S(2)}) collective-permute-start(bf16[3,32,384]{2,1,0:T(8,128)(2,1)S(1)} %get-tuple-element.21), channel_id=1, source_target_pairs={{0,16},{16,32},{32,48},{48,64},{64,80},{80,96},{96,112},{1,17},{17... | collective-permute-start | bytes 221192 | tf_op jit(solution)/shard_map/ppermute | solution.py:22
  5.9 0.8 copy.21
  6.7 0.7 reduce_window_sum.11
  7.4 0.8 select_reduce_fusion.3
  8.2 1.0 collective-permute-done.refs_1_
  9.2 0.0 copy-start.7
  9.2 0.0 copy-start.9
  9.2 0.0 copy-start.10
  9.2 0.0 copy-start.11
  9.2 0.0 copy-start.8
  9.2 2.2 %constant_dynamic-update-slice_fusion.1 = bf16[102,32,384]{2,1,0:T(8,128)(2,1)S(1)} fusion(bf16[102,32,384]{2,1,0:T(8,128)(2,1)S(1)} %constant_dynamic-update-slice_fusion.2, bf16[96,32,384]{2,1,0:T(8,128)(2,1)} %refs_0_.1), kind=kLoop, calls=%fused_computation.7 | loop fusion | bytes 4718592
  11.4 0.0 copy-done.7
  11.4 0.0 collective-permute-done.1.refs_2_
  11.4 0.0 copy-start.6
  11.5 0.2 fusion
  11.7 6.1 %collective-permute-start.3 = (bf16[102,3,384]{2,1,0:T(4,128)(2,1)S(1)}, bf16[102,3,384]{2,1,0:T(4,128)(2,1)S(1)}, u32[]{:S(2)}, u32[]{:S(2)}) collective-permute-start(bf16[102,3,384]{2,1,0:T(4,128)(2,1)S(1)} %get-tuple-element.16), channel_id=1, source_target_pairs={{1,0},{2,1},{3,2},{4,3},{5,4},{6,5},{7,6},{8,7},{9,8},{10,9},{11,1... | collective-permute-start | bytes 705032 | tf_op jit(solution)/shard_map/ppermute | solution.py:26
  17.9 1.9 %collective-permute-start.2 = (bf16[102,3,384]{2,1,0:T(4,128)(2,1)S(1)}, bf16[102,3,384]{2,1,0:T(4,128)(2,1)S(1)}, u32[]{:S(2)}, u32[]{:S(2)}) collective-permute-start(bf16[102,3,384]{2,1,0:T(4,128)(2,1)S(1)} %get-tuple-element.17), channel_id=1, source_target_pairs={{0,1},{1,2},{2,3},{3,4},{4,5},{5,6},{6,7},{7,8},{8,9},{9,10},{10,1... | collective-permute-start | bytes 705032 | tf_op jit(solution)/shard_map/ppermute | solution.py:25
  19.8 0.5 select_reduce_fusion.1
  20.3 0.1 copy.22
  20.4 0.1 copy.23
  20.5 0.0 copy-done.9
  20.5 0.0 copy-done.10
  20.5 0.0 copy-done.11
  20.6 0.1 copy.24
  20.7 0.7 reshape.47.refs_0_
  21.3 0.0 copy-done.8
  21.3 0.7 reshape.48.refs_5_
  22.0 2.9 %collective-permute-done.3.refs_4_ = bf16[102,3,384]{2,1,0:T(4,128)(2,1)S(1)} collective-permute-done((bf16[102,3,384]{2,1,0:T(4,128)(2,1)S(1)}, bf16[102,3,384]{2,1,0:T(4,128)(2,1)S(1)}, u32[]{:S(2)}, u32[]{:S(2)}) %collective-permute-start.3) | collective-permute-done | bytes 235040 | tf_op jit(solution)/shard_map/ppermute | solution.py:26
  24.8 0.0 copy-start.2
  24.8 6.2 %collective-permute-done.2.refs_3_ = bf16[102,3,384]{2,1,0:T(4,128)(2,1)S(1)} collective-permute-done((bf16[102,3,384]{2,1,0:T(4,128)(2,1)S(1)}, bf16[102,3,384]{2,1,0:T(4,128)(2,1)S(1)}, u32[]{:S(2)}, u32[]{:S(2)}) %collective-permute-start.2) | collective-permute-done | bytes 235040 | tf_op jit(solution)/shard_map/ppermute | solution.py:25
  31.1 0.0 copy-done.6
  31.1 0.0 copy-done.2
  31.1 0.0 copy-start.3
  31.1 0.7 copy-done.3
  31.8 21.8 %shard_map.113 = bf16[96,32,384]{2,1,0:T(8,128)(2,1)} custom-call(bf16[96,32,384]{2,1,0:T(8,128)(2,1)} %refs_0_.1, bf16[3,32,384]{2,1,0:T(8,128)(2,1)} %copy-done.7, bf16[3,32,384]{2,1,0:T(8,128)(2,1)} %copy-done.6, bf16[102,3,384]{2,1,0:T(4,128)(2,1)} %copy-done.3, bf16[102,3,384]{2,1,0:T(4,128)(2,1)} %copy-done.2, f32[49,384]{1,0:T(8,128)} %reshape.48.refs_5_), custom_call_target="tpu_custom_call" | custom-call | tf_op jit(solution)/shard_map/pallas_call | solution.py:88
  53.6 28.9 %shard_map.114 = (bf16[3072,384]{1,0:T(8,128)(2,1)}, bf16[768,768]{1,0:T(8,128)(2,1)}) custom-call(s32[48]{0:T(128)} %reshape.47.refs_0_, bf16[3072,384]{1,0:T(8,128)(2,1)} %bitcast.13, bf16[3072,384]{1,0:T(8,128)(2,1)} %bitcast.12, bf16[384,1536]{1,0:T(8,128)(2,1)} %refs_4_.3, bf16[1536,384]{1,0:T(8,128)(2,1)} %refs_5_.1, bf16[4,384,768]{2,1,0:T(8,128)(2,1)} %bitcast.17), custom_call_target="tpu_custom_call" | custom-call | tf_op jit(solution)/shard_map/pallas_call | solution.py:234
  82.5 31.7 %shard_map.115 = (bf16[3072,384]{1,0:T(8,128)(2,1)}, bf16[3072,384]{1,0:T(8,128)(2,1)}) custom-call(s32[48]{0:T(128)} %reshape.47.refs_0_, bf16[3072,384]{1,0:T(8,128)(2,1)} %bitcast.14, bf16[3072,384]{1,0:T(8,128)(2,1)} %get-tuple-element.7.refs_2_, bf16[768,768]{1,0:T(8,128)(2,1)} %bitcast.20, bf16[384,1536]{1,0:T(8,128)(2,1)} %refs_4_.3, ...), custom_call_target="tpu_custom_call" | custom-call | tf_op jit(solution)/shard_map/pallas_call | solution.py:234
  114.2 0.9 fusion.1
  115.2 1.9 %collective-permute-start.4 = (bf16[3,32,384]{2,1,0:T(8,128)(2,1)S(1)}, bf16[3,32,384]{2,1,0:T(8,128)(2,1)S(1)}, u32[]{:S(2)}, u32[]{:S(2)}) collective-permute-start(bf16[3,32,384]{2,1,0:T(8,128)(2,1)S(1)} %bitcast.22), channel_id=1, source_target_pairs={{0,16},{16,32},{32,48},{48,64},{64,80},{80,96},{96,112},{1,17},{17... | collective-permute-start | bytes 221192 | tf_op jit(solution)/shard_map/ppermute | solution.py:22
  117.1 3.6 %collective-permute-start.5 = (bf16[3,32,384]{2,1,0:T(8,128)(2,1)S(1)}, bf16[3,32,384]{2,1,0:T(8,128)(2,1)S(1)}, u32[]{:S(2)}, u32[]{:S(2)}) collective-permute-start(bf16[3,32,384]{2,1,0:T(8,128)(2,1)S(1)} %bitcast.21), channel_id=1, source_target_pairs={{16,0},{32,16},{48,32},{64,48},{80,64},{96,80},{112,96},{17,1},{33... | collective-permute-start | bytes 221192 | tf_op jit(solution)/shard_map/ppermute | solution.py:23
  120.8 0.1 collective-permute-done.4.refs_1_
  120.9 0.0 copy-start.4
  120.9 1.9 %collective-permute-done.5.refs_2_ = bf16[3,32,384]{2,1,0:T(8,128)(2,1)S(1)} collective-permute-done((bf16[3,32,384]{2,1,0:T(8,128)(2,1)S(1)}, bf16[3,32,384]{2,1,0:T(8,128)(2,1)S(1)}, u32[]{:S(2)}, u32[]{:S(2)}) %collective-permute-start.5) | collective-permute-done | bytes 73760 | tf_op jit(solution)/shard_map/ppermute | solution.py:23
  122.7 0.0 copy-start.5
  122.7 1.5 pad_maximum_fusion
  124.2 1.9 %collective-permute-start.7 = (bf16[102,3,384]{2,1,0:T(4,128)(2,1)S(1)}, bf16[102,3,384]{2,1,0:T(4,128)(2,1)S(1)}, u32[]{:S(2)}, u32[]{:S(2)}) collective-permute-start(bf16[102,3,384]{2,1,0:T(4,128)(2,1)S(1)} %get-tuple-element.14), channel_id=1, source_target_pairs={{1,0},{2,1},{3,2},{4,3},{5,4},{6,5},{7,6},{8,7},{9,8},{10,9},{11,1... | collective-permute-start | bytes 705032 | tf_op jit(solution)/shard_map/ppermute | solution.py:26
  126.2 3.9 %collective-permute-start.6 = (bf16[102,3,384]{2,1,0:T(4,128)(2,1)S(1)}, bf16[102,3,384]{2,1,0:T(4,128)(2,1)S(1)}, u32[]{:S(2)}, u32[]{:S(2)}) collective-permute-start(bf16[102,3,384]{2,1,0:T(4,128)(2,1)S(1)} %get-tuple-element.15), channel_id=1, source_target_pairs={{0,1},{1,2},{2,3},{3,4},{4,5},{5,6},{6,7},{7,8},{8,9},{9,10},{10,1... | collective-permute-start | bytes 705032 | tf_op jit(solution)/shard_map/ppermute | solution.py:25
  130.1 5.7 %collective-permute-done.7.refs_4_ = bf16[102,3,384]{2,1,0:T(4,128)(2,1)S(1)} collective-permute-done((bf16[102,3,384]{2,1,0:T(4,128)(2,1)S(1)}, bf16[102,3,384]{2,1,0:T(4,128)(2,1)S(1)}, u32[]{:S(2)}, u32[]{:S(2)}) %collective-permute-start.7) | collective-permute-done | bytes 235040 | tf_op jit(solution)/shard_map/ppermute | solution.py:26
  135.8 0.0 copy-start
  135.8 4.0 %collective-permute-done.6.refs_3_ = bf16[102,3,384]{2,1,0:T(4,128)(2,1)S(1)} collective-permute-done((bf16[102,3,384]{2,1,0:T(4,128)(2,1)S(1)}, bf16[102,3,384]{2,1,0:T(4,128)(2,1)S(1)}, u32[]{:S(2)}, u32[]{:S(2)}) %collective-permute-start.6) | collective-permute-done | bytes 235040 | tf_op jit(solution)/shard_map/ppermute | solution.py:25
  139.8 0.0 copy-start.1
  139.8 0.0 copy-done.4
  139.8 0.0 copy-done.5
  139.8 0.0 copy-done
  139.8 0.7 copy-done.1
  140.5 22.4 %shard_map.116 = bf16[96,32,384]{2,1,0:T(8,128)(2,1)} custom-call(bf16[96,32,384]{2,1,0:T(8,128)(2,1)} %bitcast.16, bf16[3,32,384]{2,1,0:T(8,128)(2,1)} %copy-done.4, bf16[3,32,384]{2,1,0:T(8,128)(2,1)} %copy-done.5, bf16[102,3,384]{2,1,0:T(4,128)(2,1)} %copy-done.1, bf16[102,3,384]{2,1,0:T(4,128)(2,1)} %copy-done, f32[49,384]{1,0:T(8,128)} %reshape.48.refs_5_, ...), custom_call_target="tpu_custom_call" | custom-call | tf_op jit(solution)/shard_map/pallas_call | solution.py:88
  (4 shorter events, 0.0 us)
Async XLA Ops:
  1.6 9.9 %collective-permute-start.1 = (bf16[3,32,384]{2,1,0:T(8,128)(2,1)S(1)}, bf16[3,32,384]{2,1,0:T(8,128)(2,1)S(1)}, u32[]{:S(2)}, u32[]{:S(2)}) collective-permute-start(bf16[3,32,384]{2,1,0:T(8,128)(2,1)S(1)} %get-tuple-element.20), channel_id=1, source_target_pairs={{16,0},{32,16},{48,32},{64,48},{80,64},{96,80},{112,96},{17,1},{33... | collective-permute-start | bytes 221192 | tf_op jit(solution)/shard_map/ppermute | solution.py:23
  3.5 5.7 %collective-permute-start = (bf16[3,32,384]{2,1,0:T(8,128)(2,1)S(1)}, bf16[3,32,384]{2,1,0:T(8,128)(2,1)S(1)}, u32[]{:S(2)}, u32[]{:S(2)}) collective-permute-start(bf16[3,32,384]{2,1,0:T(8,128)(2,1)S(1)} %get-tuple-element.21), channel_id=1, source_target_pairs={{0,16},{16,32},{32,48},{48,64},{64,80},{80,96},{96,112},{1,17},{17... | collective-permute-start | bytes 221192 | tf_op jit(solution)/shard_map/ppermute | solution.py:22
  9.2 2.3 %copy-start.7 = (bf16[3,32,384]{2,1,0:T(8,128)(2,1)}, bf16[3,32,384]{2,1,0:T(8,128)(2,1)S(1)}, u32[]{:S(2)}) copy-start(bf16[3,32,384]{2,1,0:T(8,128)(2,1)S(1)} %collective-permute-done.refs_1_) | copy-start | bytes 221188
  9.2 11.3 %copy-start.9 = (s32[12,4]{0,1:T(4,128)S(1)}, s32[12,4]{0,1:T(4,128)}, u32[]{:S(2)}) copy-start(s32[12,4]{0,1:T(4,128)} %param.17) | copy-start | bytes 580
  9.2 11.3 %copy-start.10 = (s32[12,4]{0,1:T(4,128)S(1)}, s32[12,4]{0,1:T(4,128)}, u32[]{:S(2)}) copy-start(s32[12,4]{0,1:T(4,128)} %param.15) | copy-start | bytes 580
  9.2 11.3 %copy-start.11 = (s32[12,4]{0,1:T(4,128)S(1)}, s32[12,4]{0,1:T(4,128)}, u32[]{:S(2)}) copy-start(s32[12,4]{0,1:T(4,128)} %param.18) | copy-start | bytes 580
  9.2 12.1 %copy-start.8 = (bf16[7,7,384]{2,1,0:T(8,128)(2,1)S(1)}, bf16[7,7,384]{2,1,0:T(8,128)(2,1)}, u32[]{:S(2)}) copy-start(bf16[7,7,384]{2,1,0:T(8,128)(2,1)} %param.11) | copy-start | bytes 112900
  11.4 19.6 %copy-start.6 = (bf16[3,32,384]{2,1,0:T(8,128)(2,1)}, bf16[3,32,384]{2,1,0:T(8,128)(2,1)S(1)}, u32[]{:S(2)}) copy-start(bf16[3,32,384]{2,1,0:T(8,128)(2,1)S(1)} %collective-permute-done.1.refs_2_) | copy-start | bytes 221188
  11.7 13.1 %collective-permute-start.3 = (bf16[102,3,384]{2,1,0:T(4,128)(2,1)S(1)}, bf16[102,3,384]{2,1,0:T(4,128)(2,1)S(1)}, u32[]{:S(2)}, u32[]{:S(2)}) collective-permute-start(bf16[102,3,384]{2,1,0:T(4,128)(2,1)S(1)} %get-tuple-element.16), channel_id=1, source_target_pairs={{1,0},{2,1},{3,2},{4,3},{5,4},{6,5},{7,6},{8,7},{9,8},{10,9},{11,1... | collective-permute-start | bytes 705032 | tf_op jit(solution)/shard_map/ppermute | solution.py:26
  17.9 13.2 %collective-permute-start.2 = (bf16[102,3,384]{2,1,0:T(4,128)(2,1)S(1)}, bf16[102,3,384]{2,1,0:T(4,128)(2,1)S(1)}, u32[]{:S(2)}, u32[]{:S(2)}) collective-permute-start(bf16[102,3,384]{2,1,0:T(4,128)(2,1)S(1)} %get-tuple-element.17), channel_id=1, source_target_pairs={{0,1},{1,2},{2,3},{3,4},{4,5},{5,6},{6,7},{7,8},{8,9},{9,10},{10,1... | collective-permute-start | bytes 705032 | tf_op jit(solution)/shard_map/ppermute | solution.py:25
  24.8 6.2 %copy-start.2 = (bf16[102,3,384]{2,1,0:T(4,128)(2,1)}, bf16[102,3,384]{2,1,0:T(4,128)(2,1)S(1)}, u32[]{:S(2)}) copy-start(bf16[102,3,384]{2,1,0:T(4,128)(2,1)S(1)} %collective-permute-done.3.refs_4_) | copy-start | bytes 705028
  31.1 0.7 copy-start.3
  115.2 5.7 %collective-permute-start.4 = (bf16[3,32,384]{2,1,0:T(8,128)(2,1)S(1)}, bf16[3,32,384]{2,1,0:T(8,128)(2,1)S(1)}, u32[]{:S(2)}, u32[]{:S(2)}) collective-permute-start(bf16[3,32,384]{2,1,0:T(8,128)(2,1)S(1)} %bitcast.22), channel_id=1, source_target_pairs={{0,16},{16,32},{32,48},{48,64},{64,80},{80,96},{96,112},{1,17},{17... | collective-permute-start | bytes 221192 | tf_op jit(solution)/shard_map/ppermute | solution.py:22
  117.1 5.6 %collective-permute-start.5 = (bf16[3,32,384]{2,1,0:T(8,128)(2,1)S(1)}, bf16[3,32,384]{2,1,0:T(8,128)(2,1)S(1)}, u32[]{:S(2)}, u32[]{:S(2)}) collective-permute-start(bf16[3,32,384]{2,1,0:T(8,128)(2,1)S(1)} %bitcast.21), channel_id=1, source_target_pairs={{16,0},{32,16},{48,32},{64,48},{80,64},{96,80},{112,96},{17,1},{33... | collective-permute-start | bytes 221192 | tf_op jit(solution)/shard_map/ppermute | solution.py:23
  120.9 19.0 %copy-start.4 = (bf16[3,32,384]{2,1,0:T(8,128)(2,1)}, bf16[3,32,384]{2,1,0:T(8,128)(2,1)S(1)}, u32[]{:S(2)}) copy-start(bf16[3,32,384]{2,1,0:T(8,128)(2,1)S(1)} %collective-permute-done.4.refs_1_) | copy-start | bytes 221188
  122.7 17.1 %copy-start.5 = (bf16[3,32,384]{2,1,0:T(8,128)(2,1)}, bf16[3,32,384]{2,1,0:T(8,128)(2,1)S(1)}, u32[]{:S(2)}) copy-start(bf16[3,32,384]{2,1,0:T(8,128)(2,1)S(1)} %collective-permute-done.5.refs_2_) | copy-start | bytes 221188
  124.2 11.5 %collective-permute-start.7 = (bf16[102,3,384]{2,1,0:T(4,128)(2,1)S(1)}, bf16[102,3,384]{2,1,0:T(4,128)(2,1)S(1)}, u32[]{:S(2)}, u32[]{:S(2)}) collective-permute-start(bf16[102,3,384]{2,1,0:T(4,128)(2,1)S(1)} %get-tuple-element.14), channel_id=1, source_target_pairs={{1,0},{2,1},{3,2},{4,3},{5,4},{6,5},{7,6},{8,7},{9,8},{10,9},{11,1... | collective-permute-start | bytes 705032 | tf_op jit(solution)/shard_map/ppermute | solution.py:26
  126.2 13.6 %collective-permute-start.6 = (bf16[102,3,384]{2,1,0:T(4,128)(2,1)S(1)}, bf16[102,3,384]{2,1,0:T(4,128)(2,1)S(1)}, u32[]{:S(2)}, u32[]{:S(2)}) collective-permute-start(bf16[102,3,384]{2,1,0:T(4,128)(2,1)S(1)} %get-tuple-element.15), channel_id=1, source_target_pairs={{0,1},{1,2},{2,3},{3,4},{4,5},{5,6},{6,7},{7,8},{8,9},{9,10},{10,1... | collective-permute-start | bytes 705032 | tf_op jit(solution)/shard_map/ppermute | solution.py:25
  135.8 4.0 %copy-start = (bf16[102,3,384]{2,1,0:T(4,128)(2,1)}, bf16[102,3,384]{2,1,0:T(4,128)(2,1)S(1)}, u32[]{:S(2)}) copy-start(bf16[102,3,384]{2,1,0:T(4,128)(2,1)S(1)} %collective-permute-done.7.refs_4_) | copy-start | bytes 705028
  139.8 0.7 copy-start.1

commit v6 on v5

--- a/solution.py
+++ b/solution.py
@@ -17,18 +17,40 @@
 def halo_pieces(cells, width):
     rows = lax.axis_size("row")
     cols = lax.axis_size("col")
-    down = [(i, i + 1) for i in range(rows - 1)]
-    up = [(i + 1, i) for i in range(rows - 1)]
-    top = lax.ppermute(cells[cells.shape[0] - width :], "row", down)
-    bottom = lax.ppermute(cells[:width], "row", up)
-    framed = jnp.concatenate([top, cells, bottom], axis=0)
-    left = lax.ppermute(framed[:, cells.shape[1] - width :], "col", [(i, i + 1) for i in range(cols - 1)])
-    right = lax.ppermute(framed[:, :width], "col", [(i + 1, i) for i in range(cols - 1)])
-    return (cells, top, bottom, left, right)
+    height, breadth = cells.shape[:2]
+
+    def arrive(piece, down, right):
+        pairs = [
+            ((r - down) * cols + (c - right), r * cols + c)
+            for r in range(rows)
+            for c in range(cols)
+            if 0 <= r - down < rows and 0 <= c - right < cols
+        ]
+        if right == 0:
+            return lax.ppermute(piece, "row", [(src // cols, dst // cols) for src, dst in pairs if src % cols == 0])
+        if down == 0:
+            return lax.ppermute(piece, "col", [(src, dst) for src, dst in pairs if src < cols])
+        return lax.ppermute(piece, ("row", "col"), pairs)
+
+    low = slice(0, width)
+    high_r = slice(height - width, height)
+    high_c = slice(breadth - width, breadth)
+    return (
+        cells,
+        arrive(cells[high_r], 1, 0),
+        arrive(cells[low], -1, 0),
+        arrive(cells[:, high_c], 0, 1),
+        arrive(cells[:, low], 0, -1),
+        arrive(cells[high_r, high_c], 1, 1),
+        arrive(cells[high_r, low], 1, -1),
+        arrive(cells[low, high_c], -1, 1),
+        arrive(cells[low, low], -1, -1),
+    )
 
 
 def depthwise_kernel(
-    image_ref, top_ref, bottom_ref, left_ref, right_ref, k_ref, *rest, reach, chunk, flip
+    image_ref, top_ref, bottom_ref, left_ref, right_ref, tl_ref, tr_ref, bl_ref, br_ref, k_ref, *rest,
+    reach, chunk, flip
 ):
     if len(rest) == 5:
         base_ref, out_ref, framed_ref, shifted_ref, total_ref = rest
@@ -40,8 +62,12 @@
     framed_ref[reach : reach + height, reach : reach + breadth, :] = image_ref[...].astype(jnp.float32)
     framed_ref[:reach, reach : reach + breadth, :] = top_ref[...].astype(jnp.float32)
     framed_ref[reach + height :, reach : reach + breadth, :] = bottom_ref[...].astype(jnp.float32)
-    framed_ref[:, :reach, :] = left_ref[...].astype(jnp.float32)
-    framed_ref[:, reach + breadth :, :] = right_ref[...].astype(jnp.float32)
+    framed_ref[reach : reach + height, :reach, :] = left_ref[...].astype(jnp.float32)
+    framed_ref[reach : reach + height, reach + breadth :, :] = right_ref[...].astype(jnp.float32)
+    framed_ref[:reach, :reach, :] = tl_ref[...].astype(jnp.float32)
+    framed_ref[:reach, reach + breadth :, :] = tr_ref[...].astype(jnp.float32)
+    framed_ref[reach + height :, :reach, :] = bl_ref[...].astype(jnp.float32)
+    framed_ref[reach + height :, reach + breadth :, :] = br_ref[...].astype(jnp.float32)
     for shift_c in range(side):
         shifted_ref[...] = framed_ref[:, shift_c : shift_c + breadth, :]
 
@@ -77,8 +103,9 @@
         pl.BlockSpec((height, breadth, lanes), lambda c: (0, 0, c)),
         pl.BlockSpec((reach, breadth, lanes), lambda c: (0, 0, c)),
         pl.BlockSpec((reach, breadth, lanes), lambda c: (0, 0, c)),
-        pl.BlockSpec((framed[0], reach, lanes), lambda c: (0, 0, c)),
-        pl.BlockSpec((framed[0], reach, lanes), lambda c: (0, 0, c)),
+        pl.BlockSpec((height, reach, lanes), lambda c: (0, 0, c)),
+        pl.BlockSpec((height, reach, lanes), lambda c: (0, 0, c)),
+    ] + [pl.BlockSpec((reach, reach, lanes), lambda c: (0, 0, c))] * 4 + [
         pl.BlockSpec((taps.shape[0], lanes), lambda c: (0, c)),
     ]
     operands = list(pieces) + [taps]

time: 164 us -> 196 us (1.20)
  starting transfers between devices: 23.8 us -> 51.6 us
  local copies, waits for them, and re-layouts: 8.19 us -> 11.1 us
  waiting for transfers between devices: 21.7 us -> 23.7 us
    ppermute x8 -> x16, starting transfers between devices: 23.8 us -> 51.6 us  [the longest x8 26.7 us: arrive(): return lax.ppermute(piece, ('row', 'col'), pairs)]
    slice x3 -> x6, local copies, waits for them, and re-layouts: 2.12 us -> 6.43 us  [the longest x2 2.96 us: halo_pieces(): cells[:, low]]
    unnamed x27 -> x33, local copies, waits for them, and re-layouts: 4.46 us -> 2.31 us
    ppermute x8 -> x16, waiting for transfers between devices: 21.7 us -> 23.7 us  [the longest x8 14.7 us: arrive(): return lax.ppermute(piece, ('row', 'col'), pairs)]
  transfers between devices with their start and end apart: 8 -> 16, of which waited for: 7 -> 6; matrix products, arithmetic and copies ran while one was open for 4% -> 5% of each run, Pallas kernels for 0% -> 0%
where the time goes in v6:
time: 196 us; the launch traced here: 195 us
  Pallas kernels  105 us (54%)
  starting transfers between devices  51.6 us (26%)
  waiting for transfers between devices  23.7 us (12%)
  local copies, waits for them, and re-layouts  11.1 us (6%)
  other arithmetic  2.79 us (1%)
    pallas_call x2, Pallas kernels, pixel_call(): pl.pallas_call(lambda *refs: kernel(*refs, layout=layout), grid_spec=pltp...  60.6 us
    pallas_call x2, Pallas kernels, depthwise(): pl.pallas_call(lambda *refs: depthwise_kernel(*refs, reach=reach, chunk=c...  44.3 us
    ppermute x8, starting transfers between devices, arrive(): return lax.ppermute(piece, ('row', 'col'), pairs)  26.7 us
    ppermute x8, waiting for transfers between devices, arrive(): return lax.ppermute(piece, ('row', 'col'), pairs)  14.7 us
    ppermute x4, starting transfers between devices, arrive(): lax.ppermute(piece, 'col', [(src, dst) for src, dst in pairs if src < cols])  13.8 us
    ppermute x4, starting transfers between devices, arrive(): lax.ppermute(piece, 'row', [(src // cols, dst // cols) for src, dst in pa...  11.1 us
    ppermute x4, waiting for transfers between devices, arrive(): lax.ppermute(piece, 'col', [(src, dst) for src, dst in pairs if src < cols])  8.9 us
  transfers between devices with their start and end apart: 16, of which 6 were waited for; matrix products, arithmetic and copies ran while one was open for 5% of the time, Pallas kernels for 0%

profile of v6, /device:TPU:26, one launch (start us, length us, event | category | flops | bytes accessed | tf_op | source)
XLA Modules:
  0.0 195.1 jit_solution(13984822794638735387)
XLA Ops:
  0.6 0.8 fusion.3
  1.4 5.5 %collective-permute-start.7 = (bf16[3,3,384]{2,1,0:T(4,128)(2,1)S(1)}, bf16[3,3,384]{2,1,0:T(4,128)(2,1)S(1)}, u32[]{:S(2)}, u32[]{:S(2)}) collective-permute-start(bf16[3,3,384]{2,1,0:T(4,128)(2,1)S(1)} %get-tuple-element.22), channel_id=1, source_target_pairs={{17,0},{18,1},{19,2},{20,3},{21,4},{22,5},{23,6},{24,7},{25,8},{26... | collective-permute-start | bytes 20744 | tf_op jit(solution)/shard_map/ppermute | solution.py:33
  7.0 1.9 collective-permute-start.6
  8.9 5.8 %collective-permute-start.5 = (bf16[3,3,384]{2,1,0:T(4,128)(2,1)S(1)}, bf16[3,3,384]{2,1,0:T(4,128)(2,1)S(1)}, u32[]{:S(2)}, u32[]{:S(2)}) collective-permute-start(bf16[3,3,384]{2,1,0:T(4,128)(2,1)S(1)} %get-tuple-element.24), channel_id=1, source_target_pairs={{1,16},{2,17},{3,18},{4,19},{5,20},{6,21},{7,22},{8,23},{9,24},{10... | collective-permute-start | bytes 20744 | tf_op jit(solution)/shard_map/ppermute | solution.py:33
  14.7 1.9 collective-permute-start.4
  16.6 0.9 fusion.5
  17.5 3.7 %collective-permute-start.1 = (bf16[3,32,384]{2,1,0:T(8,128)(2,1)S(1)}, bf16[3,32,384]{2,1,0:T(8,128)(2,1)S(1)}, u32[]{:S(2)}, u32[]{:S(2)}) collective-permute-start(bf16[3,32,384]{2,1,0:T(8,128)(2,1)S(1)} %get-tuple-element.28), channel_id=1, source_target_pairs={{16,0},{32,16},{48,32},{64,48},{80,64},{96,80},{112,96},{17,1},{33... | collective-permute-start | bytes 221192 | tf_op jit(solution)/shard_map/ppermute | solution.py:30
  21.2 1.5 fusion.4
  22.7 0.8 copy.21
  23.5 0.7 reduce_window_sum.11
  24.2 0.8 select_reduce_fusion.3
  25.0 0.5 select_reduce_fusion.1
  25.5 0.1 copy.22
  25.6 0.1 copy.23
  25.7 0.0 collective-permute-done.7.refs_8_
  25.7 1.9 collective-permute-start
  27.6 0.0 collective-permute-done.6.refs_7_
  27.7 6.0 %collective-permute-start.3 = (bf16[96,3,384]{2,1,0:T(4,128)(2,1)S(1)}, bf16[96,3,384]{2,1,0:T(4,128)(2,1)S(1)}, u32[]{:S(2)}, u32[]{:S(2)}) collective-permute-start(bf16[96,3,384]{2,1,0:T(4,128)(2,1)S(1)} %get-tuple-element.26), channel_id=1, source_target_pairs={{1,0},{2,1},{3,2},{4,3},{5,4},{6,5},{7,6},{8,7},{9,8},{10,9},{11,1... | collective-permute-start | bytes 663560 | tf_op jit(solution)/shard_map/ppermute | solution.py:32
  33.7 0.0 collective-permute-done.5.refs_6_
  33.7 1.9 collective-permute-start.2
  35.6 0.7 and_convert_fusion
  36.3 0.1 copy.24
  36.4 0.6 reshape.47.refs_0_
  37.1 1.4 reshape.48.refs_9_
  38.5 0.0 collective-permute-done.4.refs_5_
  38.5 0.0 collective-permute-done.1.refs_2_
  38.5 0.0 collective-permute-done.refs_1_
  38.5 2.4 %collective-permute-done.3.refs_4_ = bf16[96,3,384]{2,1,0:T(4,128)(2,1)S(1)} collective-permute-done((bf16[96,3,384]{2,1,0:T(4,128)(2,1)S(1)}, bf16[96,3,384]{2,1,0:T(4,128)(2,1)S(1)}, u32[]{:S(2)}, u32[]{:S(2)}) %collective-permute-start.3) | collective-permute-done | bytes 221216 | tf_op jit(solution)/shard_map/ppermute | solution.py:32
  40.9 6.5 %collective-permute-done.2.refs_3_ = bf16[96,3,384]{2,1,0:T(4,128)(2,1)S(1)} collective-permute-done((bf16[96,3,384]{2,1,0:T(4,128)(2,1)S(1)}, bf16[96,3,384]{2,1,0:T(4,128)(2,1)S(1)}, u32[]{:S(2)}, u32[]{:S(2)}) %collective-permute-start.2) | collective-permute-done | bytes 221216 | tf_op jit(solution)/shard_map/ppermute | solution.py:32
  47.4 0.0 copy-done.14
  47.5 0.0 copy-start.3
  47.5 0.7 copy-done.3
  48.2 21.9 %shard_map.113 = bf16[96,32,384]{2,1,0:T(8,128)(2,1)} custom-call(bf16[96,32,384]{2,1,0:T(8,128)(2,1)} %refs_0_.1, bf16[3,32,384]{2,1,0:T(8,128)(2,1)} %copy-done.7, bf16[3,32,384]{2,1,0:T(8,128)(2,1)} %copy-done.6, bf16[96,3,384]{2,1,0:T(4,128)(2,1)} %copy-done.3, bf16[96,3,384]{2,1,0:T(4,128)(2,1)} %copy-done.2, bf16[3,3,384]{2,1,0:T(4,128)(2,1)} %copy-done.15, ...), custom_call_target="tpu_custom_call" | custom-call | tf_op jit(solution)/shard_map/pallas_call | solution.py:115
  70.1 28.9 %shard_map.114 = (bf16[3072,384]{1,0:T(8,128)(2,1)}, bf16[768,768]{1,0:T(8,128)(2,1)}) custom-call(s32[48]{0:T(128)} %reshape.47.refs_0_, bf16[3072,384]{1,0:T(8,128)(2,1)} %bitcast.12, bf16[3072,384]{1,0:T(8,128)(2,1)} %bitcast.14, bf16[384,1536]{1,0:T(8,128)(2,1)} %refs_4_.3, bf16[1536,384]{1,0:T(8,128)(2,1)} %refs_5_.1, bf16[4,384,768]{2,1,0:T(8,128)(2,1)} %bitcast.15), custom_call_target="tpu_custom_call" | custom-call | tf_op jit(solution)/shard_map/pallas_call | solution.py:261
  99.0 31.7 %shard_map.115 = (bf16[3072,384]{1,0:T(8,128)(2,1)}, bf16[3072,384]{1,0:T(8,128)(2,1)}) custom-call(s32[48]{0:T(128)} %reshape.47.refs_0_, bf16[3072,384]{1,0:T(8,128)(2,1)} %bitcast.13, bf16[3072,384]{1,0:T(8,128)(2,1)} %get-tuple-element.7.refs_2_, bf16[768,768]{1,0:T(8,128)(2,1)} %bitcast.21, bf16[384,1536]{1,0:T(8,128)(2,1)} %refs_4_.3, ...), custom_call_target="tpu_custom_call" | custom-call | tf_op jit(solution)/shard_map/pallas_call | solution.py:261
  130.7 0.9 fusion.2
  131.6 1.9 collective-permute-start.8
  133.6 3.6 %collective-permute-start.9 = (bf16[3,32,384]{2,1,0:T(8,128)(2,1)S(1)}, bf16[3,32,384]{2,1,0:T(8,128)(2,1)S(1)}, u32[]{:S(2)}, u32[]{:S(2)}) collective-permute-start(bf16[3,32,384]{2,1,0:T(8,128)(2,1)S(1)} %bitcast.22), channel_id=1, source_target_pairs={{16,0},{32,16},{48,32},{64,48},{80,64},{96,80},{112,96},{17,1},{33... | collective-permute-start | bytes 221192 | tf_op jit(solution)/shard_map/ppermute | solution.py:30
  137.2 1.5 fusion.1
  138.7 1.9 collective-permute-start.11
  140.6 3.9 %collective-permute-start.10 = (bf16[96,3,384]{2,1,0:T(4,128)(2,1)S(1)}, bf16[96,3,384]{2,1,0:T(4,128)(2,1)S(1)}, u32[]{:S(2)}, u32[]{:S(2)}) collective-permute-start(bf16[96,3,384]{2,1,0:T(4,128)(2,1)S(1)} %get-tuple-element.19), channel_id=1, source_target_pairs={{0,1},{1,2},{2,3},{3,4},{4,5},{5,6},{6,7},{7,8},{8,9},{9,10},{10,1... | collective-permute-start | bytes 663560 | tf_op jit(solution)/shard_map/ppermute | solution.py:32
  144.6 0.8 fusion
  145.4 3.2 %collective-permute-start.15 = (bf16[3,3,384]{2,1,0:T(4,128)(2,1)S(1)}, bf16[3,3,384]{2,1,0:T(4,128)(2,1)S(1)}, u32[]{:S(2)}, u32[]{:S(2)}) collective-permute-start(bf16[3,3,384]{2,1,0:T(4,128)(2,1)S(1)} %get-tuple-element.14), channel_id=1, source_target_pairs={{17,0},{18,1},{19,2},{20,3},{21,4},{22,5},{23,6},{24,7},{25,8},{26... | collective-permute-start | bytes 20744 | tf_op jit(solution)/shard_map/ppermute | solution.py:33
  148.6 1.8 collective-permute-done.15.refs_8_
  150.3 2.0 %collective-permute-start.14 = (bf16[3,3,384]{2,1,0:T(4,128)(2,1)S(1)}, bf16[3,3,384]{2,1,0:T(4,128)(2,1)S(1)}, u32[]{:S(2)}, u32[]{:S(2)}) collective-permute-start(bf16[3,3,384]{2,1,0:T(4,128)(2,1)S(1)} %get-tuple-element.15), channel_id=1, source_target_pairs={{16,1},{17,2},{18,3},{19,4},{20,5},{21,6},{22,7},{23,8},{24,9},{25... | collective-permute-start | bytes 20744 | tf_op jit(solution)/shard_map/ppermute | solution.py:33
  152.3 5.5 %collective-permute-done.14.refs_7_ = bf16[3,3,384]{2,1,0:T(4,128)(2,1)S(1)} collective-permute-done((bf16[3,3,384]{2,1,0:T(4,128)(2,1)S(1)}, bf16[3,3,384]{2,1,0:T(4,128)(2,1)S(1)}, u32[]{:S(2)}, u32[]{:S(2)}) %collective-permute-start.14) | collective-permute-done | bytes 6944 | tf_op jit(solution)/shard_map/ppermute | solution.py:33
  157.9 4.5 %collective-permute-start.13 = (bf16[3,3,384]{2,1,0:T(4,128)(2,1)S(1)}, bf16[3,3,384]{2,1,0:T(4,128)(2,1)S(1)}, u32[]{:S(2)}, u32[]{:S(2)}) collective-permute-start(bf16[3,3,384]{2,1,0:T(4,128)(2,1)S(1)} %get-tuple-element.16), channel_id=1, source_target_pairs={{1,16},{2,17},{3,18},{4,19},{5,20},{6,21},{7,22},{8,23},{9,24},{10... | collective-permute-start | bytes 20744 | tf_op jit(solution)/shard_map/ppermute | solution.py:33
  162.4 1.4 collective-permute-done.13.refs_6_
  163.8 1.9 collective-permute-start.12
  165.7 6.1 %collective-permute-done.12.refs_5_ = bf16[3,3,384]{2,1,0:T(4,128)(2,1)S(1)} collective-permute-done((bf16[3,3,384]{2,1,0:T(4,128)(2,1)S(1)}, bf16[3,3,384]{2,1,0:T(4,128)(2,1)S(1)}, u32[]{:S(2)}, u32[]{:S(2)}) %collective-permute-start.12) | collective-permute-done | bytes 6944 | tf_op jit(solution)/shard_map/ppermute | solution.py:33
  171.8 0.0 collective-permute-done.8.refs_1_
  171.8 0.0 collective-permute-done.9.refs_2_
  171.8 0.0 collective-permute-done.11.refs_4_
  171.8 0.0 collective-permute-done.10.refs_3_
  171.8 0.0 copy-start.1
  171.8 0.0 copy-done.8
  171.8 0.0 copy-done.9
  171.8 0.0 copy-done.10
  171.8 0.5 copy-done.11
  172.4 0.0 copy-done.4
  172.4 0.0 copy-done.5
  172.4 0.1 copy-done
  172.6 0.1 copy-done.1
  172.6 22.4 %shard_map.116 = bf16[96,32,384]{2,1,0:T(8,128)(2,1)} custom-call(bf16[96,32,384]{2,1,0:T(8,128)(2,1)} %bitcast.19, bf16[3,32,384]{2,1,0:T(8,128)(2,1)} %copy-done.4, bf16[3,32,384]{2,1,0:T(8,128)(2,1)} %copy-done.5, bf16[96,3,384]{2,1,0:T(4,128)(2,1)} %copy-done.1, bf16[96,3,384]{2,1,0:T(4,128)(2,1)} %copy-done, bf16[3,3,384]{2,1,0:T(4,128)(2,1)} %copy-done.11, ...), custom_call_target="tpu_custom_call" | custom-call | tf_op jit(solution)/shard_map/pallas_call | solution.py:115
  (21 shorter events, 0.0 us)
Async XLA Ops:
  1.4 24.3 %collective-permute-start.7 = (bf16[3,3,384]{2,1,0:T(4,128)(2,1)S(1)}, bf16[3,3,384]{2,1,0:T(4,128)(2,1)S(1)}, u32[]{:S(2)}, u32[]{:S(2)}) collective-permute-start(bf16[3,3,384]{2,1,0:T(4,128)(2,1)S(1)} %get-tuple-element.22), channel_id=1, source_target_pairs={{17,0},{18,1},{19,2},{20,3},{21,4},{22,5},{23,6},{24,7},{25,8},{26... | collective-permute-start | bytes 20744 | tf_op jit(solution)/shard_map/ppermute | solution.py:33
  7.0 20.7 %collective-permute-start.6 = (bf16[3,3,384]{2,1,0:T(4,128)(2,1)S(1)}, bf16[3,3,384]{2,1,0:T(4,128)(2,1)S(1)}, u32[]{:S(2)}, u32[]{:S(2)}) collective-permute-start(bf16[3,3,384]{2,1,0:T(4,128)(2,1)S(1)} %get-tuple-element.23), channel_id=1, source_target_pairs={{16,1},{17,2},{18,3},{19,4},{20,5},{21,6},{22,7},{23,8},{24,9},{25... | collective-permute-start | bytes 20744 | tf_op jit(solution)/shard_map/ppermute | solution.py:33
  8.9 24.8 %collective-permute-start.5 = (bf16[3,3,384]{2,1,0:T(4,128)(2,1)S(1)}, bf16[3,3,384]{2,1,0:T(4,128)(2,1)S(1)}, u32[]{:S(2)}, u32[]{:S(2)}) collective-permute-start(bf16[3,3,384]{2,1,0:T(4,128)(2,1)S(1)} %get-tuple-element.24), channel_id=1, source_target_pairs={{1,16},{2,17},{3,18},{4,19},{5,20},{6,21},{7,22},{8,23},{9,24},{10... | collective-permute-start | bytes 20744 | tf_op jit(solution)/shard_map/ppermute | solution.py:33
  14.7 23.8 %collective-permute-start.4 = (bf16[3,3,384]{2,1,0:T(4,128)(2,1)S(1)}, bf16[3,3,384]{2,1,0:T(4,128)(2,1)S(1)}, u32[]{:S(2)}, u32[]{:S(2)}) collective-permute-start(bf16[3,3,384]{2,1,0:T(4,128)(2,1)S(1)} %get-tuple-element.25), channel_id=1, source_target_pairs={{0,17},{1,18},{2,19},{3,20},{4,21},{5,22},{6,23},{7,24},{8,25},{9,... | collective-permute-start | bytes 20744 | tf_op jit(solution)/shard_map/ppermute | solution.py:33
  17.5 21.0 %collective-permute-start.1 = (bf16[3,32,384]{2,1,0:T(8,128)(2,1)S(1)}, bf16[3,32,384]{2,1,0:T(8,128)(2,1)S(1)}, u32[]{:S(2)}, u32[]{:S(2)}) collective-permute-start(bf16[3,32,384]{2,1,0:T(8,128)(2,1)S(1)} %get-tuple-element.28), channel_id=1, source_target_pairs={{16,0},{32,16},{48,32},{64,48},{80,64},{96,80},{112,96},{17,1},{33... | collective-permute-start | bytes 221192 | tf_op jit(solution)/shard_map/ppermute | solution.py:30
  25.7 21.7 %copy-start.12 = (bf16[3,3,384]{2,1,0:T(4,128)(2,1)}, bf16[3,3,384]{2,1,0:T(4,128)(2,1)S(1)}, u32[]{:S(2)}) copy-start(bf16[3,3,384]{2,1,0:T(4,128)(2,1)S(1)} %collective-permute-done.7.refs_8_) | copy-start | bytes 20740
  25.7 12.8 %collective-permute-start = (bf16[3,32,384]{2,1,0:T(8,128)(2,1)S(1)}, bf16[3,32,384]{2,1,0:T(8,128)(2,1)S(1)}, u32[]{:S(2)}, u32[]{:S(2)}) collective-permute-start(bf16[3,32,384]{2,1,0:T(8,128)(2,1)S(1)} %get-tuple-element.29), channel_id=1, source_target_pairs={{0,16},{16,32},{32,48},{48,64},{64,80},{80,96},{96,112},{1,17},{17... | collective-permute-start | bytes 221192 | tf_op jit(solution)/shard_map/ppermute | solution.py:30
  27.7 19.8 %copy-start.13 = (bf16[3,3,384]{2,1,0:T(4,128)(2,1)}, bf16[3,3,384]{2,1,0:T(4,128)(2,1)S(1)}, u32[]{:S(2)}) copy-start(bf16[3,3,384]{2,1,0:T(4,128)(2,1)S(1)} %collective-permute-done.6.refs_7_) | copy-start | bytes 20740
  27.7 13.2 %collective-permute-start.3 = (bf16[96,3,384]{2,1,0:T(4,128)(2,1)S(1)}, bf16[96,3,384]{2,1,0:T(4,128)(2,1)S(1)}, u32[]{:S(2)}, u32[]{:S(2)}) collective-permute-start(bf16[96,3,384]{2,1,0:T(4,128)(2,1)S(1)} %get-tuple-element.26), channel_id=1, source_target_pairs={{1,0},{2,1},{3,2},{4,3},{5,4},{6,5},{7,6},{8,7},{9,8},{10,9},{11,1... | collective-permute-start | bytes 663560 | tf_op jit(solution)/shard_map/ppermute | solution.py:32
  33.7 13.8 %copy-start.14 = (bf16[3,3,384]{2,1,0:T(4,128)(2,1)}, bf16[3,3,384]{2,1,0:T(4,128)(2,1)S(1)}, u32[]{:S(2)}) copy-start(bf16[3,3,384]{2,1,0:T(4,128)(2,1)S(1)} %collective-permute-done.5.refs_6_) | copy-start | bytes 20740
  33.7 13.7 %collective-permute-start.2 = (bf16[96,3,384]{2,1,0:T(4,128)(2,1)S(1)}, bf16[96,3,384]{2,1,0:T(4,128)(2,1)S(1)}, u32[]{:S(2)}, u32[]{:S(2)}) collective-permute-start(bf16[96,3,384]{2,1,0:T(4,128)(2,1)S(1)} %get-tuple-element.27), channel_id=1, source_target_pairs={{0,1},{1,2},{2,3},{3,4},{4,5},{5,6},{6,7},{7,8},{8,9},{9,10},{10,1... | collective-permute-start | bytes 663560 | tf_op jit(solution)/shard_map/ppermute | solution.py:32
  38.5 9.0 %copy-start.15 = (bf16[3,3,384]{2,1,0:T(4,128)(2,1)}, bf16[3,3,384]{2,1,0:T(4,128)(2,1)S(1)}, u32[]{:S(2)}) copy-start(bf16[3,3,384]{2,1,0:T(4,128)(2,1)S(1)} %collective-permute-done.4.refs_5_) | copy-start | bytes 20740
  38.5 9.0 %copy-start.6 = (bf16[3,32,384]{2,1,0:T(8,128)(2,1)}, bf16[3,32,384]{2,1,0:T(8,128)(2,1)S(1)}, u32[]{:S(2)}) copy-start(bf16[3,32,384]{2,1,0:T(8,128)(2,1)S(1)} %collective-permute-done.1.refs_2_) | copy-start | bytes 221188
  38.5 8.9 %copy-start.7 = (bf16[3,32,384]{2,1,0:T(8,128)(2,1)}, bf16[3,32,384]{2,1,0:T(8,128)(2,1)S(1)}, u32[]{:S(2)}) copy-start(bf16[3,32,384]{2,1,0:T(8,128)(2,1)S(1)} %collective-permute-done.refs_1_) | copy-start | bytes 221188
  40.9 6.6 %copy-start.2 = (bf16[96,3,384]{2,1,0:T(4,128)(2,1)}, bf16[96,3,384]{2,1,0:T(4,128)(2,1)S(1)}, u32[]{:S(2)}) copy-start(bf16[96,3,384]{2,1,0:T(4,128)(2,1)S(1)} %collective-permute-done.3.refs_4_) | copy-start | bytes 663556
  47.5 0.7 copy-start.3
  131.6 40.1 %collective-permute-start.8 = (bf16[3,32,384]{2,1,0:T(8,128)(2,1)S(1)}, bf16[3,32,384]{2,1,0:T(8,128)(2,1)S(1)}, u32[]{:S(2)}, u32[]{:S(2)}) collective-permute-start(bf16[3,32,384]{2,1,0:T(8,128)(2,1)S(1)} %bitcast.23), channel_id=1, source_target_pairs={{0,16},{16,32},{32,48},{48,64},{64,80},{80,96},{96,112},{1,17},{17... | collective-permute-start | bytes 221192 | tf_op jit(solution)/shard_map/ppermute | solution.py:30
  133.6 38.2 %collective-permute-start.9 = (bf16[3,32,384]{2,1,0:T(8,128)(2,1)S(1)}, bf16[3,32,384]{2,1,0:T(8,128)(2,1)S(1)}, u32[]{:S(2)}, u32[]{:S(2)}) collective-permute-start(bf16[3,32,384]{2,1,0:T(8,128)(2,1)S(1)} %bitcast.22), channel_id=1, source_target_pairs={{16,0},{32,16},{48,32},{64,48},{80,64},{96,80},{112,96},{17,1},{33... | collective-permute-start | bytes 221192 | tf_op jit(solution)/shard_map/ppermute | solution.py:30
  138.7 33.1 %collective-permute-start.11 = (bf16[96,3,384]{2,1,0:T(4,128)(2,1)S(1)}, bf16[96,3,384]{2,1,0:T(4,128)(2,1)S(1)}, u32[]{:S(2)}, u32[]{:S(2)}) collective-permute-start(bf16[96,3,384]{2,1,0:T(4,128)(2,1)S(1)} %get-tuple-element.18), channel_id=1, source_target_pairs={{1,0},{2,1},{3,2},{4,3},{5,4},{6,5},{7,6},{8,7},{9,8},{10,9},{11,1... | collective-permute-start | bytes 663560 | tf_op jit(solution)/shard_map/ppermute | solution.py:32
  140.6 31.2 %collective-permute-start.10 = (bf16[96,3,384]{2,1,0:T(4,128)(2,1)S(1)}, bf16[96,3,384]{2,1,0:T(4,128)(2,1)S(1)}, u32[]{:S(2)}, u32[]{:S(2)}) collective-permute-start(bf16[96,3,384]{2,1,0:T(4,128)(2,1)S(1)} %get-tuple-element.19), channel_id=1, source_target_pairs={{0,1},{1,2},{2,3},{3,4},{4,5},{5,6},{6,7},{7,8},{8,9},{9,10},{10,1... | collective-permute-start | bytes 663560 | tf_op jit(solution)/shard_map/ppermute | solution.py:32
  145.4 5.0 %collective-permute-start.15 = (bf16[3,3,384]{2,1,0:T(4,128)(2,1)S(1)}, bf16[3,3,384]{2,1,0:T(4,128)(2,1)S(1)}, u32[]{:S(2)}, u32[]{:S(2)}) collective-permute-start(bf16[3,3,384]{2,1,0:T(4,128)(2,1)S(1)} %get-tuple-element.14), channel_id=1, source_target_pairs={{17,0},{18,1},{19,2},{20,3},{21,4},{22,5},{23,6},{24,7},{25,8},{26... | collective-permute-start | bytes 20744 | tf_op jit(solution)/shard_map/ppermute | solution.py:33
  150.3 21.5 %copy-start.8 = (bf16[3,3,384]{2,1,0:T(4,128)(2,1)}, bf16[3,3,384]{2,1,0:T(4,128)(2,1)S(1)}, u32[]{:S(2)}) copy-start(bf16[3,3,384]{2,1,0:T(4,128)(2,1)S(1)} %collective-permute-done.15.refs_8_) | copy-start | bytes 20740
  150.3 7.5 %collective-permute-start.14 = (bf16[3,3,384]{2,1,0:T(4,128)(2,1)S(1)}, bf16[3,3,384]{2,1,0:T(4,128)(2,1)S(1)}, u32[]{:S(2)}, u32[]{:S(2)}) collective-permute-start(bf16[3,3,384]{2,1,0:T(4,128)(2,1)S(1)} %get-tuple-element.15), channel_id=1, source_target_pairs={{16,1},{17,2},{18,3},{19,4},{20,5},{21,6},{22,7},{23,8},{24,9},{25... | collective-permute-start | bytes 20744 | tf_op jit(solution)/shard_map/ppermute | solution.py:33
  157.9 14.0 %copy-start.9 = (bf16[3,3,384]{2,1,0:T(4,128)(2,1)}, bf16[3,3,384]{2,1,0:T(4,128)(2,1)S(1)}, u32[]{:S(2)}) copy-start(bf16[3,3,384]{2,1,0:T(4,128)(2,1)S(1)} %collective-permute-done.14.refs_7_) | copy-start | bytes 20740
  157.9 5.9 %collective-permute-start.13 = (bf16[3,3,384]{2,1,0:T(4,128)(2,1)S(1)}, bf16[3,3,384]{2,1,0:T(4,128)(2,1)S(1)}, u32[]{:S(2)}, u32[]{:S(2)}) collective-permute-start(bf16[3,3,384]{2,1,0:T(4,128)(2,1)S(1)} %get-tuple-element.16), channel_id=1, source_target_pairs={{1,16},{2,17},{3,18},{4,19},{5,20},{6,21},{7,22},{8,23},{9,24},{10... | collective-permute-start | bytes 20744 | tf_op jit(solution)/shard_map/ppermute | solution.py:33
  163.8 8.1 %copy-start.10 = (bf16[3,3,384]{2,1,0:T(4,128)(2,1)}, bf16[3,3,384]{2,1,0:T(4,128)(2,1)S(1)}, u32[]{:S(2)}) copy-start(bf16[3,3,384]{2,1,0:T(4,128)(2,1)S(1)} %collective-permute-done.13.refs_6_) | copy-start | bytes 20740
  163.8 8.0 %collective-permute-start.12 = (bf16[3,3,384]{2,1,0:T(4,128)(2,1)S(1)}, bf16[3,3,384]{2,1,0:T(4,128)(2,1)S(1)}, u32[]{:S(2)}, u32[]{:S(2)}) collective-permute-start(bf16[3,3,384]{2,1,0:T(4,128)(2,1)S(1)} %get-tuple-element.17), channel_id=1, source_target_pairs={{0,17},{1,18},{2,19},{3,20},{4,21},{5,22},{6,23},{7,24},{8,25},{9,... | collective-permute-start | bytes 20744 | tf_op jit(solution)/shard_map/ppermute | solution.py:33
  171.7 0.6 copy-start.11
  171.8 0.6 copy-start.4
  171.8 0.7 copy-start.5
  171.8 0.8 copy-start
  171.8 0.8 copy-start.1

commit v7 on v5

--- a/solution.py
+++ b/solution.py
@@ -19,16 +19,21 @@
     cols = lax.axis_size("col")
     down = [(i, i + 1) for i in range(rows - 1)]
     up = [(i + 1, i) for i in range(rows - 1)]
+    rightward = [(i, i + 1) for i in range(cols - 1)]
+    leftward = [(i + 1, i) for i in range(cols - 1)]
     top = lax.ppermute(cells[cells.shape[0] - width :], "row", down)
     bottom = lax.ppermute(cells[:width], "row", up)
-    framed = jnp.concatenate([top, cells, bottom], axis=0)
-    left = lax.ppermute(framed[:, cells.shape[1] - width :], "col", [(i, i + 1) for i in range(cols - 1)])
-    right = lax.ppermute(framed[:, :width], "col", [(i + 1, i) for i in range(cols - 1)])
-    return (cells, top, bottom, left, right)
+    left = lax.ppermute(cells[:, cells.shape[1] - width :], "col", rightward)
+    right = lax.ppermute(cells[:, :width], "col", leftward)
+    rims = jnp.concatenate([top, bottom], axis=0)
+    left_corners = lax.ppermute(rims[:, cells.shape[1] - width :], "col", rightward)
+    right_corners = lax.ppermute(rims[:, :width], "col", leftward)
+    return (cells, top, bottom, left, right, left_corners, right_corners)
 
 
 def depthwise_kernel(
-    image_ref, top_ref, bottom_ref, left_ref, right_ref, k_ref, *rest, reach, chunk, flip
+    image_ref, top_ref, bottom_ref, left_ref, right_ref, lc_ref, rc_ref, k_ref, *rest, reach, chunk,
+    flip
 ):
     if len(rest) == 5:
         base_ref, out_ref, framed_ref, shifted_ref, total_ref = rest
@@ -40,8 +45,12 @@
     framed_ref[reach : reach + height, reach : reach + breadth, :] = image_ref[...].astype(jnp.float32)
     framed_ref[:reach, reach : reach + breadth, :] = top_ref[...].astype(jnp.float32)
     framed_ref[reach + height :, reach : reach + breadth, :] = bottom_ref[...].astype(jnp.float32)
-    framed_ref[:, :reach, :] = left_ref[...].astype(jnp.float32)
-    framed_ref[:, reach + breadth :, :] = right_ref[...].astype(jnp.float32)
+    framed_ref[reach : reach + height, :reach, :] = left_ref[...].astype(jnp.float32)
+    framed_ref[reach : reach + height, reach + breadth :, :] = right_ref[...].astype(jnp.float32)
+    framed_ref[:reach, :reach, :] = lc_ref[:reach].astype(jnp.float32)
+    framed_ref[reach + height :, :reach, :] = lc_ref[reach:].astype(jnp.float32)
+    framed_ref[:reach, reach + breadth :, :] = rc_ref[:reach].astype(jnp.float32)
+    framed_ref[reach + height :, reach + breadth :, :] = rc_ref[reach:].astype(jnp.float32)
     for shift_c in range(side):
         shifted_ref[...] = framed_ref[:, shift_c : shift_c + breadth, :]
 
@@ -77,8 +86,10 @@
         pl.BlockSpec((height, breadth, lanes), lambda c: (0, 0, c)),
         pl.BlockSpec((reach, breadth, lanes), lambda c: (0, 0, c)),
         pl.BlockSpec((reach, breadth, lanes), lambda c: (0, 0, c)),
-        pl.BlockSpec((framed[0], reach, lanes), lambda c: (0, 0, c)),
-        pl.BlockSpec((framed[0], reach, lanes), lambda c: (0, 0, c)),
+        pl.BlockSpec((height, reach, lanes), lambda c: (0, 0, c)),
+        pl.BlockSpec((height, reach, lanes), lambda c: (0, 0, c)),
+        pl.BlockSpec((2 * reach, reach, lanes), lambda c: (0, 0, c)),
+        pl.BlockSpec((2 * reach, reach, lanes), lambda c: (0, 0, c)),
         pl.BlockSpec((taps.shape[0], lanes), lambda c: (0, c)),
     ]
     operands = list(pieces) + [taps]

time: 164 us -> 167 us (1.018)
  starting transfers between devices: 23.8 us -> 38.9 us
  waiting for transfers between devices: 21.7 us -> 8.75 us
  local copies, waits for them, and re-layouts: 8.19 us -> 10.3 us
    ppermute x4 -> x8, starting transfers between devices: 13.9 us -> 29 us  [the longest x2 11.3 us: halo_pieces(): right_corners = lax.ppermute(rims[:, :width], 'col', leftward)]
    ppermute x4 -> x8, waiting for transfers between devices: 18.8 us -> 8.74 us  [the longest x2 8.72 us: halo_pieces(): lax.ppermute(rims[:, cells.shape[1] - width:], 'col', rightward)]
    slice x1 -> x4, local copies, waits for them, and re-layouts: 0.25 us -> 3 us  [the longest x2 2.96 us: halo_pieces(): right = lax.ppermute(cells[:, :width], 'col', leftward)]
    ppermute x2, waiting for transfers between devices: 1.87 us -> 0.01 us  [halo_pieces(): bottom = lax.ppermute(cells[:width], 'row', up)]
  transfers between devices with their start and end apart: 8 -> 12, of which waited for: 7 -> 2; matrix products, arithmetic and copies ran while one was open for 4% -> 5% of each run, Pallas kernels for 0% -> 0%
where the time goes in v7:
time: 167 us
  Pallas kernels  105 us (63%)
  starting transfers between devices  38.9 us (23%)
  local copies, waits for them, and re-layouts  10.3 us (6%)
  waiting for transfers between devices  8.75 us (5%)
  other arithmetic  2.79 us (2%)
    pallas_call x2, Pallas kernels, pixel_call(): pl.pallas_call(lambda *refs: kernel(*refs, layout=layout), grid_spec=pltp...  60.6 us
    pallas_call x2, Pallas kernels, depthwise(): pl.pallas_call(lambda *refs: depthwise_kernel(*refs, reach=reach, chunk=c...  44.3 us
    ppermute x2, starting transfers between devices, halo_pieces(): right_corners = lax.ppermute(rims[:, :width], 'col', leftward)  11.3 us
    ppermute x2, starting transfers between devices, halo_pieces(): right = lax.ppermute(cells[:, :width], 'col', leftward)  9.27 us
    ppermute x2, waiting for transfers between devices, halo_pieces(): lax.ppermute(rims[:, cells.shape[1] - width:], 'col', rightward)  8.72 us
    ppermute x2, starting transfers between devices, halo_pieces(): bottom = lax.ppermute(cells[:width], 'row', up)  5.56 us
    ppermute x2, starting transfers between devices, halo_pieces(): left = lax.ppermute(cells[:, cells.shape[1] - width:], 'col', rightward)  4.62 us
    ppermute x2, starting transfers between devices, halo_pieces(): top = lax.ppermute(cells[cells.shape[0] - width:], 'row', down)  4.33 us
  transfers between devices with their start and end apart: 12, of which 2 were waited for; matrix products, arithmetic and copies ran while one was open for 5% of the time, Pallas kernels for 0%

profile of v7, /device:TPU:26, one launch (start us, length us, event | category | flops | bytes accessed | tf_op | source)
XLA Modules:
  0.0 166.6 jit_solution(5695784145901503107)
XLA Ops:
  0.6 0.9 fusion.3
  1.6 1.9 %collective-permute-start.1 = (bf16[3,32,384]{2,1,0:T(8,128)(2,1)S(1)}, bf16[3,32,384]{2,1,0:T(8,128)(2,1)S(1)}, u32[]{:S(2)}, u32[]{:S(2)}) collective-permute-start(bf16[3,32,384]{2,1,0:T(8,128)(2,1)S(1)} %get-tuple-element.20), channel_id=1, source_target_pairs={{16,0},{32,16},{48,32},{64,48},{80,64},{96,80},{112,96},{17,1},{33... | collective-permute-start | bytes 221192 | tf_op jit(solution)/shard_map/ppermute | solution.py:25
  3.5 2.4 %collective-permute-start = (bf16[3,32,384]{2,1,0:T(8,128)(2,1)S(1)}, bf16[3,32,384]{2,1,0:T(8,128)(2,1)S(1)}, u32[]{:S(2)}, u32[]{:S(2)}) collective-permute-start(bf16[3,32,384]{2,1,0:T(8,128)(2,1)S(1)} %get-tuple-element.21), channel_id=1, source_target_pairs={{0,16},{16,32},{32,48},{48,64},{64,80},{80,96},{96,112},{1,17},{17... | collective-permute-start | bytes 221192 | tf_op jit(solution)/shard_map/ppermute | solution.py:24
  5.9 1.5 fusion.2
  7.4 6.1 %collective-permute-start.3 = (bf16[96,3,384]{2,1,0:T(4,128)(2,1)S(1)}, bf16[96,3,384]{2,1,0:T(4,128)(2,1)S(1)}, u32[]{:S(2)}, u32[]{:S(2)}) collective-permute-start(bf16[96,3,384]{2,1,0:T(4,128)(2,1)S(1)} %get-tuple-element.18), channel_id=1, source_target_pairs={{1,0},{2,1},{3,2},{4,3},{5,4},{6,5},{7,6},{8,7},{9,8},{10,9},{11,1... | collective-permute-start | bytes 663560 | tf_op jit(solution)/shard_map/ppermute | solution.py:27
  13.5 1.9 %collective-permute-start.2 = (bf16[96,3,384]{2,1,0:T(4,128)(2,1)S(1)}, bf16[96,3,384]{2,1,0:T(4,128)(2,1)S(1)}, u32[]{:S(2)}, u32[]{:S(2)}) collective-permute-start(bf16[96,3,384]{2,1,0:T(4,128)(2,1)S(1)} %get-tuple-element.19), channel_id=1, source_target_pairs={{0,1},{1,2},{2,3},{3,4},{4,5},{5,6},{6,7},{7,8},{8,9},{9,10},{10,1... | collective-permute-start | bytes 663560 | tf_op jit(solution)/shard_map/ppermute | solution.py:26
  15.5 0.8 copy.21
  16.2 0.7 reduce_window_sum.11
  17.0 0.8 select_reduce_fusion.3
  17.8 0.5 select_reduce_fusion.1
  18.3 0.1 copy.22
  18.4 0.1 copy.23
  18.5 0.0 collective-permute-done.refs_1_
  18.5 0.0 copy-start.7
  18.5 0.0 collective-permute-done.1.refs_2_
  18.5 0.0 copy-start.6
  18.6 6.0 %collective-permute-start.5 = (bf16[6,3,384]{2,1,0:T(4,128)(2,1)S(1)}, bf16[6,3,384]{2,1,0:T(4,128)(2,1)S(1)}, u32[]{:S(2)}, u32[]{:S(2)}) collective-permute-start(bf16[6,3,384]{2,1,0:T(4,128)(2,1)S(1)} %get-tuple-element.24), channel_id=1, source_target_pairs={{1,0},{2,1},{3,2},{4,3},{5,4},{6,5},{7,6},{8,7},{9,8},{10,9},{11,1... | collective-permute-start | bytes 41480 | tf_op jit(solution)/shard_map/ppermute | solution.py:30
  24.6 1.9 %collective-permute-start.4 = (bf16[6,3,384]{2,1,0:T(4,128)(2,1)S(1)}, bf16[6,3,384]{2,1,0:T(4,128)(2,1)S(1)}, u32[]{:S(2)}, u32[]{:S(2)}) collective-permute-start(bf16[6,3,384]{2,1,0:T(4,128)(2,1)S(1)} %get-tuple-element.25), channel_id=1, source_target_pairs={{0,1},{1,2},{2,3},{3,4},{4,5},{5,6},{6,7},{7,8},{8,9},{9,10},{10,1... | collective-permute-start | bytes 41480 | tf_op jit(solution)/shard_map/ppermute | solution.py:29
  26.6 0.7 and_convert_fusion
  27.3 0.1 copy.24
  27.4 0.7 reshape.47.refs_0_
  28.0 1.4 reshape.48.refs_7_
  29.5 0.0 collective-permute-done.5.refs_6_
  29.5 0.0 copy-start.8
  29.5 2.9 %collective-permute-done.4.refs_5_ = bf16[6,3,384]{2,1,0:T(4,128)(2,1)S(1)} collective-permute-done((bf16[6,3,384]{2,1,0:T(4,128)(2,1)S(1)}, bf16[6,3,384]{2,1,0:T(4,128)(2,1)S(1)}, u32[]{:S(2)}, u32[]{:S(2)}) %collective-permute-start.4) | collective-permute-done | bytes 13856 | tf_op jit(solution)/shard_map/ppermute | solution.py:29
  32.4 0.0 copy-start.9
  32.4 0.0 collective-permute-done.3.refs_4_
  32.4 0.0 copy-start.4
  32.4 0.0 collective-permute-done.2.refs_3_
  32.4 0.0 copy-done.7
  32.4 0.0 copy-done.6
  32.4 0.0 copy-done.8
  32.4 0.6 copy-done.9
  33.0 0.1 copy-done.4
  33.1 0.0 copy-start.5
  33.1 0.7 copy-done.5
  33.8 21.9 %shard_map.113 = bf16[96,32,384]{2,1,0:T(8,128)(2,1)} custom-call(bf16[96,32,384]{2,1,0:T(8,128)(2,1)} %refs_0_.1, bf16[3,32,384]{2,1,0:T(8,128)(2,1)} %copy-done.7, bf16[3,32,384]{2,1,0:T(8,128)(2,1)} %copy-done.6, bf16[96,3,384]{2,1,0:T(4,128)(2,1)} %copy-done.5, bf16[96,3,384]{2,1,0:T(4,128)(2,1)} %copy-done.4, bf16[6,3,384]{2,1,0:T(4,128)(2,1)} %copy-done.9, ...), custom_call_target="tpu_custom_call" | custom-call | tf_op jit(solution)/shard_map/pallas_call | solution.py:99
  55.7 28.9 %shard_map.114 = (bf16[3072,384]{1,0:T(8,128)(2,1)}, bf16[768,768]{1,0:T(8,128)(2,1)}) custom-call(s32[48]{0:T(128)} %reshape.47.refs_0_, bf16[3072,384]{1,0:T(8,128)(2,1)} %bitcast.12, bf16[3072,384]{1,0:T(8,128)(2,1)} %bitcast.14, bf16[384,1536]{1,0:T(8,128)(2,1)} %refs_4_.3, bf16[1536,384]{1,0:T(8,128)(2,1)} %refs_5_.1, bf16[4,384,768]{2,1,0:T(8,128)(2,1)} %bitcast.15), custom_call_target="tpu_custom_call" | custom-call | tf_op jit(solution)/shard_map/pallas_call | solution.py:245
  84.6 31.7 %shard_map.115 = (bf16[3072,384]{1,0:T(8,128)(2,1)}, bf16[3072,384]{1,0:T(8,128)(2,1)}) custom-call(s32[48]{0:T(128)} %reshape.47.refs_0_, bf16[3072,384]{1,0:T(8,128)(2,1)} %bitcast.13, bf16[3072,384]{1,0:T(8,128)(2,1)} %get-tuple-element.7.refs_2_, bf16[768,768]{1,0:T(8,128)(2,1)} %bitcast.20, bf16[384,1536]{1,0:T(8,128)(2,1)} %refs_4_.3, ...), custom_call_target="tpu_custom_call" | custom-call | tf_op jit(solution)/shard_map/pallas_call | solution.py:245
  116.3 0.9 fusion.1
  117.3 1.9 %collective-permute-start.6 = (bf16[3,32,384]{2,1,0:T(8,128)(2,1)S(1)}, bf16[3,32,384]{2,1,0:T(8,128)(2,1)S(1)}, u32[]{:S(2)}, u32[]{:S(2)}) collective-permute-start(bf16[3,32,384]{2,1,0:T(8,128)(2,1)S(1)} %bitcast.22), channel_id=1, source_target_pairs={{0,16},{16,32},{32,48},{48,64},{64,80},{80,96},{96,112},{1,17},{17... | collective-permute-start | bytes 221192 | tf_op jit(solution)/shard_map/ppermute | solution.py:24
  119.2 3.6 %collective-permute-start.7 = (bf16[3,32,384]{2,1,0:T(8,128)(2,1)S(1)}, bf16[3,32,384]{2,1,0:T(8,128)(2,1)S(1)}, u32[]{:S(2)}, u32[]{:S(2)}) collective-permute-start(bf16[3,32,384]{2,1,0:T(8,128)(2,1)S(1)} %bitcast.21), channel_id=1, source_target_pairs={{16,0},{32,16},{48,32},{64,48},{80,64},{96,80},{112,96},{17,1},{33... | collective-permute-start | bytes 221192 | tf_op jit(solution)/shard_map/ppermute | solution.py:25
  122.8 1.5 fusion
  124.3 3.1 %collective-permute-start.9 = (bf16[96,3,384]{2,1,0:T(4,128)(2,1)S(1)}, bf16[96,3,384]{2,1,0:T(4,128)(2,1)S(1)}, u32[]{:S(2)}, u32[]{:S(2)}) collective-permute-start(bf16[96,3,384]{2,1,0:T(4,128)(2,1)S(1)} %get-tuple-element.14), channel_id=1, source_target_pairs={{1,0},{2,1},{3,2},{4,3},{5,4},{6,5},{7,6},{8,7},{9,8},{10,9},{11,1... | collective-permute-start | bytes 663560 | tf_op jit(solution)/shard_map/ppermute | solution.py:27
  127.5 2.7 %collective-permute-start.8 = (bf16[96,3,384]{2,1,0:T(4,128)(2,1)S(1)}, bf16[96,3,384]{2,1,0:T(4,128)(2,1)S(1)}, u32[]{:S(2)}, u32[]{:S(2)}) collective-permute-start(bf16[96,3,384]{2,1,0:T(4,128)(2,1)S(1)} %get-tuple-element.15), channel_id=1, source_target_pairs={{0,1},{1,2},{2,3},{3,4},{4,5},{5,6},{6,7},{7,8},{8,9},{9,10},{10,1... | collective-permute-start | bytes 663560 | tf_op jit(solution)/shard_map/ppermute | solution.py:26
  130.2 0.0 collective-permute-done.6.refs_1_
  130.2 0.0 copy-start
  130.2 0.0 collective-permute-done.7.refs_2_
  130.2 0.0 copy-start.1
  130.3 5.3 %collective-permute-start.11 = (bf16[6,3,384]{2,1,0:T(4,128)(2,1)S(1)}, bf16[6,3,384]{2,1,0:T(4,128)(2,1)S(1)}, u32[]{:S(2)}, u32[]{:S(2)}) collective-permute-start(bf16[6,3,384]{2,1,0:T(4,128)(2,1)S(1)} %get-tuple-element.22), channel_id=1, source_target_pairs={{1,0},{2,1},{3,2},{4,3},{5,4},{6,5},{7,6},{8,7},{9,8},{10,9},{11,1... | collective-permute-start | bytes 41480 | tf_op jit(solution)/shard_map/ppermute | solution.py:30
  135.6 1.9 %collective-permute-start.10 = (bf16[6,3,384]{2,1,0:T(4,128)(2,1)S(1)}, bf16[6,3,384]{2,1,0:T(4,128)(2,1)S(1)}, u32[]{:S(2)}, u32[]{:S(2)}) collective-permute-start(bf16[6,3,384]{2,1,0:T(4,128)(2,1)S(1)} %get-tuple-element.23), channel_id=1, source_target_pairs={{0,1},{1,2},{2,3},{3,4},{4,5},{5,6},{6,7},{7,8},{8,9},{9,10},{10,1... | collective-permute-start | bytes 41480 | tf_op jit(solution)/shard_map/ppermute | solution.py:29
  137.5 0.0 collective-permute-done.11.refs_6_
  137.5 0.0 copy-start.10
  137.5 5.8 %collective-permute-done.10.refs_5_ = bf16[6,3,384]{2,1,0:T(4,128)(2,1)S(1)} collective-permute-done((bf16[6,3,384]{2,1,0:T(4,128)(2,1)S(1)}, bf16[6,3,384]{2,1,0:T(4,128)(2,1)S(1)}, u32[]{:S(2)}, u32[]{:S(2)}) %collective-permute-start.10) | collective-permute-done | bytes 13856 | tf_op jit(solution)/shard_map/ppermute | solution.py:29
  143.3 0.0 collective-permute-done.9.refs_4_
  143.3 0.0 collective-permute-done.8.refs_3_
  143.3 0.0 copy-start.3
  143.3 0.0 copy-done
  143.4 0.0 copy-done.1
  143.4 0.0 copy-done.10
  143.4 0.5 copy-done.11
  143.9 0.1 copy-done.2
  144.0 0.1 copy-done.3
  144.2 22.5 %shard_map.116 = bf16[96,32,384]{2,1,0:T(8,128)(2,1)} custom-call(bf16[96,32,384]{2,1,0:T(8,128)(2,1)} %bitcast.18, bf16[3,32,384]{2,1,0:T(8,128)(2,1)} %copy-done, bf16[3,32,384]{2,1,0:T(8,128)(2,1)} %copy-done.1, bf16[96,3,384]{2,1,0:T(4,128)(2,1)} %copy-done.3, bf16[96,3,384]{2,1,0:T(4,128)(2,1)} %copy-done.2, bf16[6,3,384]{2,1,0:T(4,128)(2,1)} %copy-done.11, ...), custom_call_target="tpu_custom_call" | custom-call | tf_op jit(solution)/shard_map/pallas_call | solution.py:99
  (9 shorter events, 0.1 us)
Async XLA Ops:
  1.6 17.0 %collective-permute-start.1 = (bf16[3,32,384]{2,1,0:T(8,128)(2,1)S(1)}, bf16[3,32,384]{2,1,0:T(8,128)(2,1)S(1)}, u32[]{:S(2)}, u32[]{:S(2)}) collective-permute-start(bf16[3,32,384]{2,1,0:T(8,128)(2,1)S(1)} %get-tuple-element.20), channel_id=1, source_target_pairs={{16,0},{32,16},{48,32},{64,48},{80,64},{96,80},{112,96},{17,1},{33... | collective-permute-start | bytes 221192 | tf_op jit(solution)/shard_map/ppermute | solution.py:25
  3.5 15.0 %collective-permute-start = (bf16[3,32,384]{2,1,0:T(8,128)(2,1)S(1)}, bf16[3,32,384]{2,1,0:T(8,128)(2,1)S(1)}, u32[]{:S(2)}, u32[]{:S(2)}) collective-permute-start(bf16[3,32,384]{2,1,0:T(8,128)(2,1)S(1)} %get-tuple-element.21), channel_id=1, source_target_pairs={{0,16},{16,32},{32,48},{48,64},{64,80},{80,96},{96,112},{1,17},{17... | collective-permute-start | bytes 221192 | tf_op jit(solution)/shard_map/ppermute | solution.py:24
  7.4 25.0 %collective-permute-start.3 = (bf16[96,3,384]{2,1,0:T(4,128)(2,1)S(1)}, bf16[96,3,384]{2,1,0:T(4,128)(2,1)S(1)}, u32[]{:S(2)}, u32[]{:S(2)}) collective-permute-start(bf16[96,3,384]{2,1,0:T(4,128)(2,1)S(1)} %get-tuple-element.18), channel_id=1, source_target_pairs={{1,0},{2,1},{3,2},{4,3},{5,4},{6,5},{7,6},{8,7},{9,8},{10,9},{11,1... | collective-permute-start | bytes 663560 | tf_op jit(solution)/shard_map/ppermute | solution.py:27
  13.5 18.9 %collective-permute-start.2 = (bf16[96,3,384]{2,1,0:T(4,128)(2,1)S(1)}, bf16[96,3,384]{2,1,0:T(4,128)(2,1)S(1)}, u32[]{:S(2)}, u32[]{:S(2)}) collective-permute-start(bf16[96,3,384]{2,1,0:T(4,128)(2,1)S(1)} %get-tuple-element.19), channel_id=1, source_target_pairs={{0,1},{1,2},{2,3},{3,4},{4,5},{5,6},{6,7},{7,8},{8,9},{9,10},{10,1... | collective-permute-start | bytes 663560 | tf_op jit(solution)/shard_map/ppermute | solution.py:26
  18.5 13.9 %copy-start.7 = (bf16[3,32,384]{2,1,0:T(8,128)(2,1)}, bf16[3,32,384]{2,1,0:T(8,128)(2,1)S(1)}, u32[]{:S(2)}) copy-start(bf16[3,32,384]{2,1,0:T(8,128)(2,1)S(1)} %collective-permute-done.refs_1_) | copy-start | bytes 221188
  18.5 13.9 %copy-start.6 = (bf16[3,32,384]{2,1,0:T(8,128)(2,1)}, bf16[3,32,384]{2,1,0:T(8,128)(2,1)S(1)}, u32[]{:S(2)}) copy-start(bf16[3,32,384]{2,1,0:T(8,128)(2,1)S(1)} %collective-permute-done.1.refs_2_) | copy-start | bytes 221188
  18.6 10.9 %collective-permute-start.5 = (bf16[6,3,384]{2,1,0:T(4,128)(2,1)S(1)}, bf16[6,3,384]{2,1,0:T(4,128)(2,1)S(1)}, u32[]{:S(2)}, u32[]{:S(2)}) collective-permute-start(bf16[6,3,384]{2,1,0:T(4,128)(2,1)S(1)} %get-tuple-element.24), channel_id=1, source_target_pairs={{1,0},{2,1},{3,2},{4,3},{5,4},{6,5},{7,6},{8,7},{9,8},{10,9},{11,1... | collective-permute-start | bytes 41480 | tf_op jit(solution)/shard_map/ppermute | solution.py:30
  24.6 7.8 %collective-permute-start.4 = (bf16[6,3,384]{2,1,0:T(4,128)(2,1)S(1)}, bf16[6,3,384]{2,1,0:T(4,128)(2,1)S(1)}, u32[]{:S(2)}, u32[]{:S(2)}) collective-permute-start(bf16[6,3,384]{2,1,0:T(4,128)(2,1)S(1)} %get-tuple-element.25), channel_id=1, source_target_pairs={{0,1},{1,2},{2,3},{3,4},{4,5},{5,6},{6,7},{7,8},{8,9},{9,10},{10,1... | collective-permute-start | bytes 41480 | tf_op jit(solution)/shard_map/ppermute | solution.py:29
  29.5 2.9 %copy-start.8 = (bf16[6,3,384]{2,1,0:T(4,128)(2,1)}, bf16[6,3,384]{2,1,0:T(4,128)(2,1)S(1)}, u32[]{:S(2)}) copy-start(bf16[6,3,384]{2,1,0:T(4,128)(2,1)S(1)} %collective-permute-done.5.refs_6_) | copy-start | bytes 41476
  32.4 0.6 copy-start.9
  32.4 0.7 copy-start.4
  33.1 0.7 copy-start.5
  117.3 12.9 %collective-permute-start.6 = (bf16[3,32,384]{2,1,0:T(8,128)(2,1)S(1)}, bf16[3,32,384]{2,1,0:T(8,128)(2,1)S(1)}, u32[]{:S(2)}, u32[]{:S(2)}) collective-permute-start(bf16[3,32,384]{2,1,0:T(8,128)(2,1)S(1)} %bitcast.22), channel_id=1, source_target_pairs={{0,16},{16,32},{32,48},{48,64},{64,80},{80,96},{96,112},{1,17},{17... | collective-permute-start | bytes 221192 | tf_op jit(solution)/shard_map/ppermute | solution.py:24
  119.2 11.0 %collective-permute-start.7 = (bf16[3,32,384]{2,1,0:T(8,128)(2,1)S(1)}, bf16[3,32,384]{2,1,0:T(8,128)(2,1)S(1)}, u32[]{:S(2)}, u32[]{:S(2)}) collective-permute-start(bf16[3,32,384]{2,1,0:T(8,128)(2,1)S(1)} %bitcast.21), channel_id=1, source_target_pairs={{16,0},{32,16},{48,32},{64,48},{80,64},{96,80},{112,96},{17,1},{33... | collective-permute-start | bytes 221192 | tf_op jit(solution)/shard_map/ppermute | solution.py:25
  124.3 19.0 %collective-permute-start.9 = (bf16[96,3,384]{2,1,0:T(4,128)(2,1)S(1)}, bf16[96,3,384]{2,1,0:T(4,128)(2,1)S(1)}, u32[]{:S(2)}, u32[]{:S(2)}) collective-permute-start(bf16[96,3,384]{2,1,0:T(4,128)(2,1)S(1)} %get-tuple-element.14), channel_id=1, source_target_pairs={{1,0},{2,1},{3,2},{4,3},{5,4},{6,5},{7,6},{8,7},{9,8},{10,9},{11,1... | collective-permute-start | bytes 663560 | tf_op jit(solution)/shard_map/ppermute | solution.py:27
  127.5 15.9 %collective-permute-start.8 = (bf16[96,3,384]{2,1,0:T(4,128)(2,1)S(1)}, bf16[96,3,384]{2,1,0:T(4,128)(2,1)S(1)}, u32[]{:S(2)}, u32[]{:S(2)}) collective-permute-start(bf16[96,3,384]{2,1,0:T(4,128)(2,1)S(1)} %get-tuple-element.15), channel_id=1, source_target_pairs={{0,1},{1,2},{2,3},{3,4},{4,5},{5,6},{6,7},{7,8},{8,9},{9,10},{10,1... | collective-permute-start | bytes 663560 | tf_op jit(solution)/shard_map/ppermute | solution.py:26
  130.2 13.1 %copy-start = (bf16[3,32,384]{2,1,0:T(8,128)(2,1)}, bf16[3,32,384]{2,1,0:T(8,128)(2,1)S(1)}, u32[]{:S(2)}) copy-start(bf16[3,32,384]{2,1,0:T(8,128)(2,1)S(1)} %collective-permute-done.6.refs_1_) | copy-start | bytes 221188
  130.2 13.1 %copy-start.1 = (bf16[3,32,384]{2,1,0:T(8,128)(2,1)}, bf16[3,32,384]{2,1,0:T(8,128)(2,1)S(1)}, u32[]{:S(2)}) copy-start(bf16[3,32,384]{2,1,0:T(8,128)(2,1)S(1)} %collective-permute-done.7.refs_2_) | copy-start | bytes 221188
  130.3 7.2 %collective-permute-start.11 = (bf16[6,3,384]{2,1,0:T(4,128)(2,1)S(1)}, bf16[6,3,384]{2,1,0:T(4,128)(2,1)S(1)}, u32[]{:S(2)}, u32[]{:S(2)}) collective-permute-start(bf16[6,3,384]{2,1,0:T(4,128)(2,1)S(1)} %get-tuple-element.22), channel_id=1, source_target_pairs={{1,0},{2,1},{3,2},{4,3},{5,4},{6,5},{7,6},{8,7},{9,8},{10,9},{11,1... | collective-permute-start | bytes 41480 | tf_op jit(solution)/shard_map/ppermute | solution.py:30
  135.6 7.8 %collective-permute-start.10 = (bf16[6,3,384]{2,1,0:T(4,128)(2,1)S(1)}, bf16[6,3,384]{2,1,0:T(4,128)(2,1)S(1)}, u32[]{:S(2)}, u32[]{:S(2)}) collective-permute-start(bf16[6,3,384]{2,1,0:T(4,128)(2,1)S(1)} %get-tuple-element.23), channel_id=1, source_target_pairs={{0,1},{1,2},{2,3},{3,4},{4,5},{5,6},{6,7},{7,8},{8,9},{9,10},{10,1... | collective-permute-start | bytes 41480 | tf_op jit(solution)/shard_map/ppermute | solution.py:29
  137.5 5.9 %copy-start.10 = (bf16[6,3,384]{2,1,0:T(4,128)(2,1)}, bf16[6,3,384]{2,1,0:T(4,128)(2,1)S(1)}, u32[]{:S(2)}) copy-start(bf16[6,3,384]{2,1,0:T(4,128)(2,1)S(1)} %collective-permute-done.11.refs_6_) | copy-start | bytes 41476
  143.3 0.6 copy-start.11
  143.3 0.7 copy-start.2
  143.3 0.8 copy-start.3

commit v8 on v5

--- a/solution.py
+++ b/solution.py
@@ -7,6 +7,7 @@
 
 KS = 7
 LIVE_DEV = 18
+SPAN = 512
 
 
 EPSILON = 1e-06
@@ -149,10 +150,18 @@
     *, layout
 ):
     normed, _ = normalize(mixed_ref[...].astype(jnp.float32))
-    hidden = jnp.dot(normed.astype(jnp.bfloat16), w_in_ref[...], preferred_element_type=jnp.float32)
-    cdf = 0.5 * (1.0 + lax.erf(hidden * ROOT_HALF))
-    activated = (hidden * cdf).astype(jnp.bfloat16)
-    branch = jnp.dot(activated, w_out_ref[...], preferred_element_type=jnp.float32)
+    normed_low = normed.astype(jnp.bfloat16)
+    branch = None
+    for start in range(0, w_in_ref.shape[1], SPAN):
+        hidden = jnp.dot(
+            normed_low, w_in_ref[:, start : start + SPAN], preferred_element_type=jnp.float32
+        )
+        cdf = 0.5 * (1.0 + lax.erf(hidden * ROOT_HALF))
+        activated = (hidden * cdf).astype(jnp.bfloat16)
+        part = jnp.dot(
+            activated, w_out_ref[start : start + SPAN, :], preferred_element_type=jnp.float32
+        )
+        branch = part if branch is None else branch + part
     branch = jnp.where(pixel_live(live, layout), branch.astype(jnp.bfloat16).astype(jnp.float32), 0.0)
     summed = (image_ref[...].astype(jnp.float32) + branch).astype(jnp.bfloat16)
     summed_ref[...] = summed
@@ -197,15 +206,22 @@
                         y * half : (y + 1) * half, k * 128 : (k + 1) * 128
                     ]
     normed, inv_std = normalize(mixed_ref[...].astype(jnp.float32))
-    hidden = jnp.dot(normed.astype(jnp.bfloat16), w_in_ref[...], preferred_element_type=jnp.float32)
-    cdf = 0.5 * (1.0 + lax.erf(hidden * ROOT_HALF))
-    slope = cdf + hidden * INV_ROOT_TAU * jnp.exp(-0.5 * hidden * hidden)
     down_normed, down_inv = normalize(summed_ref[...].astype(jnp.float32))
     grad_normed = jnp.concatenate([grad_ref[k] for k in range(grad_ref.shape[0])], axis=1)
     grad_summed = normalize_back(grad_normed, down_normed, down_inv).astype(jnp.bfloat16)
     grad_summed_ref[...] = grad_summed
-    grad_hidden = (times_transposed(grad_summed, w_out_ref[...]) * slope).astype(jnp.bfloat16)
-    grad_norm_in = times_transposed(grad_hidden, w_in_ref[...])
+    normed_low = normed.astype(jnp.bfloat16)
+    grad_norm_in = None
+    for start in range(0, w_in_ref.shape[1], SPAN):
+        w_in = w_in_ref[:, start : start + SPAN]
+        hidden = jnp.dot(normed_low, w_in, preferred_element_type=jnp.float32)
+        cdf = 0.5 * (1.0 + lax.erf(hidden * ROOT_HALF))
+        slope = cdf + hidden * INV_ROOT_TAU * jnp.exp(-0.5 * hidden * hidden)
+        grad_hidden = (
+            times_transposed(grad_summed, w_out_ref[start : start + SPAN, :]) * slope
+        ).astype(jnp.bfloat16)
+        part = times_transposed(grad_hidden, w_in)
+        grad_norm_in = part if grad_norm_in is None else grad_norm_in + part
     grad_owned_mixed = normalize_back(grad_norm_in, normed, inv_std)
     grad_mixed_ref[...] = jnp.where(pixel_live(live, layout), grad_owned_mixed, 0.0).astype(jnp.bfloat16)
 

time: 164 us -> 168 us (1.024)
  Pallas kernels: 105 us -> 109 us
    pallas_call x2, Pallas kernels: 60.6 us -> 64.6 us  [pixel_call(): pl.pallas_call(lambda *refs: kernel(*refs, layout=layout), grid_spec=pltp...]
where the time goes in v8:
time: 168 us; the launch traced here: 167 us
  Pallas kernels  109 us (65%)
  starting transfers between devices  23.8 us (14%)
  waiting for transfers between devices  21.7 us (13%)
  local copies, waits for them, and re-layouts  8.19 us (5%)
  other arithmetic  3.6 us (2%)
    pallas_call x2, Pallas kernels, pixel_call(): pl.pallas_call(lambda *refs: kernel(*refs, layout=layout), grid_spec=pltp...  64.6 us
    pallas_call x2, Pallas kernels, depthwise(): pl.pallas_call(lambda *refs: depthwise_kernel(*refs, reach=reach, chunk=c...  44.2 us
    ppermute x2, waiting for transfers between devices, halo_pieces(): lax.ppermute(framed[:, cells.shape[1] - width:], 'col', [(i, i + 1) for i...  10.3 us
    ppermute x2, waiting for transfers between devices, halo_pieces(): lax.ppermute(framed[:, :width], 'col', [(i + 1, i) for i in range(cols -...  8.52 us
    ppermute x2, starting transfers between devices, halo_pieces(): lax.ppermute(framed[:, :width], 'col', [(i + 1, i) for i in range(cols -...  8.05 us
    ppermute x2, starting transfers between devices, halo_pieces(): lax.ppermute(framed[:, cells.shape[1] - width:], 'col', [(i, i + 1) for i...  5.84 us
    ppermute x2, starting transfers between devices, halo_pieces(): bottom = lax.ppermute(cells[:width], 'row', up)  5.56 us
    unnamed x27, local copies, waits for them, and re-layouts  4.46 us
  transfers between devices with their start and end apart: 8, of which 7 were waited for; matrix products, arithmetic and copies ran while one was open for 4% of the time, Pallas kernels for 0%

profile of v8, /device:TPU:26, one launch (start us, length us, event | category | flops | bytes accessed | tf_op | source)
XLA Modules:
  0.0 166.9 jit_solution(16566990379955911888)
XLA Ops:
  0.6 0.9 fusion.2
  1.6 1.9 %collective-permute-start.1 = (bf16[3,32,384]{2,1,0:T(8,128)(2,1)S(1)}, bf16[3,32,384]{2,1,0:T(8,128)(2,1)S(1)}, u32[]{:S(2)}, u32[]{:S(2)}) collective-permute-start(bf16[3,32,384]{2,1,0:T(8,128)(2,1)S(1)} %get-tuple-element.20), channel_id=1, source_target_pairs={{16,0},{32,16},{48,32},{64,48},{80,64},{96,80},{112,96},{17,1},{33... | collective-permute-start | bytes 221192 | tf_op jit(solution)/shard_map/ppermute | solution.py:24
  3.5 2.4 %collective-permute-start = (bf16[3,32,384]{2,1,0:T(8,128)(2,1)S(1)}, bf16[3,32,384]{2,1,0:T(8,128)(2,1)S(1)}, u32[]{:S(2)}, u32[]{:S(2)}) collective-permute-start(bf16[3,32,384]{2,1,0:T(8,128)(2,1)S(1)} %get-tuple-element.21), channel_id=1, source_target_pairs={{0,16},{16,32},{32,48},{48,64},{64,80},{80,96},{96,112},{1,17},{17... | collective-permute-start | bytes 221192 | tf_op jit(solution)/shard_map/ppermute | solution.py:23
  5.9 0.8 copy.21
  6.7 0.7 reduce_window_sum.11
  7.4 0.8 select_reduce_fusion.3
  8.2 1.0 collective-permute-done.refs_1_
  9.2 0.0 copy-start.7
  9.2 0.0 copy-start.9
  9.2 0.0 copy-start.10
  9.2 0.0 copy-start.11
  9.2 0.0 copy-start.8
  9.2 2.2 %constant_dynamic-update-slice_fusion.1 = bf16[102,32,384]{2,1,0:T(8,128)(2,1)S(1)} fusion(bf16[102,32,384]{2,1,0:T(8,128)(2,1)S(1)} %constant_dynamic-update-slice_fusion.2, bf16[96,32,384]{2,1,0:T(8,128)(2,1)} %refs_0_.1), kind=kLoop, calls=%fused_computation.7 | loop fusion | bytes 4718592
  11.4 0.0 copy-done.7
  11.4 0.0 collective-permute-done.1.refs_2_
  11.4 0.0 copy-start.6
  11.5 0.2 fusion
  11.7 6.1 %collective-permute-start.3 = (bf16[102,3,384]{2,1,0:T(4,128)(2,1)S(1)}, bf16[102,3,384]{2,1,0:T(4,128)(2,1)S(1)}, u32[]{:S(2)}, u32[]{:S(2)}) collective-permute-start(bf16[102,3,384]{2,1,0:T(4,128)(2,1)S(1)} %get-tuple-element.16), channel_id=1, source_target_pairs={{1,0},{2,1},{3,2},{4,3},{5,4},{6,5},{7,6},{8,7},{9,8},{10,9},{11,1... | collective-permute-start | bytes 705032 | tf_op jit(solution)/shard_map/ppermute | solution.py:27
  17.9 1.9 %collective-permute-start.2 = (bf16[102,3,384]{2,1,0:T(4,128)(2,1)S(1)}, bf16[102,3,384]{2,1,0:T(4,128)(2,1)S(1)}, u32[]{:S(2)}, u32[]{:S(2)}) collective-permute-start(bf16[102,3,384]{2,1,0:T(4,128)(2,1)S(1)} %get-tuple-element.17), channel_id=1, source_target_pairs={{0,1},{1,2},{2,3},{3,4},{4,5},{5,6},{6,7},{7,8},{8,9},{9,10},{10,1... | collective-permute-start | bytes 705032 | tf_op jit(solution)/shard_map/ppermute | solution.py:26
  19.8 0.5 select_reduce_fusion.1
  20.3 0.1 copy.22
  20.4 0.1 copy.23
  20.5 0.0 copy-done.9
  20.5 0.0 copy-done.10
  20.5 0.0 copy-done.11
  20.6 0.1 copy.24
  20.7 0.7 reshape.47.refs_0_
  21.3 0.0 copy-done.8
  21.3 0.7 reshape.48.refs_5_
  22.0 2.9 %collective-permute-done.3.refs_4_ = bf16[102,3,384]{2,1,0:T(4,128)(2,1)S(1)} collective-permute-done((bf16[102,3,384]{2,1,0:T(4,128)(2,1)S(1)}, bf16[102,3,384]{2,1,0:T(4,128)(2,1)S(1)}, u32[]{:S(2)}, u32[]{:S(2)}) %collective-permute-start.3) | collective-permute-done | bytes 235040 | tf_op jit(solution)/shard_map/ppermute | solution.py:27
  24.8 0.0 copy-start.2
  24.8 6.2 %collective-permute-done.2.refs_3_ = bf16[102,3,384]{2,1,0:T(4,128)(2,1)S(1)} collective-permute-done((bf16[102,3,384]{2,1,0:T(4,128)(2,1)S(1)}, bf16[102,3,384]{2,1,0:T(4,128)(2,1)S(1)}, u32[]{:S(2)}, u32[]{:S(2)}) %collective-permute-start.2) | collective-permute-done | bytes 235040 | tf_op jit(solution)/shard_map/ppermute | solution.py:26
  31.1 0.0 copy-done.6
  31.1 0.0 copy-done.2
  31.1 0.0 copy-start.3
  31.1 0.7 copy-done.3
  31.8 21.8 %shard_map.113 = bf16[96,32,384]{2,1,0:T(8,128)(2,1)} custom-call(bf16[96,32,384]{2,1,0:T(8,128)(2,1)} %refs_0_.1, bf16[3,32,384]{2,1,0:T(8,128)(2,1)} %copy-done.7, bf16[3,32,384]{2,1,0:T(8,128)(2,1)} %copy-done.6, bf16[102,3,384]{2,1,0:T(4,128)(2,1)} %copy-done.3, bf16[102,3,384]{2,1,0:T(4,128)(2,1)} %copy-done.2, f32[49,384]{1,0:T(8,128)} %reshape.48.refs_5_), custom_call_target="tpu_custom_call" | custom-call | tf_op jit(solution)/shard_map/pallas_call | solution.py:89
  53.6 29.8 %shard_map.114 = (bf16[3072,384]{1,0:T(8,128)(2,1)}, bf16[768,768]{1,0:T(8,128)(2,1)}) custom-call(s32[48]{0:T(128)} %reshape.47.refs_0_, bf16[3072,384]{1,0:T(8,128)(2,1)} %bitcast.13, bf16[3072,384]{1,0:T(8,128)(2,1)} %bitcast.12, bf16[384,1536]{1,0:T(8,128)(2,1)} %refs_4_.3, bf16[1536,384]{1,0:T(8,128)(2,1)} %refs_5_.1, bf16[4,384,768]{2,1,0:T(8,128)(2,1)} %bitcast.17), custom_call_target="tpu_custom_call" | custom-call | tf_op jit(solution)/shard_map/pallas_call | solution.py:250
  83.4 34.9 %shard_map.115 = (bf16[3072,384]{1,0:T(8,128)(2,1)}, bf16[3072,384]{1,0:T(8,128)(2,1)}) custom-call(s32[48]{0:T(128)} %reshape.47.refs_0_, bf16[3072,384]{1,0:T(8,128)(2,1)} %bitcast.14, bf16[3072,384]{1,0:T(8,128)(2,1)} %get-tuple-element.7.refs_2_, bf16[768,768]{1,0:T(8,128)(2,1)} %bitcast.20, bf16[384,1536]{1,0:T(8,128)(2,1)} %refs_4_.3, ...), custom_call_target="tpu_custom_call" | custom-call | tf_op jit(solution)/shard_map/pallas_call | solution.py:250
  118.2 0.9 fusion.1
  119.2 1.9 %collective-permute-start.4 = (bf16[3,32,384]{2,1,0:T(8,128)(2,1)S(1)}, bf16[3,32,384]{2,1,0:T(8,128)(2,1)S(1)}, u32[]{:S(2)}, u32[]{:S(2)}) collective-permute-start(bf16[3,32,384]{2,1,0:T(8,128)(2,1)S(1)} %bitcast.22), channel_id=1, source_target_pairs={{0,16},{16,32},{32,48},{48,64},{64,80},{80,96},{96,112},{1,17},{17... | collective-permute-start | bytes 221192 | tf_op jit(solution)/shard_map/ppermute | solution.py:23
  121.1 3.6 %collective-permute-start.5 = (bf16[3,32,384]{2,1,0:T(8,128)(2,1)S(1)}, bf16[3,32,384]{2,1,0:T(8,128)(2,1)S(1)}, u32[]{:S(2)}, u32[]{:S(2)}) collective-permute-start(bf16[3,32,384]{2,1,0:T(8,128)(2,1)S(1)} %bitcast.21), channel_id=1, source_target_pairs={{16,0},{32,16},{48,32},{64,48},{80,64},{96,80},{112,96},{17,1},{33... | collective-permute-start | bytes 221192 | tf_op jit(solution)/shard_map/ppermute | solution.py:24
  124.8 0.1 collective-permute-done.4.refs_1_
  124.9 0.0 copy-start.4
  124.9 1.9 %collective-permute-done.5.refs_2_ = bf16[3,32,384]{2,1,0:T(8,128)(2,1)S(1)} collective-permute-done((bf16[3,32,384]{2,1,0:T(8,128)(2,1)S(1)}, bf16[3,32,384]{2,1,0:T(8,128)(2,1)S(1)}, u32[]{:S(2)}, u32[]{:S(2)}) %collective-permute-start.5) | collective-permute-done | bytes 73760 | tf_op jit(solution)/shard_map/ppermute | solution.py:24
  126.7 0.0 copy-start.5
  126.7 1.5 pad_maximum_fusion
  128.2 1.9 %collective-permute-start.7 = (bf16[102,3,384]{2,1,0:T(4,128)(2,1)S(1)}, bf16[102,3,384]{2,1,0:T(4,128)(2,1)S(1)}, u32[]{:S(2)}, u32[]{:S(2)}) collective-permute-start(bf16[102,3,384]{2,1,0:T(4,128)(2,1)S(1)} %get-tuple-element.14), channel_id=1, source_target_pairs={{1,0},{2,1},{3,2},{4,3},{5,4},{6,5},{7,6},{8,7},{9,8},{10,9},{11,1... | collective-permute-start | bytes 705032 | tf_op jit(solution)/shard_map/ppermute | solution.py:27
  130.2 3.9 %collective-permute-start.6 = (bf16[102,3,384]{2,1,0:T(4,128)(2,1)S(1)}, bf16[102,3,384]{2,1,0:T(4,128)(2,1)S(1)}, u32[]{:S(2)}, u32[]{:S(2)}) collective-permute-start(bf16[102,3,384]{2,1,0:T(4,128)(2,1)S(1)} %get-tuple-element.15), channel_id=1, source_target_pairs={{0,1},{1,2},{2,3},{3,4},{4,5},{5,6},{6,7},{7,8},{8,9},{9,10},{10,1... | collective-permute-start | bytes 705032 | tf_op jit(solution)/shard_map/ppermute | solution.py:26
  134.1 5.7 %collective-permute-done.7.refs_4_ = bf16[102,3,384]{2,1,0:T(4,128)(2,1)S(1)} collective-permute-done((bf16[102,3,384]{2,1,0:T(4,128)(2,1)S(1)}, bf16[102,3,384]{2,1,0:T(4,128)(2,1)S(1)}, u32[]{:S(2)}, u32[]{:S(2)}) %collective-permute-start.7) | collective-permute-done | bytes 235040 | tf_op jit(solution)/shard_map/ppermute | solution.py:27
  139.8 0.0 copy-start
  139.8 4.0 %collective-permute-done.6.refs_3_ = bf16[102,3,384]{2,1,0:T(4,128)(2,1)S(1)} collective-permute-done((bf16[102,3,384]{2,1,0:T(4,128)(2,1)S(1)}, bf16[102,3,384]{2,1,0:T(4,128)(2,1)S(1)}, u32[]{:S(2)}, u32[]{:S(2)}) %collective-permute-start.6) | collective-permute-done | bytes 235040 | tf_op jit(solution)/shard_map/ppermute | solution.py:26
  143.8 0.0 copy-start.1
  143.8 0.0 copy-done.4
  143.8 0.0 copy-done.5
  143.8 0.0 copy-done
  143.8 0.7 copy-done.1
  144.5 22.4 %shard_map.116 = bf16[96,32,384]{2,1,0:T(8,128)(2,1)} custom-call(bf16[96,32,384]{2,1,0:T(8,128)(2,1)} %bitcast.16, bf16[3,32,384]{2,1,0:T(8,128)(2,1)} %copy-done.4, bf16[3,32,384]{2,1,0:T(8,128)(2,1)} %copy-done.5, bf16[102,3,384]{2,1,0:T(4,128)(2,1)} %copy-done.1, bf16[102,3,384]{2,1,0:T(4,128)(2,1)} %copy-done, f32[49,384]{1,0:T(8,128)} %reshape.48.refs_5_, ...), custom_call_target="tpu_custom_call" | custom-call | tf_op jit(solution)/shard_map/pallas_call | solution.py:89
  (4 shorter events, 0.0 us)
Async XLA Ops:
  1.6 9.9 %collective-permute-start.1 = (bf16[3,32,384]{2,1,0:T(8,128)(2,1)S(1)}, bf16[3,32,384]{2,1,0:T(8,128)(2,1)S(1)}, u32[]{:S(2)}, u32[]{:S(2)}) collective-permute-start(bf16[3,32,384]{2,1,0:T(8,128)(2,1)S(1)} %get-tuple-element.20), channel_id=1, source_target_pairs={{16,0},{32,16},{48,32},{64,48},{80,64},{96,80},{112,96},{17,1},{33... | collective-permute-start | bytes 221192 | tf_op jit(solution)/shard_map/ppermute | solution.py:24
  3.5 5.7 %collective-permute-start = (bf16[3,32,384]{2,1,0:T(8,128)(2,1)S(1)}, bf16[3,32,384]{2,1,0:T(8,128)(2,1)S(1)}, u32[]{:S(2)}, u32[]{:S(2)}) collective-permute-start(bf16[3,32,384]{2,1,0:T(8,128)(2,1)S(1)} %get-tuple-element.21), channel_id=1, source_target_pairs={{0,16},{16,32},{32,48},{48,64},{64,80},{80,96},{96,112},{1,17},{17... | collective-permute-start | bytes 221192 | tf_op jit(solution)/shard_map/ppermute | solution.py:23
  9.2 2.3 %copy-start.7 = (bf16[3,32,384]{2,1,0:T(8,128)(2,1)}, bf16[3,32,384]{2,1,0:T(8,128)(2,1)S(1)}, u32[]{:S(2)}) copy-start(bf16[3,32,384]{2,1,0:T(8,128)(2,1)S(1)} %collective-permute-done.refs_1_) | copy-start | bytes 221188
  9.2 11.3 %copy-start.9 = (s32[12,4]{0,1:T(4,128)S(1)}, s32[12,4]{0,1:T(4,128)}, u32[]{:S(2)}) copy-start(s32[12,4]{0,1:T(4,128)} %param.17) | copy-start | bytes 580
  9.2 11.3 %copy-start.10 = (s32[12,4]{0,1:T(4,128)S(1)}, s32[12,4]{0,1:T(4,128)}, u32[]{:S(2)}) copy-start(s32[12,4]{0,1:T(4,128)} %param.15) | copy-start | bytes 580
  9.2 11.3 %copy-start.11 = (s32[12,4]{0,1:T(4,128)S(1)}, s32[12,4]{0,1:T(4,128)}, u32[]{:S(2)}) copy-start(s32[12,4]{0,1:T(4,128)} %param.18) | copy-start | bytes 580
  9.2 12.1 %copy-start.8 = (bf16[7,7,384]{2,1,0:T(8,128)(2,1)S(1)}, bf16[7,7,384]{2,1,0:T(8,128)(2,1)}, u32[]{:S(2)}) copy-start(bf16[7,7,384]{2,1,0:T(8,128)(2,1)} %param.11) | copy-start | bytes 112900
  11.4 19.6 %copy-start.6 = (bf16[3,32,384]{2,1,0:T(8,128)(2,1)}, bf16[3,32,384]{2,1,0:T(8,128)(2,1)S(1)}, u32[]{:S(2)}) copy-start(bf16[3,32,384]{2,1,0:T(8,128)(2,1)S(1)} %collective-permute-done.1.refs_2_) | copy-start | bytes 221188
  11.7 13.1 %collective-permute-start.3 = (bf16[102,3,384]{2,1,0:T(4,128)(2,1)S(1)}, bf16[102,3,384]{2,1,0:T(4,128)(2,1)S(1)}, u32[]{:S(2)}, u32[]{:S(2)}) collective-permute-start(bf16[102,3,384]{2,1,0:T(4,128)(2,1)S(1)} %get-tuple-element.16), channel_id=1, source_target_pairs={{1,0},{2,1},{3,2},{4,3},{5,4},{6,5},{7,6},{8,7},{9,8},{10,9},{11,1... | collective-permute-start | bytes 705032 | tf_op jit(solution)/shard_map/ppermute | solution.py:27
  17.9 13.2 %collective-permute-start.2 = (bf16[102,3,384]{2,1,0:T(4,128)(2,1)S(1)}, bf16[102,3,384]{2,1,0:T(4,128)(2,1)S(1)}, u32[]{:S(2)}, u32[]{:S(2)}) collective-permute-start(bf16[102,3,384]{2,1,0:T(4,128)(2,1)S(1)} %get-tuple-element.17), channel_id=1, source_target_pairs={{0,1},{1,2},{2,3},{3,4},{4,5},{5,6},{6,7},{7,8},{8,9},{9,10},{10,1... | collective-permute-start | bytes 705032 | tf_op jit(solution)/shard_map/ppermute | solution.py:26
  24.8 6.2 %copy-start.2 = (bf16[102,3,384]{2,1,0:T(4,128)(2,1)}, bf16[102,3,384]{2,1,0:T(4,128)(2,1)S(1)}, u32[]{:S(2)}) copy-start(bf16[102,3,384]{2,1,0:T(4,128)(2,1)S(1)} %collective-permute-done.3.refs_4_) | copy-start | bytes 705028
  31.1 0.7 copy-start.3
  119.2 5.7 %collective-permute-start.4 = (bf16[3,32,384]{2,1,0:T(8,128)(2,1)S(1)}, bf16[3,32,384]{2,1,0:T(8,128)(2,1)S(1)}, u32[]{:S(2)}, u32[]{:S(2)}) collective-permute-start(bf16[3,32,384]{2,1,0:T(8,128)(2,1)S(1)} %bitcast.22), channel_id=1, source_target_pairs={{0,16},{16,32},{32,48},{48,64},{64,80},{80,96},{96,112},{1,17},{17... | collective-permute-start | bytes 221192 | tf_op jit(solution)/shard_map/ppermute | solution.py:23
  121.1 5.6 %collective-permute-start.5 = (bf16[3,32,384]{2,1,0:T(8,128)(2,1)S(1)}, bf16[3,32,384]{2,1,0:T(8,128)(2,1)S(1)}, u32[]{:S(2)}, u32[]{:S(2)}) collective-permute-start(bf16[3,32,384]{2,1,0:T(8,128)(2,1)S(1)} %bitcast.21), channel_id=1, source_target_pairs={{16,0},{32,16},{48,32},{64,48},{80,64},{96,80},{112,96},{17,1},{33... | collective-permute-start | bytes 221192 | tf_op jit(solution)/shard_map/ppermute | solution.py:24
  124.9 19.0 %copy-start.4 = (bf16[3,32,384]{2,1,0:T(8,128)(2,1)}, bf16[3,32,384]{2,1,0:T(8,128)(2,1)S(1)}, u32[]{:S(2)}) copy-start(bf16[3,32,384]{2,1,0:T(8,128)(2,1)S(1)} %collective-permute-done.4.refs_1_) | copy-start | bytes 221188
  126.7 17.1 %copy-start.5 = (bf16[3,32,384]{2,1,0:T(8,128)(2,1)}, bf16[3,32,384]{2,1,0:T(8,128)(2,1)S(1)}, u32[]{:S(2)}) copy-start(bf16[3,32,384]{2,1,0:T(8,128)(2,1)S(1)} %collective-permute-done.5.refs_2_) | copy-start | bytes 221188
  128.2 11.5 %collective-permute-start.7 = (bf16[102,3,384]{2,1,0:T(4,128)(2,1)S(1)}, bf16[102,3,384]{2,1,0:T(4,128)(2,1)S(1)}, u32[]{:S(2)}, u32[]{:S(2)}) collective-permute-start(bf16[102,3,384]{2,1,0:T(4,128)(2,1)S(1)} %get-tuple-element.14), channel_id=1, source_target_pairs={{1,0},{2,1},{3,2},{4,3},{5,4},{6,5},{7,6},{8,7},{9,8},{10,9},{11,1... | collective-permute-start | bytes 705032 | tf_op jit(solution)/shard_map/ppermute | solution.py:27
  130.2 13.6 %collective-permute-start.6 = (bf16[102,3,384]{2,1,0:T(4,128)(2,1)S(1)}, bf16[102,3,384]{2,1,0:T(4,128)(2,1)S(1)}, u32[]{:S(2)}, u32[]{:S(2)}) collective-permute-start(bf16[102,3,384]{2,1,0:T(4,128)(2,1)S(1)} %get-tuple-element.15), channel_id=1, source_target_pairs={{0,1},{1,2},{2,3},{3,4},{4,5},{5,6},{6,7},{7,8},{8,9},{9,10},{10,1... | collective-permute-start | bytes 705032 | tf_op jit(solution)/shard_map/ppermute | solution.py:26
  139.8 4.0 %copy-start = (bf16[102,3,384]{2,1,0:T(4,128)(2,1)}, bf16[102,3,384]{2,1,0:T(4,128)(2,1)S(1)}, u32[]{:S(2)}) copy-start(bf16[102,3,384]{2,1,0:T(4,128)(2,1)S(1)} %collective-permute-done.7.refs_4_) | copy-start | bytes 705028
  143.8 0.7 copy-start.1

commit v9 on v5

--- a/solution.py
+++ b/solution.py
@@ -212,12 +212,13 @@
 
 def pixel_live(live, layout):
     block, breadth, tile_side, tile_cols = layout
+    band = block // breadth // tile_side
     place = lax.broadcasted_iota(jnp.int32, (block, 1), 0)
-    tile = (place % breadth) // tile_side
-    first = pl.program_id(0) * tile_cols
+    tile = (place // breadth // tile_side) * tile_cols + (place % breadth) // tile_side
+    first = pl.program_id(0) * band * tile_cols
     flag = jnp.zeros((block, 1), jnp.int32)
-    for column in range(tile_cols):
-        flag = jnp.where(tile == column, live[first + column], flag)
+    for index in range(band * tile_cols):
+        flag = jnp.where(tile == index, live[first + index], flag)
     return flag > 0
 
 
@@ -269,7 +270,8 @@
     routed = routed_tiles(tile_counts, tile_owner, tile_slot, peer_count, capacity)
     live = routed & (tissue_mask != 0)
     live = live.reshape(-1).astype(jnp.int32)
-    layout = (tile_side * breadth, breadth, tile_side, tile_cols)
+    band = 2 if tile_rows % 2 == 0 else 1
+    layout = (band * tile_side * breadth, breadth, tile_side, tile_cols)
     taps = depth_kernel.reshape(KS * KS, channels).astype(jnp.float32)
     mixed = depthwise(halo_pieces(image, reach), taps, reach)
     mixed = mixed.reshape(pixels, channels)

time: 164 us -> 153 us (0.933)
  Pallas kernels: 105 us -> 93.6 us
    pallas_call x2, Pallas kernels: 60.6 us -> 49.4 us  [pixel_call(): pl.pallas_call(lambda *refs: kernel(*refs, layout=layout), grid_spec=pltp...]
where the time goes in v9:
time: 153 us; the launch traced here: 152 us
  Pallas kernels  93.6 us (61%)
  starting transfers between devices  23.8 us (16%)
  waiting for transfers between devices  21.7 us (14%)
  local copies, waits for them, and re-layouts  8.19 us (5%)
  other arithmetic  3.6 us (2%)
    pallas_call x2, Pallas kernels, pixel_call(): pl.pallas_call(lambda *refs: kernel(*refs, layout=layout), grid_spec=pltp...  49.4 us
    pallas_call x2, Pallas kernels, depthwise(): pl.pallas_call(lambda *refs: depthwise_kernel(*refs, reach=reach, chunk=c...  44.2 us
    ppermute x2, waiting for transfers between devices, halo_pieces(): lax.ppermute(framed[:, cells.shape[1] - width:], 'col', [(i, i + 1) for i...  10.3 us
    ppermute x2, waiting for transfers between devices, halo_pieces(): lax.ppermute(framed[:, :width], 'col', [(i + 1, i) for i in range(cols -...  8.52 us
    ppermute x2, starting transfers between devices, halo_pieces(): lax.ppermute(framed[:, :width], 'col', [(i + 1, i) for i in range(cols -...  8.05 us
    ppermute x2, starting transfers between devices, halo_pieces(): lax.ppermute(framed[:, cells.shape[1] - width:], 'col', [(i, i + 1) for i...  5.84 us
    ppermute x2, starting transfers between devices, halo_pieces(): bottom = lax.ppermute(cells[:width], 'row', up)  5.56 us
    unnamed x27, local copies, waits for them, and re-layouts  4.46 us
  transfers between devices with their start and end apart: 8, of which 7 were waited for; matrix products, arithmetic and copies ran while one was open for 4% of the time, Pallas kernels for 0%

profile of v9, /device:TPU:26, one launch (start us, length us, event | category | flops | bytes accessed | tf_op | source)
XLA Modules:
  0.0 151.7 jit_solution(7502267245017412722)
XLA Ops:
  0.6 0.9 fusion.2
  1.6 1.9 %collective-permute-start.1 = (bf16[3,32,384]{2,1,0:T(8,128)(2,1)S(1)}, bf16[3,32,384]{2,1,0:T(8,128)(2,1)S(1)}, u32[]{:S(2)}, u32[]{:S(2)}) collective-permute-start(bf16[3,32,384]{2,1,0:T(8,128)(2,1)S(1)} %get-tuple-element.20), channel_id=1, source_target_pairs={{16,0},{32,16},{48,32},{64,48},{80,64},{96,80},{112,96},{17,1},{33... | collective-permute-start | bytes 221192 | tf_op jit(solution)/shard_map/ppermute | solution.py:23
  3.5 2.4 %collective-permute-start = (bf16[3,32,384]{2,1,0:T(8,128)(2,1)S(1)}, bf16[3,32,384]{2,1,0:T(8,128)(2,1)S(1)}, u32[]{:S(2)}, u32[]{:S(2)}) collective-permute-start(bf16[3,32,384]{2,1,0:T(8,128)(2,1)S(1)} %get-tuple-element.21), channel_id=1, source_target_pairs={{0,16},{16,32},{32,48},{48,64},{64,80},{80,96},{96,112},{1,17},{17... | collective-permute-start | bytes 221192 | tf_op jit(solution)/shard_map/ppermute | solution.py:22
  5.9 0.8 copy.21
  6.7 0.7 reduce_window_sum.11
  7.4 0.8 select_reduce_fusion.3
  8.2 1.0 collective-permute-done.refs_1_
  9.2 0.0 copy-start.7
  9.2 0.0 copy-start.9
  9.2 0.0 copy-start.10
  9.2 0.0 copy-start.11
  9.2 0.0 copy-start.8
  9.2 2.2 %constant_dynamic-update-slice_fusion.1 = bf16[102,32,384]{2,1,0:T(8,128)(2,1)S(1)} fusion(bf16[102,32,384]{2,1,0:T(8,128)(2,1)S(1)} %constant_dynamic-update-slice_fusion.2, bf16[96,32,384]{2,1,0:T(8,128)(2,1)} %refs_0_.1), kind=kLoop, calls=%fused_computation.7 | loop fusion | bytes 4718592
  11.4 0.0 copy-done.7
  11.4 0.0 collective-permute-done.1.refs_2_
  11.4 0.0 copy-start.6
  11.5 0.2 fusion
  11.7 6.1 %collective-permute-start.3 = (bf16[102,3,384]{2,1,0:T(4,128)(2,1)S(1)}, bf16[102,3,384]{2,1,0:T(4,128)(2,1)S(1)}, u32[]{:S(2)}, u32[]{:S(2)}) collective-permute-start(bf16[102,3,384]{2,1,0:T(4,128)(2,1)S(1)} %get-tuple-element.16), channel_id=1, source_target_pairs={{1,0},{2,1},{3,2},{4,3},{5,4},{6,5},{7,6},{8,7},{9,8},{10,9},{11,1... | collective-permute-start | bytes 705032 | tf_op jit(solution)/shard_map/ppermute | solution.py:26
  17.9 1.9 %collective-permute-start.2 = (bf16[102,3,384]{2,1,0:T(4,128)(2,1)S(1)}, bf16[102,3,384]{2,1,0:T(4,128)(2,1)S(1)}, u32[]{:S(2)}, u32[]{:S(2)}) collective-permute-start(bf16[102,3,384]{2,1,0:T(4,128)(2,1)S(1)} %get-tuple-element.17), channel_id=1, source_target_pairs={{0,1},{1,2},{2,3},{3,4},{4,5},{5,6},{6,7},{7,8},{8,9},{9,10},{10,1... | collective-permute-start | bytes 705032 | tf_op jit(solution)/shard_map/ppermute | solution.py:25
  19.8 0.5 select_reduce_fusion.1
  20.3 0.1 copy.22
  20.4 0.1 copy.23
  20.5 0.0 copy-done.9
  20.5 0.0 copy-done.10
  20.5 0.0 copy-done.11
  20.6 0.1 copy.24
  20.7 0.7 reshape.47.refs_0_
  21.3 0.0 copy-done.8
  21.3 0.7 reshape.48.refs_5_
  22.0 2.9 %collective-permute-done.3.refs_4_ = bf16[102,3,384]{2,1,0:T(4,128)(2,1)S(1)} collective-permute-done((bf16[102,3,384]{2,1,0:T(4,128)(2,1)S(1)}, bf16[102,3,384]{2,1,0:T(4,128)(2,1)S(1)}, u32[]{:S(2)}, u32[]{:S(2)}) %collective-permute-start.3) | collective-permute-done | bytes 235040 | tf_op jit(solution)/shard_map/ppermute | solution.py:26
  24.8 0.0 copy-start.2
  24.8 6.2 %collective-permute-done.2.refs_3_ = bf16[102,3,384]{2,1,0:T(4,128)(2,1)S(1)} collective-permute-done((bf16[102,3,384]{2,1,0:T(4,128)(2,1)S(1)}, bf16[102,3,384]{2,1,0:T(4,128)(2,1)S(1)}, u32[]{:S(2)}, u32[]{:S(2)}) %collective-permute-start.2) | collective-permute-done | bytes 235040 | tf_op jit(solution)/shard_map/ppermute | solution.py:25
  31.1 0.0 copy-done.6
  31.1 0.0 copy-done.2
  31.1 0.0 copy-start.3
  31.1 0.7 copy-done.3
  31.8 21.8 %shard_map.113 = bf16[96,32,384]{2,1,0:T(8,128)(2,1)} custom-call(bf16[96,32,384]{2,1,0:T(8,128)(2,1)} %refs_0_.1, bf16[3,32,384]{2,1,0:T(8,128)(2,1)} %copy-done.7, bf16[3,32,384]{2,1,0:T(8,128)(2,1)} %copy-done.6, bf16[102,3,384]{2,1,0:T(4,128)(2,1)} %copy-done.3, bf16[102,3,384]{2,1,0:T(4,128)(2,1)} %copy-done.2, f32[49,384]{1,0:T(8,128)} %reshape.48.refs_5_), custom_call_target="tpu_custom_call" | custom-call | tf_op jit(solution)/shard_map/pallas_call | solution.py:88
  53.6 22.7 %shard_map.114 = (bf16[3072,384]{1,0:T(8,128)(2,1)}, bf16[768,768]{1,0:T(8,128)(2,1)}) custom-call(s32[48]{0:T(128)} %reshape.47.refs_0_, bf16[3072,384]{1,0:T(8,128)(2,1)} %bitcast.13, bf16[3072,384]{1,0:T(8,128)(2,1)} %bitcast.12, bf16[384,1536]{1,0:T(8,128)(2,1)} %refs_4_.3, bf16[1536,384]{1,0:T(8,128)(2,1)} %refs_5_.1, bf16[4,384,768]{2,1,0:T(8,128)(2,1)} %bitcast.17), custom_call_target="tpu_custom_call" | custom-call | tf_op jit(solution)/shard_map/pallas_call | solution.py:235
  76.3 26.7 %shard_map.115 = (bf16[3072,384]{1,0:T(8,128)(2,1)}, bf16[3072,384]{1,0:T(8,128)(2,1)}) custom-call(s32[48]{0:T(128)} %reshape.47.refs_0_, bf16[3072,384]{1,0:T(8,128)(2,1)} %bitcast.14, bf16[3072,384]{1,0:T(8,128)(2,1)} %get-tuple-element.7.refs_2_, bf16[768,768]{1,0:T(8,128)(2,1)} %bitcast.20, bf16[384,1536]{1,0:T(8,128)(2,1)} %refs_4_.3, ...), custom_call_target="tpu_custom_call" | custom-call | tf_op jit(solution)/shard_map/pallas_call | solution.py:235
  103.0 0.9 fusion.1
  104.0 1.9 %collective-permute-start.4 = (bf16[3,32,384]{2,1,0:T(8,128)(2,1)S(1)}, bf16[3,32,384]{2,1,0:T(8,128)(2,1)S(1)}, u32[]{:S(2)}, u32[]{:S(2)}) collective-permute-start(bf16[3,32,384]{2,1,0:T(8,128)(2,1)S(1)} %bitcast.22), channel_id=1, source_target_pairs={{0,16},{16,32},{32,48},{48,64},{64,80},{80,96},{96,112},{1,17},{17... | collective-permute-start | bytes 221192 | tf_op jit(solution)/shard_map/ppermute | solution.py:22
  105.9 3.6 %collective-permute-start.5 = (bf16[3,32,384]{2,1,0:T(8,128)(2,1)S(1)}, bf16[3,32,384]{2,1,0:T(8,128)(2,1)S(1)}, u32[]{:S(2)}, u32[]{:S(2)}) collective-permute-start(bf16[3,32,384]{2,1,0:T(8,128)(2,1)S(1)} %bitcast.21), channel_id=1, source_target_pairs={{16,0},{32,16},{48,32},{64,48},{80,64},{96,80},{112,96},{17,1},{33... | collective-permute-start | bytes 221192 | tf_op jit(solution)/shard_map/ppermute | solution.py:23
  109.5 0.1 collective-permute-done.4.refs_1_
  109.6 0.0 copy-start.4
  109.6 1.9 %collective-permute-done.5.refs_2_ = bf16[3,32,384]{2,1,0:T(8,128)(2,1)S(1)} collective-permute-done((bf16[3,32,384]{2,1,0:T(8,128)(2,1)S(1)}, bf16[3,32,384]{2,1,0:T(8,128)(2,1)S(1)}, u32[]{:S(2)}, u32[]{:S(2)}) %collective-permute-start.5) | collective-permute-done | bytes 73760 | tf_op jit(solution)/shard_map/ppermute | solution.py:23
  111.5 0.0 copy-start.5
  111.5 1.5 %pad_maximum_fusion = (bf16[102,3,384]{2,1,0:T(4,128)(2,1)S(1)}, bf16[102,3,384]{2,1,0:T(4,128)(2,1)S(1)}) fusion(bf16[3,32,384]{2,1,0:T(8,128)(2,1)S(1)} %collective-permute-done.5.refs_2_, bf16[96,32,384]{2,1,0:T(8,128)(2,1)} %bitcast.15, bf16[3,32,384]{2,1,0:T(8,128)(2,1)S(1)} %collective-permute-done.4.refs_1_), kind=kLoop, calls=%fused_computation | loop fusion | flops 1410048 | bytes 2976768 | tf_op jit(solution)/shard_map/concatenate | solution.py:24
  113.0 1.9 %collective-permute-start.7 = (bf16[102,3,384]{2,1,0:T(4,128)(2,1)S(1)}, bf16[102,3,384]{2,1,0:T(4,128)(2,1)S(1)}, u32[]{:S(2)}, u32[]{:S(2)}) collective-permute-start(bf16[102,3,384]{2,1,0:T(4,128)(2,1)S(1)} %get-tuple-element.14), channel_id=1, source_target_pairs={{1,0},{2,1},{3,2},{4,3},{5,4},{6,5},{7,6},{8,7},{9,8},{10,9},{11,1... | collective-permute-start | bytes 705032 | tf_op jit(solution)/shard_map/ppermute | solution.py:26
  115.0 3.9 %collective-permute-start.6 = (bf16[102,3,384]{2,1,0:T(4,128)(2,1)S(1)}, bf16[102,3,384]{2,1,0:T(4,128)(2,1)S(1)}, u32[]{:S(2)}, u32[]{:S(2)}) collective-permute-start(bf16[102,3,384]{2,1,0:T(4,128)(2,1)S(1)} %get-tuple-element.15), channel_id=1, source_target_pairs={{0,1},{1,2},{2,3},{3,4},{4,5},{5,6},{6,7},{7,8},{8,9},{9,10},{10,1... | collective-permute-start | bytes 705032 | tf_op jit(solution)/shard_map/ppermute | solution.py:25
  118.9 5.7 %collective-permute-done.7.refs_4_ = bf16[102,3,384]{2,1,0:T(4,128)(2,1)S(1)} collective-permute-done((bf16[102,3,384]{2,1,0:T(4,128)(2,1)S(1)}, bf16[102,3,384]{2,1,0:T(4,128)(2,1)S(1)}, u32[]{:S(2)}, u32[]{:S(2)}) %collective-permute-start.7) | collective-permute-done | bytes 235040 | tf_op jit(solution)/shard_map/ppermute | solution.py:26
  124.5 0.0 copy-start
  124.6 4.0 %collective-permute-done.6.refs_3_ = bf16[102,3,384]{2,1,0:T(4,128)(2,1)S(1)} collective-permute-done((bf16[102,3,384]{2,1,0:T(4,128)(2,1)S(1)}, bf16[102,3,384]{2,1,0:T(4,128)(2,1)S(1)}, u32[]{:S(2)}, u32[]{:S(2)}) %collective-permute-start.6) | collective-permute-done | bytes 235040 | tf_op jit(solution)/shard_map/ppermute | solution.py:25
  128.6 0.0 copy-start.1
  128.6 0.0 copy-done.4
  128.6 0.0 copy-done.5
  128.6 0.0 copy-done
  128.6 0.7 copy-done.1
  129.3 22.4 %shard_map.116 = bf16[96,32,384]{2,1,0:T(8,128)(2,1)} custom-call(bf16[96,32,384]{2,1,0:T(8,128)(2,1)} %bitcast.16, bf16[3,32,384]{2,1,0:T(8,128)(2,1)} %copy-done.4, bf16[3,32,384]{2,1,0:T(8,128)(2,1)} %copy-done.5, bf16[102,3,384]{2,1,0:T(4,128)(2,1)} %copy-done.1, bf16[102,3,384]{2,1,0:T(4,128)(2,1)} %copy-done, f32[49,384]{1,0:T(8,128)} %reshape.48.refs_5_, ...), custom_call_target="tpu_custom_call" | custom-call | tf_op jit(solution)/shard_map/pallas_call | solution.py:88
  (4 shorter events, 0.0 us)
Async XLA Ops:
  1.6 9.9 %collective-permute-start.1 = (bf16[3,32,384]{2,1,0:T(8,128)(2,1)S(1)}, bf16[3,32,384]{2,1,0:T(8,128)(2,1)S(1)}, u32[]{:S(2)}, u32[]{:S(2)}) collective-permute-start(bf16[3,32,384]{2,1,0:T(8,128)(2,1)S(1)} %get-tuple-element.20), channel_id=1, source_target_pairs={{16,0},{32,16},{48,32},{64,48},{80,64},{96,80},{112,96},{17,1},{33... | collective-permute-start | bytes 221192 | tf_op jit(solution)/shard_map/ppermute | solution.py:23
  3.5 5.7 %collective-permute-start = (bf16[3,32,384]{2,1,0:T(8,128)(2,1)S(1)}, bf16[3,32,384]{2,1,0:T(8,128)(2,1)S(1)}, u32[]{:S(2)}, u32[]{:S(2)}) collective-permute-start(bf16[3,32,384]{2,1,0:T(8,128)(2,1)S(1)} %get-tuple-element.21), channel_id=1, source_target_pairs={{0,16},{16,32},{32,48},{48,64},{64,80},{80,96},{96,112},{1,17},{17... | collective-permute-start | bytes 221192 | tf_op jit(solution)/shard_map/ppermute | solution.py:22
  9.2 2.3 %copy-start.7 = (bf16[3,32,384]{2,1,0:T(8,128)(2,1)}, bf16[3,32,384]{2,1,0:T(8,128)(2,1)S(1)}, u32[]{:S(2)}) copy-start(bf16[3,32,384]{2,1,0:T(8,128)(2,1)S(1)} %collective-permute-done.refs_1_) | copy-start | bytes 221188
  9.2 11.3 %copy-start.9 = (s32[12,4]{0,1:T(4,128)S(1)}, s32[12,4]{0,1:T(4,128)}, u32[]{:S(2)}) copy-start(s32[12,4]{0,1:T(4,128)} %param.17) | copy-start | bytes 580
  9.2 11.3 %copy-start.10 = (s32[12,4]{0,1:T(4,128)S(1)}, s32[12,4]{0,1:T(4,128)}, u32[]{:S(2)}) copy-start(s32[12,4]{0,1:T(4,128)} %param.15) | copy-start | bytes 580
  9.2 11.3 %copy-start.11 = (s32[12,4]{0,1:T(4,128)S(1)}, s32[12,4]{0,1:T(4,128)}, u32[]{:S(2)}) copy-start(s32[12,4]{0,1:T(4,128)} %param.18) | copy-start | bytes 580
  9.2 12.1 %copy-start.8 = (bf16[7,7,384]{2,1,0:T(8,128)(2,1)S(1)}, bf16[7,7,384]{2,1,0:T(8,128)(2,1)}, u32[]{:S(2)}) copy-start(bf16[7,7,384]{2,1,0:T(8,128)(2,1)} %param.11) | copy-start | bytes 112900
  11.4 19.6 %copy-start.6 = (bf16[3,32,384]{2,1,0:T(8,128)(2,1)}, bf16[3,32,384]{2,1,0:T(8,128)(2,1)S(1)}, u32[]{:S(2)}) copy-start(bf16[3,32,384]{2,1,0:T(8,128)(2,1)S(1)} %collective-permute-done.1.refs_2_) | copy-start | bytes 221188
  11.7 13.1 %collective-permute-start.3 = (bf16[102,3,384]{2,1,0:T(4,128)(2,1)S(1)}, bf16[102,3,384]{2,1,0:T(4,128)(2,1)S(1)}, u32[]{:S(2)}, u32[]{:S(2)}) collective-permute-start(bf16[102,3,384]{2,1,0:T(4,128)(2,1)S(1)} %get-tuple-element.16), channel_id=1, source_target_pairs={{1,0},{2,1},{3,2},{4,3},{5,4},{6,5},{7,6},{8,7},{9,8},{10,9},{11,1... | collective-permute-start | bytes 705032 | tf_op jit(solution)/shard_map/ppermute | solution.py:26
  17.9 13.2 %collective-permute-start.2 = (bf16[102,3,384]{2,1,0:T(4,128)(2,1)S(1)}, bf16[102,3,384]{2,1,0:T(4,128)(2,1)S(1)}, u32[]{:S(2)}, u32[]{:S(2)}) collective-permute-start(bf16[102,3,384]{2,1,0:T(4,128)(2,1)S(1)} %get-tuple-element.17), channel_id=1, source_target_pairs={{0,1},{1,2},{2,3},{3,4},{4,5},{5,6},{6,7},{7,8},{8,9},{9,10},{10,1... | collective-permute-start | bytes 705032 | tf_op jit(solution)/shard_map/ppermute | solution.py:25
  24.8 6.2 %copy-start.2 = (bf16[102,3,384]{2,1,0:T(4,128)(2,1)}, bf16[102,3,384]{2,1,0:T(4,128)(2,1)S(1)}, u32[]{:S(2)}) copy-start(bf16[102,3,384]{2,1,0:T(4,128)(2,1)S(1)} %collective-permute-done.3.refs_4_) | copy-start | bytes 705028
  31.1 0.7 copy-start.3
  104.0 5.7 %collective-permute-start.4 = (bf16[3,32,384]{2,1,0:T(8,128)(2,1)S(1)}, bf16[3,32,384]{2,1,0:T(8,128)(2,1)S(1)}, u32[]{:S(2)}, u32[]{:S(2)}) collective-permute-start(bf16[3,32,384]{2,1,0:T(8,128)(2,1)S(1)} %bitcast.22), channel_id=1, source_target_pairs={{0,16},{16,32},{32,48},{48,64},{64,80},{80,96},{96,112},{1,17},{17... | collective-permute-start | bytes 221192 | tf_op jit(solution)/shard_map/ppermute | solution.py:22
  105.9 5.6 %collective-permute-start.5 = (bf16[3,32,384]{2,1,0:T(8,128)(2,1)S(1)}, bf16[3,32,384]{2,1,0:T(8,128)(2,1)S(1)}, u32[]{:S(2)}, u32[]{:S(2)}) collective-permute-start(bf16[3,32,384]{2,1,0:T(8,128)(2,1)S(1)} %bitcast.21), channel_id=1, source_target_pairs={{16,0},{32,16},{48,32},{64,48},{80,64},{96,80},{112,96},{17,1},{33... | collective-permute-start | bytes 221192 | tf_op jit(solution)/shard_map/ppermute | solution.py:23
  109.6 19.0 %copy-start.4 = (bf16[3,32,384]{2,1,0:T(8,128)(2,1)}, bf16[3,32,384]{2,1,0:T(8,128)(2,1)S(1)}, u32[]{:S(2)}) copy-start(bf16[3,32,384]{2,1,0:T(8,128)(2,1)S(1)} %collective-permute-done.4.refs_1_) | copy-start | bytes 221188
  111.5 17.1 %copy-start.5 = (bf16[3,32,384]{2,1,0:T(8,128)(2,1)}, bf16[3,32,384]{2,1,0:T(8,128)(2,1)S(1)}, u32[]{:S(2)}) copy-start(bf16[3,32,384]{2,1,0:T(8,128)(2,1)S(1)} %collective-permute-done.5.refs_2_) | copy-start | bytes 221188
  113.0 11.5 %collective-permute-start.7 = (bf16[102,3,384]{2,1,0:T(4,128)(2,1)S(1)}, bf16[102,3,384]{2,1,0:T(4,128)(2,1)S(1)}, u32[]{:S(2)}, u32[]{:S(2)}) collective-permute-start(bf16[102,3,384]{2,1,0:T(4,128)(2,1)S(1)} %get-tuple-element.14), channel_id=1, source_target_pairs={{1,0},{2,1},{3,2},{4,3},{5,4},{6,5},{7,6},{8,7},{9,8},{10,9},{11,1... | collective-permute-start | bytes 705032 | tf_op jit(solution)/shard_map/ppermute | solution.py:26
  115.0 13.6 %collective-permute-start.6 = (bf16[102,3,384]{2,1,0:T(4,128)(2,1)S(1)}, bf16[102,3,384]{2,1,0:T(4,128)(2,1)S(1)}, u32[]{:S(2)}, u32[]{:S(2)}) collective-permute-start(bf16[102,3,384]{2,1,0:T(4,128)(2,1)S(1)} %get-tuple-element.15), channel_id=1, source_target_pairs={{0,1},{1,2},{2,3},{3,4},{4,5},{5,6},{6,7},{7,8},{8,9},{9,10},{10,1... | collective-permute-start | bytes 705032 | tf_op jit(solution)/shard_map/ppermute | solution.py:25
  124.5 4.0 %copy-start = (bf16[102,3,384]{2,1,0:T(4,128)(2,1)}, bf16[102,3,384]{2,1,0:T(4,128)(2,1)S(1)}, u32[]{:S(2)}) copy-start(bf16[102,3,384]{2,1,0:T(4,128)(2,1)S(1)} %collective-permute-done.7.refs_4_) | copy-start | bytes 705028
  128.6 0.7 copy-start.1

commit v10 on v9

--- a/solution.py
+++ b/solution.py
@@ -270,7 +270,7 @@
     routed = routed_tiles(tile_counts, tile_owner, tile_slot, peer_count, capacity)
     live = routed & (tissue_mask != 0)
     live = live.reshape(-1).astype(jnp.int32)
-    band = 2 if tile_rows % 2 == 0 else 1
+    band = 4 if tile_rows % 4 == 0 else 1
     layout = (band * tile_side * breadth, breadth, tile_side, tile_cols)
     taps = depth_kernel.reshape(KS * KS, channels).astype(jnp.float32)
     mixed = depthwise(halo_pieces(image, reach), taps, reach)

time: 153 us -> 153 us (level)
  no operation moved by 1% of the time
where the time goes in v10:
time: 153 us; the launch traced here: 152 us
  Pallas kernels  93.6 us (61%)
  starting transfers between devices  23.8 us (16%)
  waiting for transfers between devices  21.7 us (14%)
  local copies, waits for them, and re-layouts  8.19 us (5%)
  other arithmetic  3.6 us (2%)
    pallas_call x2, Pallas kernels, pixel_call(): pl.pallas_call(lambda *refs: kernel(*refs, layout=layout), grid_spec=pltp...  49.4 us
    pallas_call x2, Pallas kernels, depthwise(): pl.pallas_call(lambda *refs: depthwise_kernel(*refs, reach=reach, chunk=c...  44.2 us
    ppermute x2, waiting for transfers between devices, halo_pieces(): lax.ppermute(framed[:, cells.shape[1] - width:], 'col', [(i, i + 1) for i...  10.3 us
    ppermute x2, waiting for transfers between devices, halo_pieces(): lax.ppermute(framed[:, :width], 'col', [(i + 1, i) for i in range(cols -...  8.52 us
    ppermute x2, starting transfers between devices, halo_pieces(): lax.ppermute(framed[:, :width], 'col', [(i + 1, i) for i in range(cols -...  8.05 us
    ppermute x2, starting transfers between devices, halo_pieces(): lax.ppermute(framed[:, cells.shape[1] - width:], 'col', [(i, i + 1) for i...  5.84 us
    ppermute x2, starting transfers between devices, halo_pieces(): bottom = lax.ppermute(cells[:width], 'row', up)  5.56 us
    unnamed x27, local copies, waits for them, and re-layouts  4.46 us
  transfers between devices with their start and end apart: 8, of which 7 were waited for; matrix products, arithmetic and copies ran while one was open for 4% of the time, Pallas kernels for 0%

profile of v10, /device:TPU:26, one launch (start us, length us, event | category | flops | bytes accessed | tf_op | source)
XLA Modules:
  0.0 151.7 jit_solution(18001385968367375621)
XLA Ops:
  0.6 0.9 fusion.2
  1.6 1.9 %collective-permute-start.1 = (bf16[3,32,384]{2,1,0:T(8,128)(2,1)S(1)}, bf16[3,32,384]{2,1,0:T(8,128)(2,1)S(1)}, u32[]{:S(2)}, u32[]{:S(2)}) collective-permute-start(bf16[3,32,384]{2,1,0:T(8,128)(2,1)S(1)} %get-tuple-element.20), channel_id=1, source_target_pairs={{16,0},{32,16},{48,32},{64,48},{80,64},{96,80},{112,96},{17,1},{33... | collective-permute-start | bytes 221192 | tf_op jit(solution)/shard_map/ppermute | solution.py:23
  3.5 2.4 %collective-permute-start = (bf16[3,32,384]{2,1,0:T(8,128)(2,1)S(1)}, bf16[3,32,384]{2,1,0:T(8,128)(2,1)S(1)}, u32[]{:S(2)}, u32[]{:S(2)}) collective-permute-start(bf16[3,32,384]{2,1,0:T(8,128)(2,1)S(1)} %get-tuple-element.21), channel_id=1, source_target_pairs={{0,16},{16,32},{32,48},{48,64},{64,80},{80,96},{96,112},{1,17},{17... | collective-permute-start | bytes 221192 | tf_op jit(solution)/shard_map/ppermute | solution.py:22
  5.9 0.8 copy.21
  6.7 0.7 reduce_window_sum.11
  7.4 0.8 select_reduce_fusion.3
  8.2 1.0 collective-permute-done.refs_1_
  9.2 0.0 copy-start.7
  9.2 0.0 copy-start.9
  9.2 0.0 copy-start.10
  9.2 0.0 copy-start.11
  9.2 0.0 copy-start.8
  9.2 2.2 %constant_dynamic-update-slice_fusion.1 = bf16[102,32,384]{2,1,0:T(8,128)(2,1)S(1)} fusion(bf16[102,32,384]{2,1,0:T(8,128)(2,1)S(1)} %constant_dynamic-update-slice_fusion.2, bf16[96,32,384]{2,1,0:T(8,128)(2,1)} %refs_0_.1), kind=kLoop, calls=%fused_computation.7 | loop fusion | bytes 4718592
  11.4 0.0 copy-done.7
  11.4 0.0 collective-permute-done.1.refs_2_
  11.4 0.0 copy-start.6
  11.5 0.2 fusion
  11.7 6.1 %collective-permute-start.3 = (bf16[102,3,384]{2,1,0:T(4,128)(2,1)S(1)}, bf16[102,3,384]{2,1,0:T(4,128)(2,1)S(1)}, u32[]{:S(2)}, u32[]{:S(2)}) collective-permute-start(bf16[102,3,384]{2,1,0:T(4,128)(2,1)S(1)} %get-tuple-element.16), channel_id=1, source_target_pairs={{1,0},{2,1},{3,2},{4,3},{5,4},{6,5},{7,6},{8,7},{9,8},{10,9},{11,1... | collective-permute-start | bytes 705032 | tf_op jit(solution)/shard_map/ppermute | solution.py:26
  17.9 1.9 %collective-permute-start.2 = (bf16[102,3,384]{2,1,0:T(4,128)(2,1)S(1)}, bf16[102,3,384]{2,1,0:T(4,128)(2,1)S(1)}, u32[]{:S(2)}, u32[]{:S(2)}) collective-permute-start(bf16[102,3,384]{2,1,0:T(4,128)(2,1)S(1)} %get-tuple-element.17), channel_id=1, source_target_pairs={{0,1},{1,2},{2,3},{3,4},{4,5},{5,6},{6,7},{7,8},{8,9},{9,10},{10,1... | collective-permute-start | bytes 705032 | tf_op jit(solution)/shard_map/ppermute | solution.py:25
  19.8 0.5 select_reduce_fusion.1
  20.3 0.1 copy.22
  20.4 0.1 copy.23
  20.5 0.0 copy-done.9
  20.5 0.0 copy-done.10
  20.5 0.0 copy-done.11
  20.6 0.1 copy.24
  20.7 0.7 reshape.47.refs_0_
  21.3 0.0 copy-done.8
  21.3 0.7 reshape.48.refs_5_
  22.0 2.9 %collective-permute-done.3.refs_4_ = bf16[102,3,384]{2,1,0:T(4,128)(2,1)S(1)} collective-permute-done((bf16[102,3,384]{2,1,0:T(4,128)(2,1)S(1)}, bf16[102,3,384]{2,1,0:T(4,128)(2,1)S(1)}, u32[]{:S(2)}, u32[]{:S(2)}) %collective-permute-start.3) | collective-permute-done | bytes 235040 | tf_op jit(solution)/shard_map/ppermute | solution.py:26
  24.8 0.0 copy-start.2
  24.8 6.2 %collective-permute-done.2.refs_3_ = bf16[102,3,384]{2,1,0:T(4,128)(2,1)S(1)} collective-permute-done((bf16[102,3,384]{2,1,0:T(4,128)(2,1)S(1)}, bf16[102,3,384]{2,1,0:T(4,128)(2,1)S(1)}, u32[]{:S(2)}, u32[]{:S(2)}) %collective-permute-start.2) | collective-permute-done | bytes 235040 | tf_op jit(solution)/shard_map/ppermute | solution.py:25
  31.1 0.0 copy-done.6
  31.1 0.0 copy-done.2
  31.1 0.0 copy-start.3
  31.1 0.7 copy-done.3
  31.8 21.8 %shard_map.113 = bf16[96,32,384]{2,1,0:T(8,128)(2,1)} custom-call(bf16[96,32,384]{2,1,0:T(8,128)(2,1)} %refs_0_.1, bf16[3,32,384]{2,1,0:T(8,128)(2,1)} %copy-done.7, bf16[3,32,384]{2,1,0:T(8,128)(2,1)} %copy-done.6, bf16[102,3,384]{2,1,0:T(4,128)(2,1)} %copy-done.3, bf16[102,3,384]{2,1,0:T(4,128)(2,1)} %copy-done.2, f32[49,384]{1,0:T(8,128)} %reshape.48.refs_5_), custom_call_target="tpu_custom_call" | custom-call | tf_op jit(solution)/shard_map/pallas_call | solution.py:88
  53.6 22.2 %shard_map.114 = (bf16[3072,384]{1,0:T(8,128)(2,1)}, bf16[768,768]{1,0:T(8,128)(2,1)}) custom-call(s32[48]{0:T(128)} %reshape.47.refs_0_, bf16[3072,384]{1,0:T(8,128)(2,1)} %bitcast.13, bf16[3072,384]{1,0:T(8,128)(2,1)} %bitcast.12, bf16[384,1536]{1,0:T(8,128)(2,1)} %refs_4_.3, bf16[1536,384]{1,0:T(8,128)(2,1)} %refs_5_.1, bf16[4,384,768]{2,1,0:T(8,128)(2,1)} %bitcast.17), custom_call_target="tpu_custom_call" | custom-call | tf_op jit(solution)/shard_map/pallas_call | solution.py:235
  75.8 27.2 %shard_map.115 = (bf16[3072,384]{1,0:T(8,128)(2,1)}, bf16[3072,384]{1,0:T(8,128)(2,1)}) custom-call(s32[48]{0:T(128)} %reshape.47.refs_0_, bf16[3072,384]{1,0:T(8,128)(2,1)} %bitcast.14, bf16[3072,384]{1,0:T(8,128)(2,1)} %get-tuple-element.7.refs_2_, bf16[768,768]{1,0:T(8,128)(2,1)} %bitcast.20, bf16[384,1536]{1,0:T(8,128)(2,1)} %refs_4_.3, ...), custom_call_target="tpu_custom_call" | custom-call | tf_op jit(solution)/shard_map/pallas_call | solution.py:235
  103.0 0.9 fusion.1
  103.9 1.9 %collective-permute-start.4 = (bf16[3,32,384]{2,1,0:T(8,128)(2,1)S(1)}, bf16[3,32,384]{2,1,0:T(8,128)(2,1)S(1)}, u32[]{:S(2)}, u32[]{:S(2)}) collective-permute-start(bf16[3,32,384]{2,1,0:T(8,128)(2,1)S(1)} %bitcast.22), channel_id=1, source_target_pairs={{0,16},{16,32},{32,48},{48,64},{64,80},{80,96},{96,112},{1,17},{17... | collective-permute-start | bytes 221192 | tf_op jit(solution)/shard_map/ppermute | solution.py:22
  105.9 3.6 %collective-permute-start.5 = (bf16[3,32,384]{2,1,0:T(8,128)(2,1)S(1)}, bf16[3,32,384]{2,1,0:T(8,128)(2,1)S(1)}, u32[]{:S(2)}, u32[]{:S(2)}) collective-permute-start(bf16[3,32,384]{2,1,0:T(8,128)(2,1)S(1)} %bitcast.21), channel_id=1, source_target_pairs={{16,0},{32,16},{48,32},{64,48},{80,64},{96,80},{112,96},{17,1},{33... | collective-permute-start | bytes 221192 | tf_op jit(solution)/shard_map/ppermute | solution.py:23
  109.5 0.1 collective-permute-done.4.refs_1_
  109.6 0.0 copy-start.4
  109.6 1.9 %collective-permute-done.5.refs_2_ = bf16[3,32,384]{2,1,0:T(8,128)(2,1)S(1)} collective-permute-done((bf16[3,32,384]{2,1,0:T(8,128)(2,1)S(1)}, bf16[3,32,384]{2,1,0:T(8,128)(2,1)S(1)}, u32[]{:S(2)}, u32[]{:S(2)}) %collective-permute-start.5) | collective-permute-done | bytes 73760 | tf_op jit(solution)/shard_map/ppermute | solution.py:23
  111.5 0.0 copy-start.5
  111.5 1.5 %pad_maximum_fusion = (bf16[102,3,384]{2,1,0:T(4,128)(2,1)S(1)}, bf16[102,3,384]{2,1,0:T(4,128)(2,1)S(1)}) fusion(bf16[3,32,384]{2,1,0:T(8,128)(2,1)S(1)} %collective-permute-done.5.refs_2_, bf16[96,32,384]{2,1,0:T(8,128)(2,1)} %bitcast.15, bf16[3,32,384]{2,1,0:T(8,128)(2,1)S(1)} %collective-permute-done.4.refs_1_), kind=kLoop, calls=%fused_computation | loop fusion | flops 1410048 | bytes 2976768 | tf_op jit(solution)/shard_map/concatenate | solution.py:24
  113.0 1.9 %collective-permute-start.7 = (bf16[102,3,384]{2,1,0:T(4,128)(2,1)S(1)}, bf16[102,3,384]{2,1,0:T(4,128)(2,1)S(1)}, u32[]{:S(2)}, u32[]{:S(2)}) collective-permute-start(bf16[102,3,384]{2,1,0:T(4,128)(2,1)S(1)} %get-tuple-element.14), channel_id=1, source_target_pairs={{1,0},{2,1},{3,2},{4,3},{5,4},{6,5},{7,6},{8,7},{9,8},{10,9},{11,1... | collective-permute-start | bytes 705032 | tf_op jit(solution)/shard_map/ppermute | solution.py:26
  114.9 3.9 %collective-permute-start.6 = (bf16[102,3,384]{2,1,0:T(4,128)(2,1)S(1)}, bf16[102,3,384]{2,1,0:T(4,128)(2,1)S(1)}, u32[]{:S(2)}, u32[]{:S(2)}) collective-permute-start(bf16[102,3,384]{2,1,0:T(4,128)(2,1)S(1)} %get-tuple-element.15), channel_id=1, source_target_pairs={{0,1},{1,2},{2,3},{3,4},{4,5},{5,6},{6,7},{7,8},{8,9},{9,10},{10,1... | collective-permute-start | bytes 705032 | tf_op jit(solution)/shard_map/ppermute | solution.py:25
  118.9 5.7 %collective-permute-done.7.refs_4_ = bf16[102,3,384]{2,1,0:T(4,128)(2,1)S(1)} collective-permute-done((bf16[102,3,384]{2,1,0:T(4,128)(2,1)S(1)}, bf16[102,3,384]{2,1,0:T(4,128)(2,1)S(1)}, u32[]{:S(2)}, u32[]{:S(2)}) %collective-permute-start.7) | collective-permute-done | bytes 235040 | tf_op jit(solution)/shard_map/ppermute | solution.py:26
  124.5 0.0 copy-start
  124.5 4.0 %collective-permute-done.6.refs_3_ = bf16[102,3,384]{2,1,0:T(4,128)(2,1)S(1)} collective-permute-done((bf16[102,3,384]{2,1,0:T(4,128)(2,1)S(1)}, bf16[102,3,384]{2,1,0:T(4,128)(2,1)S(1)}, u32[]{:S(2)}, u32[]{:S(2)}) %collective-permute-start.6) | collective-permute-done | bytes 235040 | tf_op jit(solution)/shard_map/ppermute | solution.py:25
  128.6 0.0 copy-start.1
  128.6 0.0 copy-done.4
  128.6 0.0 copy-done.5
  128.6 0.0 copy-done
  128.6 0.7 copy-done.1
  129.3 22.4 %shard_map.116 = bf16[96,32,384]{2,1,0:T(8,128)(2,1)} custom-call(bf16[96,32,384]{2,1,0:T(8,128)(2,1)} %bitcast.16, bf16[3,32,384]{2,1,0:T(8,128)(2,1)} %copy-done.4, bf16[3,32,384]{2,1,0:T(8,128)(2,1)} %copy-done.5, bf16[102,3,384]{2,1,0:T(4,128)(2,1)} %copy-done.1, bf16[102,3,384]{2,1,0:T(4,128)(2,1)} %copy-done, f32[49,384]{1,0:T(8,128)} %reshape.48.refs_5_, ...), custom_call_target="tpu_custom_call" | custom-call | tf_op jit(solution)/shard_map/pallas_call | solution.py:88
  (4 shorter events, 0.0 us)
Async XLA Ops:
  1.6 9.9 %collective-permute-start.1 = (bf16[3,32,384]{2,1,0:T(8,128)(2,1)S(1)}, bf16[3,32,384]{2,1,0:T(8,128)(2,1)S(1)}, u32[]{:S(2)}, u32[]{:S(2)}) collective-permute-start(bf16[3,32,384]{2,1,0:T(8,128)(2,1)S(1)} %get-tuple-element.20), channel_id=1, source_target_pairs={{16,0},{32,16},{48,32},{64,48},{80,64},{96,80},{112,96},{17,1},{33... | collective-permute-start | bytes 221192 | tf_op jit(solution)/shard_map/ppermute | solution.py:23
  3.5 5.7 %collective-permute-start = (bf16[3,32,384]{2,1,0:T(8,128)(2,1)S(1)}, bf16[3,32,384]{2,1,0:T(8,128)(2,1)S(1)}, u32[]{:S(2)}, u32[]{:S(2)}) collective-permute-start(bf16[3,32,384]{2,1,0:T(8,128)(2,1)S(1)} %get-tuple-element.21), channel_id=1, source_target_pairs={{0,16},{16,32},{32,48},{48,64},{64,80},{80,96},{96,112},{1,17},{17... | collective-permute-start | bytes 221192 | tf_op jit(solution)/shard_map/ppermute | solution.py:22
  9.2 2.3 %copy-start.7 = (bf16[3,32,384]{2,1,0:T(8,128)(2,1)}, bf16[3,32,384]{2,1,0:T(8,128)(2,1)S(1)}, u32[]{:S(2)}) copy-start(bf16[3,32,384]{2,1,0:T(8,128)(2,1)S(1)} %collective-permute-done.refs_1_) | copy-start | bytes 221188
  9.2 11.3 %copy-start.9 = (s32[12,4]{0,1:T(4,128)S(1)}, s32[12,4]{0,1:T(4,128)}, u32[]{:S(2)}) copy-start(s32[12,4]{0,1:T(4,128)} %param.17) | copy-start | bytes 580
  9.2 11.3 %copy-start.10 = (s32[12,4]{0,1:T(4,128)S(1)}, s32[12,4]{0,1:T(4,128)}, u32[]{:S(2)}) copy-start(s32[12,4]{0,1:T(4,128)} %param.15) | copy-start | bytes 580
  9.2 11.3 %copy-start.11 = (s32[12,4]{0,1:T(4,128)S(1)}, s32[12,4]{0,1:T(4,128)}, u32[]{:S(2)}) copy-start(s32[12,4]{0,1:T(4,128)} %param.18) | copy-start | bytes 580
  9.2 12.1 %copy-start.8 = (bf16[7,7,384]{2,1,0:T(8,128)(2,1)S(1)}, bf16[7,7,384]{2,1,0:T(8,128)(2,1)}, u32[]{:S(2)}) copy-start(bf16[7,7,384]{2,1,0:T(8,128)(2,1)} %param.11) | copy-start | bytes 112900
  11.4 19.6 %copy-start.6 = (bf16[3,32,384]{2,1,0:T(8,128)(2,1)}, bf16[3,32,384]{2,1,0:T(8,128)(2,1)S(1)}, u32[]{:S(2)}) copy-start(bf16[3,32,384]{2,1,0:T(8,128)(2,1)S(1)} %collective-permute-done.1.refs_2_) | copy-start | bytes 221188
  11.7 13.1 %collective-permute-start.3 = (bf16[102,3,384]{2,1,0:T(4,128)(2,1)S(1)}, bf16[102,3,384]{2,1,0:T(4,128)(2,1)S(1)}, u32[]{:S(2)}, u32[]{:S(2)}) collective-permute-start(bf16[102,3,384]{2,1,0:T(4,128)(2,1)S(1)} %get-tuple-element.16), channel_id=1, source_target_pairs={{1,0},{2,1},{3,2},{4,3},{5,4},{6,5},{7,6},{8,7},{9,8},{10,9},{11,1... | collective-permute-start | bytes 705032 | tf_op jit(solution)/shard_map/ppermute | solution.py:26
  17.9 13.2 %collective-permute-start.2 = (bf16[102,3,384]{2,1,0:T(4,128)(2,1)S(1)}, bf16[102,3,384]{2,1,0:T(4,128)(2,1)S(1)}, u32[]{:S(2)}, u32[]{:S(2)}) collective-permute-start(bf16[102,3,384]{2,1,0:T(4,128)(2,1)S(1)} %get-tuple-element.17), channel_id=1, source_target_pairs={{0,1},{1,2},{2,3},{3,4},{4,5},{5,6},{6,7},{7,8},{8,9},{9,10},{10,1... | collective-permute-start | bytes 705032 | tf_op jit(solution)/shard_map/ppermute | solution.py:25
  24.8 6.2 %copy-start.2 = (bf16[102,3,384]{2,1,0:T(4,128)(2,1)}, bf16[102,3,384]{2,1,0:T(4,128)(2,1)S(1)}, u32[]{:S(2)}) copy-start(bf16[102,3,384]{2,1,0:T(4,128)(2,1)S(1)} %collective-permute-done.3.refs_4_) | copy-start | bytes 705028
  31.1 0.7 copy-start.3
  103.9 5.7 %collective-permute-start.4 = (bf16[3,32,384]{2,1,0:T(8,128)(2,1)S(1)}, bf16[3,32,384]{2,1,0:T(8,128)(2,1)S(1)}, u32[]{:S(2)}, u32[]{:S(2)}) collective-permute-start(bf16[3,32,384]{2,1,0:T(8,128)(2,1)S(1)} %bitcast.22), channel_id=1, source_target_pairs={{0,16},{16,32},{32,48},{48,64},{64,80},{80,96},{96,112},{1,17},{17... | collective-permute-start | bytes 221192 | tf_op jit(solution)/shard_map/ppermute | solution.py:22
  105.9 5.6 %collective-permute-start.5 = (bf16[3,32,384]{2,1,0:T(8,128)(2,1)S(1)}, bf16[3,32,384]{2,1,0:T(8,128)(2,1)S(1)}, u32[]{:S(2)}, u32[]{:S(2)}) collective-permute-start(bf16[3,32,384]{2,1,0:T(8,128)(2,1)S(1)} %bitcast.21), channel_id=1, source_target_pairs={{16,0},{32,16},{48,32},{64,48},{80,64},{96,80},{112,96},{17,1},{33... | collective-permute-start | bytes 221192 | tf_op jit(solution)/shard_map/ppermute | solution.py:23
  109.6 19.0 %copy-start.4 = (bf16[3,32,384]{2,1,0:T(8,128)(2,1)}, bf16[3,32,384]{2,1,0:T(8,128)(2,1)S(1)}, u32[]{:S(2)}) copy-start(bf16[3,32,384]{2,1,0:T(8,128)(2,1)S(1)} %collective-permute-done.4.refs_1_) | copy-start | bytes 221188
  111.5 17.1 %copy-start.5 = (bf16[3,32,384]{2,1,0:T(8,128)(2,1)}, bf16[3,32,384]{2,1,0:T(8,128)(2,1)S(1)}, u32[]{:S(2)}) copy-start(bf16[3,32,384]{2,1,0:T(8,128)(2,1)S(1)} %collective-permute-done.5.refs_2_) | copy-start | bytes 221188
  113.0 11.5 %collective-permute-start.7 = (bf16[102,3,384]{2,1,0:T(4,128)(2,1)S(1)}, bf16[102,3,384]{2,1,0:T(4,128)(2,1)S(1)}, u32[]{:S(2)}, u32[]{:S(2)}) collective-permute-start(bf16[102,3,384]{2,1,0:T(4,128)(2,1)S(1)} %get-tuple-element.14), channel_id=1, source_target_pairs={{1,0},{2,1},{3,2},{4,3},{5,4},{6,5},{7,6},{8,7},{9,8},{10,9},{11,1... | collective-permute-start | bytes 705032 | tf_op jit(solution)/shard_map/ppermute | solution.py:26
  114.9 13.6 %collective-permute-start.6 = (bf16[102,3,384]{2,1,0:T(4,128)(2,1)S(1)}, bf16[102,3,384]{2,1,0:T(4,128)(2,1)S(1)}, u32[]{:S(2)}, u32[]{:S(2)}) collective-permute-start(bf16[102,3,384]{2,1,0:T(4,128)(2,1)S(1)} %get-tuple-element.15), channel_id=1, source_target_pairs={{0,1},{1,2},{2,3},{3,4},{4,5},{5,6},{6,7},{7,8},{8,9},{9,10},{10,1... | collective-permute-start | bytes 705032 | tf_op jit(solution)/shard_map/ppermute | solution.py:25
  124.5 4.0 %copy-start = (bf16[102,3,384]{2,1,0:T(4,128)(2,1)}, bf16[102,3,384]{2,1,0:T(4,128)(2,1)S(1)}, u32[]{:S(2)}) copy-start(bf16[102,3,384]{2,1,0:T(4,128)(2,1)S(1)} %collective-permute-done.7.refs_4_) | copy-start | bytes 705028
  128.6 0.7 copy-start.1

commit v11 on v9

--- a/solution.py
+++ b/solution.py
@@ -66,7 +66,7 @@
                 total_ref[pl.ds(start, chunk)] = total
             return carry
 
-        lax.fori_loop(0, height // chunk, body, 0)
+        lax.fori_loop(0, height // chunk, body, 0, unroll=2)
 
 
 def depthwise(pieces, taps, reach, base=None, flip=False, lanes=128, chunk=8):

time: 153 us -> 151 us (0.987)
  Pallas kernels: 93.6 us -> 91.4 us
    pallas_call x2, Pallas kernels: 44.2 us -> 42.1 us  [depthwise(): pl.pallas_call(lambda *refs: depthwise_kernel(*refs, reach=reach, chunk=c...]
where the time goes in v11:
time: 151 us; the launch traced here: 149 us
  Pallas kernels  91.4 us (61%)
  starting transfers between devices  23.8 us (16%)
  waiting for transfers between devices  21.7 us (14%)
  local copies, waits for them, and re-layouts  8.19 us (5%)
  other arithmetic  3.6 us (2%)
    pallas_call x2, Pallas kernels, pixel_call(): pl.pallas_call(lambda *refs: kernel(*refs, layout=layout), grid_spec=pltp...  49.4 us
    pallas_call x2, Pallas kernels, depthwise(): pl.pallas_call(lambda *refs: depthwise_kernel(*refs, reach=reach, chunk=c...  42.1 us
    ppermute x2, waiting for transfers between devices, halo_pieces(): lax.ppermute(framed[:, cells.shape[1] - width:], 'col', [(i, i + 1) for i...  10.3 us
    ppermute x2, waiting for transfers between devices, halo_pieces(): lax.ppermute(framed[:, :width], 'col', [(i + 1, i) for i in range(cols -...  8.48 us
    ppermute x2, starting transfers between devices, halo_pieces(): lax.ppermute(framed[:, :width], 'col', [(i + 1, i) for i in range(cols -...  8.05 us
    ppermute x2, starting transfers between devices, halo_pieces(): lax.ppermute(framed[:, cells.shape[1] - width:], 'col', [(i, i + 1) for i...  5.84 us
    ppermute x2, starting transfers between devices, halo_pieces(): bottom = lax.ppermute(cells[:width], 'row', up)  5.56 us
    unnamed x27, local copies, waits for them, and re-layouts  4.46 us
  transfers between devices with their start and end apart: 8, of which 7 were waited for; matrix products, arithmetic and copies ran while one was open for 4% of the time, Pallas kernels for 0%

profile of v11, /device:TPU:26, one launch (start us, length us, event | category | flops | bytes accessed | tf_op | source)
XLA Modules:
  0.0 149.5 jit_solution(3334649589630420733)
XLA Ops:
  0.6 0.9 fusion.2
  1.6 1.9 %collective-permute-start.1 = (bf16[3,32,384]{2,1,0:T(8,128)(2,1)S(1)}, bf16[3,32,384]{2,1,0:T(8,128)(2,1)S(1)}, u32[]{:S(2)}, u32[]{:S(2)}) collective-permute-start(bf16[3,32,384]{2,1,0:T(8,128)(2,1)S(1)} %get-tuple-element.20), channel_id=1, source_target_pairs={{16,0},{32,16},{48,32},{64,48},{80,64},{96,80},{112,96},{17,1},{33... | collective-permute-start | bytes 221192 | tf_op jit(solution)/shard_map/ppermute | solution.py:23
  3.5 2.4 %collective-permute-start = (bf16[3,32,384]{2,1,0:T(8,128)(2,1)S(1)}, bf16[3,32,384]{2,1,0:T(8,128)(2,1)S(1)}, u32[]{:S(2)}, u32[]{:S(2)}) collective-permute-start(bf16[3,32,384]{2,1,0:T(8,128)(2,1)S(1)} %get-tuple-element.21), channel_id=1, source_target_pairs={{0,16},{16,32},{32,48},{48,64},{64,80},{80,96},{96,112},{1,17},{17... | collective-permute-start | bytes 221192 | tf_op jit(solution)/shard_map/ppermute | solution.py:22
  5.9 0.8 copy.21
  6.7 0.7 reduce_window_sum.11
  7.4 0.8 select_reduce_fusion.3
  8.2 1.0 collective-permute-done.refs_1_
  9.2 0.0 copy-start.7
  9.2 0.0 copy-start.9
  9.2 0.0 copy-start.10
  9.2 0.0 copy-start.11
  9.2 0.0 copy-start.8
  9.2 2.2 %constant_dynamic-update-slice_fusion.1 = bf16[102,32,384]{2,1,0:T(8,128)(2,1)S(1)} fusion(bf16[102,32,384]{2,1,0:T(8,128)(2,1)S(1)} %constant_dynamic-update-slice_fusion.2, bf16[96,32,384]{2,1,0:T(8,128)(2,1)} %refs_0_.1), kind=kLoop, calls=%fused_computation.7 | loop fusion | bytes 4718592
  11.4 0.0 copy-done.7
  11.4 0.0 collective-permute-done.1.refs_2_
  11.4 0.0 copy-start.6
  11.5 0.2 fusion
  11.7 6.1 %collective-permute-start.3 = (bf16[102,3,384]{2,1,0:T(4,128)(2,1)S(1)}, bf16[102,3,384]{2,1,0:T(4,128)(2,1)S(1)}, u32[]{:S(2)}, u32[]{:S(2)}) collective-permute-start(bf16[102,3,384]{2,1,0:T(4,128)(2,1)S(1)} %get-tuple-element.16), channel_id=1, source_target_pairs={{1,0},{2,1},{3,2},{4,3},{5,4},{6,5},{7,6},{8,7},{9,8},{10,9},{11,1... | collective-permute-start | bytes 705032 | tf_op jit(solution)/shard_map/ppermute | solution.py:26
  17.9 1.9 %collective-permute-start.2 = (bf16[102,3,384]{2,1,0:T(4,128)(2,1)S(1)}, bf16[102,3,384]{2,1,0:T(4,128)(2,1)S(1)}, u32[]{:S(2)}, u32[]{:S(2)}) collective-permute-start(bf16[102,3,384]{2,1,0:T(4,128)(2,1)S(1)} %get-tuple-element.17), channel_id=1, source_target_pairs={{0,1},{1,2},{2,3},{3,4},{4,5},{5,6},{6,7},{7,8},{8,9},{9,10},{10,1... | collective-permute-start | bytes 705032 | tf_op jit(solution)/shard_map/ppermute | solution.py:25
  19.8 0.5 select_reduce_fusion.1
  20.3 0.1 copy.22
  20.4 0.1 copy.23
  20.5 0.0 copy-done.9
  20.5 0.0 copy-done.10
  20.5 0.0 copy-done.11
  20.6 0.1 copy.24
  20.7 0.7 reshape.47.refs_0_
  21.3 0.0 copy-done.8
  21.3 0.7 reshape.48.refs_5_
  22.0 2.9 %collective-permute-done.3.refs_4_ = bf16[102,3,384]{2,1,0:T(4,128)(2,1)S(1)} collective-permute-done((bf16[102,3,384]{2,1,0:T(4,128)(2,1)S(1)}, bf16[102,3,384]{2,1,0:T(4,128)(2,1)S(1)}, u32[]{:S(2)}, u32[]{:S(2)}) %collective-permute-start.3) | collective-permute-done | bytes 235040 | tf_op jit(solution)/shard_map/ppermute | solution.py:26
  24.8 0.0 copy-start.2
  24.8 6.2 %collective-permute-done.2.refs_3_ = bf16[102,3,384]{2,1,0:T(4,128)(2,1)S(1)} collective-permute-done((bf16[102,3,384]{2,1,0:T(4,128)(2,1)S(1)}, bf16[102,3,384]{2,1,0:T(4,128)(2,1)S(1)}, u32[]{:S(2)}, u32[]{:S(2)}) %collective-permute-start.2) | collective-permute-done | bytes 235040 | tf_op jit(solution)/shard_map/ppermute | solution.py:25
  31.1 0.0 copy-done.6
  31.1 0.0 copy-done.2
  31.1 0.0 copy-start.3
  31.1 0.7 copy-done.3
  31.8 20.7 %shard_map.113 = bf16[96,32,384]{2,1,0:T(8,128)(2,1)} custom-call(bf16[96,32,384]{2,1,0:T(8,128)(2,1)} %refs_0_.1, bf16[3,32,384]{2,1,0:T(8,128)(2,1)} %copy-done.7, bf16[3,32,384]{2,1,0:T(8,128)(2,1)} %copy-done.6, bf16[102,3,384]{2,1,0:T(4,128)(2,1)} %copy-done.3, bf16[102,3,384]{2,1,0:T(4,128)(2,1)} %copy-done.2, f32[49,384]{1,0:T(8,128)} %reshape.48.refs_5_), custom_call_target="tpu_custom_call" | custom-call | tf_op jit(solution)/shard_map/pallas_call | solution.py:88
  52.5 22.7 %shard_map.114 = (bf16[3072,384]{1,0:T(8,128)(2,1)}, bf16[768,768]{1,0:T(8,128)(2,1)}) custom-call(s32[48]{0:T(128)} %reshape.47.refs_0_, bf16[3072,384]{1,0:T(8,128)(2,1)} %bitcast.13, bf16[3072,384]{1,0:T(8,128)(2,1)} %bitcast.12, bf16[384,1536]{1,0:T(8,128)(2,1)} %refs_4_.3, bf16[1536,384]{1,0:T(8,128)(2,1)} %refs_5_.1, bf16[4,384,768]{2,1,0:T(8,128)(2,1)} %bitcast.17), custom_call_target="tpu_custom_call" | custom-call | tf_op jit(solution)/shard_map/pallas_call | solution.py:235
  75.2 26.6 %shard_map.115 = (bf16[3072,384]{1,0:T(8,128)(2,1)}, bf16[3072,384]{1,0:T(8,128)(2,1)}) custom-call(s32[48]{0:T(128)} %reshape.47.refs_0_, bf16[3072,384]{1,0:T(8,128)(2,1)} %bitcast.14, bf16[3072,384]{1,0:T(8,128)(2,1)} %get-tuple-element.7.refs_2_, bf16[768,768]{1,0:T(8,128)(2,1)} %bitcast.20, bf16[384,1536]{1,0:T(8,128)(2,1)} %refs_4_.3, ...), custom_call_target="tpu_custom_call" | custom-call | tf_op jit(solution)/shard_map/pallas_call | solution.py:235
  101.9 0.9 fusion.1
  102.8 1.9 %collective-permute-start.4 = (bf16[3,32,384]{2,1,0:T(8,128)(2,1)S(1)}, bf16[3,32,384]{2,1,0:T(8,128)(2,1)S(1)}, u32[]{:S(2)}, u32[]{:S(2)}) collective-permute-start(bf16[3,32,384]{2,1,0:T(8,128)(2,1)S(1)} %bitcast.22), channel_id=1, source_target_pairs={{0,16},{16,32},{32,48},{48,64},{64,80},{80,96},{96,112},{1,17},{17... | collective-permute-start | bytes 221192 | tf_op jit(solution)/shard_map/ppermute | solution.py:22
  104.7 3.6 %collective-permute-start.5 = (bf16[3,32,384]{2,1,0:T(8,128)(2,1)S(1)}, bf16[3,32,384]{2,1,0:T(8,128)(2,1)S(1)}, u32[]{:S(2)}, u32[]{:S(2)}) collective-permute-start(bf16[3,32,384]{2,1,0:T(8,128)(2,1)S(1)} %bitcast.21), channel_id=1, source_target_pairs={{16,0},{32,16},{48,32},{64,48},{80,64},{96,80},{112,96},{17,1},{33... | collective-permute-start | bytes 221192 | tf_op jit(solution)/shard_map/ppermute | solution.py:23
  108.4 0.1 collective-permute-done.4.refs_1_
  108.5 0.0 copy-start.4
  108.5 1.9 %collective-permute-done.5.refs_2_ = bf16[3,32,384]{2,1,0:T(8,128)(2,1)S(1)} collective-permute-done((bf16[3,32,384]{2,1,0:T(8,128)(2,1)S(1)}, bf16[3,32,384]{2,1,0:T(8,128)(2,1)S(1)}, u32[]{:S(2)}, u32[]{:S(2)}) %collective-permute-start.5) | collective-permute-done | bytes 73760 | tf_op jit(solution)/shard_map/ppermute | solution.py:23
  110.4 0.0 copy-start.5
  110.4 1.5 %pad_maximum_fusion = (bf16[102,3,384]{2,1,0:T(4,128)(2,1)S(1)}, bf16[102,3,384]{2,1,0:T(4,128)(2,1)S(1)}) fusion(bf16[3,32,384]{2,1,0:T(8,128)(2,1)S(1)} %collective-permute-done.5.refs_2_, bf16[96,32,384]{2,1,0:T(8,128)(2,1)} %bitcast.15, bf16[3,32,384]{2,1,0:T(8,128)(2,1)S(1)} %collective-permute-done.4.refs_1_), kind=kLoop, calls=%fused_computation | loop fusion | flops 1410048 | bytes 2976768 | tf_op jit(solution)/shard_map/concatenate | solution.py:24
  111.9 1.9 %collective-permute-start.7 = (bf16[102,3,384]{2,1,0:T(4,128)(2,1)S(1)}, bf16[102,3,384]{2,1,0:T(4,128)(2,1)S(1)}, u32[]{:S(2)}, u32[]{:S(2)}) collective-permute-start(bf16[102,3,384]{2,1,0:T(4,128)(2,1)S(1)} %get-tuple-element.14), channel_id=1, source_target_pairs={{1,0},{2,1},{3,2},{4,3},{5,4},{6,5},{7,6},{8,7},{9,8},{10,9},{11,1... | collective-permute-start | bytes 705032 | tf_op jit(solution)/shard_map/ppermute | solution.py:26
  113.8 3.9 %collective-permute-start.6 = (bf16[102,3,384]{2,1,0:T(4,128)(2,1)S(1)}, bf16[102,3,384]{2,1,0:T(4,128)(2,1)S(1)}, u32[]{:S(2)}, u32[]{:S(2)}) collective-permute-start(bf16[102,3,384]{2,1,0:T(4,128)(2,1)S(1)} %get-tuple-element.15), channel_id=1, source_target_pairs={{0,1},{1,2},{2,3},{3,4},{4,5},{5,6},{6,7},{7,8},{8,9},{9,10},{10,1... | collective-permute-start | bytes 705032 | tf_op jit(solution)/shard_map/ppermute | solution.py:25
  117.7 5.6 %collective-permute-done.7.refs_4_ = bf16[102,3,384]{2,1,0:T(4,128)(2,1)S(1)} collective-permute-done((bf16[102,3,384]{2,1,0:T(4,128)(2,1)S(1)}, bf16[102,3,384]{2,1,0:T(4,128)(2,1)S(1)}, u32[]{:S(2)}, u32[]{:S(2)}) %collective-permute-start.7) | collective-permute-done | bytes 235040 | tf_op jit(solution)/shard_map/ppermute | solution.py:26
  123.4 0.0 copy-start
  123.4 4.0 %collective-permute-done.6.refs_3_ = bf16[102,3,384]{2,1,0:T(4,128)(2,1)S(1)} collective-permute-done((bf16[102,3,384]{2,1,0:T(4,128)(2,1)S(1)}, bf16[102,3,384]{2,1,0:T(4,128)(2,1)S(1)}, u32[]{:S(2)}, u32[]{:S(2)}) %collective-permute-start.6) | collective-permute-done | bytes 235040 | tf_op jit(solution)/shard_map/ppermute | solution.py:25
  127.4 0.0 copy-start.1
  127.4 0.0 copy-done.4
  127.4 0.0 copy-done.5
  127.4 0.0 copy-done
  127.4 0.7 copy-done.1
  128.1 21.3 %shard_map.116 = bf16[96,32,384]{2,1,0:T(8,128)(2,1)} custom-call(bf16[96,32,384]{2,1,0:T(8,128)(2,1)} %bitcast.16, bf16[3,32,384]{2,1,0:T(8,128)(2,1)} %copy-done.4, bf16[3,32,384]{2,1,0:T(8,128)(2,1)} %copy-done.5, bf16[102,3,384]{2,1,0:T(4,128)(2,1)} %copy-done.1, bf16[102,3,384]{2,1,0:T(4,128)(2,1)} %copy-done, f32[49,384]{1,0:T(8,128)} %reshape.48.refs_5_, ...), custom_call_target="tpu_custom_call" | custom-call | tf_op jit(solution)/shard_map/pallas_call | solution.py:88
  (4 shorter events, 0.0 us)
Async XLA Ops:
  1.6 9.9 %collective-permute-start.1 = (bf16[3,32,384]{2,1,0:T(8,128)(2,1)S(1)}, bf16[3,32,384]{2,1,0:T(8,128)(2,1)S(1)}, u32[]{:S(2)}, u32[]{:S(2)}) collective-permute-start(bf16[3,32,384]{2,1,0:T(8,128)(2,1)S(1)} %get-tuple-element.20), channel_id=1, source_target_pairs={{16,0},{32,16},{48,32},{64,48},{80,64},{96,80},{112,96},{17,1},{33... | collective-permute-start | bytes 221192 | tf_op jit(solution)/shard_map/ppermute | solution.py:23
  3.5 5.7 %collective-permute-start = (bf16[3,32,384]{2,1,0:T(8,128)(2,1)S(1)}, bf16[3,32,384]{2,1,0:T(8,128)(2,1)S(1)}, u32[]{:S(2)}, u32[]{:S(2)}) collective-permute-start(bf16[3,32,384]{2,1,0:T(8,128)(2,1)S(1)} %get-tuple-element.21), channel_id=1, source_target_pairs={{0,16},{16,32},{32,48},{48,64},{64,80},{80,96},{96,112},{1,17},{17... | collective-permute-start | bytes 221192 | tf_op jit(solution)/shard_map/ppermute | solution.py:22
  9.2 2.3 %copy-start.7 = (bf16[3,32,384]{2,1,0:T(8,128)(2,1)}, bf16[3,32,384]{2,1,0:T(8,128)(2,1)S(1)}, u32[]{:S(2)}) copy-start(bf16[3,32,384]{2,1,0:T(8,128)(2,1)S(1)} %collective-permute-done.refs_1_) | copy-start | bytes 221188
  9.2 11.3 %copy-start.9 = (s32[12,4]{0,1:T(4,128)S(1)}, s32[12,4]{0,1:T(4,128)}, u32[]{:S(2)}) copy-start(s32[12,4]{0,1:T(4,128)} %param.17) | copy-start | bytes 580
  9.2 11.3 %copy-start.10 = (s32[12,4]{0,1:T(4,128)S(1)}, s32[12,4]{0,1:T(4,128)}, u32[]{:S(2)}) copy-start(s32[12,4]{0,1:T(4,128)} %param.15) | copy-start | bytes 580
  9.2 11.3 %copy-start.11 = (s32[12,4]{0,1:T(4,128)S(1)}, s32[12,4]{0,1:T(4,128)}, u32[]{:S(2)}) copy-start(s32[12,4]{0,1:T(4,128)} %param.18) | copy-start | bytes 580
  9.2 12.1 %copy-start.8 = (bf16[7,7,384]{2,1,0:T(8,128)(2,1)S(1)}, bf16[7,7,384]{2,1,0:T(8,128)(2,1)}, u32[]{:S(2)}) copy-start(bf16[7,7,384]{2,1,0:T(8,128)(2,1)} %param.11) | copy-start | bytes 112900
  11.4 19.6 %copy-start.6 = (bf16[3,32,384]{2,1,0:T(8,128)(2,1)}, bf16[3,32,384]{2,1,0:T(8,128)(2,1)S(1)}, u32[]{:S(2)}) copy-start(bf16[3,32,384]{2,1,0:T(8,128)(2,1)S(1)} %collective-permute-done.1.refs_2_) | copy-start | bytes 221188
  11.7 13.1 %collective-permute-start.3 = (bf16[102,3,384]{2,1,0:T(4,128)(2,1)S(1)}, bf16[102,3,384]{2,1,0:T(4,128)(2,1)S(1)}, u32[]{:S(2)}, u32[]{:S(2)}) collective-permute-start(bf16[102,3,384]{2,1,0:T(4,128)(2,1)S(1)} %get-tuple-element.16), channel_id=1, source_target_pairs={{1,0},{2,1},{3,2},{4,3},{5,4},{6,5},{7,6},{8,7},{9,8},{10,9},{11,1... | collective-permute-start | bytes 705032 | tf_op jit(solution)/shard_map/ppermute | solution.py:26
  17.9 13.2 %collective-permute-start.2 = (bf16[102,3,384]{2,1,0:T(4,128)(2,1)S(1)}, bf16[102,3,384]{2,1,0:T(4,128)(2,1)S(1)}, u32[]{:S(2)}, u32[]{:S(2)}) collective-permute-start(bf16[102,3,384]{2,1,0:T(4,128)(2,1)S(1)} %get-tuple-element.17), channel_id=1, source_target_pairs={{0,1},{1,2},{2,3},{3,4},{4,5},{5,6},{6,7},{7,8},{8,9},{9,10},{10,1... | collective-permute-start | bytes 705032 | tf_op jit(solution)/shard_map/ppermute | solution.py:25
  24.8 6.2 %copy-start.2 = (bf16[102,3,384]{2,1,0:T(4,128)(2,1)}, bf16[102,3,384]{2,1,0:T(4,128)(2,1)S(1)}, u32[]{:S(2)}) copy-start(bf16[102,3,384]{2,1,0:T(4,128)(2,1)S(1)} %collective-permute-done.3.refs_4_) | copy-start | bytes 705028
  31.1 0.7 copy-start.3
  102.8 5.7 %collective-permute-start.4 = (bf16[3,32,384]{2,1,0:T(8,128)(2,1)S(1)}, bf16[3,32,384]{2,1,0:T(8,128)(2,1)S(1)}, u32[]{:S(2)}, u32[]{:S(2)}) collective-permute-start(bf16[3,32,384]{2,1,0:T(8,128)(2,1)S(1)} %bitcast.22), channel_id=1, source_target_pairs={{0,16},{16,32},{32,48},{48,64},{64,80},{80,96},{96,112},{1,17},{17... | collective-permute-start | bytes 221192 | tf_op jit(solution)/shard_map/ppermute | solution.py:22
  104.7 5.6 %collective-permute-start.5 = (bf16[3,32,384]{2,1,0:T(8,128)(2,1)S(1)}, bf16[3,32,384]{2,1,0:T(8,128)(2,1)S(1)}, u32[]{:S(2)}, u32[]{:S(2)}) collective-permute-start(bf16[3,32,384]{2,1,0:T(8,128)(2,1)S(1)} %bitcast.21), channel_id=1, source_target_pairs={{16,0},{32,16},{48,32},{64,48},{80,64},{96,80},{112,96},{17,1},{33... | collective-permute-start | bytes 221192 | tf_op jit(solution)/shard_map/ppermute | solution.py:23
  108.5 18.9 %copy-start.4 = (bf16[3,32,384]{2,1,0:T(8,128)(2,1)}, bf16[3,32,384]{2,1,0:T(8,128)(2,1)S(1)}, u32[]{:S(2)}) copy-start(bf16[3,32,384]{2,1,0:T(8,128)(2,1)S(1)} %collective-permute-done.4.refs_1_) | copy-start | bytes 221188
  110.4 17.0 %copy-start.5 = (bf16[3,32,384]{2,1,0:T(8,128)(2,1)}, bf16[3,32,384]{2,1,0:T(8,128)(2,1)S(1)}, u32[]{:S(2)}) copy-start(bf16[3,32,384]{2,1,0:T(8,128)(2,1)S(1)} %collective-permute-done.5.refs_2_) | copy-start | bytes 221188
  111.9 11.5 %collective-permute-start.7 = (bf16[102,3,384]{2,1,0:T(4,128)(2,1)S(1)}, bf16[102,3,384]{2,1,0:T(4,128)(2,1)S(1)}, u32[]{:S(2)}, u32[]{:S(2)}) collective-permute-start(bf16[102,3,384]{2,1,0:T(4,128)(2,1)S(1)} %get-tuple-element.14), channel_id=1, source_target_pairs={{1,0},{2,1},{3,2},{4,3},{5,4},{6,5},{7,6},{8,7},{9,8},{10,9},{11,1... | collective-permute-start | bytes 705032 | tf_op jit(solution)/shard_map/ppermute | solution.py:26
  113.8 13.6 %collective-permute-start.6 = (bf16[102,3,384]{2,1,0:T(4,128)(2,1)S(1)}, bf16[102,3,384]{2,1,0:T(4,128)(2,1)S(1)}, u32[]{:S(2)}, u32[]{:S(2)}) collective-permute-start(bf16[102,3,384]{2,1,0:T(4,128)(2,1)S(1)} %get-tuple-element.15), channel_id=1, source_target_pairs={{0,1},{1,2},{2,3},{3,4},{4,5},{5,6},{6,7},{7,8},{8,9},{9,10},{10,1... | collective-permute-start | bytes 705032 | tf_op jit(solution)/shard_map/ppermute | solution.py:25
  123.4 4.0 %copy-start = (bf16[102,3,384]{2,1,0:T(4,128)(2,1)}, bf16[102,3,384]{2,1,0:T(4,128)(2,1)S(1)}, u32[]{:S(2)}) copy-start(bf16[102,3,384]{2,1,0:T(4,128)(2,1)S(1)} %collective-permute-done.7.refs_4_) | copy-start | bytes 705028
  127.4 0.7 copy-start.1

commit v12 on v11

--- a/solution.py
+++ b/solution.py
@@ -66,7 +66,7 @@
                 total_ref[pl.ds(start, chunk)] = total
             return carry
 
-        lax.fori_loop(0, height // chunk, body, 0, unroll=2)
+        lax.fori_loop(0, height // chunk, body, 0, unroll=4)
 
 
 def depthwise(pieces, taps, reach, base=None, flip=False, lanes=128, chunk=8):

time: 151 us -> 150 us (level)
  no operation moved by 1% of the time
where the time goes in v12:
time: 150 us; the launch traced here: 148 us
  Pallas kernels  90.4 us (60%)
  starting transfers between devices  24 us (16%)
  waiting for transfers between devices  21.5 us (14%)
  local copies, waits for them, and re-layouts  8.19 us (5%)
  other arithmetic  3.6 us (2%)
    pallas_call x2, Pallas kernels, pixel_call(): pl.pallas_call(lambda *refs: kernel(*refs, layout=layout), grid_spec=pltp...  49.3 us
    pallas_call x2, Pallas kernels, depthwise(): pl.pallas_call(lambda *refs: depthwise_kernel(*refs, reach=reach, chunk=c...  41 us
    ppermute x2, waiting for transfers between devices, halo_pieces(): lax.ppermute(framed[:, cells.shape[1] - width:], 'col', [(i, i + 1) for i...  10.3 us
    ppermute x2, waiting for transfers between devices, halo_pieces(): lax.ppermute(framed[:, :width], 'col', [(i + 1, i) for i in range(cols -...  8.28 us
    ppermute x2, starting transfers between devices, halo_pieces(): lax.ppermute(framed[:, :width], 'col', [(i + 1, i) for i in range(cols -...  8.05 us
    ppermute x2, starting transfers between devices, halo_pieces(): lax.ppermute(framed[:, cells.shape[1] - width:], 'col', [(i, i + 1) for i...  6.02 us
    ppermute x2, starting transfers between devices, halo_pieces(): bottom = lax.ppermute(cells[:width], 'row', up)  5.56 us
    unnamed x27, local copies, waits for them, and re-layouts  4.46 us
  transfers between devices with their start and end apart: 8, of which 7 were waited for; matrix products, arithmetic and copies ran while one was open for 4% of the time, Pallas kernels for 0%

profile of v12, /device:TPU:26, one launch (start us, length us, event | category | flops | bytes accessed | tf_op | source)
XLA Modules:
  0.0 148.4 jit_solution(18282779737904622049)
XLA Ops:
  0.6 0.9 fusion.2
  1.6 1.9 %collective-permute-start.1 = (bf16[3,32,384]{2,1,0:T(8,128)(2,1)S(1)}, bf16[3,32,384]{2,1,0:T(8,128)(2,1)S(1)}, u32[]{:S(2)}, u32[]{:S(2)}) collective-permute-start(bf16[3,32,384]{2,1,0:T(8,128)(2,1)S(1)} %get-tuple-element.20), channel_id=1, source_target_pairs={{16,0},{32,16},{48,32},{64,48},{80,64},{96,80},{112,96},{17,1},{33... | collective-permute-start | bytes 221192 | tf_op jit(solution)/shard_map/ppermute | solution.py:23
  3.5 2.4 %collective-permute-start = (bf16[3,32,384]{2,1,0:T(8,128)(2,1)S(1)}, bf16[3,32,384]{2,1,0:T(8,128)(2,1)S(1)}, u32[]{:S(2)}, u32[]{:S(2)}) collective-permute-start(bf16[3,32,384]{2,1,0:T(8,128)(2,1)S(1)} %get-tuple-element.21), channel_id=1, source_target_pairs={{0,16},{16,32},{32,48},{48,64},{64,80},{80,96},{96,112},{1,17},{17... | collective-permute-start | bytes 221192 | tf_op jit(solution)/shard_map/ppermute | solution.py:22
  5.9 0.8 copy.21
  6.7 0.7 reduce_window_sum.11
  7.4 0.8 select_reduce_fusion.3
  8.2 1.0 collective-permute-done.refs_1_
  9.2 0.0 copy-start.7
  9.2 0.0 copy-start.9
  9.2 0.0 copy-start.10
  9.2 0.0 copy-start.11
  9.2 0.0 copy-start.8
  9.2 2.2 %constant_dynamic-update-slice_fusion.1 = bf16[102,32,384]{2,1,0:T(8,128)(2,1)S(1)} fusion(bf16[102,32,384]{2,1,0:T(8,128)(2,1)S(1)} %constant_dynamic-update-slice_fusion.2, bf16[96,32,384]{2,1,0:T(8,128)(2,1)} %refs_0_.1), kind=kLoop, calls=%fused_computation.7 | loop fusion | bytes 4718592
  11.4 0.0 copy-done.7
  11.4 0.0 collective-permute-done.1.refs_2_
  11.4 0.0 copy-start.6
  11.5 0.2 fusion
  11.7 6.1 %collective-permute-start.3 = (bf16[102,3,384]{2,1,0:T(4,128)(2,1)S(1)}, bf16[102,3,384]{2,1,0:T(4,128)(2,1)S(1)}, u32[]{:S(2)}, u32[]{:S(2)}) collective-permute-start(bf16[102,3,384]{2,1,0:T(4,128)(2,1)S(1)} %get-tuple-element.16), channel_id=1, source_target_pairs={{1,0},{2,1},{3,2},{4,3},{5,4},{6,5},{7,6},{8,7},{9,8},{10,9},{11,1... | collective-permute-start | bytes 705032 | tf_op jit(solution)/shard_map/ppermute | solution.py:26
  17.9 1.9 %collective-permute-start.2 = (bf16[102,3,384]{2,1,0:T(4,128)(2,1)S(1)}, bf16[102,3,384]{2,1,0:T(4,128)(2,1)S(1)}, u32[]{:S(2)}, u32[]{:S(2)}) collective-permute-start(bf16[102,3,384]{2,1,0:T(4,128)(2,1)S(1)} %get-tuple-element.17), channel_id=1, source_target_pairs={{0,1},{1,2},{2,3},{3,4},{4,5},{5,6},{6,7},{7,8},{8,9},{9,10},{10,1... | collective-permute-start | bytes 705032 | tf_op jit(solution)/shard_map/ppermute | solution.py:25
  19.8 0.5 select_reduce_fusion.1
  20.3 0.1 copy.22
  20.4 0.1 copy.23
  20.5 0.0 copy-done.9
  20.5 0.0 copy-done.10
  20.5 0.0 copy-done.11
  20.6 0.1 copy.24
  20.7 0.7 reshape.47.refs_0_
  21.3 0.0 copy-done.8
  21.3 0.7 reshape.48.refs_5_
  22.0 2.9 %collective-permute-done.3.refs_4_ = bf16[102,3,384]{2,1,0:T(4,128)(2,1)S(1)} collective-permute-done((bf16[102,3,384]{2,1,0:T(4,128)(2,1)S(1)}, bf16[102,3,384]{2,1,0:T(4,128)(2,1)S(1)}, u32[]{:S(2)}, u32[]{:S(2)}) %collective-permute-start.3) | collective-permute-done | bytes 235040 | tf_op jit(solution)/shard_map/ppermute | solution.py:26
  24.8 0.0 copy-start.2
  24.8 6.2 %collective-permute-done.2.refs_3_ = bf16[102,3,384]{2,1,0:T(4,128)(2,1)S(1)} collective-permute-done((bf16[102,3,384]{2,1,0:T(4,128)(2,1)S(1)}, bf16[102,3,384]{2,1,0:T(4,128)(2,1)S(1)}, u32[]{:S(2)}, u32[]{:S(2)}) %collective-permute-start.2) | collective-permute-done | bytes 235040 | tf_op jit(solution)/shard_map/ppermute | solution.py:25
  31.1 0.0 copy-done.6
  31.1 0.0 copy-done.2
  31.1 0.0 copy-start.3
  31.1 0.7 copy-done.3
  31.8 20.2 %shard_map.113 = bf16[96,32,384]{2,1,0:T(8,128)(2,1)} custom-call(bf16[96,32,384]{2,1,0:T(8,128)(2,1)} %refs_0_.1, bf16[3,32,384]{2,1,0:T(8,128)(2,1)} %copy-done.7, bf16[3,32,384]{2,1,0:T(8,128)(2,1)} %copy-done.6, bf16[102,3,384]{2,1,0:T(4,128)(2,1)} %copy-done.3, bf16[102,3,384]{2,1,0:T(4,128)(2,1)} %copy-done.2, f32[49,384]{1,0:T(8,128)} %reshape.48.refs_5_), custom_call_target="tpu_custom_call" | custom-call | tf_op jit(solution)/shard_map/pallas_call | solution.py:88
  52.0 22.7 %shard_map.114 = (bf16[3072,384]{1,0:T(8,128)(2,1)}, bf16[768,768]{1,0:T(8,128)(2,1)}) custom-call(s32[48]{0:T(128)} %reshape.47.refs_0_, bf16[3072,384]{1,0:T(8,128)(2,1)} %bitcast.13, bf16[3072,384]{1,0:T(8,128)(2,1)} %bitcast.12, bf16[384,1536]{1,0:T(8,128)(2,1)} %refs_4_.3, bf16[1536,384]{1,0:T(8,128)(2,1)} %refs_5_.1, bf16[4,384,768]{2,1,0:T(8,128)(2,1)} %bitcast.17), custom_call_target="tpu_custom_call" | custom-call | tf_op jit(solution)/shard_map/pallas_call | solution.py:235
  74.7 26.6 %shard_map.115 = (bf16[3072,384]{1,0:T(8,128)(2,1)}, bf16[3072,384]{1,0:T(8,128)(2,1)}) custom-call(s32[48]{0:T(128)} %reshape.47.refs_0_, bf16[3072,384]{1,0:T(8,128)(2,1)} %bitcast.14, bf16[3072,384]{1,0:T(8,128)(2,1)} %get-tuple-element.7.refs_2_, bf16[768,768]{1,0:T(8,128)(2,1)} %bitcast.20, bf16[384,1536]{1,0:T(8,128)(2,1)} %refs_4_.3, ...), custom_call_target="tpu_custom_call" | custom-call | tf_op jit(solution)/shard_map/pallas_call | solution.py:235
  101.3 0.9 fusion.1
  102.3 1.9 %collective-permute-start.4 = (bf16[3,32,384]{2,1,0:T(8,128)(2,1)S(1)}, bf16[3,32,384]{2,1,0:T(8,128)(2,1)S(1)}, u32[]{:S(2)}, u32[]{:S(2)}) collective-permute-start(bf16[3,32,384]{2,1,0:T(8,128)(2,1)S(1)} %bitcast.22), channel_id=1, source_target_pairs={{0,16},{16,32},{32,48},{48,64},{64,80},{80,96},{96,112},{1,17},{17... | collective-permute-start | bytes 221192 | tf_op jit(solution)/shard_map/ppermute | solution.py:22
  104.2 3.6 %collective-permute-start.5 = (bf16[3,32,384]{2,1,0:T(8,128)(2,1)S(1)}, bf16[3,32,384]{2,1,0:T(8,128)(2,1)S(1)}, u32[]{:S(2)}, u32[]{:S(2)}) collective-permute-start(bf16[3,32,384]{2,1,0:T(8,128)(2,1)S(1)} %bitcast.21), channel_id=1, source_target_pairs={{16,0},{32,16},{48,32},{64,48},{80,64},{96,80},{112,96},{17,1},{33... | collective-permute-start | bytes 221192 | tf_op jit(solution)/shard_map/ppermute | solution.py:23
  107.8 0.1 collective-permute-done.4.refs_1_
  107.9 0.0 copy-start.4
  107.9 1.9 %collective-permute-done.5.refs_2_ = bf16[3,32,384]{2,1,0:T(8,128)(2,1)S(1)} collective-permute-done((bf16[3,32,384]{2,1,0:T(8,128)(2,1)S(1)}, bf16[3,32,384]{2,1,0:T(8,128)(2,1)S(1)}, u32[]{:S(2)}, u32[]{:S(2)}) %collective-permute-start.5) | collective-permute-done | bytes 73760 | tf_op jit(solution)/shard_map/ppermute | solution.py:23
  109.8 0.0 copy-start.5
  109.8 1.5 %pad_maximum_fusion = (bf16[102,3,384]{2,1,0:T(4,128)(2,1)S(1)}, bf16[102,3,384]{2,1,0:T(4,128)(2,1)S(1)}) fusion(bf16[3,32,384]{2,1,0:T(8,128)(2,1)S(1)} %collective-permute-done.5.refs_2_, bf16[96,32,384]{2,1,0:T(8,128)(2,1)} %bitcast.15, bf16[3,32,384]{2,1,0:T(8,128)(2,1)S(1)} %collective-permute-done.4.refs_1_), kind=kLoop, calls=%fused_computation | loop fusion | flops 1410048 | bytes 2976768 | tf_op jit(solution)/shard_map/concatenate | solution.py:24
  111.3 1.9 %collective-permute-start.7 = (bf16[102,3,384]{2,1,0:T(4,128)(2,1)S(1)}, bf16[102,3,384]{2,1,0:T(4,128)(2,1)S(1)}, u32[]{:S(2)}, u32[]{:S(2)}) collective-permute-start(bf16[102,3,384]{2,1,0:T(4,128)(2,1)S(1)} %get-tuple-element.14), channel_id=1, source_target_pairs={{1,0},{2,1},{3,2},{4,3},{5,4},{6,5},{7,6},{8,7},{9,8},{10,9},{11,1... | collective-permute-start | bytes 705032 | tf_op jit(solution)/shard_map/ppermute | solution.py:26
  113.3 4.1 %collective-permute-start.6 = (bf16[102,3,384]{2,1,0:T(4,128)(2,1)S(1)}, bf16[102,3,384]{2,1,0:T(4,128)(2,1)S(1)}, u32[]{:S(2)}, u32[]{:S(2)}) collective-permute-start(bf16[102,3,384]{2,1,0:T(4,128)(2,1)S(1)} %get-tuple-element.15), channel_id=1, source_target_pairs={{0,1},{1,2},{2,3},{3,4},{4,5},{5,6},{6,7},{7,8},{8,9},{9,10},{10,1... | collective-permute-start | bytes 705032 | tf_op jit(solution)/shard_map/ppermute | solution.py:25
  117.4 5.4 %collective-permute-done.7.refs_4_ = bf16[102,3,384]{2,1,0:T(4,128)(2,1)S(1)} collective-permute-done((bf16[102,3,384]{2,1,0:T(4,128)(2,1)S(1)}, bf16[102,3,384]{2,1,0:T(4,128)(2,1)S(1)}, u32[]{:S(2)}, u32[]{:S(2)}) %collective-permute-start.7) | collective-permute-done | bytes 235040 | tf_op jit(solution)/shard_map/ppermute | solution.py:26
  122.8 0.0 copy-start
  122.8 4.0 %collective-permute-done.6.refs_3_ = bf16[102,3,384]{2,1,0:T(4,128)(2,1)S(1)} collective-permute-done((bf16[102,3,384]{2,1,0:T(4,128)(2,1)S(1)}, bf16[102,3,384]{2,1,0:T(4,128)(2,1)S(1)}, u32[]{:S(2)}, u32[]{:S(2)}) %collective-permute-start.6) | collective-permute-done | bytes 235040 | tf_op jit(solution)/shard_map/ppermute | solution.py:25
  126.8 0.0 copy-start.1
  126.8 0.0 copy-done.4
  126.8 0.0 copy-done.5
  126.8 0.0 copy-done
  126.8 0.7 copy-done.1
  127.6 20.8 %shard_map.116 = bf16[96,32,384]{2,1,0:T(8,128)(2,1)} custom-call(bf16[96,32,384]{2,1,0:T(8,128)(2,1)} %bitcast.16, bf16[3,32,384]{2,1,0:T(8,128)(2,1)} %copy-done.4, bf16[3,32,384]{2,1,0:T(8,128)(2,1)} %copy-done.5, bf16[102,3,384]{2,1,0:T(4,128)(2,1)} %copy-done.1, bf16[102,3,384]{2,1,0:T(4,128)(2,1)} %copy-done, f32[49,384]{1,0:T(8,128)} %reshape.48.refs_5_, ...), custom_call_target="tpu_custom_call" | custom-call | tf_op jit(solution)/shard_map/pallas_call | solution.py:88
  (4 shorter events, 0.0 us)
Async XLA Ops:
  1.6 9.9 %collective-permute-start.1 = (bf16[3,32,384]{2,1,0:T(8,128)(2,1)S(1)}, bf16[3,32,384]{2,1,0:T(8,128)(2,1)S(1)}, u32[]{:S(2)}, u32[]{:S(2)}) collective-permute-start(bf16[3,32,384]{2,1,0:T(8,128)(2,1)S(1)} %get-tuple-element.20), channel_id=1, source_target_pairs={{16,0},{32,16},{48,32},{64,48},{80,64},{96,80},{112,96},{17,1},{33... | collective-permute-start | bytes 221192 | tf_op jit(solution)/shard_map/ppermute | solution.py:23
  3.5 5.7 %collective-permute-start = (bf16[3,32,384]{2,1,0:T(8,128)(2,1)S(1)}, bf16[3,32,384]{2,1,0:T(8,128)(2,1)S(1)}, u32[]{:S(2)}, u32[]{:S(2)}) collective-permute-start(bf16[3,32,384]{2,1,0:T(8,128)(2,1)S(1)} %get-tuple-element.21), channel_id=1, source_target_pairs={{0,16},{16,32},{32,48},{48,64},{64,80},{80,96},{96,112},{1,17},{17... | collective-permute-start | bytes 221192 | tf_op jit(solution)/shard_map/ppermute | solution.py:22
  9.2 2.3 %copy-start.7 = (bf16[3,32,384]{2,1,0:T(8,128)(2,1)}, bf16[3,32,384]{2,1,0:T(8,128)(2,1)S(1)}, u32[]{:S(2)}) copy-start(bf16[3,32,384]{2,1,0:T(8,128)(2,1)S(1)} %collective-permute-done.refs_1_) | copy-start | bytes 221188
  9.2 11.3 %copy-start.9 = (s32[12,4]{0,1:T(4,128)S(1)}, s32[12,4]{0,1:T(4,128)}, u32[]{:S(2)}) copy-start(s32[12,4]{0,1:T(4,128)} %param.17) | copy-start | bytes 580
  9.2 11.3 %copy-start.10 = (s32[12,4]{0,1:T(4,128)S(1)}, s32[12,4]{0,1:T(4,128)}, u32[]{:S(2)}) copy-start(s32[12,4]{0,1:T(4,128)} %param.15) | copy-start | bytes 580
  9.2 11.3 %copy-start.11 = (s32[12,4]{0,1:T(4,128)S(1)}, s32[12,4]{0,1:T(4,128)}, u32[]{:S(2)}) copy-start(s32[12,4]{0,1:T(4,128)} %param.18) | copy-start | bytes 580
  9.2 12.1 %copy-start.8 = (bf16[7,7,384]{2,1,0:T(8,128)(2,1)S(1)}, bf16[7,7,384]{2,1,0:T(8,128)(2,1)}, u32[]{:S(2)}) copy-start(bf16[7,7,384]{2,1,0:T(8,128)(2,1)} %param.11) | copy-start | bytes 112900
  11.4 19.6 %copy-start.6 = (bf16[3,32,384]{2,1,0:T(8,128)(2,1)}, bf16[3,32,384]{2,1,0:T(8,128)(2,1)S(1)}, u32[]{:S(2)}) copy-start(bf16[3,32,384]{2,1,0:T(8,128)(2,1)S(1)} %collective-permute-done.1.refs_2_) | copy-start | bytes 221188
  11.7 13.1 %collective-permute-start.3 = (bf16[102,3,384]{2,1,0:T(4,128)(2,1)S(1)}, bf16[102,3,384]{2,1,0:T(4,128)(2,1)S(1)}, u32[]{:S(2)}, u32[]{:S(2)}) collective-permute-start(bf16[102,3,384]{2,1,0:T(4,128)(2,1)S(1)} %get-tuple-element.16), channel_id=1, source_target_pairs={{1,0},{2,1},{3,2},{4,3},{5,4},{6,5},{7,6},{8,7},{9,8},{10,9},{11,1... | collective-permute-start | bytes 705032 | tf_op jit(solution)/shard_map/ppermute | solution.py:26
  17.9 13.2 %collective-permute-start.2 = (bf16[102,3,384]{2,1,0:T(4,128)(2,1)S(1)}, bf16[102,3,384]{2,1,0:T(4,128)(2,1)S(1)}, u32[]{:S(2)}, u32[]{:S(2)}) collective-permute-start(bf16[102,3,384]{2,1,0:T(4,128)(2,1)S(1)} %get-tuple-element.17), channel_id=1, source_target_pairs={{0,1},{1,2},{2,3},{3,4},{4,5},{5,6},{6,7},{7,8},{8,9},{9,10},{10,1... | collective-permute-start | bytes 705032 | tf_op jit(solution)/shard_map/ppermute | solution.py:25
  24.8 6.2 %copy-start.2 = (bf16[102,3,384]{2,1,0:T(4,128)(2,1)}, bf16[102,3,384]{2,1,0:T(4,128)(2,1)S(1)}, u32[]{:S(2)}) copy-start(bf16[102,3,384]{2,1,0:T(4,128)(2,1)S(1)} %collective-permute-done.3.refs_4_) | copy-start | bytes 705028
  31.1 0.7 copy-start.3
  102.3 5.7 %collective-permute-start.4 = (bf16[3,32,384]{2,1,0:T(8,128)(2,1)S(1)}, bf16[3,32,384]{2,1,0:T(8,128)(2,1)S(1)}, u32[]{:S(2)}, u32[]{:S(2)}) collective-permute-start(bf16[3,32,384]{2,1,0:T(8,128)(2,1)S(1)} %bitcast.22), channel_id=1, source_target_pairs={{0,16},{16,32},{32,48},{48,64},{64,80},{80,96},{96,112},{1,17},{17... | collective-permute-start | bytes 221192 | tf_op jit(solution)/shard_map/ppermute | solution.py:22
  104.2 5.6 %collective-permute-start.5 = (bf16[3,32,384]{2,1,0:T(8,128)(2,1)S(1)}, bf16[3,32,384]{2,1,0:T(8,128)(2,1)S(1)}, u32[]{:S(2)}, u32[]{:S(2)}) collective-permute-start(bf16[3,32,384]{2,1,0:T(8,128)(2,1)S(1)} %bitcast.21), channel_id=1, source_target_pairs={{16,0},{32,16},{48,32},{64,48},{80,64},{96,80},{112,96},{17,1},{33... | collective-permute-start | bytes 221192 | tf_op jit(solution)/shard_map/ppermute | solution.py:23
  107.9 18.9 %copy-start.4 = (bf16[3,32,384]{2,1,0:T(8,128)(2,1)}, bf16[3,32,384]{2,1,0:T(8,128)(2,1)S(1)}, u32[]{:S(2)}) copy-start(bf16[3,32,384]{2,1,0:T(8,128)(2,1)S(1)} %collective-permute-done.4.refs_1_) | copy-start | bytes 221188
  109.8 17.0 %copy-start.5 = (bf16[3,32,384]{2,1,0:T(8,128)(2,1)}, bf16[3,32,384]{2,1,0:T(8,128)(2,1)S(1)}, u32[]{:S(2)}) copy-start(bf16[3,32,384]{2,1,0:T(8,128)(2,1)S(1)} %collective-permute-done.5.refs_2_) | copy-start | bytes 221188
  111.3 11.5 %collective-permute-start.7 = (bf16[102,3,384]{2,1,0:T(4,128)(2,1)S(1)}, bf16[102,3,384]{2,1,0:T(4,128)(2,1)S(1)}, u32[]{:S(2)}, u32[]{:S(2)}) collective-permute-start(bf16[102,3,384]{2,1,0:T(4,128)(2,1)S(1)} %get-tuple-element.14), channel_id=1, source_target_pairs={{1,0},{2,1},{3,2},{4,3},{5,4},{6,5},{7,6},{8,7},{9,8},{10,9},{11,1... | collective-permute-start | bytes 705032 | tf_op jit(solution)/shard_map/ppermute | solution.py:26
  113.3 13.6 %collective-permute-start.6 = (bf16[102,3,384]{2,1,0:T(4,128)(2,1)S(1)}, bf16[102,3,384]{2,1,0:T(4,128)(2,1)S(1)}, u32[]{:S(2)}, u32[]{:S(2)}) collective-permute-start(bf16[102,3,384]{2,1,0:T(4,128)(2,1)S(1)} %get-tuple-element.15), channel_id=1, source_target_pairs={{0,1},{1,2},{2,3},{3,4},{4,5},{5,6},{6,7},{7,8},{8,9},{9,10},{10,1... | collective-permute-start | bytes 705032 | tf_op jit(solution)/shard_map/ppermute | solution.py:25
  122.8 4.0 %copy-start = (bf16[102,3,384]{2,1,0:T(4,128)(2,1)}, bf16[102,3,384]{2,1,0:T(4,128)(2,1)S(1)}, u32[]{:S(2)}) copy-start(bf16[102,3,384]{2,1,0:T(4,128)(2,1)S(1)} %collective-permute-done.7.refs_4_) | copy-start | bytes 705028
  126.8 0.7 copy-start.1

commit v13 on v12

--- a/solution.py
+++ b/solution.py
@@ -66,7 +66,7 @@
                 total_ref[pl.ds(start, chunk)] = total
             return carry
 
-        lax.fori_loop(0, height // chunk, body, 0, unroll=4)
+        lax.fori_loop(0, height // chunk, body, 0, unroll=True)
 
 
 def depthwise(pieces, taps, reach, base=None, flip=False, lanes=128, chunk=8):

time: 150 us -> 152 us (1.013)
  Pallas kernels: 90.4 us -> 93.1 us
    pallas_call x2, Pallas kernels: 41 us -> 43.5 us  [depthwise(): pl.pallas_call(lambda *refs: depthwise_kernel(*refs, reach=reach, chunk=c...]
where the time goes in v13:
time: 152 us; the launch traced here: 151 us
  Pallas kernels  93.1 us (61%)
  starting transfers between devices  23.8 us (16%)
  waiting for transfers between devices  21.7 us (14%)
  local copies, waits for them, and re-layouts  8.19 us (5%)
  other arithmetic  3.6 us (2%)
    pallas_call x2, Pallas kernels, pixel_call(): pl.pallas_call(lambda *refs: kernel(*refs, layout=layout), grid_spec=pltp...  49.6 us
    pallas_call x2, Pallas kernels, depthwise(): pl.pallas_call(lambda *refs: depthwise_kernel(*refs, reach=reach, chunk=c...  43.5 us
    ppermute x2, waiting for transfers between devices, halo_pieces(): lax.ppermute(framed[:, cells.shape[1] - width:], 'col', [(i, i + 1) for i...  10.3 us
    ppermute x2, waiting for transfers between devices, halo_pieces(): lax.ppermute(framed[:, :width], 'col', [(i + 1, i) for i in range(cols -...  8.52 us
    ppermute x2, starting transfers between devices, halo_pieces(): lax.ppermute(framed[:, :width], 'col', [(i + 1, i) for i in range(cols -...  8.05 us
    ppermute x2, starting transfers between devices, halo_pieces(): lax.ppermute(framed[:, cells.shape[1] - width:], 'col', [(i, i + 1) for i...  5.84 us
    ppermute x2, starting transfers between devices, halo_pieces(): bottom = lax.ppermute(cells[:width], 'row', up)  5.56 us
    unnamed x27, local copies, waits for them, and re-layouts  4.46 us
  transfers between devices with their start and end apart: 8, of which 7 were waited for; matrix products, arithmetic and copies ran while one was open for 4% of the time, Pallas kernels for 0%

profile of v13, /device:TPU:26, one launch (start us, length us, event | category | flops | bytes accessed | tf_op | source)
XLA Modules:
  0.0 151.2 jit_solution(3112826759450897093)
XLA Ops:
  0.6 0.9 fusion.2
  1.6 1.9 %collective-permute-start.1 = (bf16[3,32,384]{2,1,0:T(8,128)(2,1)S(1)}, bf16[3,32,384]{2,1,0:T(8,128)(2,1)S(1)}, u32[]{:S(2)}, u32[]{:S(2)}) collective-permute-start(bf16[3,32,384]{2,1,0:T(8,128)(2,1)S(1)} %get-tuple-element.20), channel_id=1, source_target_pairs={{16,0},{32,16},{48,32},{64,48},{80,64},{96,80},{112,96},{17,1},{33... | collective-permute-start | bytes 221192 | tf_op jit(solution)/shard_map/ppermute | solution.py:23
  3.5 2.4 %collective-permute-start = (bf16[3,32,384]{2,1,0:T(8,128)(2,1)S(1)}, bf16[3,32,384]{2,1,0:T(8,128)(2,1)S(1)}, u32[]{:S(2)}, u32[]{:S(2)}) collective-permute-start(bf16[3,32,384]{2,1,0:T(8,128)(2,1)S(1)} %get-tuple-element.21), channel_id=1, source_target_pairs={{0,16},{16,32},{32,48},{48,64},{64,80},{80,96},{96,112},{1,17},{17... | collective-permute-start | bytes 221192 | tf_op jit(solution)/shard_map/ppermute | solution.py:22
  5.9 0.8 copy.21
  6.7 0.7 reduce_window_sum.11
  7.4 0.8 select_reduce_fusion.3
  8.2 1.0 collective-permute-done.refs_1_
  9.2 0.0 copy-start.7
  9.2 0.0 copy-start.9
  9.2 0.0 copy-start.10
  9.2 0.0 copy-start.11
  9.2 0.0 copy-start.8
  9.2 2.2 %constant_dynamic-update-slice_fusion.1 = bf16[102,32,384]{2,1,0:T(8,128)(2,1)S(1)} fusion(bf16[102,32,384]{2,1,0:T(8,128)(2,1)S(1)} %constant_dynamic-update-slice_fusion.2, bf16[96,32,384]{2,1,0:T(8,128)(2,1)} %refs_0_.1), kind=kLoop, calls=%fused_computation.7 | loop fusion | bytes 4718592
  11.4 0.0 copy-done.7
  11.4 0.0 collective-permute-done.1.refs_2_
  11.4 0.0 copy-start.6
  11.5 0.2 fusion
  11.7 6.1 %collective-permute-start.3 = (bf16[102,3,384]{2,1,0:T(4,128)(2,1)S(1)}, bf16[102,3,384]{2,1,0:T(4,128)(2,1)S(1)}, u32[]{:S(2)}, u32[]{:S(2)}) collective-permute-start(bf16[102,3,384]{2,1,0:T(4,128)(2,1)S(1)} %get-tuple-element.16), channel_id=1, source_target_pairs={{1,0},{2,1},{3,2},{4,3},{5,4},{6,5},{7,6},{8,7},{9,8},{10,9},{11,1... | collective-permute-start | bytes 705032 | tf_op jit(solution)/shard_map/ppermute | solution.py:26
  17.9 1.9 %collective-permute-start.2 = (bf16[102,3,384]{2,1,0:T(4,128)(2,1)S(1)}, bf16[102,3,384]{2,1,0:T(4,128)(2,1)S(1)}, u32[]{:S(2)}, u32[]{:S(2)}) collective-permute-start(bf16[102,3,384]{2,1,0:T(4,128)(2,1)S(1)} %get-tuple-element.17), channel_id=1, source_target_pairs={{0,1},{1,2},{2,3},{3,4},{4,5},{5,6},{6,7},{7,8},{8,9},{9,10},{10,1... | collective-permute-start | bytes 705032 | tf_op jit(solution)/shard_map/ppermute | solution.py:25
  19.8 0.5 select_reduce_fusion.1
  20.3 0.1 copy.22
  20.4 0.1 copy.23
  20.5 0.0 copy-done.9
  20.5 0.0 copy-done.10
  20.5 0.0 copy-done.11
  20.6 0.1 copy.24
  20.7 0.7 reshape.47.refs_0_
  21.3 0.0 copy-done.8
  21.3 0.7 reshape.48.refs_5_
  22.0 2.9 %collective-permute-done.3.refs_4_ = bf16[102,3,384]{2,1,0:T(4,128)(2,1)S(1)} collective-permute-done((bf16[102,3,384]{2,1,0:T(4,128)(2,1)S(1)}, bf16[102,3,384]{2,1,0:T(4,128)(2,1)S(1)}, u32[]{:S(2)}, u32[]{:S(2)}) %collective-permute-start.3) | collective-permute-done | bytes 235040 | tf_op jit(solution)/shard_map/ppermute | solution.py:26
  24.8 0.0 copy-start.2
  24.8 6.2 %collective-permute-done.2.refs_3_ = bf16[102,3,384]{2,1,0:T(4,128)(2,1)S(1)} collective-permute-done((bf16[102,3,384]{2,1,0:T(4,128)(2,1)S(1)}, bf16[102,3,384]{2,1,0:T(4,128)(2,1)S(1)}, u32[]{:S(2)}, u32[]{:S(2)}) %collective-permute-start.2) | collective-permute-done | bytes 235040 | tf_op jit(solution)/shard_map/ppermute | solution.py:25
  31.1 0.0 copy-done.6
  31.1 0.0 copy-done.2
  31.1 0.0 copy-start.3
  31.1 0.7 copy-done.3
  31.8 21.4 %shard_map.113 = bf16[96,32,384]{2,1,0:T(8,128)(2,1)} custom-call(bf16[96,32,384]{2,1,0:T(8,128)(2,1)} %refs_0_.1, bf16[3,32,384]{2,1,0:T(8,128)(2,1)} %copy-done.7, bf16[3,32,384]{2,1,0:T(8,128)(2,1)} %copy-done.6, bf16[102,3,384]{2,1,0:T(4,128)(2,1)} %copy-done.3, bf16[102,3,384]{2,1,0:T(4,128)(2,1)} %copy-done.2, f32[49,384]{1,0:T(8,128)} %reshape.48.refs_5_), custom_call_target="tpu_custom_call" | custom-call | tf_op jit(solution)/shard_map/pallas_call | solution.py:88
  53.2 22.7 %shard_map.114 = (bf16[3072,384]{1,0:T(8,128)(2,1)}, bf16[768,768]{1,0:T(8,128)(2,1)}) custom-call(s32[48]{0:T(128)} %reshape.47.refs_0_, bf16[3072,384]{1,0:T(8,128)(2,1)} %bitcast.13, bf16[3072,384]{1,0:T(8,128)(2,1)} %bitcast.12, bf16[384,1536]{1,0:T(8,128)(2,1)} %refs_4_.3, bf16[1536,384]{1,0:T(8,128)(2,1)} %refs_5_.1, bf16[4,384,768]{2,1,0:T(8,128)(2,1)} %bitcast.17), custom_call_target="tpu_custom_call" | custom-call | tf_op jit(solution)/shard_map/pallas_call | solution.py:235
  75.9 26.9 %shard_map.115 = (bf16[3072,384]{1,0:T(8,128)(2,1)}, bf16[3072,384]{1,0:T(8,128)(2,1)}) custom-call(s32[48]{0:T(128)} %reshape.47.refs_0_, bf16[3072,384]{1,0:T(8,128)(2,1)} %bitcast.14, bf16[3072,384]{1,0:T(8,128)(2,1)} %get-tuple-element.7.refs_2_, bf16[768,768]{1,0:T(8,128)(2,1)} %bitcast.20, bf16[384,1536]{1,0:T(8,128)(2,1)} %refs_4_.3, ...), custom_call_target="tpu_custom_call" | custom-call | tf_op jit(solution)/shard_map/pallas_call | solution.py:235
  102.7 0.9 fusion.1
  103.7 1.9 %collective-permute-start.4 = (bf16[3,32,384]{2,1,0:T(8,128)(2,1)S(1)}, bf16[3,32,384]{2,1,0:T(8,128)(2,1)S(1)}, u32[]{:S(2)}, u32[]{:S(2)}) collective-permute-start(bf16[3,32,384]{2,1,0:T(8,128)(2,1)S(1)} %bitcast.22), channel_id=1, source_target_pairs={{0,16},{16,32},{32,48},{48,64},{64,80},{80,96},{96,112},{1,17},{17... | collective-permute-start | bytes 221192 | tf_op jit(solution)/shard_map/ppermute | solution.py:22
  105.6 3.6 %collective-permute-start.5 = (bf16[3,32,384]{2,1,0:T(8,128)(2,1)S(1)}, bf16[3,32,384]{2,1,0:T(8,128)(2,1)S(1)}, u32[]{:S(2)}, u32[]{:S(2)}) collective-permute-start(bf16[3,32,384]{2,1,0:T(8,128)(2,1)S(1)} %bitcast.21), channel_id=1, source_target_pairs={{16,0},{32,16},{48,32},{64,48},{80,64},{96,80},{112,96},{17,1},{33... | collective-permute-start | bytes 221192 | tf_op jit(solution)/shard_map/ppermute | solution.py:23
  109.3 0.1 collective-permute-done.4.refs_1_
  109.4 0.0 copy-start.4
  109.4 1.9 %collective-permute-done.5.refs_2_ = bf16[3,32,384]{2,1,0:T(8,128)(2,1)S(1)} collective-permute-done((bf16[3,32,384]{2,1,0:T(8,128)(2,1)S(1)}, bf16[3,32,384]{2,1,0:T(8,128)(2,1)S(1)}, u32[]{:S(2)}, u32[]{:S(2)}) %collective-permute-start.5) | collective-permute-done | bytes 73760 | tf_op jit(solution)/shard_map/ppermute | solution.py:23
  111.2 0.0 copy-start.5
  111.2 1.5 %pad_maximum_fusion = (bf16[102,3,384]{2,1,0:T(4,128)(2,1)S(1)}, bf16[102,3,384]{2,1,0:T(4,128)(2,1)S(1)}) fusion(bf16[3,32,384]{2,1,0:T(8,128)(2,1)S(1)} %collective-permute-done.5.refs_2_, bf16[96,32,384]{2,1,0:T(8,128)(2,1)} %bitcast.15, bf16[3,32,384]{2,1,0:T(8,128)(2,1)S(1)} %collective-permute-done.4.refs_1_), kind=kLoop, calls=%fused_computation | loop fusion | flops 1410048 | bytes 2976768 | tf_op jit(solution)/shard_map/concatenate | solution.py:24
  112.8 1.9 %collective-permute-start.7 = (bf16[102,3,384]{2,1,0:T(4,128)(2,1)S(1)}, bf16[102,3,384]{2,1,0:T(4,128)(2,1)S(1)}, u32[]{:S(2)}, u32[]{:S(2)}) collective-permute-start(bf16[102,3,384]{2,1,0:T(4,128)(2,1)S(1)} %get-tuple-element.14), channel_id=1, source_target_pairs={{1,0},{2,1},{3,2},{4,3},{5,4},{6,5},{7,6},{8,7},{9,8},{10,9},{11,1... | collective-permute-start | bytes 705032 | tf_op jit(solution)/shard_map/ppermute | solution.py:26
  114.7 3.9 %collective-permute-start.6 = (bf16[102,3,384]{2,1,0:T(4,128)(2,1)S(1)}, bf16[102,3,384]{2,1,0:T(4,128)(2,1)S(1)}, u32[]{:S(2)}, u32[]{:S(2)}) collective-permute-start(bf16[102,3,384]{2,1,0:T(4,128)(2,1)S(1)} %get-tuple-element.15), channel_id=1, source_target_pairs={{0,1},{1,2},{2,3},{3,4},{4,5},{5,6},{6,7},{7,8},{8,9},{9,10},{10,1... | collective-permute-start | bytes 705032 | tf_op jit(solution)/shard_map/ppermute | solution.py:25
  118.6 5.7 %collective-permute-done.7.refs_4_ = bf16[102,3,384]{2,1,0:T(4,128)(2,1)S(1)} collective-permute-done((bf16[102,3,384]{2,1,0:T(4,128)(2,1)S(1)}, bf16[102,3,384]{2,1,0:T(4,128)(2,1)S(1)}, u32[]{:S(2)}, u32[]{:S(2)}) %collective-permute-start.7) | collective-permute-done | bytes 235040 | tf_op jit(solution)/shard_map/ppermute | solution.py:26
  124.3 0.0 copy-start
  124.3 4.0 %collective-permute-done.6.refs_3_ = bf16[102,3,384]{2,1,0:T(4,128)(2,1)S(1)} collective-permute-done((bf16[102,3,384]{2,1,0:T(4,128)(2,1)S(1)}, bf16[102,3,384]{2,1,0:T(4,128)(2,1)S(1)}, u32[]{:S(2)}, u32[]{:S(2)}) %collective-permute-start.6) | collective-permute-done | bytes 235040 | tf_op jit(solution)/shard_map/ppermute | solution.py:25
  128.3 0.0 copy-start.1
  128.3 0.0 copy-done.4
  128.3 0.0 copy-done.5
  128.3 0.0 copy-done
  128.3 0.7 copy-done.1
  129.0 22.2 %shard_map.116 = bf16[96,32,384]{2,1,0:T(8,128)(2,1)} custom-call(bf16[96,32,384]{2,1,0:T(8,128)(2,1)} %bitcast.16, bf16[3,32,384]{2,1,0:T(8,128)(2,1)} %copy-done.4, bf16[3,32,384]{2,1,0:T(8,128)(2,1)} %copy-done.5, bf16[102,3,384]{2,1,0:T(4,128)(2,1)} %copy-done.1, bf16[102,3,384]{2,1,0:T(4,128)(2,1)} %copy-done, f32[49,384]{1,0:T(8,128)} %reshape.48.refs_5_, ...), custom_call_target="tpu_custom_call" | custom-call | tf_op jit(solution)/shard_map/pallas_call | solution.py:88
  (4 shorter events, 0.0 us)
Async XLA Ops:
  1.6 9.9 %collective-permute-start.1 = (bf16[3,32,384]{2,1,0:T(8,128)(2,1)S(1)}, bf16[3,32,384]{2,1,0:T(8,128)(2,1)S(1)}, u32[]{:S(2)}, u32[]{:S(2)}) collective-permute-start(bf16[3,32,384]{2,1,0:T(8,128)(2,1)S(1)} %get-tuple-element.20), channel_id=1, source_target_pairs={{16,0},{32,16},{48,32},{64,48},{80,64},{96,80},{112,96},{17,1},{33... | collective-permute-start | bytes 221192 | tf_op jit(solution)/shard_map/ppermute | solution.py:23
  3.5 5.7 %collective-permute-start = (bf16[3,32,384]{2,1,0:T(8,128)(2,1)S(1)}, bf16[3,32,384]{2,1,0:T(8,128)(2,1)S(1)}, u32[]{:S(2)}, u32[]{:S(2)}) collective-permute-start(bf16[3,32,384]{2,1,0:T(8,128)(2,1)S(1)} %get-tuple-element.21), channel_id=1, source_target_pairs={{0,16},{16,32},{32,48},{48,64},{64,80},{80,96},{96,112},{1,17},{17... | collective-permute-start | bytes 221192 | tf_op jit(solution)/shard_map/ppermute | solution.py:22
  9.2 2.3 %copy-start.7 = (bf16[3,32,384]{2,1,0:T(8,128)(2,1)}, bf16[3,32,384]{2,1,0:T(8,128)(2,1)S(1)}, u32[]{:S(2)}) copy-start(bf16[3,32,384]{2,1,0:T(8,128)(2,1)S(1)} %collective-permute-done.refs_1_) | copy-start | bytes 221188
  9.2 11.3 %copy-start.9 = (s32[12,4]{0,1:T(4,128)S(1)}, s32[12,4]{0,1:T(4,128)}, u32[]{:S(2)}) copy-start(s32[12,4]{0,1:T(4,128)} %param.17) | copy-start | bytes 580
  9.2 11.3 %copy-start.10 = (s32[12,4]{0,1:T(4,128)S(1)}, s32[12,4]{0,1:T(4,128)}, u32[]{:S(2)}) copy-start(s32[12,4]{0,1:T(4,128)} %param.15) | copy-start | bytes 580
  9.2 11.3 %copy-start.11 = (s32[12,4]{0,1:T(4,128)S(1)}, s32[12,4]{0,1:T(4,128)}, u32[]{:S(2)}) copy-start(s32[12,4]{0,1:T(4,128)} %param.18) | copy-start | bytes 580
  9.2 12.1 %copy-start.8 = (bf16[7,7,384]{2,1,0:T(8,128)(2,1)S(1)}, bf16[7,7,384]{2,1,0:T(8,128)(2,1)}, u32[]{:S(2)}) copy-start(bf16[7,7,384]{2,1,0:T(8,128)(2,1)} %param.11) | copy-start | bytes 112900
  11.4 19.6 %copy-start.6 = (bf16[3,32,384]{2,1,0:T(8,128)(2,1)}, bf16[3,32,384]{2,1,0:T(8,128)(2,1)S(1)}, u32[]{:S(2)}) copy-start(bf16[3,32,384]{2,1,0:T(8,128)(2,1)S(1)} %collective-permute-done.1.refs_2_) | copy-start | bytes 221188
  11.7 13.1 %collective-permute-start.3 = (bf16[102,3,384]{2,1,0:T(4,128)(2,1)S(1)}, bf16[102,3,384]{2,1,0:T(4,128)(2,1)S(1)}, u32[]{:S(2)}, u32[]{:S(2)}) collective-permute-start(bf16[102,3,384]{2,1,0:T(4,128)(2,1)S(1)} %get-tuple-element.16), channel_id=1, source_target_pairs={{1,0},{2,1},{3,2},{4,3},{5,4},{6,5},{7,6},{8,7},{9,8},{10,9},{11,1... | collective-permute-start | bytes 705032 | tf_op jit(solution)/shard_map/ppermute | solution.py:26
  17.9 13.2 %collective-permute-start.2 = (bf16[102,3,384]{2,1,0:T(4,128)(2,1)S(1)}, bf16[102,3,384]{2,1,0:T(4,128)(2,1)S(1)}, u32[]{:S(2)}, u32[]{:S(2)}) collective-permute-start(bf16[102,3,384]{2,1,0:T(4,128)(2,1)S(1)} %get-tuple-element.17), channel_id=1, source_target_pairs={{0,1},{1,2},{2,3},{3,4},{4,5},{5,6},{6,7},{7,8},{8,9},{9,10},{10,1... | collective-permute-start | bytes 705032 | tf_op jit(solution)/shard_map/ppermute | solution.py:25
  24.8 6.2 %copy-start.2 = (bf16[102,3,384]{2,1,0:T(4,128)(2,1)}, bf16[102,3,384]{2,1,0:T(4,128)(2,1)S(1)}, u32[]{:S(2)}) copy-start(bf16[102,3,384]{2,1,0:T(4,128)(2,1)S(1)} %collective-permute-done.3.refs_4_) | copy-start | bytes 705028
  31.1 0.7 copy-start.3
  103.7 5.7 %collective-permute-start.4 = (bf16[3,32,384]{2,1,0:T(8,128)(2,1)S(1)}, bf16[3,32,384]{2,1,0:T(8,128)(2,1)S(1)}, u32[]{:S(2)}, u32[]{:S(2)}) collective-permute-start(bf16[3,32,384]{2,1,0:T(8,128)(2,1)S(1)} %bitcast.22), channel_id=1, source_target_pairs={{0,16},{16,32},{32,48},{48,64},{64,80},{80,96},{96,112},{1,17},{17... | collective-permute-start | bytes 221192 | tf_op jit(solution)/shard_map/ppermute | solution.py:22
  105.6 5.6 %collective-permute-start.5 = (bf16[3,32,384]{2,1,0:T(8,128)(2,1)S(1)}, bf16[3,32,384]{2,1,0:T(8,128)(2,1)S(1)}, u32[]{:S(2)}, u32[]{:S(2)}) collective-permute-start(bf16[3,32,384]{2,1,0:T(8,128)(2,1)S(1)} %bitcast.21), channel_id=1, source_target_pairs={{16,0},{32,16},{48,32},{64,48},{80,64},{96,80},{112,96},{17,1},{33... | collective-permute-start | bytes 221192 | tf_op jit(solution)/shard_map/ppermute | solution.py:23
  109.4 19.0 %copy-start.4 = (bf16[3,32,384]{2,1,0:T(8,128)(2,1)}, bf16[3,32,384]{2,1,0:T(8,128)(2,1)S(1)}, u32[]{:S(2)}) copy-start(bf16[3,32,384]{2,1,0:T(8,128)(2,1)S(1)} %collective-permute-done.4.refs_1_) | copy-start | bytes 221188
  111.2 17.1 %copy-start.5 = (bf16[3,32,384]{2,1,0:T(8,128)(2,1)}, bf16[3,32,384]{2,1,0:T(8,128)(2,1)S(1)}, u32[]{:S(2)}) copy-start(bf16[3,32,384]{2,1,0:T(8,128)(2,1)S(1)} %collective-permute-done.5.refs_2_) | copy-start | bytes 221188
  112.8 11.5 %collective-permute-start.7 = (bf16[102,3,384]{2,1,0:T(4,128)(2,1)S(1)}, bf16[102,3,384]{2,1,0:T(4,128)(2,1)S(1)}, u32[]{:S(2)}, u32[]{:S(2)}) collective-permute-start(bf16[102,3,384]{2,1,0:T(4,128)(2,1)S(1)} %get-tuple-element.14), channel_id=1, source_target_pairs={{1,0},{2,1},{3,2},{4,3},{5,4},{6,5},{7,6},{8,7},{9,8},{10,9},{11,1... | collective-permute-start | bytes 705032 | tf_op jit(solution)/shard_map/ppermute | solution.py:26
  114.7 13.6 %collective-permute-start.6 = (bf16[102,3,384]{2,1,0:T(4,128)(2,1)S(1)}, bf16[102,3,384]{2,1,0:T(4,128)(2,1)S(1)}, u32[]{:S(2)}, u32[]{:S(2)}) collective-permute-start(bf16[102,3,384]{2,1,0:T(4,128)(2,1)S(1)} %get-tuple-element.15), channel_id=1, source_target_pairs={{0,1},{1,2},{2,3},{3,4},{4,5},{5,6},{6,7},{7,8},{8,9},{9,10},{10,1... | collective-permute-start | bytes 705032 | tf_op jit(solution)/shard_map/ppermute | solution.py:25
  124.3 4.0 %copy-start = (bf16[102,3,384]{2,1,0:T(4,128)(2,1)}, bf16[102,3,384]{2,1,0:T(4,128)(2,1)S(1)}, u32[]{:S(2)}) copy-start(bf16[102,3,384]{2,1,0:T(4,128)(2,1)S(1)} %collective-permute-done.7.refs_4_) | copy-start | bytes 705028
  128.3 0.7 copy-start.1

commit v14 on v12

--- a/solution.py
+++ b/solution.py
@@ -69,7 +69,7 @@
         lax.fori_loop(0, height // chunk, body, 0, unroll=4)
 
 
-def depthwise(pieces, taps, reach, base=None, flip=False, lanes=128, chunk=8):
+def depthwise(pieces, taps, reach, base=None, flip=False, lanes=128, chunk=4):
     image = pieces[0]
     height, breadth, channels = image.shape
     framed = (height + 2 * reach, breadth + 2 * reach)

time: 150 us -> 151 us (level)
  no operation moved by 1% of the time
where the time goes in v14:
time: 151 us; the launch traced here: 150 us
  Pallas kernels  91.5 us (61%)
  starting transfers between devices  23.8 us (16%)
  waiting for transfers between devices  21.8 us (14%)
  local copies, waits for them, and re-layouts  8.19 us (5%)
  other arithmetic  3.6 us (2%)
    pallas_call x2, Pallas kernels, pixel_call(): pl.pallas_call(lambda *refs: kernel(*refs, layout=layout), grid_spec=pltp...  49.4 us
    pallas_call x2, Pallas kernels, depthwise(): pl.pallas_call(lambda *refs: depthwise_kernel(*refs, reach=reach, chunk=c...  42.1 us
    ppermute x2, waiting for transfers between devices, halo_pieces(): lax.ppermute(framed[:, cells.shape[1] - width:], 'col', [(i, i + 1) for i...  10.3 us
    ppermute x2, waiting for transfers between devices, halo_pieces(): lax.ppermute(framed[:, :width], 'col', [(i + 1, i) for i in range(cols -...  8.58 us
    ppermute x2, starting transfers between devices, halo_pieces(): lax.ppermute(framed[:, :width], 'col', [(i + 1, i) for i in range(cols -...  8.05 us
    ppermute x2, starting transfers between devices, halo_pieces(): lax.ppermute(framed[:, cells.shape[1] - width:], 'col', [(i, i + 1) for i...  5.84 us
    ppermute x2, starting transfers between devices, halo_pieces(): bottom = lax.ppermute(cells[:width], 'row', up)  5.56 us
    unnamed x27, local copies, waits for them, and re-layouts  4.46 us
  transfers between devices with their start and end apart: 8, of which 7 were waited for; matrix products, arithmetic and copies ran while one was open for 4% of the time, Pallas kernels for 0%

profile of v14, /device:TPU:26, one launch (start us, length us, event | category | flops | bytes accessed | tf_op | source)
XLA Modules:
  0.0 149.6 jit_solution(19263994438428157)
XLA Ops:
  0.6 0.9 fusion.2
  1.6 1.9 %collective-permute-start.1 = (bf16[3,32,384]{2,1,0:T(8,128)(2,1)S(1)}, bf16[3,32,384]{2,1,0:T(8,128)(2,1)S(1)}, u32[]{:S(2)}, u32[]{:S(2)}) collective-permute-start(bf16[3,32,384]{2,1,0:T(8,128)(2,1)S(1)} %get-tuple-element.20), channel_id=1, source_target_pairs={{16,0},{32,16},{48,32},{64,48},{80,64},{96,80},{112,96},{17,1},{33... | collective-permute-start | bytes 221192 | tf_op jit(solution)/shard_map/ppermute | solution.py:23
  3.5 2.4 %collective-permute-start = (bf16[3,32,384]{2,1,0:T(8,128)(2,1)S(1)}, bf16[3,32,384]{2,1,0:T(8,128)(2,1)S(1)}, u32[]{:S(2)}, u32[]{:S(2)}) collective-permute-start(bf16[3,32,384]{2,1,0:T(8,128)(2,1)S(1)} %get-tuple-element.21), channel_id=1, source_target_pairs={{0,16},{16,32},{32,48},{48,64},{64,80},{80,96},{96,112},{1,17},{17... | collective-permute-start | bytes 221192 | tf_op jit(solution)/shard_map/ppermute | solution.py:22
  5.9 0.8 copy.21
  6.7 0.7 reduce_window_sum.11
  7.4 0.8 select_reduce_fusion.3
  8.2 1.0 collective-permute-done.refs_1_
  9.2 0.0 copy-start.7
  9.2 0.0 copy-start.9
  9.2 0.0 copy-start.10
  9.2 0.0 copy-start.11
  9.2 0.0 copy-start.8
  9.2 2.2 %constant_dynamic-update-slice_fusion.1 = bf16[102,32,384]{2,1,0:T(8,128)(2,1)S(1)} fusion(bf16[102,32,384]{2,1,0:T(8,128)(2,1)S(1)} %constant_dynamic-update-slice_fusion.2, bf16[96,32,384]{2,1,0:T(8,128)(2,1)} %refs_0_.1), kind=kLoop, calls=%fused_computation.7 | loop fusion | bytes 4718592
  11.4 0.0 copy-done.7
  11.4 0.0 collective-permute-done.1.refs_2_
  11.4 0.0 copy-start.6
  11.5 0.2 fusion
  11.7 6.1 %collective-permute-start.3 = (bf16[102,3,384]{2,1,0:T(4,128)(2,1)S(1)}, bf16[102,3,384]{2,1,0:T(4,128)(2,1)S(1)}, u32[]{:S(2)}, u32[]{:S(2)}) collective-permute-start(bf16[102,3,384]{2,1,0:T(4,128)(2,1)S(1)} %get-tuple-element.16), channel_id=1, source_target_pairs={{1,0},{2,1},{3,2},{4,3},{5,4},{6,5},{7,6},{8,7},{9,8},{10,9},{11,1... | collective-permute-start | bytes 705032 | tf_op jit(solution)/shard_map/ppermute | solution.py:26
  17.9 1.9 %collective-permute-start.2 = (bf16[102,3,384]{2,1,0:T(4,128)(2,1)S(1)}, bf16[102,3,384]{2,1,0:T(4,128)(2,1)S(1)}, u32[]{:S(2)}, u32[]{:S(2)}) collective-permute-start(bf16[102,3,384]{2,1,0:T(4,128)(2,1)S(1)} %get-tuple-element.17), channel_id=1, source_target_pairs={{0,1},{1,2},{2,3},{3,4},{4,5},{5,6},{6,7},{7,8},{8,9},{9,10},{10,1... | collective-permute-start | bytes 705032 | tf_op jit(solution)/shard_map/ppermute | solution.py:25
  19.8 0.5 select_reduce_fusion.1
  20.3 0.1 copy.22
  20.4 0.1 copy.23
  20.5 0.0 copy-done.9
  20.5 0.0 copy-done.10
  20.5 0.0 copy-done.11
  20.6 0.1 copy.24
  20.7 0.7 reshape.47.refs_0_
  21.3 0.0 copy-done.8
  21.3 0.7 reshape.48.refs_5_
  22.0 2.9 %collective-permute-done.3.refs_4_ = bf16[102,3,384]{2,1,0:T(4,128)(2,1)S(1)} collective-permute-done((bf16[102,3,384]{2,1,0:T(4,128)(2,1)S(1)}, bf16[102,3,384]{2,1,0:T(4,128)(2,1)S(1)}, u32[]{:S(2)}, u32[]{:S(2)}) %collective-permute-start.3) | collective-permute-done | bytes 235040 | tf_op jit(solution)/shard_map/ppermute | solution.py:26
  24.8 0.0 copy-start.2
  24.8 6.2 %collective-permute-done.2.refs_3_ = bf16[102,3,384]{2,1,0:T(4,128)(2,1)S(1)} collective-permute-done((bf16[102,3,384]{2,1,0:T(4,128)(2,1)S(1)}, bf16[102,3,384]{2,1,0:T(4,128)(2,1)S(1)}, u32[]{:S(2)}, u32[]{:S(2)}) %collective-permute-start.2) | collective-permute-done | bytes 235040 | tf_op jit(solution)/shard_map/ppermute | solution.py:25
  31.1 0.0 copy-done.6
  31.1 0.0 copy-done.2
  31.1 0.0 copy-start.3
  31.1 0.7 copy-done.3
  31.8 20.7 %shard_map.113 = bf16[96,32,384]{2,1,0:T(8,128)(2,1)} custom-call(bf16[96,32,384]{2,1,0:T(8,128)(2,1)} %refs_0_.1, bf16[3,32,384]{2,1,0:T(8,128)(2,1)} %copy-done.7, bf16[3,32,384]{2,1,0:T(8,128)(2,1)} %copy-done.6, bf16[102,3,384]{2,1,0:T(4,128)(2,1)} %copy-done.3, bf16[102,3,384]{2,1,0:T(4,128)(2,1)} %copy-done.2, f32[49,384]{1,0:T(8,128)} %reshape.48.refs_5_), custom_call_target="tpu_custom_call" | custom-call | tf_op jit(solution)/shard_map/pallas_call | solution.py:88
  52.5 22.7 %shard_map.114 = (bf16[3072,384]{1,0:T(8,128)(2,1)}, bf16[768,768]{1,0:T(8,128)(2,1)}) custom-call(s32[48]{0:T(128)} %reshape.47.refs_0_, bf16[3072,384]{1,0:T(8,128)(2,1)} %bitcast.13, bf16[3072,384]{1,0:T(8,128)(2,1)} %bitcast.12, bf16[384,1536]{1,0:T(8,128)(2,1)} %refs_4_.3, bf16[1536,384]{1,0:T(8,128)(2,1)} %refs_5_.1, bf16[4,384,768]{2,1,0:T(8,128)(2,1)} %bitcast.17), custom_call_target="tpu_custom_call" | custom-call | tf_op jit(solution)/shard_map/pallas_call | solution.py:235
  75.2 26.7 %shard_map.115 = (bf16[3072,384]{1,0:T(8,128)(2,1)}, bf16[3072,384]{1,0:T(8,128)(2,1)}) custom-call(s32[48]{0:T(128)} %reshape.47.refs_0_, bf16[3072,384]{1,0:T(8,128)(2,1)} %bitcast.14, bf16[3072,384]{1,0:T(8,128)(2,1)} %get-tuple-element.7.refs_2_, bf16[768,768]{1,0:T(8,128)(2,1)} %bitcast.20, bf16[384,1536]{1,0:T(8,128)(2,1)} %refs_4_.3, ...), custom_call_target="tpu_custom_call" | custom-call | tf_op jit(solution)/shard_map/pallas_call | solution.py:235
  101.9 0.9 fusion.1
  102.9 1.9 %collective-permute-start.4 = (bf16[3,32,384]{2,1,0:T(8,128)(2,1)S(1)}, bf16[3,32,384]{2,1,0:T(8,128)(2,1)S(1)}, u32[]{:S(2)}, u32[]{:S(2)}) collective-permute-start(bf16[3,32,384]{2,1,0:T(8,128)(2,1)S(1)} %bitcast.22), channel_id=1, source_target_pairs={{0,16},{16,32},{32,48},{48,64},{64,80},{80,96},{96,112},{1,17},{17... | collective-permute-start | bytes 221192 | tf_op jit(solution)/shard_map/ppermute | solution.py:22
  104.8 3.6 %collective-permute-start.5 = (bf16[3,32,384]{2,1,0:T(8,128)(2,1)S(1)}, bf16[3,32,384]{2,1,0:T(8,128)(2,1)S(1)}, u32[]{:S(2)}, u32[]{:S(2)}) collective-permute-start(bf16[3,32,384]{2,1,0:T(8,128)(2,1)S(1)} %bitcast.21), channel_id=1, source_target_pairs={{16,0},{32,16},{48,32},{64,48},{80,64},{96,80},{112,96},{17,1},{33... | collective-permute-start | bytes 221192 | tf_op jit(solution)/shard_map/ppermute | solution.py:23
  108.4 0.1 collective-permute-done.4.refs_1_
  108.5 0.0 copy-start.4
  108.5 1.9 %collective-permute-done.5.refs_2_ = bf16[3,32,384]{2,1,0:T(8,128)(2,1)S(1)} collective-permute-done((bf16[3,32,384]{2,1,0:T(8,128)(2,1)S(1)}, bf16[3,32,384]{2,1,0:T(8,128)(2,1)S(1)}, u32[]{:S(2)}, u32[]{:S(2)}) %collective-permute-start.5) | collective-permute-done | bytes 73760 | tf_op jit(solution)/shard_map/ppermute | solution.py:23
  110.4 0.0 copy-start.5
  110.4 1.5 %pad_maximum_fusion = (bf16[102,3,384]{2,1,0:T(4,128)(2,1)S(1)}, bf16[102,3,384]{2,1,0:T(4,128)(2,1)S(1)}) fusion(bf16[3,32,384]{2,1,0:T(8,128)(2,1)S(1)} %collective-permute-done.5.refs_2_, bf16[96,32,384]{2,1,0:T(8,128)(2,1)} %bitcast.15, bf16[3,32,384]{2,1,0:T(8,128)(2,1)S(1)} %collective-permute-done.4.refs_1_), kind=kLoop, calls=%fused_computation | loop fusion | flops 1410048 | bytes 2976768 | tf_op jit(solution)/shard_map/concatenate | solution.py:24
  111.9 1.9 %collective-permute-start.7 = (bf16[102,3,384]{2,1,0:T(4,128)(2,1)S(1)}, bf16[102,3,384]{2,1,0:T(4,128)(2,1)S(1)}, u32[]{:S(2)}, u32[]{:S(2)}) collective-permute-start(bf16[102,3,384]{2,1,0:T(4,128)(2,1)S(1)} %get-tuple-element.14), channel_id=1, source_target_pairs={{1,0},{2,1},{3,2},{4,3},{5,4},{6,5},{7,6},{8,7},{9,8},{10,9},{11,1... | collective-permute-start | bytes 705032 | tf_op jit(solution)/shard_map/ppermute | solution.py:26
  113.9 3.9 %collective-permute-start.6 = (bf16[102,3,384]{2,1,0:T(4,128)(2,1)S(1)}, bf16[102,3,384]{2,1,0:T(4,128)(2,1)S(1)}, u32[]{:S(2)}, u32[]{:S(2)}) collective-permute-start(bf16[102,3,384]{2,1,0:T(4,128)(2,1)S(1)} %get-tuple-element.15), channel_id=1, source_target_pairs={{0,1},{1,2},{2,3},{3,4},{4,5},{5,6},{6,7},{7,8},{8,9},{9,10},{10,1... | collective-permute-start | bytes 705032 | tf_op jit(solution)/shard_map/ppermute | solution.py:25
  117.8 5.7 %collective-permute-done.7.refs_4_ = bf16[102,3,384]{2,1,0:T(4,128)(2,1)S(1)} collective-permute-done((bf16[102,3,384]{2,1,0:T(4,128)(2,1)S(1)}, bf16[102,3,384]{2,1,0:T(4,128)(2,1)S(1)}, u32[]{:S(2)}, u32[]{:S(2)}) %collective-permute-start.7) | collective-permute-done | bytes 235040 | tf_op jit(solution)/shard_map/ppermute | solution.py:26
  123.5 0.0 copy-start
  123.5 4.0 %collective-permute-done.6.refs_3_ = bf16[102,3,384]{2,1,0:T(4,128)(2,1)S(1)} collective-permute-done((bf16[102,3,384]{2,1,0:T(4,128)(2,1)S(1)}, bf16[102,3,384]{2,1,0:T(4,128)(2,1)S(1)}, u32[]{:S(2)}, u32[]{:S(2)}) %collective-permute-start.6) | collective-permute-done | bytes 235040 | tf_op jit(solution)/shard_map/ppermute | solution.py:25
  127.6 0.0 copy-start.1
  127.6 0.0 copy-done.4
  127.6 0.0 copy-done.5
  127.6 0.0 copy-done
  127.6 0.7 copy-done.1
  128.3 21.3 %shard_map.116 = bf16[96,32,384]{2,1,0:T(8,128)(2,1)} custom-call(bf16[96,32,384]{2,1,0:T(8,128)(2,1)} %bitcast.16, bf16[3,32,384]{2,1,0:T(8,128)(2,1)} %copy-done.4, bf16[3,32,384]{2,1,0:T(8,128)(2,1)} %copy-done.5, bf16[102,3,384]{2,1,0:T(4,128)(2,1)} %copy-done.1, bf16[102,3,384]{2,1,0:T(4,128)(2,1)} %copy-done, f32[49,384]{1,0:T(8,128)} %reshape.48.refs_5_, ...), custom_call_target="tpu_custom_call" | custom-call | tf_op jit(solution)/shard_map/pallas_call | solution.py:88
  (4 shorter events, 0.0 us)
Async XLA Ops:
  1.6 9.9 %collective-permute-start.1 = (bf16[3,32,384]{2,1,0:T(8,128)(2,1)S(1)}, bf16[3,32,384]{2,1,0:T(8,128)(2,1)S(1)}, u32[]{:S(2)}, u32[]{:S(2)}) collective-permute-start(bf16[3,32,384]{2,1,0:T(8,128)(2,1)S(1)} %get-tuple-element.20), channel_id=1, source_target_pairs={{16,0},{32,16},{48,32},{64,48},{80,64},{96,80},{112,96},{17,1},{33... | collective-permute-start | bytes 221192 | tf_op jit(solution)/shard_map/ppermute | solution.py:23
  3.5 5.7 %collective-permute-start = (bf16[3,32,384]{2,1,0:T(8,128)(2,1)S(1)}, bf16[3,32,384]{2,1,0:T(8,128)(2,1)S(1)}, u32[]{:S(2)}, u32[]{:S(2)}) collective-permute-start(bf16[3,32,384]{2,1,0:T(8,128)(2,1)S(1)} %get-tuple-element.21), channel_id=1, source_target_pairs={{0,16},{16,32},{32,48},{48,64},{64,80},{80,96},{96,112},{1,17},{17... | collective-permute-start | bytes 221192 | tf_op jit(solution)/shard_map/ppermute | solution.py:22
  9.2 2.3 %copy-start.7 = (bf16[3,32,384]{2,1,0:T(8,128)(2,1)}, bf16[3,32,384]{2,1,0:T(8,128)(2,1)S(1)}, u32[]{:S(2)}) copy-start(bf16[3,32,384]{2,1,0:T(8,128)(2,1)S(1)} %collective-permute-done.refs_1_) | copy-start | bytes 221188
  9.2 11.3 %copy-start.9 = (s32[12,4]{0,1:T(4,128)S(1)}, s32[12,4]{0,1:T(4,128)}, u32[]{:S(2)}) copy-start(s32[12,4]{0,1:T(4,128)} %param.17) | copy-start | bytes 580
  9.2 11.3 %copy-start.10 = (s32[12,4]{0,1:T(4,128)S(1)}, s32[12,4]{0,1:T(4,128)}, u32[]{:S(2)}) copy-start(s32[12,4]{0,1:T(4,128)} %param.15) | copy-start | bytes 580
  9.2 11.3 %copy-start.11 = (s32[12,4]{0,1:T(4,128)S(1)}, s32[12,4]{0,1:T(4,128)}, u32[]{:S(2)}) copy-start(s32[12,4]{0,1:T(4,128)} %param.18) | copy-start | bytes 580
  9.2 12.1 %copy-start.8 = (bf16[7,7,384]{2,1,0:T(8,128)(2,1)S(1)}, bf16[7,7,384]{2,1,0:T(8,128)(2,1)}, u32[]{:S(2)}) copy-start(bf16[7,7,384]{2,1,0:T(8,128)(2,1)} %param.11) | copy-start | bytes 112900
  11.4 19.6 %copy-start.6 = (bf16[3,32,384]{2,1,0:T(8,128)(2,1)}, bf16[3,32,384]{2,1,0:T(8,128)(2,1)S(1)}, u32[]{:S(2)}) copy-start(bf16[3,32,384]{2,1,0:T(8,128)(2,1)S(1)} %collective-permute-done.1.refs_2_) | copy-start | bytes 221188
  11.7 13.1 %collective-permute-start.3 = (bf16[102,3,384]{2,1,0:T(4,128)(2,1)S(1)}, bf16[102,3,384]{2,1,0:T(4,128)(2,1)S(1)}, u32[]{:S(2)}, u32[]{:S(2)}) collective-permute-start(bf16[102,3,384]{2,1,0:T(4,128)(2,1)S(1)} %get-tuple-element.16), channel_id=1, source_target_pairs={{1,0},{2,1},{3,2},{4,3},{5,4},{6,5},{7,6},{8,7},{9,8},{10,9},{11,1... | collective-permute-start | bytes 705032 | tf_op jit(solution)/shard_map/ppermute | solution.py:26
  17.9 13.2 %collective-permute-start.2 = (bf16[102,3,384]{2,1,0:T(4,128)(2,1)S(1)}, bf16[102,3,384]{2,1,0:T(4,128)(2,1)S(1)}, u32[]{:S(2)}, u32[]{:S(2)}) collective-permute-start(bf16[102,3,384]{2,1,0:T(4,128)(2,1)S(1)} %get-tuple-element.17), channel_id=1, source_target_pairs={{0,1},{1,2},{2,3},{3,4},{4,5},{5,6},{6,7},{7,8},{8,9},{9,10},{10,1... | collective-permute-start | bytes 705032 | tf_op jit(solution)/shard_map/ppermute | solution.py:25
  24.8 6.2 %copy-start.2 = (bf16[102,3,384]{2,1,0:T(4,128)(2,1)}, bf16[102,3,384]{2,1,0:T(4,128)(2,1)S(1)}, u32[]{:S(2)}) copy-start(bf16[102,3,384]{2,1,0:T(4,128)(2,1)S(1)} %collective-permute-done.3.refs_4_) | copy-start | bytes 705028
  31.1 0.7 copy-start.3
  102.9 5.7 %collective-permute-start.4 = (bf16[3,32,384]{2,1,0:T(8,128)(2,1)S(1)}, bf16[3,32,384]{2,1,0:T(8,128)(2,1)S(1)}, u32[]{:S(2)}, u32[]{:S(2)}) collective-permute-start(bf16[3,32,384]{2,1,0:T(8,128)(2,1)S(1)} %bitcast.22), channel_id=1, source_target_pairs={{0,16},{16,32},{32,48},{48,64},{64,80},{80,96},{96,112},{1,17},{17... | collective-permute-start | bytes 221192 | tf_op jit(solution)/shard_map/ppermute | solution.py:22
  104.8 5.6 %collective-permute-start.5 = (bf16[3,32,384]{2,1,0:T(8,128)(2,1)S(1)}, bf16[3,32,384]{2,1,0:T(8,128)(2,1)S(1)}, u32[]{:S(2)}, u32[]{:S(2)}) collective-permute-start(bf16[3,32,384]{2,1,0:T(8,128)(2,1)S(1)} %bitcast.21), channel_id=1, source_target_pairs={{16,0},{32,16},{48,32},{64,48},{80,64},{96,80},{112,96},{17,1},{33... | collective-permute-start | bytes 221192 | tf_op jit(solution)/shard_map/ppermute | solution.py:23
  108.5 19.0 %copy-start.4 = (bf16[3,32,384]{2,1,0:T(8,128)(2,1)}, bf16[3,32,384]{2,1,0:T(8,128)(2,1)S(1)}, u32[]{:S(2)}) copy-start(bf16[3,32,384]{2,1,0:T(8,128)(2,1)S(1)} %collective-permute-done.4.refs_1_) | copy-start | bytes 221188
  110.4 17.2 %copy-start.5 = (bf16[3,32,384]{2,1,0:T(8,128)(2,1)}, bf16[3,32,384]{2,1,0:T(8,128)(2,1)S(1)}, u32[]{:S(2)}) copy-start(bf16[3,32,384]{2,1,0:T(8,128)(2,1)S(1)} %collective-permute-done.5.refs_2_) | copy-start | bytes 221188
  111.9 11.6 %collective-permute-start.7 = (bf16[102,3,384]{2,1,0:T(4,128)(2,1)S(1)}, bf16[102,3,384]{2,1,0:T(4,128)(2,1)S(1)}, u32[]{:S(2)}, u32[]{:S(2)}) collective-permute-start(bf16[102,3,384]{2,1,0:T(4,128)(2,1)S(1)} %get-tuple-element.14), channel_id=1, source_target_pairs={{1,0},{2,1},{3,2},{4,3},{5,4},{6,5},{7,6},{8,7},{9,8},{10,9},{11,1... | collective-permute-start | bytes 705032 | tf_op jit(solution)/shard_map/ppermute | solution.py:26
  113.9 13.7 %collective-permute-start.6 = (bf16[102,3,384]{2,1,0:T(4,128)(2,1)S(1)}, bf16[102,3,384]{2,1,0:T(4,128)(2,1)S(1)}, u32[]{:S(2)}, u32[]{:S(2)}) collective-permute-start(bf16[102,3,384]{2,1,0:T(4,128)(2,1)S(1)} %get-tuple-element.15), channel_id=1, source_target_pairs={{0,1},{1,2},{2,3},{3,4},{4,5},{5,6},{6,7},{7,8},{8,9},{9,10},{10,1... | collective-permute-start | bytes 705032 | tf_op jit(solution)/shard_map/ppermute | solution.py:25
  123.5 4.0 %copy-start = (bf16[102,3,384]{2,1,0:T(4,128)(2,1)}, bf16[102,3,384]{2,1,0:T(4,128)(2,1)S(1)}, u32[]{:S(2)}) copy-start(bf16[102,3,384]{2,1,0:T(4,128)(2,1)S(1)} %collective-permute-done.7.refs_4_) | copy-start | bytes 705028
  127.6 0.7 copy-start.1

commit v15 on v12

--- a/solution.py
+++ b/solution.py
@@ -21,9 +21,11 @@
     up = [(i + 1, i) for i in range(rows - 1)]
     top = lax.ppermute(cells[cells.shape[0] - width :], "row", down)
     bottom = lax.ppermute(cells[:width], "row", up)
-    framed = jnp.concatenate([top, cells, bottom], axis=0)
-    left = lax.ppermute(framed[:, cells.shape[1] - width :], "col", [(i, i + 1) for i in range(cols - 1)])
-    right = lax.ppermute(framed[:, :width], "col", [(i + 1, i) for i in range(cols - 1)])
+    edge = cells.shape[1] - width
+    left_strip = jnp.concatenate([top[:, edge:], cells[:, edge:], bottom[:, edge:]], axis=0)
+    right_strip = jnp.concatenate([top[:, :width], cells[:, :width], bottom[:, :width]], axis=0)
+    left = lax.ppermute(left_strip, "col", [(i, i + 1) for i in range(cols - 1)])
+    right = lax.ppermute(right_strip, "col", [(i + 1, i) for i in range(cols - 1)])
     return (cells, top, bottom, left, right)
 
 

time: 150 us -> 144 us (0.960)
  waiting for transfers between devices: 21.5 us -> 13.3 us
  starting transfers between devices: 24 us -> 26.3 us
    ppermute x4, waiting for transfers between devices: 18.5 us -> 12.9 us  [the longest x2 8.42 us: halo_pieces(): lax.ppermute(left_strip, 'col', [(i, i + 1) for i in range(cols - 1)])]
    slice x1 -> x6, local copies, waits for them, and re-layouts: 0.25 us -> 3.01 us  [the longest x2 2.96 us: halo_pieces(): cells[:, :width]]
    ppermute x4, starting transfers between devices: 14.1 us -> 16.4 us  [the longest x2 8.82 us: halo_pieces(): lax.ppermute(right_strip, 'col', [(i + 1, i) for i in range(cols - 1)])]
    unnamed x27 -> x25, local copies, waits for them, and re-layouts: 4.46 us -> 2.25 us
  transfers between devices with their start and end apart: 8 -> 8, of which waited for: 7 -> 5; matrix products, arithmetic and copies ran while one was open for 4% -> 6% of each run, Pallas kernels for 0% -> 0%
where the time goes in v15:
time: 144 us; the launch traced here: 143 us
  Pallas kernels  90.4 us (63%)
  starting transfers between devices  26.3 us (18%)
  waiting for transfers between devices  13.3 us (9%)
  local copies, waits for them, and re-layouts  8.76 us (6%)
  other arithmetic  2.99 us (2%)
    pallas_call x2, Pallas kernels, pixel_call(): pl.pallas_call(lambda *refs: kernel(*refs, layout=layout), grid_spec=pltp...  49.4 us
    pallas_call x2, Pallas kernels, depthwise(): pl.pallas_call(lambda *refs: depthwise_kernel(*refs, reach=reach, chunk=c...  41 us
    ppermute x2, starting transfers between devices, halo_pieces(): lax.ppermute(right_strip, 'col', [(i + 1, i) for i in range(cols - 1)])  8.82 us
    ppermute x2, waiting for transfers between devices, halo_pieces(): lax.ppermute(left_strip, 'col', [(i, i + 1) for i in range(cols - 1)])  8.42 us
    ppermute x2, starting transfers between devices, halo_pieces(): lax.ppermute(left_strip, 'col', [(i, i + 1) for i in range(cols - 1)])  7.56 us
    ppermute x2, starting transfers between devices, halo_pieces(): bottom = lax.ppermute(cells[:width], 'row', up)  5.45 us
    ppermute x2, waiting for transfers between devices, halo_pieces(): lax.ppermute(right_strip, 'col', [(i + 1, i) for i in range(cols - 1)])  4.49 us
    ppermute x2, starting transfers between devices, halo_pieces(): top = lax.ppermute(cells[cells.shape[0] - width:], 'row', down)  4.44 us
  transfers between devices with their start and end apart: 8, of which 5 were waited for; matrix products, arithmetic and copies ran while one was open for 6% of the time, Pallas kernels for 0%

profile of v15, /device:TPU:26, one launch (start us, length us, event | category | flops | bytes accessed | tf_op | source)
XLA Modules:
  0.0 142.7 jit_solution(17495483376973825046)
XLA Ops:
  0.6 0.0 copy-start.9
  0.6 0.0 copy-start.11
  0.7 0.0 copy-start.10
  0.7 0.0 copy-start.8
  0.7 1.0 fusion.3
  1.6 1.9 %collective-permute-start.1 = (bf16[3,32,384]{2,1,0:T(8,128)(2,1)S(1)}, bf16[3,32,384]{2,1,0:T(8,128)(2,1)S(1)}, u32[]{:S(2)}, u32[]{:S(2)}) collective-permute-start(bf16[3,32,384]{2,1,0:T(8,128)(2,1)S(1)} %get-tuple-element.20), channel_id=1, source_target_pairs={{16,0},{32,16},{48,32},{64,48},{80,64},{96,80},{112,96},{17,1},{33... | collective-permute-start | bytes 221192 | tf_op jit(solution)/shard_map/ppermute | solution.py:23
  3.6 2.4 %collective-permute-start = (bf16[3,32,384]{2,1,0:T(8,128)(2,1)S(1)}, bf16[3,32,384]{2,1,0:T(8,128)(2,1)S(1)}, u32[]{:S(2)}, u32[]{:S(2)}) collective-permute-start(bf16[3,32,384]{2,1,0:T(8,128)(2,1)S(1)} %get-tuple-element.21), channel_id=1, source_target_pairs={{0,16},{16,32},{32,48},{48,64},{64,80},{80,96},{96,112},{1,17},{17... | collective-permute-start | bytes 221192 | tf_op jit(solution)/shard_map/ppermute | solution.py:22
  6.0 1.5 %fusion.2 = (bf16[96,3,384]{2,1,0:T(4,128)(2,1)S(1)}, bf16[96,3,384]{2,1,0:T(4,128)(2,1)S(1)}) fusion(bf16[96,32,384]{2,1,0:T(8,128)(2,1)} %refs_0_.1), kind=kLoop, calls=%fused_computation.13 | loop fusion | bytes 884736 | tf_op jit(solution)/shard_map/slice | solution.py:26
  7.5 0.8 copy.21
  8.3 0.7 reduce_window_sum.11
  9.0 0.8 select_reduce_fusion.3
  9.8 0.0 collective-permute-done.1.refs_2_
  9.8 0.0 copy-start.6
  9.8 0.0 collective-permute-done.refs_1_
  9.8 0.0 copy-start.7
  9.8 0.2 pad_maximum_fusion
  10.1 3.8 %collective-permute-start.2 = (bf16[102,3,384]{2,1,0:T(4,128)(2,1)S(1)}, bf16[102,3,384]{2,1,0:T(4,128)(2,1)S(1)}, u32[]{:S(2)}, u32[]{:S(2)}) collective-permute-start(bf16[102,3,384]{2,1,0:T(4,128)(2,1)S(1)} %pad_maximum_fusion), channel_id=1, source_target_pairs={{0,1},{1,2},{2,3},{3,4},{4,5},{5,6},{6,7},{7,8},{8,9},{9,10},{10,1... | collective-permute-start | bytes 705032 | tf_op jit(solution)/shard_map/ppermute | solution.py:27
  13.9 0.2 pad_maximum_fusion.1
  14.2 4.2 %collective-permute-start.3 = (bf16[102,3,384]{2,1,0:T(4,128)(2,1)S(1)}, bf16[102,3,384]{2,1,0:T(4,128)(2,1)S(1)}, u32[]{:S(2)}, u32[]{:S(2)}) collective-permute-start(bf16[102,3,384]{2,1,0:T(4,128)(2,1)S(1)} %pad_maximum_fusion.1), channel_id=1, source_target_pairs={{1,0},{2,1},{3,2},{4,3},{5,4},{6,5},{7,6},{8,7},{9,8},{10,9},{11,1... | collective-permute-start | bytes 705032 | tf_op jit(solution)/shard_map/ppermute | solution.py:28
  18.4 0.5 select_reduce_fusion.1
  18.9 0.1 copy.22
  19.0 0.1 copy.23
  19.1 0.0 copy-done.9
  19.1 0.0 copy-done.11
  19.1 0.0 copy-done.10
  19.1 0.1 copy.24
  19.2 0.7 reshape.47.refs_0_
  19.9 0.0 copy-done.8
  19.9 0.7 reshape.48.refs_5_
  20.6 3.5 %collective-permute-done.2.refs_3_ = bf16[102,3,384]{2,1,0:T(4,128)(2,1)S(1)} collective-permute-done((bf16[102,3,384]{2,1,0:T(4,128)(2,1)S(1)}, bf16[102,3,384]{2,1,0:T(4,128)(2,1)S(1)}, u32[]{:S(2)}, u32[]{:S(2)}) %collective-permute-start.2) | collective-permute-done | bytes 235040 | tf_op jit(solution)/shard_map/ppermute | solution.py:27
  24.0 0.0 copy-start.2
  24.0 2.2 %collective-permute-done.3.refs_4_ = bf16[102,3,384]{2,1,0:T(4,128)(2,1)S(1)} collective-permute-done((bf16[102,3,384]{2,1,0:T(4,128)(2,1)S(1)}, bf16[102,3,384]{2,1,0:T(4,128)(2,1)S(1)}, u32[]{:S(2)}, u32[]{:S(2)}) %collective-permute-start.3) | collective-permute-done | bytes 235040 | tf_op jit(solution)/shard_map/ppermute | solution.py:28
  26.3 0.0 copy-done.6
  26.3 0.0 copy-done.7
  26.3 0.0 copy-done.2
  26.3 0.0 copy-start.3
  26.3 0.7 copy-done.3
  27.0 20.2 %shard_map.113 = bf16[96,32,384]{2,1,0:T(8,128)(2,1)} custom-call(bf16[96,32,384]{2,1,0:T(8,128)(2,1)} %refs_0_.1, bf16[3,32,384]{2,1,0:T(8,128)(2,1)} %copy-done.7, bf16[3,32,384]{2,1,0:T(8,128)(2,1)} %copy-done.6, bf16[102,3,384]{2,1,0:T(4,128)(2,1)} %copy-done.2, bf16[102,3,384]{2,1,0:T(4,128)(2,1)} %copy-done.3, f32[49,384]{1,0:T(8,128)} %reshape.48.refs_5_), custom_call_target="tpu_custom_call" | custom-call | tf_op jit(solution)/shard_map/pallas_call | solution.py:90
  47.2 22.7 %shard_map.114 = (bf16[3072,384]{1,0:T(8,128)(2,1)}, bf16[768,768]{1,0:T(8,128)(2,1)}) custom-call(s32[48]{0:T(128)} %reshape.47.refs_0_, bf16[3072,384]{1,0:T(8,128)(2,1)} %bitcast.12, bf16[3072,384]{1,0:T(8,128)(2,1)} %bitcast.14, bf16[384,1536]{1,0:T(8,128)(2,1)} %refs_4_.3, bf16[1536,384]{1,0:T(8,128)(2,1)} %refs_5_.1, bf16[4,384,768]{2,1,0:T(8,128)(2,1)} %bitcast.15), custom_call_target="tpu_custom_call" | custom-call | tf_op jit(solution)/shard_map/pallas_call | solution.py:237
  69.9 26.7 %shard_map.115 = (bf16[3072,384]{1,0:T(8,128)(2,1)}, bf16[3072,384]{1,0:T(8,128)(2,1)}) custom-call(s32[48]{0:T(128)} %reshape.47.refs_0_, bf16[3072,384]{1,0:T(8,128)(2,1)} %bitcast.13, bf16[3072,384]{1,0:T(8,128)(2,1)} %get-tuple-element.7.refs_2_, bf16[768,768]{1,0:T(8,128)(2,1)} %bitcast.20, bf16[384,1536]{1,0:T(8,128)(2,1)} %refs_4_.3, ...), custom_call_target="tpu_custom_call" | custom-call | tf_op jit(solution)/shard_map/pallas_call | solution.py:237
  96.6 0.9 fusion.1
  97.5 2.0 %collective-permute-start.4 = (bf16[3,32,384]{2,1,0:T(8,128)(2,1)S(1)}, bf16[3,32,384]{2,1,0:T(8,128)(2,1)S(1)}, u32[]{:S(2)}, u32[]{:S(2)}) collective-permute-start(bf16[3,32,384]{2,1,0:T(8,128)(2,1)S(1)} %bitcast.22), channel_id=1, source_target_pairs={{0,16},{16,32},{32,48},{48,64},{64,80},{80,96},{96,112},{1,17},{17... | collective-permute-start | bytes 221192 | tf_op jit(solution)/shard_map/ppermute | solution.py:22
  99.6 3.5 %collective-permute-start.5 = (bf16[3,32,384]{2,1,0:T(8,128)(2,1)S(1)}, bf16[3,32,384]{2,1,0:T(8,128)(2,1)S(1)}, u32[]{:S(2)}, u32[]{:S(2)}) collective-permute-start(bf16[3,32,384]{2,1,0:T(8,128)(2,1)S(1)} %bitcast.21), channel_id=1, source_target_pairs={{16,0},{32,16},{48,32},{64,48},{80,64},{96,80},{112,96},{17,1},{33... | collective-permute-start | bytes 221192 | tf_op jit(solution)/shard_map/ppermute | solution.py:23
  103.1 1.5 %fusion = (bf16[96,3,384]{2,1,0:T(4,128)(2,1)S(1)}, bf16[96,3,384]{2,1,0:T(4,128)(2,1)S(1)}) fusion(bf16[96,32,384]{2,1,0:T(8,128)(2,1)} %bitcast.17), kind=kLoop, calls=%fused_computation.11 | loop fusion | bytes 884736 | tf_op jit(solution)/shard_map/slice | solution.py:26
  104.6 0.0 collective-permute-done.4.refs_1_
  104.6 0.0 copy-start.4
  104.7 0.4 collective-permute-done.5.refs_2_
  105.1 0.0 copy-start.5
  105.1 0.2 pad_maximum_fusion.2
  105.3 3.7 %collective-permute-start.6 = (bf16[102,3,384]{2,1,0:T(4,128)(2,1)S(1)}, bf16[102,3,384]{2,1,0:T(4,128)(2,1)S(1)}, u32[]{:S(2)}, u32[]{:S(2)}) collective-permute-start(bf16[102,3,384]{2,1,0:T(4,128)(2,1)S(1)} %pad_maximum_fusion.2), channel_id=1, source_target_pairs={{0,1},{1,2},{2,3},{3,4},{4,5},{5,6},{6,7},{7,8},{8,9},{9,10},{10,1... | collective-permute-start | bytes 705032 | tf_op jit(solution)/shard_map/ppermute | solution.py:27
  109.1 0.2 pad_maximum_fusion.3
  109.3 4.6 %collective-permute-start.7 = (bf16[102,3,384]{2,1,0:T(4,128)(2,1)S(1)}, bf16[102,3,384]{2,1,0:T(4,128)(2,1)S(1)}, u32[]{:S(2)}, u32[]{:S(2)}) collective-permute-start(bf16[102,3,384]{2,1,0:T(4,128)(2,1)S(1)} %pad_maximum_fusion.3), channel_id=1, source_target_pairs={{1,0},{2,1},{3,2},{4,3},{5,4},{6,5},{7,6},{8,7},{9,8},{10,9},{11,1... | collective-permute-start | bytes 705032 | tf_op jit(solution)/shard_map/ppermute | solution.py:28
  113.9 4.9 %collective-permute-done.6.refs_3_ = bf16[102,3,384]{2,1,0:T(4,128)(2,1)S(1)} collective-permute-done((bf16[102,3,384]{2,1,0:T(4,128)(2,1)S(1)}, bf16[102,3,384]{2,1,0:T(4,128)(2,1)S(1)}, u32[]{:S(2)}, u32[]{:S(2)}) %collective-permute-start.6) | collective-permute-done | bytes 235040 | tf_op jit(solution)/shard_map/ppermute | solution.py:27
  118.9 0.0 copy-start
  118.9 2.2 %collective-permute-done.7.refs_4_ = bf16[102,3,384]{2,1,0:T(4,128)(2,1)S(1)} collective-permute-done((bf16[102,3,384]{2,1,0:T(4,128)(2,1)S(1)}, bf16[102,3,384]{2,1,0:T(4,128)(2,1)S(1)}, u32[]{:S(2)}, u32[]{:S(2)}) %collective-permute-start.7) | collective-permute-done | bytes 235040 | tf_op jit(solution)/shard_map/ppermute | solution.py:28
  121.1 0.0 copy-start.1
  121.1 0.0 copy-done.4
  121.1 0.0 copy-done.5
  121.1 0.0 copy-done
  121.1 0.7 copy-done.1
  121.9 20.8 %shard_map.116 = bf16[96,32,384]{2,1,0:T(8,128)(2,1)} custom-call(bf16[96,32,384]{2,1,0:T(8,128)(2,1)} %bitcast.18, bf16[3,32,384]{2,1,0:T(8,128)(2,1)} %copy-done.4, bf16[3,32,384]{2,1,0:T(8,128)(2,1)} %copy-done.5, bf16[102,3,384]{2,1,0:T(4,128)(2,1)} %copy-done, bf16[102,3,384]{2,1,0:T(4,128)(2,1)} %copy-done.1, f32[49,384]{1,0:T(8,128)} %reshape.48.refs_5_, ...), custom_call_target="tpu_custom_call" | custom-call | tf_op jit(solution)/shard_map/pallas_call | solution.py:90
  (6 shorter events, 0.1 us)
Async XLA Ops:
  0.6 18.5 %copy-start.9 = (s32[12,4]{0,1:T(4,128)S(1)}, s32[12,4]{0,1:T(4,128)}, u32[]{:S(2)}) copy-start(s32[12,4]{0,1:T(4,128)} %param.17) | copy-start | bytes 580
  0.6 18.5 %copy-start.11 = (s32[12,4]{0,1:T(4,128)S(1)}, s32[12,4]{0,1:T(4,128)}, u32[]{:S(2)}) copy-start(s32[12,4]{0,1:T(4,128)} %param.18) | copy-start | bytes 580
  0.7 18.5 %copy-start.10 = (s32[12,4]{0,1:T(4,128)S(1)}, s32[12,4]{0,1:T(4,128)}, u32[]{:S(2)}) copy-start(s32[12,4]{0,1:T(4,128)} %param.15) | copy-start | bytes 580
  0.7 19.2 %copy-start.8 = (bf16[7,7,384]{2,1,0:T(8,128)(2,1)S(1)}, bf16[7,7,384]{2,1,0:T(8,128)(2,1)}, u32[]{:S(2)}) copy-start(bf16[7,7,384]{2,1,0:T(8,128)(2,1)} %param.11) | copy-start | bytes 112900
  1.6 8.1 %collective-permute-start.1 = (bf16[3,32,384]{2,1,0:T(8,128)(2,1)S(1)}, bf16[3,32,384]{2,1,0:T(8,128)(2,1)S(1)}, u32[]{:S(2)}, u32[]{:S(2)}) collective-permute-start(bf16[3,32,384]{2,1,0:T(8,128)(2,1)S(1)} %get-tuple-element.20), channel_id=1, source_target_pairs={{16,0},{32,16},{48,32},{64,48},{80,64},{96,80},{112,96},{17,1},{33... | collective-permute-start | bytes 221192 | tf_op jit(solution)/shard_map/ppermute | solution.py:23
  3.6 6.2 %collective-permute-start = (bf16[3,32,384]{2,1,0:T(8,128)(2,1)S(1)}, bf16[3,32,384]{2,1,0:T(8,128)(2,1)S(1)}, u32[]{:S(2)}, u32[]{:S(2)}) collective-permute-start(bf16[3,32,384]{2,1,0:T(8,128)(2,1)S(1)} %get-tuple-element.21), channel_id=1, source_target_pairs={{0,16},{16,32},{32,48},{48,64},{64,80},{80,96},{96,112},{1,17},{17... | collective-permute-start | bytes 221192 | tf_op jit(solution)/shard_map/ppermute | solution.py:22
  9.8 16.5 %copy-start.6 = (bf16[3,32,384]{2,1,0:T(8,128)(2,1)}, bf16[3,32,384]{2,1,0:T(8,128)(2,1)S(1)}, u32[]{:S(2)}) copy-start(bf16[3,32,384]{2,1,0:T(8,128)(2,1)S(1)} %collective-permute-done.1.refs_2_) | copy-start | bytes 221188
  9.8 16.5 %copy-start.7 = (bf16[3,32,384]{2,1,0:T(8,128)(2,1)}, bf16[3,32,384]{2,1,0:T(8,128)(2,1)S(1)}, u32[]{:S(2)}) copy-start(bf16[3,32,384]{2,1,0:T(8,128)(2,1)S(1)} %collective-permute-done.refs_1_) | copy-start | bytes 221188
  10.1 14.0 %collective-permute-start.2 = (bf16[102,3,384]{2,1,0:T(4,128)(2,1)S(1)}, bf16[102,3,384]{2,1,0:T(4,128)(2,1)S(1)}, u32[]{:S(2)}, u32[]{:S(2)}) collective-permute-start(bf16[102,3,384]{2,1,0:T(4,128)(2,1)S(1)} %pad_maximum_fusion), channel_id=1, source_target_pairs={{0,1},{1,2},{2,3},{3,4},{4,5},{5,6},{6,7},{7,8},{8,9},{9,10},{10,1... | collective-permute-start | bytes 705032 | tf_op jit(solution)/shard_map/ppermute | solution.py:27
  14.2 12.1 %collective-permute-start.3 = (bf16[102,3,384]{2,1,0:T(4,128)(2,1)S(1)}, bf16[102,3,384]{2,1,0:T(4,128)(2,1)S(1)}, u32[]{:S(2)}, u32[]{:S(2)}) collective-permute-start(bf16[102,3,384]{2,1,0:T(4,128)(2,1)S(1)} %pad_maximum_fusion.1), channel_id=1, source_target_pairs={{1,0},{2,1},{3,2},{4,3},{5,4},{6,5},{7,6},{8,7},{9,8},{10,9},{11,1... | collective-permute-start | bytes 705032 | tf_op jit(solution)/shard_map/ppermute | solution.py:28
  24.0 2.3 %copy-start.2 = (bf16[102,3,384]{2,1,0:T(4,128)(2,1)}, bf16[102,3,384]{2,1,0:T(4,128)(2,1)S(1)}, u32[]{:S(2)}) copy-start(bf16[102,3,384]{2,1,0:T(4,128)(2,1)S(1)} %collective-permute-done.2.refs_3_) | copy-start | bytes 705028
  26.3 0.7 copy-start.3
  97.5 7.1 %collective-permute-start.4 = (bf16[3,32,384]{2,1,0:T(8,128)(2,1)S(1)}, bf16[3,32,384]{2,1,0:T(8,128)(2,1)S(1)}, u32[]{:S(2)}, u32[]{:S(2)}) collective-permute-start(bf16[3,32,384]{2,1,0:T(8,128)(2,1)S(1)} %bitcast.22), channel_id=1, source_target_pairs={{0,16},{16,32},{32,48},{48,64},{64,80},{80,96},{96,112},{1,17},{17... | collective-permute-start | bytes 221192 | tf_op jit(solution)/shard_map/ppermute | solution.py:22
  99.6 5.5 %collective-permute-start.5 = (bf16[3,32,384]{2,1,0:T(8,128)(2,1)S(1)}, bf16[3,32,384]{2,1,0:T(8,128)(2,1)S(1)}, u32[]{:S(2)}, u32[]{:S(2)}) collective-permute-start(bf16[3,32,384]{2,1,0:T(8,128)(2,1)S(1)} %bitcast.21), channel_id=1, source_target_pairs={{16,0},{32,16},{48,32},{64,48},{80,64},{96,80},{112,96},{17,1},{33... | collective-permute-start | bytes 221192 | tf_op jit(solution)/shard_map/ppermute | solution.py:23
  104.6 16.5 %copy-start.4 = (bf16[3,32,384]{2,1,0:T(8,128)(2,1)}, bf16[3,32,384]{2,1,0:T(8,128)(2,1)S(1)}, u32[]{:S(2)}) copy-start(bf16[3,32,384]{2,1,0:T(8,128)(2,1)S(1)} %collective-permute-done.4.refs_1_) | copy-start | bytes 221188
  105.1 16.0 %copy-start.5 = (bf16[3,32,384]{2,1,0:T(8,128)(2,1)}, bf16[3,32,384]{2,1,0:T(8,128)(2,1)S(1)}, u32[]{:S(2)}) copy-start(bf16[3,32,384]{2,1,0:T(8,128)(2,1)S(1)} %collective-permute-done.5.refs_2_) | copy-start | bytes 221188
  105.3 13.5 %collective-permute-start.6 = (bf16[102,3,384]{2,1,0:T(4,128)(2,1)S(1)}, bf16[102,3,384]{2,1,0:T(4,128)(2,1)S(1)}, u32[]{:S(2)}, u32[]{:S(2)}) collective-permute-start(bf16[102,3,384]{2,1,0:T(4,128)(2,1)S(1)} %pad_maximum_fusion.2), channel_id=1, source_target_pairs={{0,1},{1,2},{2,3},{3,4},{4,5},{5,6},{6,7},{7,8},{8,9},{9,10},{10,1... | collective-permute-start | bytes 705032 | tf_op jit(solution)/shard_map/ppermute | solution.py:27
  109.3 11.8 %collective-permute-start.7 = (bf16[102,3,384]{2,1,0:T(4,128)(2,1)S(1)}, bf16[102,3,384]{2,1,0:T(4,128)(2,1)S(1)}, u32[]{:S(2)}, u32[]{:S(2)}) collective-permute-start(bf16[102,3,384]{2,1,0:T(4,128)(2,1)S(1)} %pad_maximum_fusion.3), channel_id=1, source_target_pairs={{1,0},{2,1},{3,2},{4,3},{5,4},{6,5},{7,6},{8,7},{9,8},{10,9},{11,1... | collective-permute-start | bytes 705032 | tf_op jit(solution)/shard_map/ppermute | solution.py:28
  118.9 2.3 %copy-start = (bf16[102,3,384]{2,1,0:T(4,128)(2,1)}, bf16[102,3,384]{2,1,0:T(4,128)(2,1)S(1)}, u32[]{:S(2)}) copy-start(bf16[102,3,384]{2,1,0:T(4,128)(2,1)S(1)} %collective-permute-done.6.refs_3_) | copy-start | bytes 705028
  121.1 0.7 copy-start.1

commit v16 on v15

--- a/solution.py
+++ b/solution.py
@@ -45,7 +45,8 @@
     framed_ref[:, :reach, :] = left_ref[...].astype(jnp.float32)
     framed_ref[:, reach + breadth :, :] = right_ref[...].astype(jnp.float32)
     for shift_c in range(side):
-        shifted_ref[...] = framed_ref[:, shift_c : shift_c + breadth, :]
+        if shift_c > 0:
+            shifted_ref[...] = framed_ref[:, shift_c : shift_c + breadth, :]
 
         def body(step, carry, shift_c=shift_c):
             start = pl.multiple_of(step * chunk, chunk)
@@ -61,7 +62,11 @@
                 else:
                     index = shift_r * side + shift_c
                 tap = k_ref[pl.ds(index, 1), :]
-                total = total + shifted_ref[pl.ds(start + shift_r, chunk)] * tap[None]
+                if shift_c > 0:
+                    window = shifted_ref[pl.ds(start + shift_r, chunk)]
+                else:
+                    window = framed_ref[pl.ds(start + shift_r, chunk), pl.ds(0, breadth), :]
+                total = total + window * tap[None]
             if shift_c == side - 1:
                 out_ref[pl.ds(start, chunk)] = total.astype(out_ref.dtype)
             else:

time: 144 us -> 144 us (level)
  no operation moved by 1% of the time
where the time goes in v16:
time: 144 us; the launch traced here: 142 us
  Pallas kernels  89.6 us (62%)
  starting transfers between devices  26.3 us (18%)
  waiting for transfers between devices  13.4 us (9%)
  local copies, waits for them, and re-layouts  8.76 us (6%)
  other arithmetic  2.99 us (2%)
    pallas_call x2, Pallas kernels, pixel_call(): pl.pallas_call(lambda *refs: kernel(*refs, layout=layout), grid_spec=pltp...  49.4 us
    pallas_call x2, Pallas kernels, depthwise(): pl.pallas_call(lambda *refs: depthwise_kernel(*refs, reach=reach, chunk=c...  40.2 us
    ppermute x2, starting transfers between devices, halo_pieces(): lax.ppermute(right_strip, 'col', [(i + 1, i) for i in range(cols - 1)])  8.82 us
    ppermute x2, waiting for transfers between devices, halo_pieces(): lax.ppermute(left_strip, 'col', [(i, i + 1) for i in range(cols - 1)])  8.43 us
    ppermute x2, starting transfers between devices, halo_pieces(): lax.ppermute(left_strip, 'col', [(i, i + 1) for i in range(cols - 1)])  7.61 us
    ppermute x2, starting transfers between devices, halo_pieces(): bottom = lax.ppermute(cells[:width], 'row', up)  5.41 us
    ppermute x2, waiting for transfers between devices, halo_pieces(): lax.ppermute(right_strip, 'col', [(i + 1, i) for i in range(cols - 1)])  4.53 us
    ppermute x2, starting transfers between devices, halo_pieces(): top = lax.ppermute(cells[cells.shape[0] - width:], 'row', down)  4.48 us
  transfers between devices with their start and end apart: 8, of which 5 were waited for; matrix products, arithmetic and copies ran while one was open for 6% of the time, Pallas kernels for 0%

profile of v16, /device:TPU:26, one launch (start us, length us, event | category | flops | bytes accessed | tf_op | source)
XLA Modules:
  0.0 142.0 jit_solution(18096274526373809943)
XLA Ops:
  0.6 0.0 copy-start.9
  0.6 0.0 copy-start.11
  0.7 0.0 copy-start.10
  0.7 0.0 copy-start.8
  0.7 1.0 fusion.3
  1.6 1.9 %collective-permute-start.1 = (bf16[3,32,384]{2,1,0:T(8,128)(2,1)S(1)}, bf16[3,32,384]{2,1,0:T(8,128)(2,1)S(1)}, u32[]{:S(2)}, u32[]{:S(2)}) collective-permute-start(bf16[3,32,384]{2,1,0:T(8,128)(2,1)S(1)} %get-tuple-element.20), channel_id=1, source_target_pairs={{16,0},{32,16},{48,32},{64,48},{80,64},{96,80},{112,96},{17,1},{33... | collective-permute-start | bytes 221192 | tf_op jit(solution)/shard_map/ppermute | solution.py:23
  3.6 2.4 %collective-permute-start = (bf16[3,32,384]{2,1,0:T(8,128)(2,1)S(1)}, bf16[3,32,384]{2,1,0:T(8,128)(2,1)S(1)}, u32[]{:S(2)}, u32[]{:S(2)}) collective-permute-start(bf16[3,32,384]{2,1,0:T(8,128)(2,1)S(1)} %get-tuple-element.21), channel_id=1, source_target_pairs={{0,16},{16,32},{32,48},{48,64},{64,80},{80,96},{96,112},{1,17},{17... | collective-permute-start | bytes 221192 | tf_op jit(solution)/shard_map/ppermute | solution.py:22
  6.0 1.5 %fusion.2 = (bf16[96,3,384]{2,1,0:T(4,128)(2,1)S(1)}, bf16[96,3,384]{2,1,0:T(4,128)(2,1)S(1)}) fusion(bf16[96,32,384]{2,1,0:T(8,128)(2,1)} %refs_0_.1), kind=kLoop, calls=%fused_computation.13 | loop fusion | bytes 884736 | tf_op jit(solution)/shard_map/slice | solution.py:26
  7.5 0.8 copy.21
  8.3 0.7 reduce_window_sum.11
  9.0 0.8 select_reduce_fusion.3
  9.8 0.0 collective-permute-done.1.refs_2_
  9.8 0.0 copy-start.6
  9.8 0.0 collective-permute-done.refs_1_
  9.8 0.0 copy-start.7
  9.8 0.2 pad_maximum_fusion
  10.1 3.8 %collective-permute-start.2 = (bf16[102,3,384]{2,1,0:T(4,128)(2,1)S(1)}, bf16[102,3,384]{2,1,0:T(4,128)(2,1)S(1)}, u32[]{:S(2)}, u32[]{:S(2)}) collective-permute-start(bf16[102,3,384]{2,1,0:T(4,128)(2,1)S(1)} %pad_maximum_fusion), channel_id=1, source_target_pairs={{0,1},{1,2},{2,3},{3,4},{4,5},{5,6},{6,7},{7,8},{8,9},{9,10},{10,1... | collective-permute-start | bytes 705032 | tf_op jit(solution)/shard_map/ppermute | solution.py:27
  13.9 0.2 pad_maximum_fusion.1
  14.2 4.2 %collective-permute-start.3 = (bf16[102,3,384]{2,1,0:T(4,128)(2,1)S(1)}, bf16[102,3,384]{2,1,0:T(4,128)(2,1)S(1)}, u32[]{:S(2)}, u32[]{:S(2)}) collective-permute-start(bf16[102,3,384]{2,1,0:T(4,128)(2,1)S(1)} %pad_maximum_fusion.1), channel_id=1, source_target_pairs={{1,0},{2,1},{3,2},{4,3},{5,4},{6,5},{7,6},{8,7},{9,8},{10,9},{11,1... | collective-permute-start | bytes 705032 | tf_op jit(solution)/shard_map/ppermute | solution.py:28
  18.4 0.5 select_reduce_fusion.1
  18.9 0.1 copy.22
  19.0 0.1 copy.23
  19.1 0.0 copy-done.9
  19.1 0.0 copy-done.11
  19.1 0.0 copy-done.10
  19.1 0.1 copy.24
  19.2 0.7 reshape.47.refs_0_
  19.9 0.0 copy-done.8
  19.9 0.7 reshape.48.refs_5_
  20.6 3.5 %collective-permute-done.2.refs_3_ = bf16[102,3,384]{2,1,0:T(4,128)(2,1)S(1)} collective-permute-done((bf16[102,3,384]{2,1,0:T(4,128)(2,1)S(1)}, bf16[102,3,384]{2,1,0:T(4,128)(2,1)S(1)}, u32[]{:S(2)}, u32[]{:S(2)}) %collective-permute-start.2) | collective-permute-done | bytes 235040 | tf_op jit(solution)/shard_map/ppermute | solution.py:27
  24.0 0.0 copy-start.2
  24.0 2.2 %collective-permute-done.3.refs_4_ = bf16[102,3,384]{2,1,0:T(4,128)(2,1)S(1)} collective-permute-done((bf16[102,3,384]{2,1,0:T(4,128)(2,1)S(1)}, bf16[102,3,384]{2,1,0:T(4,128)(2,1)S(1)}, u32[]{:S(2)}, u32[]{:S(2)}) %collective-permute-start.3) | collective-permute-done | bytes 235040 | tf_op jit(solution)/shard_map/ppermute | solution.py:28
  26.3 0.0 copy-done.6
  26.3 0.0 copy-done.7
  26.3 0.0 copy-done.2
  26.3 0.0 copy-start.3
  26.3 0.7 copy-done.3
  27.0 19.8 %shard_map.113 = bf16[96,32,384]{2,1,0:T(8,128)(2,1)} custom-call(bf16[96,32,384]{2,1,0:T(8,128)(2,1)} %refs_0_.1, bf16[3,32,384]{2,1,0:T(8,128)(2,1)} %copy-done.7, bf16[3,32,384]{2,1,0:T(8,128)(2,1)} %copy-done.6, bf16[102,3,384]{2,1,0:T(4,128)(2,1)} %copy-done.2, bf16[102,3,384]{2,1,0:T(4,128)(2,1)} %copy-done.3, f32[49,384]{1,0:T(8,128)} %reshape.48.refs_5_), custom_call_target="tpu_custom_call" | custom-call | tf_op jit(solution)/shard_map/pallas_call | solution.py:95
  46.8 22.7 %shard_map.114 = (bf16[3072,384]{1,0:T(8,128)(2,1)}, bf16[768,768]{1,0:T(8,128)(2,1)}) custom-call(s32[48]{0:T(128)} %reshape.47.refs_0_, bf16[3072,384]{1,0:T(8,128)(2,1)} %bitcast.12, bf16[3072,384]{1,0:T(8,128)(2,1)} %bitcast.14, bf16[384,1536]{1,0:T(8,128)(2,1)} %refs_4_.3, bf16[1536,384]{1,0:T(8,128)(2,1)} %refs_5_.1, bf16[4,384,768]{2,1,0:T(8,128)(2,1)} %bitcast.15), custom_call_target="tpu_custom_call" | custom-call | tf_op jit(solution)/shard_map/pallas_call | solution.py:242
  69.5 26.6 %shard_map.115 = (bf16[3072,384]{1,0:T(8,128)(2,1)}, bf16[3072,384]{1,0:T(8,128)(2,1)}) custom-call(s32[48]{0:T(128)} %reshape.47.refs_0_, bf16[3072,384]{1,0:T(8,128)(2,1)} %bitcast.13, bf16[3072,384]{1,0:T(8,128)(2,1)} %get-tuple-element.7.refs_2_, bf16[768,768]{1,0:T(8,128)(2,1)} %bitcast.20, bf16[384,1536]{1,0:T(8,128)(2,1)} %refs_4_.3, ...), custom_call_target="tpu_custom_call" | custom-call | tf_op jit(solution)/shard_map/pallas_call | solution.py:242
  96.2 0.9 fusion.1
  97.1 2.1 %collective-permute-start.4 = (bf16[3,32,384]{2,1,0:T(8,128)(2,1)S(1)}, bf16[3,32,384]{2,1,0:T(8,128)(2,1)S(1)}, u32[]{:S(2)}, u32[]{:S(2)}) collective-permute-start(bf16[3,32,384]{2,1,0:T(8,128)(2,1)S(1)} %bitcast.22), channel_id=1, source_target_pairs={{0,16},{16,32},{32,48},{48,64},{64,80},{80,96},{96,112},{1,17},{17... | collective-permute-start | bytes 221192 | tf_op jit(solution)/shard_map/ppermute | solution.py:22
  99.2 3.5 %collective-permute-start.5 = (bf16[3,32,384]{2,1,0:T(8,128)(2,1)S(1)}, bf16[3,32,384]{2,1,0:T(8,128)(2,1)S(1)}, u32[]{:S(2)}, u32[]{:S(2)}) collective-permute-start(bf16[3,32,384]{2,1,0:T(8,128)(2,1)S(1)} %bitcast.21), channel_id=1, source_target_pairs={{16,0},{32,16},{48,32},{64,48},{80,64},{96,80},{112,96},{17,1},{33... | collective-permute-start | bytes 221192 | tf_op jit(solution)/shard_map/ppermute | solution.py:23
  102.7 1.5 %fusion = (bf16[96,3,384]{2,1,0:T(4,128)(2,1)S(1)}, bf16[96,3,384]{2,1,0:T(4,128)(2,1)S(1)}) fusion(bf16[96,32,384]{2,1,0:T(8,128)(2,1)} %bitcast.17), kind=kLoop, calls=%fused_computation.11 | loop fusion | bytes 884736 | tf_op jit(solution)/shard_map/slice | solution.py:26
  104.2 0.0 collective-permute-done.4.refs_1_
  104.2 0.0 copy-start.4
  104.2 0.4 collective-permute-done.5.refs_2_
  104.7 0.0 copy-start.5
  104.7 0.2 pad_maximum_fusion.2
  104.9 3.8 %collective-permute-start.6 = (bf16[102,3,384]{2,1,0:T(4,128)(2,1)S(1)}, bf16[102,3,384]{2,1,0:T(4,128)(2,1)S(1)}, u32[]{:S(2)}, u32[]{:S(2)}) collective-permute-start(bf16[102,3,384]{2,1,0:T(4,128)(2,1)S(1)} %pad_maximum_fusion.2), channel_id=1, source_target_pairs={{0,1},{1,2},{2,3},{3,4},{4,5},{5,6},{6,7},{7,8},{8,9},{9,10},{10,1... | collective-permute-start | bytes 705032 | tf_op jit(solution)/shard_map/ppermute | solution.py:27
  108.7 0.2 pad_maximum_fusion.3
  108.9 4.6 %collective-permute-start.7 = (bf16[102,3,384]{2,1,0:T(4,128)(2,1)S(1)}, bf16[102,3,384]{2,1,0:T(4,128)(2,1)S(1)}, u32[]{:S(2)}, u32[]{:S(2)}) collective-permute-start(bf16[102,3,384]{2,1,0:T(4,128)(2,1)S(1)} %pad_maximum_fusion.3), channel_id=1, source_target_pairs={{1,0},{2,1},{3,2},{4,3},{5,4},{6,5},{7,6},{8,7},{9,8},{10,9},{11,1... | collective-permute-start | bytes 705032 | tf_op jit(solution)/shard_map/ppermute | solution.py:28
  113.6 4.9 %collective-permute-done.6.refs_3_ = bf16[102,3,384]{2,1,0:T(4,128)(2,1)S(1)} collective-permute-done((bf16[102,3,384]{2,1,0:T(4,128)(2,1)S(1)}, bf16[102,3,384]{2,1,0:T(4,128)(2,1)S(1)}, u32[]{:S(2)}, u32[]{:S(2)}) %collective-permute-start.6) | collective-permute-done | bytes 235040 | tf_op jit(solution)/shard_map/ppermute | solution.py:27
  118.5 0.0 copy-start
  118.5 2.3 %collective-permute-done.7.refs_4_ = bf16[102,3,384]{2,1,0:T(4,128)(2,1)S(1)} collective-permute-done((bf16[102,3,384]{2,1,0:T(4,128)(2,1)S(1)}, bf16[102,3,384]{2,1,0:T(4,128)(2,1)S(1)}, u32[]{:S(2)}, u32[]{:S(2)}) %collective-permute-start.7) | collective-permute-done | bytes 235040 | tf_op jit(solution)/shard_map/ppermute | solution.py:28
  120.8 0.0 copy-start.1
  120.8 0.0 copy-done.4
  120.8 0.0 copy-done.5
  120.8 0.0 copy-done
  120.8 0.7 copy-done.1
  121.5 20.4 %shard_map.116 = bf16[96,32,384]{2,1,0:T(8,128)(2,1)} custom-call(bf16[96,32,384]{2,1,0:T(8,128)(2,1)} %bitcast.18, bf16[3,32,384]{2,1,0:T(8,128)(2,1)} %copy-done.4, bf16[3,32,384]{2,1,0:T(8,128)(2,1)} %copy-done.5, bf16[102,3,384]{2,1,0:T(4,128)(2,1)} %copy-done, bf16[102,3,384]{2,1,0:T(4,128)(2,1)} %copy-done.1, f32[49,384]{1,0:T(8,128)} %reshape.48.refs_5_, ...), custom_call_target="tpu_custom_call" | custom-call | tf_op jit(solution)/shard_map/pallas_call | solution.py:95
  (6 shorter events, 0.1 us)
Async XLA Ops:
  0.6 18.5 %copy-start.9 = (s32[12,4]{0,1:T(4,128)S(1)}, s32[12,4]{0,1:T(4,128)}, u32[]{:S(2)}) copy-start(s32[12,4]{0,1:T(4,128)} %param.17) | copy-start | bytes 580
  0.6 18.5 %copy-start.11 = (s32[12,4]{0,1:T(4,128)S(1)}, s32[12,4]{0,1:T(4,128)}, u32[]{:S(2)}) copy-start(s32[12,4]{0,1:T(4,128)} %param.18) | copy-start | bytes 580
  0.7 18.5 %copy-start.10 = (s32[12,4]{0,1:T(4,128)S(1)}, s32[12,4]{0,1:T(4,128)}, u32[]{:S(2)}) copy-start(s32[12,4]{0,1:T(4,128)} %param.15) | copy-start | bytes 580
  0.7 19.2 %copy-start.8 = (bf16[7,7,384]{2,1,0:T(8,128)(2,1)S(1)}, bf16[7,7,384]{2,1,0:T(8,128)(2,1)}, u32[]{:S(2)}) copy-start(bf16[7,7,384]{2,1,0:T(8,128)(2,1)} %param.11) | copy-start | bytes 112900
  1.6 8.1 %collective-permute-start.1 = (bf16[3,32,384]{2,1,0:T(8,128)(2,1)S(1)}, bf16[3,32,384]{2,1,0:T(8,128)(2,1)S(1)}, u32[]{:S(2)}, u32[]{:S(2)}) collective-permute-start(bf16[3,32,384]{2,1,0:T(8,128)(2,1)S(1)} %get-tuple-element.20), channel_id=1, source_target_pairs={{16,0},{32,16},{48,32},{64,48},{80,64},{96,80},{112,96},{17,1},{33... | collective-permute-start | bytes 221192 | tf_op jit(solution)/shard_map/ppermute | solution.py:23
  3.6 6.2 %collective-permute-start = (bf16[3,32,384]{2,1,0:T(8,128)(2,1)S(1)}, bf16[3,32,384]{2,1,0:T(8,128)(2,1)S(1)}, u32[]{:S(2)}, u32[]{:S(2)}) collective-permute-start(bf16[3,32,384]{2,1,0:T(8,128)(2,1)S(1)} %get-tuple-element.21), channel_id=1, source_target_pairs={{0,16},{16,32},{32,48},{48,64},{64,80},{80,96},{96,112},{1,17},{17... | collective-permute-start | bytes 221192 | tf_op jit(solution)/shard_map/ppermute | solution.py:22
  9.8 16.5 %copy-start.6 = (bf16[3,32,384]{2,1,0:T(8,128)(2,1)}, bf16[3,32,384]{2,1,0:T(8,128)(2,1)S(1)}, u32[]{:S(2)}) copy-start(bf16[3,32,384]{2,1,0:T(8,128)(2,1)S(1)} %collective-permute-done.1.refs_2_) | copy-start | bytes 221188
  9.8 16.5 %copy-start.7 = (bf16[3,32,384]{2,1,0:T(8,128)(2,1)}, bf16[3,32,384]{2,1,0:T(8,128)(2,1)S(1)}, u32[]{:S(2)}) copy-start(bf16[3,32,384]{2,1,0:T(8,128)(2,1)S(1)} %collective-permute-done.refs_1_) | copy-start | bytes 221188
  10.1 14.0 %collective-permute-start.2 = (bf16[102,3,384]{2,1,0:T(4,128)(2,1)S(1)}, bf16[102,3,384]{2,1,0:T(4,128)(2,1)S(1)}, u32[]{:S(2)}, u32[]{:S(2)}) collective-permute-start(bf16[102,3,384]{2,1,0:T(4,128)(2,1)S(1)} %pad_maximum_fusion), channel_id=1, source_target_pairs={{0,1},{1,2},{2,3},{3,4},{4,5},{5,6},{6,7},{7,8},{8,9},{9,10},{10,1... | collective-permute-start | bytes 705032 | tf_op jit(solution)/shard_map/ppermute | solution.py:27
  14.2 12.1 %collective-permute-start.3 = (bf16[102,3,384]{2,1,0:T(4,128)(2,1)S(1)}, bf16[102,3,384]{2,1,0:T(4,128)(2,1)S(1)}, u32[]{:S(2)}, u32[]{:S(2)}) collective-permute-start(bf16[102,3,384]{2,1,0:T(4,128)(2,1)S(1)} %pad_maximum_fusion.1), channel_id=1, source_target_pairs={{1,0},{2,1},{3,2},{4,3},{5,4},{6,5},{7,6},{8,7},{9,8},{10,9},{11,1... | collective-permute-start | bytes 705032 | tf_op jit(solution)/shard_map/ppermute | solution.py:28
  24.0 2.3 %copy-start.2 = (bf16[102,3,384]{2,1,0:T(4,128)(2,1)}, bf16[102,3,384]{2,1,0:T(4,128)(2,1)S(1)}, u32[]{:S(2)}) copy-start(bf16[102,3,384]{2,1,0:T(4,128)(2,1)S(1)} %collective-permute-done.2.refs_3_) | copy-start | bytes 705028
  26.3 0.7 copy-start.3
  97.1 7.1 %collective-permute-start.4 = (bf16[3,32,384]{2,1,0:T(8,128)(2,1)S(1)}, bf16[3,32,384]{2,1,0:T(8,128)(2,1)S(1)}, u32[]{:S(2)}, u32[]{:S(2)}) collective-permute-start(bf16[3,32,384]{2,1,0:T(8,128)(2,1)S(1)} %bitcast.22), channel_id=1, source_target_pairs={{0,16},{16,32},{32,48},{48,64},{64,80},{80,96},{96,112},{1,17},{17... | collective-permute-start | bytes 221192 | tf_op jit(solution)/shard_map/ppermute | solution.py:22
  99.2 5.5 %collective-permute-start.5 = (bf16[3,32,384]{2,1,0:T(8,128)(2,1)S(1)}, bf16[3,32,384]{2,1,0:T(8,128)(2,1)S(1)}, u32[]{:S(2)}, u32[]{:S(2)}) collective-permute-start(bf16[3,32,384]{2,1,0:T(8,128)(2,1)S(1)} %bitcast.21), channel_id=1, source_target_pairs={{16,0},{32,16},{48,32},{64,48},{80,64},{96,80},{112,96},{17,1},{33... | collective-permute-start | bytes 221192 | tf_op jit(solution)/shard_map/ppermute | solution.py:23
  104.2 16.6 %copy-start.4 = (bf16[3,32,384]{2,1,0:T(8,128)(2,1)}, bf16[3,32,384]{2,1,0:T(8,128)(2,1)S(1)}, u32[]{:S(2)}) copy-start(bf16[3,32,384]{2,1,0:T(8,128)(2,1)S(1)} %collective-permute-done.4.refs_1_) | copy-start | bytes 221188
  104.7 16.1 %copy-start.5 = (bf16[3,32,384]{2,1,0:T(8,128)(2,1)}, bf16[3,32,384]{2,1,0:T(8,128)(2,1)S(1)}, u32[]{:S(2)}) copy-start(bf16[3,32,384]{2,1,0:T(8,128)(2,1)S(1)} %collective-permute-done.5.refs_2_) | copy-start | bytes 221188
  104.9 13.6 %collective-permute-start.6 = (bf16[102,3,384]{2,1,0:T(4,128)(2,1)S(1)}, bf16[102,3,384]{2,1,0:T(4,128)(2,1)S(1)}, u32[]{:S(2)}, u32[]{:S(2)}) collective-permute-start(bf16[102,3,384]{2,1,0:T(4,128)(2,1)S(1)} %pad_maximum_fusion.2), channel_id=1, source_target_pairs={{0,1},{1,2},{2,3},{3,4},{4,5},{5,6},{6,7},{7,8},{8,9},{9,10},{10,1... | collective-permute-start | bytes 705032 | tf_op jit(solution)/shard_map/ppermute | solution.py:27
  108.9 11.8 %collective-permute-start.7 = (bf16[102,3,384]{2,1,0:T(4,128)(2,1)S(1)}, bf16[102,3,384]{2,1,0:T(4,128)(2,1)S(1)}, u32[]{:S(2)}, u32[]{:S(2)}) collective-permute-start(bf16[102,3,384]{2,1,0:T(4,128)(2,1)S(1)} %pad_maximum_fusion.3), channel_id=1, source_target_pairs={{1,0},{2,1},{3,2},{4,3},{5,4},{6,5},{7,6},{8,7},{9,8},{10,9},{11,1... | collective-permute-start | bytes 705032 | tf_op jit(solution)/shard_map/ppermute | solution.py:28
  118.5 2.3 %copy-start = (bf16[102,3,384]{2,1,0:T(4,128)(2,1)}, bf16[102,3,384]{2,1,0:T(4,128)(2,1)S(1)}, u32[]{:S(2)}) copy-start(bf16[102,3,384]{2,1,0:T(4,128)(2,1)S(1)} %collective-permute-done.6.refs_3_) | copy-start | bytes 705028
  120.8 0.7 copy-start.1
